TPU v7x, 128 devices: a whole 4x4x4 slice. The times are simulated.
128 devices in a mesh: seq: 32 (over y, x, core), head: 4 (over z).
Axes of the slice: x: 4, y: 4, z: 4, core: 2. Of those that a mesh axis runs over, the one named last changes fastest.
Arguments:
- queries: bfloat16 [8192, 4096], P(('seq', 'head')), may hold values from -8 to 8
- keys: bfloat16 [8192, 1024], P(('seq', 'head')), may hold values from -8 to 8
- values: bfloat16 [8192, 1024], P(('seq', 'head')), may hold values from -6 to 6
- slash: int32 [8, 4], replicated, may hold values from 0 to 3, all different within a row
- vertical: int32 [8, 32], replicated, may hold values from 0 to 127, as said below
Outputs:
- attended: bfloat16 [8192, 4096], P('seq', 'head')
Inputs may be any that keep to these rules, and one draw needn't show every extreme that they name: `slash`: each row holds 4 different values. `vertical`: each row names 32 different blocks; at most 2 of them lie in one range of 4 blocks k * 4 to (k + 1) * 4 - 1, and every row has exactly 2 in some such range.
All inputs are finite; a program needn't handle non-finite values.
Results may differ from a plain program's by a relative error of at most 0.0045.
Values may be sent and summed in bfloat16 or wider, within the bound.
No kernel may reach another device: no remote copies, remote signals or barrier semaphores. Data moves between devices by JAX's collectives and lax.ppermute only.
A program may use at most 128 MiB of HBM per device.

v0:
```python
import jax
import jax.numpy as jnp
from jax import lax
from jax.sharding import PartitionSpec as P

HEAD_WIDTH = 128
BLOCK_TOKENS = 64
EXTRA_DIAGONALS = 4


def shifted(value, axis, by):
    size = lax.axis_size(axis)
    pairs = [(i, i + by) for i in range(size) if 0 <= i + by < size]
    return lax.ppermute(value, axis, pairs)


def attend_head(
    query_rows,
    slash_keys_picked,
    slash_values_picked,
    mask_s,
    vertical_key_rows,
    vertical_value_rows,
    vert_ok,
    softmax_scale,
):
    slash_score = (
        jnp.einsum(
            "gxh,gvih->gxvi", query_rows, slash_keys_picked, preferred_element_type=jnp.float32
        )
        * softmax_scale
    )
    slash_score = jnp.where(mask_s, slash_score, -jnp.inf)
    vertical_score = (
        jnp.einsum(
            "ulo,ezo->ulez", query_rows, vertical_key_rows, preferred_element_type=jnp.float32
        )
        * softmax_scale
    )
    vertical_score = jnp.where(vert_ok[:, None, :, None], vertical_score, -jnp.inf)
    top = jnp.maximum(jnp.max(slash_score, axis=(2, 3)), jnp.max(vertical_score, axis=(2, 3)))
    slash_weight = jnp.exp(slash_score - top[:, :, None, None])
    vertical_weight = jnp.exp(vertical_score - top[:, :, None, None])
    total = jnp.sum(slash_weight, axis=(2, 3)) + jnp.sum(vertical_weight, axis=(2, 3))
    summed_scores = jnp.einsum(
        "zirc,zrcp->zip",
        slash_weight.astype(jnp.bfloat16),
        slash_values_picked,
        preferred_element_type=jnp.float32,
    )
    summed_scores = summed_scores + jnp.einsum(
        "wenc,ncp->wep",
        vertical_weight.astype(jnp.bfloat16),
        vertical_value_rows,
        preferred_element_type=jnp.float32,
    )
    result = (summed_scores / total[:, :, None]).astype(jnp.bfloat16)
    return result.reshape(-1, result.shape[2])


def local(queries, keys, values, slash, vertical):
    softmax_scale = HEAD_WIDTH ** (-0.5)
    seq_index = lax.axis_index("seq")
    head_index = lax.axis_index("head")
    q_all, k_all, v_all = (
        lax.all_to_all(queries, "head", split_axis=1, concat_axis=0, tiled=True),
        lax.all_to_all(keys, "head", split_axis=1, concat_axis=0, tiled=True),
        lax.all_to_all(values, "head", split_axis=1, concat_axis=0, tiled=True),
    )
    rows = q_all.shape[0]
    nbd = rows // BLOCK_TOKENS
    kv_local = k_all.shape[1] // HEAD_WIDTH
    query_group = q_all.shape[1] // HEAD_WIDTH // kv_local
    width = EXTRA_DIAGONALS + 1
    prev_k, prev_v = shifted((k_all, v_all), "seq", 1)
    window_k = jnp.concatenate([prev_k, k_all], 0).reshape(
        2 * nbd, BLOCK_TOKENS, kv_local, HEAD_WIDTH
    )
    window_v = jnp.concatenate([prev_v, v_all], 0).reshape(
        2 * nbd, BLOCK_TOKENS, kv_local, HEAD_WIDTH
    )
    own_k = k_all.reshape(nbd, BLOCK_TOKENS, kv_local, HEAD_WIDTH)
    own_v = v_all.reshape(nbd, BLOCK_TOKENS, kv_local, HEAD_WIDTH)
    first_head = head_index * kv_local
    local_slash = lax.dynamic_slice_in_dim(slash, first_head, kv_local, 0) + 1
    diagonal_offsets = jnp.concatenate([jnp.zeros((kv_local, 1), jnp.int32), local_slash], 1)
    local_vert = lax.dynamic_slice_in_dim(vertical, first_head, kv_local, 0)
    owner = local_vert // nbd
    inner = local_vert % nbd
    mine = owner == seq_index
    pieces = []
    for group_member in range(kv_local):
        picked = jnp.stack(
            [
                own_k[:, :, group_member][inner[group_member]],
                own_v[:, :, group_member][inner[group_member]],
            ],
            0,
        )
        pieces.append(
            jnp.where(mine[group_member][None, :, None, None], picked.astype(jnp.float32), 0.0)
        )
    fetched = lax.psum(jnp.stack(pieces, 0).astype(jnp.bfloat16), "seq")
    vert_keys = fetched[:, 0]
    vert_vals = fetched[:, 1]
    qblocks = seq_index * nbd + jnp.arange(nbd, dtype=jnp.int32)
    spots = jnp.arange(BLOCK_TOKENS)
    causal = spots[None, :] <= spots[:, None]
    beyond = jnp.arange(width) > 0
    outputs = []
    for group_member in range(kv_local):
        offset = diagonal_offsets[group_member]
        slab_k = window_k[:, :, group_member]
        slab_v = window_v[:, :, group_member]
        slash_keys_picked = jnp.stack(
            [lax.dynamic_slice_in_dim(slab_k, nbd - offset[j], nbd, 0) for j in range(width)], 1
        )
        slash_values_picked = jnp.stack(
            [lax.dynamic_slice_in_dim(slab_v, nbd - offset[j], nbd, 0) for j in range(width)], 1
        )
        slash_ok = qblocks[:, None] - offset[None, :] >= 0
        mask_s = slash_ok[:, None, :, None] & (
            beyond[None, None, :, None] | causal[None, :, None, :]
        )
        dist = qblocks[:, None] - local_vert[group_member][None, :]
        hit = jnp.any(dist[:, :, None] == offset[None, None, :], axis=2)
        vert_ok = (dist > 0) & jnp.logical_not(hit)
        for inside in range(query_group):
            head = group_member * query_group + inside
            query_rows = q_all[:, head * HEAD_WIDTH : (head + 1) * HEAD_WIDTH].reshape(
                nbd, BLOCK_TOKENS, HEAD_WIDTH
            )
            outputs.append(
                attend_head(
                    query_rows,
                    slash_keys_picked,
                    slash_values_picked,
                    mask_s,
                    vert_keys[group_member],
                    vert_vals[group_member],
                    vert_ok,
                    softmax_scale,
                )
            )
    return jnp.concatenate(outputs, 1)


def solution(mesh):
    return jax.shard_map(
        local,
        mesh=mesh,
        in_specs=(
            P(("seq", "head"), None),
            P(("seq", "head"), None),
            P(("seq", "head"), None),
            P(),
            P(),
        ),
        out_specs=P("seq", "head"),
        check_vma=False,
    )
```

profile of v0, /device:TPU:1, one launch (start us, length us, event | category | flops | bytes accessed | tf_op | source)
XLA Modules:
  0.0 204.7 jit_solution(9577444136500928972)
XLA Ops:
  6.5 1.5 copy.329
  8.1 5.8 %all-to-all-start.2 = ((bf16[64,4,256]{2,0,1:T(8,128)(2,1)}), bf16[64,4,256]{2,0,1:T(8,128)(2,1)S(1)}, u32[]{:S(2)}, u32[]{:S(2)}) async-start(bf16[64,4,256]{2,0,1:T(8,128)(2,1)} %bitcast.527), calls=%async_computation.2 | async-start | bytes 262144 | tf_op jit(solution)/shard_map/all_to_all | solution.py:68
  14.0 0.7 fusion.207
  14.7 0.8 fusion.206
  15.7 0.7 broadcast_or_fusion
  16.7 0.7 fusion.233
  27.3 1.6 copy.330
  28.9 1.9 copy.328
  31.0 4.2 %all-to-all-start = ((bf16[64,4,256]{2,0,1:T(8,128)(2,1)}), bf16[64,4,256]{2,0,1:T(8,128)(2,1)S(1)}, u32[]{:S(2)}, u32[]{:S(2)}) async-start(bf16[64,4,256]{2,0,1:T(8,128)(2,1)} %bitcast.528), calls=%async_computation | async-start | bytes 262144 | tf_op jit(solution)/shard_map/all_to_all | solution.py:67
  35.3 4.5 %collective-permute-start.1 = (bf16[256,256]{1,0:T(8,128)(2,1)S(1)}, bf16[256,256]{1,0:T(8,128)(2,1)S(1)}, u32[]{:S(2)}, u32[]{:S(2)}) collective-permute-start(bf16[256,256]{1,0:T(8,128)(2,1)S(1)} %bitcast.534), channel_id=1, source_target_pairs={{0,4},{4,8},{8,12},{12,16},{16,20},{20,24},{24,28},{28,32},{32,36}... | collective-permute-start | bytes 393224 | tf_op jit(solution)/shard_map/ppermute | solution.py:14
  40.1 4.2 %all-to-all-start.1 = ((bf16[64,4,1024]{2,0,1:T(8,128)(2,1)}), bf16[64,4,1024]{2,0,1:T(8,128)(2,1)S(1)}, u32[]{:S(2)}, u32[]{:S(2)}) async-start(bf16[64,4,1024]{2,0,1:T(8,128)(2,1)} %bitcast.526), calls=%async_computation.1 | async-start | bytes 1048576 | tf_op jit(solution)/shard_map/all_to_all | solution.py:66
  44.3 5.0 %collective-permute-start = (bf16[256,256]{1,0:T(8,128)(2,1)S(1)}, bf16[256,256]{1,0:T(8,128)(2,1)S(1)}, u32[]{:S(2)}, u32[]{:S(2)}) collective-permute-start(bf16[256,256]{1,0:T(8,128)(2,1)S(1)} %bitcast.537), channel_id=1, source_target_pairs={{0,4},{4,8},{8,12},{12,16},{16,20},{20,24},{24,28},{28,32},{32,36}... | collective-permute-start | bytes 393224 | tf_op jit(solution)/shard_map/ppermute | solution.py:14
  49.8 0.6 gather_fusion.3
  50.5 0.6 gather_fusion.2
  51.1 0.6 gather_fusion.1
  51.8 0.6 gather_fusion
  53.0 1.5 pad_maximum_fusion
  56.1 1.7 constant_dynamic-slice_fusion
  57.9 1.7 constant_dynamic-slice_fusion.4
  60.0 0.5 copy-done.17
  60.8 2.8 %fusion.234 = (f32[4,64]{1,0:T(4,128)}, f32[4,64,5,64]{1,3,2,0:T(8,128)}) fusion(bf16[4,5,64,128]{3,2,1,0:T(8,128)(2,1)} %copy-done.17, bf16[4,64,128,1]{2,1,3,0:T(8,128)(2,1)S(1)} %bitcast.551, pred[64,5,64]{0,2,1:T(8,128)(4,1)S(1)} %copy-done.13, pred[4,5]{1,0:T(4,128)(4,1)S(1)} %get-tuple-element.78), kind=kOutput, calls=%fused_computation.289 | convolution fusion | flops 21298944 | bytes 742420 | tf_op jit(solution)/shard_map/gxh,gvih->gxvi/dot_general | solution.py:28
  63.7 2.6 %fusion.235 = (f32[4,64]{1,0:T(4,128)}, f32[4,64,5,64]{1,3,2,0:T(8,128)}) fusion(bf16[4,5,64,128]{3,2,1,0:T(8,128)(2,1)} %copy-done.17, bf16[4,64,128,1]{2,1,3,0:T(8,128)(2,1)S(1)} %bitcast.549, pred[64,5,64]{0,2,1:T(8,128)(4,1)S(1)} %copy-done.13, pred[4,5]{1,0:T(4,128)(4,1)S(1)} %get-tuple-element.78), kind=kOutput, calls=%fused_computation.290 | convolution fusion | flops 21298944 | bytes 742420 | tf_op jit(solution)/shard_map/gxh,gvih->gxvi/dot_general | solution.py:28
  66.3 2.7 %fusion.236 = (f32[4,64]{1,0:T(4,128)}, f32[4,64,5,64]{1,3,2,0:T(8,128)}) fusion(bf16[4,5,64,128]{3,2,1,0:T(8,128)(2,1)} %copy-done.17, bf16[4,64,128,1]{2,1,3,0:T(8,128)(2,1)S(1)} %bitcast.557, pred[64,5,64]{0,2,1:T(8,128)(4,1)S(1)} %copy-done.13, pred[4,5]{1,0:T(4,128)(4,1)S(1)} %get-tuple-element.78), kind=kOutput, calls=%fused_computation.291 | convolution fusion | flops 21298944 | bytes 742420 | tf_op jit(solution)/shard_map/gxh,gvih->gxvi/dot_general | solution.py:28
  69.0 1.7 fusion.237
  70.7 0.9 fusion.238
  71.5 0.9 fusion.239
  72.7 0.9 fusion.241
  73.6 89.2 %all-reduce.3.cloned.1.call-done = bf16[2,2,32,64,128]{4,3,2,1,0:T(8,128)(2,1)} async-done(((bf16[2,2,32,64,128]{4,3,2,1,0:T(8,128)(2,1)}), bf16[2,2,32,64,128]{4,3,2,1,0:T(8,128)(2,1)}) %all-reduce.3.cloned.1.call-update) | async-done | bytes 2097168 | tf_op jit(solution)/shard_map/psum | solution.py:103
  162.8 1.9 fusion.179
  164.8 1.5 fusion.19
  166.7 0.7 fusion.177
  167.5 5.0 %fusion.6 = (f32[4,64]{1,0:T(4,128)S(1)}, f32[4,64]{1,0:T(4,128)S(1)}, f32[4,64]{1,0:T(4,128)S(1)}, f32[4,64]{1,0:T(4,128)S(1)}, f32[32,64,4,64]{3,1,2,0:T(8,128)}) fusion(f32[32,64,4,64]{3,1,2,0:T(8,128)S(1)} %get-tuple-element.83, f32[4,64]{1,0:T(4,128)S(1)} %max.59, pred[4,32]{0,1:T(8,128)(4,1)S(1)} %copy.194, f32[32,64,4,64]{3,1,2,0:T(8,128)S(1)} %fusion.177, ...), kind=kOutput, calls=%fused_computation.26 | convolution fusion | flops 141556736 | bytes 15282176 | tf_op jit(solution)/shard_map/ulo,ezo->ulez/dot_general | solution.py:35
  173.8 0.7 fusion.183
  174.6 1.4 fusion.23
  176.5 0.7 fusion.181
  177.2 3.5 %fusion.14 = (f32[4,64]{1,0:T(4,128)S(1)}, f32[4,64]{1,0:T(4,128)S(1)}, f32[4,64]{1,0:T(4,128)S(1)}, f32[4,64]{1,0:T(4,128)S(1)}, f32[32,64,4,64]{3,1,2,0:T(8,128)S(1)}) fusion(f32[32,64,4,64]{3,1,2,0:T(8,128)S(1)} %get-tuple-element.93, f32[4,64]{1,0:T(4,128)S(1)} %max.63, pred[4,32]{0,1:T(8,128)(4,1)S(1)} %copy.216, f32[32,64,4,64]{3,1,2,0:T(8,128)S(1)} %fusion.181, ...), kind=kOutput, calls=%fused_computation.34 | convolution fusion | flops 141556736 | bytes 15282176 | tf_op jit(solution)/shard_map/ulo,ezo->ulez/dot_general | solution.py:35
  182.0 1.2 fusion.115
  183.2 0.8 copy-done.1
  184.0 2.2 %fusion.4 = (f32[4,64]{1,0:T(4,128)S(1)}, f32[4,64]{1,0:T(4,128)S(1)}) fusion(f32[32,64,4,64]{3,1,2,0:T(8,128)S(1)} %fusion.177, f32[4,64]{1,0:T(4,128)S(1)} %max.58, pred[4,32]{0,1:T(8,128)(4,1)S(1)} %copy.194, f32[4,64]{1,0:T(4,128)S(1)} %max.57, f32[32,64,4,64]{3,1,2,0:T(8,128)S(1)} %copy-done.1), kind=kLoop, calls=%fused_computation.24 | loop fusion | flops 4193792 | bytes 4198528 | tf_op jit(solution)/shard_map/reduce_sum | solution.py:44
  186.2 2.2 %fusion.12 = (f32[4,64]{1,0:T(4,128)S(1)}, f32[4,64]{1,0:T(4,128)S(1)}) fusion(f32[32,64,4,64]{3,1,2,0:T(8,128)S(1)} %fusion.181, f32[4,64]{1,0:T(4,128)S(1)} %max.62, pred[4,32]{0,1:T(8,128)(4,1)S(1)} %copy.216, f32[4,64]{1,0:T(4,128)S(1)} %max.61, f32[32,64,4,64]{3,1,2,0:T(8,128)S(1)} %get-tuple-element.96), kind=kLoop, calls=%fused_computation.32 | loop fusion | flops 4193792 | bytes 4198528 | tf_op jit(solution)/shard_map/reduce_sum | solution.py:44
  188.5 1.2 fusion.121
  189.8 1.2 fusion.127
  191.0 1.2 fusion.133
  192.3 1.2 fusion.139
  193.5 1.2 fusion.145
  194.8 1.2 fusion.151
  196.0 1.2 fusion.157
  197.2 0.6 constant_dynamic-update-slice_fusion
  (149 shorter events, 8.2 us)
Async XLA Ops:
  8.1 22.9 %all-to-all-start.2 = ((bf16[64,4,256]{2,0,1:T(8,128)(2,1)}), bf16[64,4,256]{2,0,1:T(8,128)(2,1)S(1)}, u32[]{:S(2)}, u32[]{:S(2)}) async-start(bf16[64,4,256]{2,0,1:T(8,128)(2,1)} %bitcast.527), calls=%async_computation.2 | async-start | bytes 262144 | tf_op jit(solution)/shard_map/all_to_all | solution.py:68
  16.5 55.9 %copy-start.26 = (pred[4,5]{1,0:T(4,128)(4,1)}, pred[4,5]{1,0:T(4,128)(4,1)S(1)}, u32[]{:S(2)}) copy-start(pred[4,5]{1,0:T(4,128)(4,1)S(1)} %get-tuple-element.77) | copy-start | bytes 64
  31.0 9.1 %all-to-all-start = ((bf16[64,4,256]{2,0,1:T(8,128)(2,1)}), bf16[64,4,256]{2,0,1:T(8,128)(2,1)S(1)}, u32[]{:S(2)}, u32[]{:S(2)}) async-start(bf16[64,4,256]{2,0,1:T(8,128)(2,1)} %bitcast.528), calls=%async_computation | async-start | bytes 262144 | tf_op jit(solution)/shard_map/all_to_all | solution.py:67
  35.3 19.2 %collective-permute-start.1 = (bf16[256,256]{1,0:T(8,128)(2,1)S(1)}, bf16[256,256]{1,0:T(8,128)(2,1)S(1)}, u32[]{:S(2)}, u32[]{:S(2)}) collective-permute-start(bf16[256,256]{1,0:T(8,128)(2,1)S(1)} %bitcast.534), channel_id=1, source_target_pairs={{0,4},{4,8},{8,12},{12,16},{16,20},{20,24},{24,28},{28,32},{32,36}... | collective-permute-start | bytes 393224 | tf_op jit(solution)/shard_map/ppermute | solution.py:14
  40.1 19.9 %all-to-all-start.1 = ((bf16[64,4,1024]{2,0,1:T(8,128)(2,1)}), bf16[64,4,1024]{2,0,1:T(8,128)(2,1)S(1)}, u32[]{:S(2)}, u32[]{:S(2)}) async-start(bf16[64,4,1024]{2,0,1:T(8,128)(2,1)} %bitcast.526), calls=%async_computation.1 | async-start | bytes 1048576 | tf_op jit(solution)/shard_map/all_to_all | solution.py:66
  44.3 118.5 %all-reduce.3.cloned.1.call-start = ((), (), s32[]{:S(2)}) async-start(), calls=%async_computation.3 | async-start | bytes 4194304 | tf_op jit(solution)/shard_map/psum | solution.py:103
  44.3 11.0 %collective-permute-start = (bf16[256,256]{1,0:T(8,128)(2,1)S(1)}, bf16[256,256]{1,0:T(8,128)(2,1)S(1)}, u32[]{:S(2)}, u32[]{:S(2)}) collective-permute-start(bf16[256,256]{1,0:T(8,128)(2,1)S(1)} %bitcast.537), channel_id=1, source_target_pairs={{0,4},{4,8},{8,12},{12,16},{16,20},{20,24},{24,28},{28,32},{32,36}... | collective-permute-start | bytes 393224 | tf_op jit(solution)/shard_map/ppermute | solution.py:14
  56.1 4.7 %copy-start.13 = (pred[64,5,64]{0,2,1:T(8,128)(4,1)S(1)}, pred[64,5,64]{0,2,1:T(8,128)(4,1)}, u32[]{:S(2)}) copy-start(pred[64,5,64]{0,2,1:T(8,128)(4,1)} %broadcast_or_fusion) | copy-start | bytes 61444
  59.7 0.7 copy-start.17
  59.9 0.7 copy-start.15
  60.7 8.3 %copy-start.18 = (bf16[4,5,64,128]{3,2,1,0:T(8,128)(2,1)S(1)}, bf16[4,5,64,128]{3,2,1,0:T(8,128)(2,1)}, u32[]{:S(2)}) copy-start(bf16[4,5,64,128]{3,2,1,0:T(8,128)(2,1)} %copy-done.17) | copy-start | bytes 983044
  60.7 10.0 %copy-start.16 = (bf16[4,5,64,128]{3,2,1,0:T(8,128)(2,1)S(1)}, bf16[4,5,64,128]{3,2,1,0:T(8,128)(2,1)}, u32[]{:S(2)}) copy-start(bf16[4,5,64,128]{3,2,1,0:T(8,128)(2,1)} %copy-done.15) | copy-start | bytes 983044
  60.7 11.7 %copy-start.14 = (pred[64,5,64]{0,2,1:T(8,128)(4,1)S(1)}, pred[64,5,64]{0,2,1:T(8,128)(4,1)}, u32[]{:S(2)}) copy-start(pred[64,5,64]{0,2,1:T(8,128)(4,1)} %broadcast_or_fusion) | copy-start | bytes 61444
  60.8 9.9 %copy-start.6 = (bf16[256,128]{1,0:T(8,128)(2,1)}, bf16[256,128]{1,0:T(8,128)(2,1)S(1)}, u32[]{:S(2)}) copy-start(bf16[256,128]{1,0:T(8,128)(2,1)S(1)} %get-tuple-element.29) | copy-start | bytes 196612
  60.8 9.8 %copy-start.8 = (bf16[256,128]{1,0:T(8,128)(2,1)}, bf16[256,128]{1,0:T(8,128)(2,1)S(1)}, u32[]{:S(2)}) copy-start(bf16[256,128]{1,0:T(8,128)(2,1)S(1)} %get-tuple-element.32) | copy-start | bytes 196612
  60.8 9.8 %copy-start.11 = (bf16[256,128]{1,0:T(8,128)(2,1)}, bf16[256,128]{1,0:T(8,128)(2,1)S(1)}, u32[]{:S(2)}) copy-start(bf16[256,128]{1,0:T(8,128)(2,1)S(1)} %get-tuple-element.31) | copy-start | bytes 196612
  60.8 11.9 %copy-start.9 = (bf16[256,128]{1,0:T(8,128)(2,1)}, bf16[256,128]{1,0:T(8,128)(2,1)S(1)}, u32[]{:S(2)}) copy-start(bf16[256,128]{1,0:T(8,128)(2,1)S(1)} %get-tuple-element.27) | copy-start | bytes 196612
  162.8 1.9 copy-start
  162.8 1.9 copy-start.7
  164.7 1.5 copy-start.25
  164.8 1.5 copy-start.5
  164.8 1.9 copy-start.24
  166.2 1.2 copy-start.12
  167.5 5.0 %copy-start.23 = (f32[4,64]{1,0:T(4,128)S(1)}, f32[4,64]{1,0:T(4,128)}, u32[]{:S(2)}) copy-start(f32[4,64]{1,0:T(4,128)} %get-tuple-element.87) | copy-start | bytes 3076
  167.5 5.0 %copy-start.4 = (f32[4,64,5,64]{1,3,2,0:T(8,128)S(1)}, f32[4,64,5,64]{1,3,2,0:T(8,128)}, u32[]{:S(2)}) copy-start(f32[4,64,5,64]{1,3,2,0:T(8,128)} %get-tuple-element.88) | copy-start | bytes 983044
  167.5 5.5 %copy-start.22 = (f32[4,64]{1,0:T(4,128)S(1)}, f32[4,64]{1,0:T(4,128)}, u32[]{:S(2)}) copy-start(f32[4,64]{1,0:T(4,128)} %get-tuple-element.89) | copy-start | bytes 3076
  167.5 5.5 %copy-start.3 = (f32[4,64,5,64]{1,3,2,0:T(8,128)S(1)}, f32[4,64,5,64]{1,3,2,0:T(8,128)}, u32[]{:S(2)}) copy-start(f32[4,64,5,64]{1,3,2,0:T(8,128)} %get-tuple-element.90) | copy-start | bytes 983044
  167.5 5.9 %copy-start.2 = (f32[4,64,5,64]{1,3,2,0:T(8,128)S(1)}, f32[4,64,5,64]{1,3,2,0:T(8,128)}, u32[]{:S(2)}) copy-start(f32[4,64,5,64]{1,3,2,0:T(8,128)} %get-tuple-element.85) | copy-start | bytes 983044
  174.5 1.5 copy-start.21
  174.5 1.9 copy-start.20
  176.0 1.2 copy-start.10
  181.8 2.2 %copy-start.1 = (f32[32,64,4,64]{3,1,2,0:T(8,128)S(1)}, f32[32,64,4,64]{3,1,2,0:T(8,128)}, u32[]{:S(2)}) copy-start(f32[32,64,4,64]{3,1,2,0:T(8,128)} %get-tuple-element.86) | copy-start | bytes 6291460
  196.0 1.2 copy-start.19
Sparse Core Ops, SparseCore 0:
  54.6 108.1 all-reduce.2
where the time goes:
time: 206 us; the launch traced here: 205 us
  waiting for transfers between devices  89.5 us (43%)
  matrix products  40.1 us (19%)
  between operations  24.3 us (12%)
  starting transfers between devices  23.8 us (12%)
  local copies, waits for them, and re-layouts  16.8 us (8%)
  other arithmetic  10.1 us (5%)
    psum x1, waiting for transfers between devices, local(): fetched = lax.psum(jnp.stack(pieces, 0).astype(jnp.bfloat16), 'seq')  89.2 us
    dot_general x8, matrix products, attend_head(): jnp.einsum('ulo,ezo->ulez', query_rows, vertical_key_rows, preferred_elem...  15.4 us
    dot_general x8, matrix products, attend_head(): jnp.einsum('gxh,gvih->gxvi', query_rows, slash_keys_picked, preferred_ele...  12.8 us
    dot_general x8, matrix products, attend_head(): jnp.einsum('wenc,ncp->wep', vertical_weight.astype(jnp.bfloat16), vertica...  9.68 us
    ppermute x2, starting transfers between devices, shifted(): return lax.ppermute(value, axis, pairs)  9.48 us
    all_to_all x1, starting transfers between devices, local(): lax.all_to_all(values, 'head', split_axis=1, concat_axis=0, tiled=True)  5.84 us
    reduce_sum x2, other arithmetic, attend_head(): jnp.sum(vertical_weight, axis=(2, 3))  4.45 us
    all_to_all x1, starting transfers between devices, local(): lax.all_to_all(keys, 'head', split_axis=1, concat_axis=0, tiled=True)  4.25 us
  transfers between devices with their start and end apart: 6, of which 2 were waited for; matrix products, arithmetic and copies ran while one was open for 15% of the time, Pallas kernels for 0%

commit v1 on v0

--- a/solution.py
+++ b/solution.py
@@ -87,20 +87,28 @@
     local_vert = lax.dynamic_slice_in_dim(vertical, first_head, kv_local, 0)
     owner = local_vert // nbd
     inner = local_vert % nbd
-    mine = owner == seq_index
+    listed = local_vert.shape[1]
+    earlier = jnp.arange(listed)[None, :] < jnp.arange(listed)[:, None]
+    same_owner = owner[:, :, None] == owner[:, None, :]
+    rank = jnp.sum(same_owner & earlier[None], axis=2)
+    slots = 2
+    mine = (owner == seq_index)[:, None, :] & (rank[:, None, :] == jnp.arange(slots)[None, :, None])
+    pick = jnp.sum(jnp.where(mine, inner[:, None, :], 0), axis=2)
     pieces = []
     for group_member in range(kv_local):
-        picked = jnp.stack(
-            [
-                own_k[:, :, group_member][inner[group_member]],
-                own_v[:, :, group_member][inner[group_member]],
-            ],
-            0,
+        pieces.append(
+            jnp.stack(
+                [
+                    own_k[:, :, group_member][pick[group_member]],
+                    own_v[:, :, group_member][pick[group_member]],
+                ],
+                1,
+            )
         )
-        pieces.append(
-            jnp.where(mine[group_member][None, :, None, None], picked.astype(jnp.float32), 0.0)
-        )
-    fetched = lax.psum(jnp.stack(pieces, 0).astype(jnp.bfloat16), "seq")
+    gathered = lax.all_gather(jnp.stack(pieces, 0), "seq", axis=0, tiled=False)
+    heads_idx = jnp.arange(kv_local)[:, None]
+    fetched = gathered[owner, heads_idx, rank]
+    fetched = jnp.moveaxis(fetched, 2, 1)
     vert_keys = fetched[:, 0]
     vert_vals = fetched[:, 1]
     qblocks = seq_index * nbd + jnp.arange(nbd, dtype=jnp.int32)

time: 206 us -> 134 us (0.65)
  waiting for transfers between devices: 89.5 us -> 4.47 us
  matrix products: 40.1 us -> 47.8 us
  local copies, waits for them, and re-layouts: 16.8 us -> 22.9 us
    psum x1 -> x0, waiting for transfers between devices: 89.2 us -> none  [local(): fetched = lax.psum(jnp.stack(pieces, 0).astype(jnp.bfloat16), 'seq')]
    dot_general x8, matrix products: 12.8 us -> 19.8 us  [attend_head(): jnp.einsum('gxh,gvih->gxvi', query_rows, slash_keys_picked, preferred_ele...]
    all_gather x0 -> x1, waiting for transfers between devices: none -> 4.36 us  [local(): gathered = lax.all_gather(jnp.stack(pieces, 0), 'seq', axis=0, tiled=False)]
    gather x4 -> x6, local copies, waits for them, and re-layouts: 2.59 us -> 5.66 us  [the longest x2 3.42 us: local(): fetched = gathered[owner, heads_idx, rank]]
    dot_general x8, matrix products: 2.28 us -> 4.88 us  [attend_head(): jnp.einsum('zirc,zrcp->zip', slash_weight.astype(jnp.bfloat16), slash_val...]
  transfers between devices with their start and end apart: 6 -> 6, of which waited for: 2 -> 2; matrix products, arithmetic and copies ran while one was open for 15% -> 30% of each run, Pallas kernels for 0% -> 0%
where the time goes in v1:
time: 134 us; the launch traced here: 133 us
  matrix products  47.8 us (36%)
  between operations  24.4 us (18%)
  starting transfers between devices  23.8 us (18%)
  local copies, waits for them, and re-layouts  22.9 us (17%)
  other arithmetic  9.3 us (7%)
  waiting for transfers between devices  4.47 us (3%)
    dot_general x8, matrix products, attend_head(): jnp.einsum('gxh,gvih->gxvi', query_rows, slash_keys_picked, preferred_ele...  19.8 us
    dot_general x8, matrix products, attend_head(): jnp.einsum('ulo,ezo->ulez', query_rows, vertical_key_rows, preferred_elem...  13.5 us
    dot_general x8, matrix products, attend_head(): jnp.einsum('wenc,ncp->wep', vertical_weight.astype(jnp.bfloat16), vertica...  9.66 us
    ppermute x2, starting transfers between devices, shifted(): return lax.ppermute(value, axis, pairs)  9.23 us
    all_to_all x1, starting transfers between devices, local(): lax.all_to_all(values, 'head', split_axis=1, concat_axis=0, tiled=True)  5.84 us
    dot_general x8, matrix products, attend_head(): jnp.einsum('zirc,zrcp->zip', slash_weight.astype(jnp.bfloat16), slash_val...  4.88 us
    reduce_sum x2, other arithmetic, attend_head(): jnp.sum(vertical_weight, axis=(2, 3))  4.68 us
    all_to_all x1, starting transfers between devices, local(): lax.all_to_all(queries, 'head', split_axis=1, concat_axis=0, tiled=True)  4.46 us
  transfers between devices with their start and end apart: 6, of which 2 were waited for; matrix products, arithmetic and copies ran while one was open for 30% of the time, Pallas kernels for 0%

profile of v1, /device:TPU:1, one launch (start us, length us, event | category | flops | bytes accessed | tf_op | source)
XLA Modules:
  0.0 132.7 jit_solution(1322329869511600869)
XLA Ops:
  6.5 1.5 %copy.341 = bf16[8,4,8,256]{3,2,0,1:T(8,128)(2,1)} copy(bf16[8,4,8,256]{3,2,1,0:T(8,128)(2,1)} %bitcast.582) | data formatting | bytes 262144 | tf_op jit(solution)/shard_map/all_to_all | solution.py:68
  8.1 5.8 %all-to-all-start.2 = ((bf16[64,4,256]{2,0,1:T(8,128)(2,1)}), bf16[64,4,256]{2,0,1:T(8,128)(2,1)S(1)}, u32[]{:S(2)}, u32[]{:S(2)}) async-start(bf16[64,4,256]{2,0,1:T(8,128)(2,1)} %bitcast.542), calls=%async_computation.2 | async-start | bytes 262144 | tf_op jit(solution)/shard_map/all_to_all | solution.py:68
  14.0 1.6 %copy.342 = bf16[8,4,8,256]{3,2,0,1:T(8,128)(2,1)} copy(bf16[8,4,8,256]{3,2,1,0:T(8,128)(2,1)} %bitcast.583) | data formatting | bytes 262144 | tf_op jit(solution)/shard_map/all_to_all | solution.py:67
  15.5 1.9 %copy.340 = bf16[8,4,8,1024]{3,2,0,1:T(8,128)(2,1)} copy(bf16[8,4,8,1024]{3,2,1,0:T(8,128)(2,1)} %bitcast.569) | data formatting | bytes 1048576 | tf_op jit(solution)/shard_map/all_to_all | solution.py:66
  17.4 0.8 fusion.207
  18.4 0.7 and_select_fusion.1
  19.5 0.7 broadcast_or_fusion
  20.4 4.2 %all-to-all-start = ((bf16[64,4,256]{2,0,1:T(8,128)(2,1)}), bf16[64,4,256]{2,0,1:T(8,128)(2,1)S(1)}, u32[]{:S(2)}, u32[]{:S(2)}) async-start(bf16[64,4,256]{2,0,1:T(8,128)(2,1)} %bitcast.543), calls=%async_computation | async-start | bytes 262144 | tf_op jit(solution)/shard_map/all_to_all | solution.py:67
  24.7 4.5 %collective-permute-start.1 = (bf16[256,256]{1,0:T(8,128)(2,1)S(1)}, bf16[256,256]{1,0:T(8,128)(2,1)S(1)}, u32[]{:S(2)}, u32[]{:S(2)}) collective-permute-start(bf16[256,256]{1,0:T(8,128)(2,1)S(1)} %bitcast.562), channel_id=1, source_target_pairs={{0,4},{4,8},{8,12},{12,16},{16,20},{20,24},{24,28},{28,32},{32,36}... | collective-permute-start | bytes 393224 | tf_op jit(solution)/shard_map/ppermute | solution.py:14
  29.5 4.5 %all-to-all-start.1 = ((bf16[64,4,1024]{2,0,1:T(8,128)(2,1)}), bf16[64,4,1024]{2,0,1:T(8,128)(2,1)S(1)}, u32[]{:S(2)}, u32[]{:S(2)}) async-start(bf16[64,4,1024]{2,0,1:T(8,128)(2,1)} %bitcast.541), calls=%async_computation.1 | async-start | bytes 1048576 | tf_op jit(solution)/shard_map/all_to_all | solution.py:66
  36.5 0.7 copy.206
  37.2 0.7 subtract_compare_fusion
  37.9 4.7 %collective-permute-start = (bf16[256,256]{1,0:T(8,128)(2,1)S(1)}, bf16[256,256]{1,0:T(8,128)(2,1)S(1)}, u32[]{:S(2)}, u32[]{:S(2)}) collective-permute-start(bf16[256,256]{1,0:T(8,128)(2,1)S(1)} %bitcast.566), channel_id=1, source_target_pairs={{0,4},{4,8},{8,12},{12,16},{16,20},{20,24},{24,28},{28,32},{32,36}... | collective-permute-start | bytes 393224 | tf_op jit(solution)/shard_map/ppermute | solution.py:14
  42.6 0.7 fusion.240
  54.3 1.7 %constant_dynamic-slice_fusion = (bf16[4,64,1,128]{3,2,1,0:T(2,128)(2,1)S(1)}, bf16[4,64,1,128]{3,2,1,0:T(2,128)(2,1)S(1)}, bf16[4,64,1,128]{3,2,1,0:T(2,128)(2,...) fusion(bf16[8,64,1,128]{3,2,1,0:T(2,128)(2,1)S(1)} %get-tuple-e, ...), kind=kLoop, calls=%fused_computation.222 | loop fusion | bytes 1048608 | tf_op jit(solution)/shard_map/dynamic_slice | solution.py:127
  56.5 1.7 %constant_dynamic-slice_fusion.4 = (bf16[4,64,1,128]{3,2,1,0:T(2,128)(2,1)S(1)}, bf16[4,64,1,128]{3,2,1,0:T(2,128)(2,1)S(1)}, bf16[4,64,1,128]{3,2,1,0:T(2,128)(...) fusion(bf16[8,64,1,128]{3,2,1,0:T(2,128)(2,1)S(1)} %get-tuple-e, ...), kind=kLoop, calls=%fused_computation.226 | loop fusion | bytes 1048608 | tf_op jit(solution)/shard_map/dynamic_slice | solution.py:124
  62.3 2.8 %fusion.241 = (f32[4,64]{1,0:T(4,128)}, f32[4,64,5,64]{1,3,2,0:T(8,128)}) fusion(bf16[4,5,64,128]{3,2,1,0:T(8,128)(2,1)} %copy-done.24, bf16[4,64,128,1]{2,1,3,0:T(8,128)(2,1)S(1)} %bitcast.580, pred[64,5,64]{0,2,1:T(8,128)(4,1)} %broadcast_or_fusion, pred[4,5]{1,0:T(4,128)(4,1)S(1)} %get-tuple-element.80), kind=kOutput, calls=%fused_computation.302 | convolution fusion | flops 21298944 | bytes 742420 | tf_op jit(solution)/shard_map/gxh,gvih->gxvi/dot_general | solution.py:28
  65.1 2.7 %fusion.242 = (f32[4,64]{1,0:T(4,128)}, f32[4,64,5,64]{1,3,2,0:T(8,128)}) fusion(bf16[4,5,64,128]{3,2,1,0:T(8,128)(2,1)} %copy-done.24, bf16[4,64,128,1]{2,1,3,0:T(8,128)(2,1)S(1)} %bitcast.578, pred[64,5,64]{0,2,1:T(8,128)(4,1)} %broadcast_or_fusion, pred[4,5]{1,0:T(4,128)(4,1)S(1)} %get-tuple-element.80), kind=kOutput, calls=%fused_computation.303 | convolution fusion | flops 21298944 | bytes 742420 | tf_op jit(solution)/shard_map/gxh,gvih->gxvi/dot_general | solution.py:28
  67.8 2.1 %fusion.243 = (f32[4,64]{1,0:T(4,128)S(1)}, f32[4,64,5,64]{1,3,2,0:T(8,128)}) fusion(bf16[4,5,64,128]{3,2,1,0:T(8,128)(2,1)} %copy-done.24, bf16[4,64,128,1]{2,1,3,0:T(8,128)(2,1)S(1)} %bitcast.590, pred[64,5,64]{0,2,1:T(8,128)(4,1)S(1)} %copy-done.23, pred[4,5]{1,0:T(4,128)(4,1)} %copy-done.37), kind=kOutput, calls=%fused_computation.304 | convolution fusion | flops 21298944 | bytes 742420 | tf_op jit(solution)/shard_map/gxh,gvih->gxvi/dot_general | solution.py:28
  69.8 2.3 %fusion.244 = (f32[4,64]{1,0:T(4,128)}, f32[4,64,5,64]{1,3,2,0:T(8,128)}) fusion(bf16[4,5,64,128]{3,2,1,0:T(8,128)(2,1)S(1)} %copy-done.25, bf16[4,64,128,1]{2,1,3,0:T(8,128)(2,1)S(1)} %bitcast.576, pred[64,5,64]{0,2,1:T(8,128)(4,1)S(1)} %copy-done.23, pred[4,5]{1,0:T(4,128)(4,1)} %copy-done.37), kind=kOutput, calls=%fused_computation.305 | convolution fusion | flops 21298944 | bytes 742420 | tf_op jit(solution)/shard_map/gxh,gvih->gxvi/dot_general | solution.py:28
  72.2 2.7 %fusion.245 = (f32[4,64]{1,0:T(4,128)}, f32[4,64,5,64]{1,3,2,0:T(8,128)}) fusion(bf16[4,5,64,128]{3,2,1,0:T(8,128)(2,1)} %bitcast_dynamic-update-slice_fusion.4, bf16[4,64,128,1]{2,1,3,0:T(8,128)(2,1)S(1)} %bitcast.574, pred[64,5,64]{0,2,1:T(8,128)(4,1)S(1)} %copy-done.23, pred[4,5]{1,0:T(4,128)(4,1)S(1)} %copy-done.36), kind=kOutput, calls=%fused_computation.306 | convolution fusion | flops 21298944 | bytes 742420 | tf_op jit(solution)/shard_map/gxh,gvih->gxvi/dot_general | solution.py:28
  74.9 1.9 %fusion.246 = (f32[4,64]{1,0:T(4,128)}, f32[4,64,5,64]{1,3,2,0:T(8,128)S(1)}) fusion(bf16[4,5,64,128]{3,2,1,0:T(8,128)(2,1)} %bitcast_dynamic-update-slice_fusion.4, bf16[4,64,128,1]{2,1,3,0:T(8,128)(2,1)S(1)} %bitcast.572, pred[64,5,64]{0,2,1:T(8,128)(4,1)S(1)} %copy-done.23, pred[4,5]{1,0:T(4,128)(4,1)S(1)} %copy-done.36), kind=kOutput, calls=%fused_computation.307 | convolution fusion | flops 21298944 | bytes 742420 | tf_op jit(solution)/shard_map/gxh,gvih->gxvi/dot_general | solution.py:28
  76.8 2.7 %fusion.247 = (f32[4,64]{1,0:T(4,128)}, f32[4,64,5,64]{1,3,2,0:T(8,128)}) fusion(bf16[4,5,64,128]{3,2,1,0:T(8,128)(2,1)} %bitcast_dynamic-update-slice_fusion.4, bf16[4,64,128,1]{2,1,3,0:T(8,128)(2,1)S(1)} %bitcast.588, pred[64,5,64]{0,2,1:T(8,128)(4,1)S(1)} %copy-done.23, pred[4,5]{1,0:T(4,128)(4,1)S(1)} %copy-done.36), kind=kOutput, calls=%fused_computation.308 | convolution fusion | flops 21298944 | bytes 742420 | tf_op jit(solution)/shard_map/gxh,gvih->gxvi/dot_general | solution.py:28
  79.5 2.7 %fusion.248 = (f32[4,64]{1,0:T(4,128)}, f32[4,64,5,64]{1,3,2,0:T(8,128)}) fusion(bf16[4,5,64,128]{3,2,1,0:T(8,128)(2,1)} %bitcast_dynamic-update-slice_fusion.4, bf16[4,64,128,1]{2,1,3,0:T(8,128)(2,1)S(1)} %bitcast.570, pred[64,5,64]{0,2,1:T(8,128)(4,1)S(1)} %copy-done.23, pred[4,5]{1,0:T(4,128)(4,1)S(1)} %copy-done.36), kind=kOutput, calls=%fused_computation.309 | convolution fusion | flops 21298944 | bytes 742420 | tf_op jit(solution)/shard_map/gxh,gvih->gxvi/dot_general | solution.py:28
  82.2 4.4 %all-gather.3.cloned.1.call-done = bf16[64,2,2,64,128]{4,3,2,1,0:T(8,128)(2,1)} async-done(((bf16[2,2,2,64,128]{4,3,2,1,0:T(8,128)(2,1)}), bf16[64,2,2,64,128]{4,3,2,1,0:T(8,128)(2,1)}) %all-gather.3.cloned.1.call-update) | async-done | bytes 4194320 | tf_op jit(solution)/shard_map/all_gather | solution.py:108
  86.5 3.2 %gather_fusion.4 = bf16[64,2,64,128]{3,2,1,0:T(8,128)(2,1)S(1)} fusion(bf16[32,2,2,2,64,128]{5,4,3,2,1,0:T(8,128)(2,1)} %bitcast.568, s32[64]{0:T(128)S(1)} %reshape.595), kind=kCustom, calls=%fused_computation.4 | custom fusion | bytes 4195072 | tf_op jit(solution)/shard_map/gather | solution.py:110
  90.6 0.7 fusion.179
  91.3 1.5 %fusion.19 = (f32[4,64]{1,0:T(4,128)S(1)}, f32[4,64]{1,0:T(4,128)S(1)}, f32[32,64,4,64]{3,1,2,0:T(8,128)S(1)}) fusion(pred[4,32]{0,1:T(8,128)(4,1)S(1)} %copy.202, f32[32,64,4,64]{3,1,2,0:T(8,128)S(1)} %fusion.179, bf16[4,64,128,1]{2,1,0,3:T(8,128)(2,1)S(1)} %bitcast.579, bf16[2,2,32,64,128]{4,3,2,1,0:T(8,128)(2,1)S(1)} %bitcast.545), kind=kOutput, calls=%fused_computation.40 | convolution fusion | flops 137362944 | bytes 6887424 | tf_op jit(solution)/shard_map/ulo,ezo->ulez/dot_general | solution.py:35
  93.0 0.9 convolution_bitcast_fusion.7
  93.9 0.7 fusion.177
  94.7 4.2 %fusion.6 = (f32[4,64]{1,0:T(4,128)}, f32[4,64]{1,0:T(4,128)S(1)}, f32[4,64]{1,0:T(4,128)S(1)}, f32[4,64]{1,0:T(4,128)}, f32[32,64,4,64]{3,1,2,0:T(8,128)S(1)}) fusion(f32[32,64,4,64]{3,1,2,0:T(8,128)S(1)} %get-tuple-element.83, f32[4,64]{1,0:T(4,128)S(1)} %max.59, pred[4,32]{0,1:T(8,128)(4,1)S(1)} %copy.202, f32[32,64,4,64]{3,1,2,0:T(8,128)S(1)} %fusion.177, ...), kind=kOutput, calls=%fused_computation.27 | convolution fusion | flops 141556736 | bytes 15282176 | tf_op jit(solution)/shard_map/ulo,ezo->ulez/dot_general | solution.py:35
  99.0 0.9 convolution_bitcast_fusion.6
  100.1 0.9 convolution_bitcast_fusion.5
  101.1 0.9 convolution_bitcast_fusion.4
  102.2 0.7 fusion.183
  102.9 1.4 %fusion.23 = (f32[4,64]{1,0:T(4,128)S(1)}, f32[4,64]{1,0:T(4,128)S(1)}, f32[32,64,4,64]{3,1,2,0:T(8,128)S(1)}) fusion(pred[4,32]{0,1:T(8,128)(4,1)S(1)} %copy.226, f32[32,64,4,64]{3,1,2,0:T(8,128)S(1)} %fusion.183, bf16[4,64,128,1]{2,1,0,3:T(8,128)(2,1)S(1)} %bitcast.573, bf16[2,2,32,64,128]{4,3,2,1,0:T(8,128)(2,1)S(1)} %bitcast.549), kind=kOutput, calls=%fused_computation.44 | convolution fusion | flops 137362944 | bytes 6887424 | tf_op jit(solution)/shard_map/ulo,ezo->ulez/dot_general | solution.py:35
  104.9 0.7 fusion.181
  105.7 3.4 %fusion.14 = (f32[4,64]{1,0:T(4,128)S(1)}, f32[4,64]{1,0:T(4,128)S(1)}, f32[4,64]{1,0:T(4,128)S(1)}, f32[4,64]{1,0:T(4,128)S(1)}, f32[32,64,4,64]{3,1,2,0:T(8,128)S(1)}) fusion(f32[32,64,4,64]{3,1,2,0:T(8,128)S(1)} %get-tuple-element.93, f32[4,64]{1,0:T(4,128)S(1)} %max.63, pred[4,32]{0,1:T(8,128)(4,1)S(1)} %copy.226, f32[32,64,4,64]{3,1,2,0:T(8,128)S(1)} %fusion.181, ...), kind=kOutput, calls=%fused_computation.35 | convolution fusion | flops 141556736 | bytes 15282176 | tf_op jit(solution)/shard_map/ulo,ezo->ulez/dot_general | solution.py:35
  110.5 1.2 fusion.115
  111.7 2.5 %fusion.4 = (f32[4,64]{1,0:T(4,128)S(1)}, f32[4,64]{1,0:T(4,128)S(1)}) fusion(f32[32,64,4,64]{3,1,2,0:T(8,128)S(1)} %fusion.177, f32[4,64]{1,0:T(4,128)S(1)} %max.58, pred[4,32]{0,1:T(8,128)(4,1)S(1)} %copy.202, f32[4,64]{1,0:T(4,128)S(1)} %max.57, f32[32,64,4,64]{3,1,2,0:T(8,128)S(1)} %get-tuple-element.86), kind=kLoop, calls=%fused_computation.25 | loop fusion | flops 4193792 | bytes 4198528 | tf_op jit(solution)/shard_map/reduce_sum | solution.py:44
  114.2 2.2 %fusion.12 = (f32[4,64]{1,0:T(4,128)S(1)}, f32[4,64]{1,0:T(4,128)S(1)}) fusion(f32[32,64,4,64]{3,1,2,0:T(8,128)S(1)} %fusion.181, f32[4,64]{1,0:T(4,128)S(1)} %max.62, pred[4,32]{0,1:T(8,128)(4,1)S(1)} %copy.226, f32[4,64]{1,0:T(4,128)S(1)} %max.61, f32[32,64,4,64]{3,1,2,0:T(8,128)S(1)} %get-tuple-element.96), kind=kLoop, calls=%fused_computation.33 | loop fusion | flops 4193792 | bytes 4198528 | tf_op jit(solution)/shard_map/reduce_sum | solution.py:44
  116.5 1.2 fusion.121
  117.7 1.2 fusion.127
  119.0 1.2 fusion.133
  120.3 1.2 fusion.139
  121.5 1.2 fusion.145
  122.8 1.2 fusion.151
  124.0 1.2 fusion.157
  (178 shorter events, 13.0 us)
Async XLA Ops:
  8.1 12.3 %all-to-all-start.2 = ((bf16[64,4,256]{2,0,1:T(8,128)(2,1)}), bf16[64,4,256]{2,0,1:T(8,128)(2,1)S(1)}, u32[]{:S(2)}, u32[]{:S(2)}) async-start(bf16[64,4,256]{2,0,1:T(8,128)(2,1)} %bitcast.542), calls=%async_computation.2 | async-start | bytes 262144 | tf_op jit(solution)/shard_map/all_to_all | solution.py:68
  20.4 9.1 %all-to-all-start = ((bf16[64,4,256]{2,0,1:T(8,128)(2,1)}), bf16[64,4,256]{2,0,1:T(8,128)(2,1)S(1)}, u32[]{:S(2)}, u32[]{:S(2)}) async-start(bf16[64,4,256]{2,0,1:T(8,128)(2,1)} %bitcast.543), calls=%async_computation | async-start | bytes 262144 | tf_op jit(solution)/shard_map/all_to_all | solution.py:67
  24.7 28.9 %collective-permute-start.1 = (bf16[256,256]{1,0:T(8,128)(2,1)S(1)}, bf16[256,256]{1,0:T(8,128)(2,1)S(1)}, u32[]{:S(2)}, u32[]{:S(2)}) collective-permute-start(bf16[256,256]{1,0:T(8,128)(2,1)S(1)} %bitcast.562), channel_id=1, source_target_pairs={{0,4},{4,8},{8,12},{12,16},{16,20},{20,24},{24,28},{28,32},{32,36}... | collective-permute-start | bytes 393224 | tf_op jit(solution)/shard_map/ppermute | solution.py:14
  29.5 32.6 %all-to-all-start.1 = ((bf16[64,4,1024]{2,0,1:T(8,128)(2,1)}), bf16[64,4,1024]{2,0,1:T(8,128)(2,1)S(1)}, u32[]{:S(2)}, u32[]{:S(2)}) async-start(bf16[64,4,1024]{2,0,1:T(8,128)(2,1)} %bitcast.541), calls=%async_computation.1 | async-start | bytes 1048576 | tf_op jit(solution)/shard_map/all_to_all | solution.py:66
  34.0 52.6 %all-gather.3.cloned.1.call-start = ((), (), s32[]{:S(2)}) async-start(), calls=%async_computation.3 | async-start | bytes 4325376 | tf_op jit(solution)/shard_map/all_gather | solution.py:108
  37.9 29.9 %copy-start.37 = (pred[4,5]{1,0:T(4,128)(4,1)}, pred[4,5]{1,0:T(4,128)(4,1)S(1)}, u32[]{:S(2)}) copy-start(pred[4,5]{1,0:T(4,128)(4,1)S(1)} %get-tuple-element.80) | copy-start | bytes 64
  37.9 15.8 %collective-permute-start = (bf16[256,256]{1,0:T(8,128)(2,1)S(1)}, bf16[256,256]{1,0:T(8,128)(2,1)S(1)}, u32[]{:S(2)}, u32[]{:S(2)}) collective-permute-start(bf16[256,256]{1,0:T(8,128)(2,1)S(1)} %bitcast.566), channel_id=1, source_target_pairs={{0,4},{4,8},{8,12},{12,16},{16,20},{20,24},{24,28},{28,32},{32,36}... | collective-permute-start | bytes 393224 | tf_op jit(solution)/shard_map/ppermute | solution.py:14
  58.4 9.4 %copy-start.23 = (pred[64,5,64]{0,2,1:T(8,128)(4,1)S(1)}, pred[64,5,64]{0,2,1:T(8,128)(4,1)}, u32[]{:S(2)}) copy-start(pred[64,5,64]{0,2,1:T(8,128)(4,1)} %broadcast_or_fusion) | copy-start | bytes 61444
  59.3 12.9 %copy-start.36 = (pred[4,5]{1,0:T(4,128)(4,1)S(1)}, pred[4,5]{1,0:T(4,128)(4,1)}, u32[]{:S(2)}) copy-start(pred[4,5]{1,0:T(4,128)(4,1)} %get-tuple-element.79) | copy-start | bytes 64
  59.4 2.0 %copy-start.24 = (bf16[4,5,64,128]{3,2,1,0:T(8,128)(2,1)}, bf16[4,5,64,128]{3,2,1,0:T(8,128)(2,1)S(1)}, u32[]{:S(2)}) copy-start(bf16[4,5,64,128]{3,2,1,0:T(8,128)(2,1)S(1)} %bitcast_dynamic-update-slice_fusion.12) | copy-start | bytes 983044
  62.1 7.7 %copy-start.25 = (bf16[4,5,64,128]{3,2,1,0:T(8,128)(2,1)S(1)}, bf16[4,5,64,128]{3,2,1,0:T(8,128)(2,1)}, u32[]{:S(2)}) copy-start(bf16[4,5,64,128]{3,2,1,0:T(8,128)(2,1)} %copy-done.24) | copy-start | bytes 983044
  62.2 12.7 %copy-start.7 = (bf16[256,128]{1,0:T(8,128)(2,1)}, bf16[256,128]{1,0:T(8,128)(2,1)S(1)}, u32[]{:S(2)}) copy-start(bf16[256,128]{1,0:T(8,128)(2,1)S(1)} %get-tuple-element.30) | copy-start | bytes 196612
  62.2 12.6 %copy-start.9 = (bf16[256,128]{1,0:T(8,128)(2,1)}, bf16[256,128]{1,0:T(8,128)(2,1)S(1)}, u32[]{:S(2)}) copy-start(bf16[256,128]{1,0:T(8,128)(2,1)S(1)} %get-tuple-element.32) | copy-start | bytes 196612
  62.2 17.2 %copy-start.11 = (bf16[256,128]{1,0:T(8,128)(2,1)}, bf16[256,128]{1,0:T(8,128)(2,1)S(1)}, u32[]{:S(2)}) copy-start(bf16[256,128]{1,0:T(8,128)(2,1)S(1)} %get-tuple-element.31) | copy-start | bytes 196612
  62.3 17.2 %copy-start.13 = (bf16[256,128]{1,0:T(8,128)(2,1)}, bf16[256,128]{1,0:T(8,128)(2,1)S(1)}, u32[]{:S(2)}) copy-start(bf16[256,128]{1,0:T(8,128)(2,1)S(1)} %get-tuple-element.34) | copy-start | bytes 196612
  62.3 17.2 %copy-start.19 = (bf16[256,128]{1,0:T(8,128)(2,1)}, bf16[256,128]{1,0:T(8,128)(2,1)S(1)}, u32[]{:S(2)}) copy-start(bf16[256,128]{1,0:T(8,128)(2,1)S(1)} %get-tuple-element.29) | copy-start | bytes 196612
  62.3 17.2 %copy-start.21 = (bf16[256,128]{1,0:T(8,128)(2,1)}, bf16[256,128]{1,0:T(8,128)(2,1)S(1)}, u32[]{:S(2)}) copy-start(bf16[256,128]{1,0:T(8,128)(2,1)S(1)} %get-tuple-element.33) | copy-start | bytes 196612
  89.7 0.8 copy-start.14
  89.7 1.6 %copy-start.12 = (bf16[256,128]{1,0:T(8,128)(2,1)S(1)}, bf16[256,128]{1,0:T(8,128)(2,1)}, u32[]{:S(2)}) copy-start(bf16[256,128]{1,0:T(8,128)(2,1)} %copy-done.11) | copy-start | bytes 196612
  91.3 1.5 %copy-start.35 = (f32[4,64]{1,0:T(4,128)S(1)}, f32[4,64]{1,0:T(4,128)}, u32[]{:S(2)}) copy-start(f32[4,64]{1,0:T(4,128)} %get-tuple-element.81) | copy-start | bytes 3076
  91.3 1.5 %copy-start.6 = (f32[4,64,5,64]{1,3,2,0:T(8,128)S(1)}, f32[4,64,5,64]{1,3,2,0:T(8,128)}, u32[]{:S(2)}) copy-start(f32[4,64,5,64]{1,3,2,0:T(8,128)} %get-tuple-element.82) | copy-start | bytes 983044
  91.3 2.6 %copy-start.10 = (bf16[256,128]{1,0:T(8,128)(2,1)S(1)}, bf16[256,128]{1,0:T(8,128)(2,1)}, u32[]{:S(2)}) copy-start(bf16[256,128]{1,0:T(8,128)(2,1)} %copy-done.9) | copy-start | bytes 196612
  92.8 1.9 %copy-start.34 = (f32[4,64]{1,0:T(4,128)S(1)}, f32[4,64]{1,0:T(4,128)}, u32[]{:S(2)}) copy-start(f32[4,64]{1,0:T(4,128)} %get-tuple-element.84) | copy-start | bytes 3076
  92.8 1.9 %copy-start.22 = (bf16[256,128]{1,0:T(8,128)(2,1)S(1)}, bf16[256,128]{1,0:T(8,128)(2,1)}, u32[]{:S(2)}) copy-start(bf16[256,128]{1,0:T(8,128)(2,1)} %copy-done.21) | copy-start | bytes 196612
  94.7 4.3 %copy-start.5 = (f32[4,64,5,64]{1,3,2,0:T(8,128)S(1)}, f32[4,64,5,64]{1,3,2,0:T(8,128)}, u32[]{:S(2)}) copy-start(f32[4,64,5,64]{1,3,2,0:T(8,128)} %get-tuple-element.88) | copy-start | bytes 983044
  94.7 5.3 %copy-start.33 = (f32[4,64]{1,0:T(4,128)S(1)}, f32[4,64]{1,0:T(4,128)}, u32[]{:S(2)}) copy-start(f32[4,64]{1,0:T(4,128)} %get-tuple-element.89) | copy-start | bytes 3076
  94.7 5.3 %copy-start.4 = (f32[4,64,5,64]{1,3,2,0:T(8,128)S(1)}, f32[4,64,5,64]{1,3,2,0:T(8,128)}, u32[]{:S(2)}) copy-start(f32[4,64,5,64]{1,3,2,0:T(8,128)} %get-tuple-element.90) | copy-start | bytes 983044
  94.7 6.4 %copy-start.3 = (f32[4,64,5,64]{1,3,2,0:T(8,128)S(1)}, f32[4,64,5,64]{1,3,2,0:T(8,128)}, u32[]{:S(2)}) copy-start(f32[4,64,5,64]{1,3,2,0:T(8,128)} %get-tuple-element.85) | copy-start | bytes 983044
  99.0 3.2 %copy-start.8 = (bf16[256,128]{1,0:T(8,128)(2,1)S(1)}, bf16[256,128]{1,0:T(8,128)(2,1)}, u32[]{:S(2)}) copy-start(bf16[256,128]{1,0:T(8,128)(2,1)} %copy-done.7) | copy-start | bytes 196612
  102.9 1.5 %copy-start.31 = (f32[4,64]{1,0:T(4,128)S(1)}, f32[4,64]{1,0:T(4,128)}, u32[]{:S(2)}) copy-start(f32[4,64]{1,0:T(4,128)} %get-tuple-element.91) | copy-start | bytes 3076
  102.9 1.5 %copy-start.2 = (f32[4,64,5,64]{1,3,2,0:T(8,128)S(1)}, f32[4,64,5,64]{1,3,2,0:T(8,128)}, u32[]{:S(2)}) copy-start(f32[4,64,5,64]{1,3,2,0:T(8,128)} %get-tuple-element.92) | copy-start | bytes 983044
  104.4 1.2 copy-start.30
  104.4 1.2 copy-start.20
  105.6 3.5 %copy-start.29 = (f32[4,64]{1,0:T(4,128)S(1)}, f32[4,64]{1,0:T(4,128)}, u32[]{:S(2)}) copy-start(f32[4,64]{1,0:T(4,128)} %get-tuple-element.97) | copy-start | bytes 3076
  105.6 3.5 %copy-start.1 = (f32[4,64,5,64]{1,3,2,0:T(8,128)S(1)}, f32[4,64,5,64]{1,3,2,0:T(8,128)}, u32[]{:S(2)}) copy-start(f32[4,64,5,64]{1,3,2,0:T(8,128)} %get-tuple-element.98) | copy-start | bytes 983044
  105.6 3.9 %copy-start.28 = (f32[4,64]{1,0:T(4,128)S(1)}, f32[4,64]{1,0:T(4,128)}, u32[]{:S(2)}) copy-start(f32[4,64]{1,0:T(4,128)} %get-tuple-element.99) | copy-start | bytes 3076
  105.7 4.0 %copy-start = (f32[4,64,5,64]{1,3,2,0:T(8,128)S(1)}, f32[4,64,5,64]{1,3,2,0:T(8,128)}, u32[]{:S(2)}) copy-start(f32[4,64,5,64]{1,3,2,0:T(8,128)} %get-tuple-element.100) | copy-start | bytes 983044
  109.1 1.4 %copy-start.32 = (f32[4,64]{1,0:T(4,128)S(1)}, f32[4,64]{1,0:T(4,128)}, u32[]{:S(2)}) copy-start(f32[4,64]{1,0:T(4,128)} %get-tuple-element.16) | copy-start | bytes 3076
  109.1 1.4 %copy-start.17 = (f32[4,64,128]{2,1,0:T(8,128)S(1)}, f32[4,64,128]{2,1,0:T(8,128)}, u32[]{:S(2)}) copy-start(f32[4,64,128]{2,1,0:T(8,128)} %convolution_bitcast_fusion.7) | copy-start | bytes 393220
  114.2 2.3 %copy-start.18 = (f32[4,64,128]{2,1,0:T(8,128)S(1)}, f32[4,64,128]{2,1,0:T(8,128)}, u32[]{:S(2)}) copy-start(f32[4,64,128]{2,1,0:T(8,128)} %convolution_bitcast_fusion.6) | copy-start | bytes 393220
  116.4 1.3 copy-start.16
  117.7 1.3 copy-start.27
  117.7 1.3 copy-start.15
  124.0 1.2 copy-start.26
Sparse Core Ops, SparseCore 0:
  37.4 49.1 all-gather.2

commit v2 on v1

v2 whole, which is shorter than its diff:
```python
import jax
import jax.numpy as jnp
from jax import lax
from jax.experimental import pallas as pl
from jax.sharding import PartitionSpec as P

HEAD_WIDTH = 128
BLOCK_TOKENS = 64
EXTRA_DIAGONALS = 4
SLASH_SLOTS = 6
INTERPRET = False


def shifted(value, axis, by):
    size = lax.axis_size(axis)
    pairs = [(i, i + by) for i in range(size) if 0 <= i + by < size]
    return lax.ppermute(value, axis, pairs)


def attend_kernel(q_ref, ks_ref, vs_ref, kv_ref, vv_ref, ms_ref, mv_ref, o_ref, *, group, scale):
    rows = BLOCK_TOKENS * group
    q = q_ref[...]
    q_stack = jnp.concatenate(
        [q[:, h * HEAD_WIDTH : (h + 1) * HEAD_WIDTH] for h in range(group)], axis=0
    )
    nt = (((1,), (1,)), ((), ()))
    s_slash = (
        lax.dot_general(q_stack, ks_ref[0, 0], nt, preferred_element_type=jnp.float32) * scale
    )
    s_vert = lax.dot_general(q_stack, kv_ref[0], nt, preferred_element_type=jnp.float32) * scale
    width = s_slash.shape[1]
    row = jnp.bitwise_and(lax.broadcasted_iota(jnp.int32, (rows, width), 0), BLOCK_TOKENS - 1)
    col = lax.broadcasted_iota(jnp.int32, (rows, width), 1)
    ok_slash = (ms_ref[0, 0] > 0) & ((col >= BLOCK_TOKENS) | (col <= row))
    s_slash = jnp.where(ok_slash, s_slash, -jnp.inf)
    s_vert = jnp.where(mv_ref[0, 0] > 0, s_vert, -jnp.inf)
    top = jnp.maximum(
        jnp.max(s_slash, axis=1, keepdims=True), jnp.max(s_vert, axis=1, keepdims=True)
    )
    w_slash = jnp.exp(s_slash - top)
    w_vert = jnp.exp(s_vert - top)
    total = jnp.sum(w_slash, axis=1, keepdims=True) + jnp.sum(w_vert, axis=1, keepdims=True)
    acc = jnp.dot(w_slash.astype(jnp.bfloat16), vs_ref[0, 0], preferred_element_type=jnp.float32)
    acc = acc + jnp.dot(
        w_vert.astype(jnp.bfloat16), vv_ref[0], preferred_element_type=jnp.float32
    )
    res = (acc / total).astype(o_ref.dtype)
    for h in range(group):
        o_ref[:, h * HEAD_WIDTH : (h + 1) * HEAD_WIDTH] = res[
            h * BLOCK_TOKENS : (h + 1) * BLOCK_TOKENS
        ]


def attend(q_all, ks, vs, kv, vv, ms, mv, group, scale):
    kv_local, nbd = ks.shape[0], ks.shape[1]
    slash_rows = ks.shape[2]
    vert_rows = kv.shape[1]
    cols = group * HEAD_WIDTH
    rows = BLOCK_TOKENS * group
    steps = kv_local * nbd
    flops = steps * 4 * rows * (slash_rows + vert_rows) * HEAD_WIDTH
    cost = pl.CostEstimate(
        flops=flops,
        transcendentals=steps * rows * (slash_rows + vert_rows),
        bytes_accessed=2 * (2 * q_all.size + ks.size + vs.size + kv.size + vv.size),
    )
    kernel = lambda *refs: attend_kernel(*refs, group=group, scale=scale)
    return pl.pallas_call(
        kernel,
        grid=(kv_local, nbd),
        in_specs=[
            pl.BlockSpec((BLOCK_TOKENS, cols), lambda g, i: (i, g)),
            pl.BlockSpec((1, 1, slash_rows, HEAD_WIDTH), lambda g, i: (g, i, 0, 0)),
            pl.BlockSpec((1, 1, slash_rows, HEAD_WIDTH), lambda g, i: (g, i, 0, 0)),
            pl.BlockSpec((1, vert_rows, HEAD_WIDTH), lambda g, i: (g, 0, 0)),
            pl.BlockSpec((1, vert_rows, HEAD_WIDTH), lambda g, i: (g, 0, 0)),
            pl.BlockSpec((1, 1, 1, slash_rows), lambda g, i: (g, i, 0, 0)),
            pl.BlockSpec((1, 1, 1, vert_rows), lambda g, i: (g, i, 0, 0)),
        ],
        out_specs=pl.BlockSpec((BLOCK_TOKENS, cols), lambda g, i: (i, g)),
        out_shape=jax.ShapeDtypeStruct(q_all.shape, q_all.dtype),
        cost_estimate=cost,
        interpret=INTERPRET,
    )(q_all, ks, vs, kv, vv, ms, mv)


def local(queries, keys, values, slash, vertical):
    softmax_scale = HEAD_WIDTH ** (-0.5)
    seq_index = lax.axis_index("seq")
    head_index = lax.axis_index("head")
    q_all, k_all, v_all = (
        lax.all_to_all(queries, "head", split_axis=1, concat_axis=0, tiled=True),
        lax.all_to_all(keys, "head", split_axis=1, concat_axis=0, tiled=True),
        lax.all_to_all(values, "head", split_axis=1, concat_axis=0, tiled=True),
    )
    rows = q_all.shape[0]
    nbd = rows // BLOCK_TOKENS
    kv_local = k_all.shape[1] // HEAD_WIDTH
    query_group = q_all.shape[1] // HEAD_WIDTH // kv_local
    width = EXTRA_DIAGONALS + 1
    prev_k, prev_v = shifted((k_all, v_all), "seq", 1)
    window_k = jnp.concatenate([prev_k, k_all], 0).reshape(
        2 * nbd, BLOCK_TOKENS, kv_local, HEAD_WIDTH
    )
    window_v = jnp.concatenate([prev_v, v_all], 0).reshape(
        2 * nbd, BLOCK_TOKENS, kv_local, HEAD_WIDTH
    )
    own_k = k_all.reshape(nbd, BLOCK_TOKENS, kv_local, HEAD_WIDTH)
    own_v = v_all.reshape(nbd, BLOCK_TOKENS, kv_local, HEAD_WIDTH)
    first_head = head_index * kv_local
    local_slash = lax.dynamic_slice_in_dim(slash, first_head, kv_local, 0) + 1
    diagonal_offsets = jnp.concatenate([jnp.zeros((kv_local, 1), jnp.int32), local_slash], 1)
    local_vert = lax.dynamic_slice_in_dim(vertical, first_head, kv_local, 0)
    owner = local_vert // nbd
    inner = local_vert % nbd
    listed = local_vert.shape[1]
    earlier = jnp.arange(listed)[None, :] < jnp.arange(listed)[:, None]
    same_owner = owner[:, :, None] == owner[:, None, :]
    rank = jnp.sum(same_owner & earlier[None], axis=2)
    slots = 2
    mine = (owner == seq_index)[:, None, :] & (rank[:, None, :] == jnp.arange(slots)[None, :, None])
    pick = jnp.sum(jnp.where(mine, inner[:, None, :], 0), axis=2)
    pieces = []
    for group_member in range(kv_local):
        pieces.append(
            jnp.stack(
                [
                    own_k[:, :, group_member][pick[group_member]],
                    own_v[:, :, group_member][pick[group_member]],
                ],
                1,
            )
        )
    gathered = lax.all_gather(jnp.stack(pieces, 0), "seq", axis=0, tiled=False)
    heads_idx = jnp.arange(kv_local)[:, None]
    fetched = gathered[owner, heads_idx, rank]
    vert_keys = fetched[:, :, 0].reshape(kv_local, listed * BLOCK_TOKENS, HEAD_WIDTH)
    vert_vals = fetched[:, :, 1].reshape(kv_local, listed * BLOCK_TOKENS, HEAD_WIDTH)
    qblocks = seq_index * nbd + jnp.arange(nbd, dtype=jnp.int32)
    pad = jnp.zeros((nbd, SLASH_SLOTS - width, BLOCK_TOKENS, HEAD_WIDTH), k_all.dtype)
    slash_k, slash_v, slash_ok, vert_ok = [], [], [], []
    for group_member in range(kv_local):
        offset = diagonal_offsets[group_member]
        slab_k = window_k[:, :, group_member]
        slab_v = window_v[:, :, group_member]
        picked_k = jnp.stack(
            [lax.dynamic_slice_in_dim(slab_k, nbd - offset[j], nbd, 0) for j in range(width)], 1
        )
        picked_v = jnp.stack(
            [lax.dynamic_slice_in_dim(slab_v, nbd - offset[j], nbd, 0) for j in range(width)], 1
        )
        slash_k.append(jnp.concatenate([picked_k, pad], 1))
        slash_v.append(jnp.concatenate([picked_v, pad], 1))
        block_ok = qblocks[:, None] - offset[None, :] >= 0
        block_ok = jnp.concatenate(
            [block_ok, jnp.zeros((nbd, SLASH_SLOTS - width), jnp.bool_)], 1
        )
        slash_ok.append(jnp.repeat(block_ok, BLOCK_TOKENS, axis=1))
        dist = qblocks[:, None] - local_vert[group_member][None, :]
        hit = jnp.any(dist[:, :, None] == offset[None, None, :], axis=2)
        ok = (dist > 0) & jnp.logical_not(hit)
        vert_ok.append(jnp.repeat(ok, BLOCK_TOKENS, axis=1))
    ks = jnp.stack(slash_k, 0).reshape(kv_local, nbd, SLASH_SLOTS * BLOCK_TOKENS, HEAD_WIDTH)
    vs = jnp.stack(slash_v, 0).reshape(kv_local, nbd, SLASH_SLOTS * BLOCK_TOKENS, HEAD_WIDTH)
    ms = jnp.stack(slash_ok, 0).astype(jnp.int32)[:, :, None, :]
    mv = jnp.stack(vert_ok, 0).astype(jnp.int32)[:, :, None, :]
    return attend(q_all, ks, vs, vert_keys, vert_vals, ms, mv, query_group, softmax_scale)


def solution(mesh):
    return jax.shard_map(
        local,
        mesh=mesh,
        in_specs=(
            P(("seq", "head"), None),
            P(("seq", "head"), None),
            P(("seq", "head"), None),
            P(),
            P(),
        ),
        out_specs=P("seq", "head"),
        check_vma=False,
    )
```

time: 134 us -> 111 us (0.83)
  matrix products: 47.8 us -> 0 us
  waiting for transfers between devices: 4.47 us -> 26.7 us
  Pallas kernels: 0 us -> 13.1 us
  other arithmetic: 9.3 us -> 3.53 us
  starting transfers between devices: 23.8 us -> 21 us
    dot_general x32 -> x0, matrix products: 47.8 us -> none  [the longest x8 19.8 us: attend_head(): jnp.einsum('gxh,gvih->gxvi', query_rows, slash_keys_picked, preferred_ele...]
    all_gather x1, waiting for transfers between devices: 4.36 us -> 21.6 us  [local(): gathered = lax.all_gather(jnp.stack(pieces, 0), 'seq', axis=0, tiled=False)]
    pallas_call x0 -> x1, Pallas kernels: none -> 13.1 us  [attend(): pl.pallas_call(kernel, grid=(kv_local, nbd), in_specs=[pl.BlockSpec((BLOC...]
    reduce_sum x10 -> x0, other arithmetic: 5.7 us -> none  [the longest x2 4.68 us: attend_head(): jnp.sum(vertical_weight, axis=(2, 3))]
    all_to_all x1, waiting for transfers between devices: 0.01 us -> 4.78 us  [local(): lax.all_to_all(values, 'head', split_axis=1, concat_axis=0, tiled=True)]
    unnamed x98 -> x22, local copies, waits for them, and re-layouts: 3.7 us -> 1.19 us
    another operation x0 -> x2, other arithmetic: none -> 1.96 us  [the longest x1 1 us: local(): jnp.stack(slash_v, 0)]
    all_to_all x1, starting transfers between devices: 5.84 us -> 3.92 us  [local(): lax.all_to_all(values, 'head', split_axis=1, concat_axis=0, tiled=True)]
  transfers between devices with their start and end apart: 6 -> 6, of which waited for: 2 -> 3; matrix products, arithmetic and copies ran while one was open for 30% -> 21% of each run, Pallas kernels for 0% -> 0%
where the time goes in v2:
time: 111 us; the launch traced here: 110 us
  waiting for transfers between devices  26.7 us (24%)
  between operations  23.8 us (21%)
  local copies, waits for them, and re-layouts  22.3 us (20%)
  starting transfers between devices  21 us (19%)
  Pallas kernels  13.1 us (12%)
  other arithmetic  3.53 us (3%)
    all_gather x1, waiting for transfers between devices, local(): gathered = lax.all_gather(jnp.stack(pieces, 0), 'seq', axis=0, tiled=False)  21.6 us
    pallas_call x1, Pallas kernels, attend(): pl.pallas_call(kernel, grid=(kv_local, nbd), in_specs=[pl.BlockSpec((BLOC...  13.1 us
    ppermute x2, starting transfers between devices, shifted(): return lax.ppermute(value, axis, pairs)  7.58 us
    all_to_all x1, starting transfers between devices, local(): lax.all_to_all(keys, 'head', split_axis=1, concat_axis=0, tiled=True)  5.84 us
    all_to_all x1, waiting for transfers between devices, local(): lax.all_to_all(values, 'head', split_axis=1, concat_axis=0, tiled=True)  4.78 us
    all_to_all x1, starting transfers between devices, local(): lax.all_to_all(values, 'head', split_axis=1, concat_axis=0, tiled=True)  3.92 us
    all_to_all x1, starting transfers between devices, local(): lax.all_to_all(queries, 'head', split_axis=1, concat_axis=0, tiled=True)  3.6 us
    gather x1, local copies, waits for them, and re-layouts, local(): fetched = gathered[owner, heads_idx, rank]  3.2 us
  transfers between devices with their start and end apart: 6, of which 3 were waited for; matrix products, arithmetic and copies ran while one was open for 21% of the time, Pallas kernels for 0%

profile of v2, /device:TPU:1, one launch (start us, length us, event | category | flops | bytes accessed | tf_op | source)
XLA Modules:
  0.0 110.4 jit_solution(1972684375974150345)
XLA Ops:
  6.5 1.6 %copy.185 = bf16[8,4,8,256]{3,2,0,1:T(8,128)(2,1)} copy(bf16[8,4,8,256]{3,2,1,0:T(8,128)(2,1)} %bitcast.147) | data formatting | bytes 262144 | tf_op jit(solution)/shard_map/all_to_all | solution.py:93
  8.1 5.8 %all-to-all-start.1 = ((bf16[64,4,256]{2,0,1:T(8,128)(2,1)}), bf16[64,4,256]{2,0,1:T(8,128)(2,1)S(1)}, u32[]{:S(2)}, u32[]{:S(2)}) async-start(bf16[64,4,256]{2,0,1:T(8,128)(2,1)} %bitcast.130), calls=%async_computation.1 | async-start | bytes 262144 | tf_op jit(solution)/shard_map/all_to_all | solution.py:93
  14.0 0.7 and_select_fusion.1
  14.7 0.2 convert_reduce_fusion
  14.9 0.2 fusion.4
  15.0 1.6 %copy.184 = bf16[8,4,8,256]{3,2,0,1:T(8,128)(2,1)} copy(bf16[8,4,8,256]{3,2,1,0:T(8,128)(2,1)} %bitcast.148) | data formatting | bytes 262144 | tf_op jit(solution)/shard_map/all_to_all | solution.py:94
  16.6 1.9 %copy.183 = bf16[8,4,8,1024]{3,2,0,1:T(8,128)(2,1)} copy(bf16[8,4,8,1024]{3,2,1,0:T(8,128)(2,1)} %bitcast.145) | data formatting | bytes 1048576 | tf_op jit(solution)/shard_map/all_to_all | solution.py:92
  18.5 0.3 all-to-all-done.1
  18.8 3.9 %all-to-all-start.2 = ((bf16[64,4,256]{2,0,1:T(8,128)(2,1)}), bf16[64,4,256]{2,0,1:T(8,128)(2,1)S(1)}, u32[]{:S(2)}, u32[]{:S(2)}) async-start(bf16[64,4,256]{2,0,1:T(8,128)(2,1)} %bitcast.129), calls=%async_computation.2 | async-start | bytes 262144 | tf_op jit(solution)/shard_map/all_to_all | solution.py:94
  22.7 4.8 %all-to-all-done.2 = bf16[64,4,256]{2,0,1:T(8,128)(2,1)S(1)} async-done(((bf16[64,4,256]{2,0,1:T(8,128)(2,1)}), bf16[64,4,256]{2,0,1:T(8,128)(2,1)S(1)}, u32[]{:S(2)}, u32[]{:S(2)}) %all-to-all-start.2) | async-done | bytes 131104 | tf_op jit(solution)/shard_map/all_to_all | solution.py:94
  27.5 3.6 %all-to-all-start = ((bf16[64,4,1024]{2,0,1:T(8,128)(2,1)}), bf16[64,4,1024]{2,0,1:T(8,128)(2,1)S(1)}, u32[]{:S(2)}, u32[]{:S(2)}) async-start(bf16[64,4,1024]{2,0,1:T(8,128)(2,1)} %bitcast.128), calls=%async_computation | async-start | bytes 1048576 | tf_op jit(solution)/shard_map/all_to_all | solution.py:92
  31.2 0.2 fusion.21
  31.4 0.2 fusion.20
  31.6 0.6 gather_fusion.3
  32.2 0.6 gather_fusion.2
  32.8 0.6 gather_fusion.1
  33.4 0.6 gather_fusion
  34.0 0.7 copy.118
  34.7 0.1 fusion.5
  34.7 0.2 fusion.2
  35.0 0.1 compare_reduce_fusion
  35.1 0.1 not_and_fusion.1
  35.2 0.1 broadcast_in_dim.33
  35.3 0.1 stack.157
  35.4 0.1 broadcast_in_dim.34
  35.5 0.1 stack.158
  35.6 0.1 subtract_compare_fusion.1
  35.7 5.7 %collective-permute-start.1 = (bf16[256,256]{1,0:T(8,128)(2,1)S(1)}, bf16[256,256]{1,0:T(8,128)(2,1)S(1)}, u32[]{:S(2)}, u32[]{:S(2)}) collective-permute-start(bf16[256,256]{1,0:T(8,128)(2,1)S(1)} %bitcast.140), channel_id=1, source_target_pairs={{0,4},{4,8},{8,12},{12,16},{16,20},{20,24},{24,28},{28,32},{32,36}... | collective-permute-start | bytes 393224 | tf_op jit(solution)/shard_map/ppermute | solution.py:17
  41.4 0.7 fusion.22
  42.1 0.1 stack.155
  42.3 0.1 stack.154
  42.4 1.9 %collective-permute-start = (bf16[256,256]{1,0:T(8,128)(2,1)S(1)}, bf16[256,256]{1,0:T(8,128)(2,1)S(1)}, u32[]{:S(2)}, u32[]{:S(2)}) collective-permute-start(bf16[256,256]{1,0:T(8,128)(2,1)S(1)} %bitcast.137), channel_id=1, source_target_pairs={{0,4},{4,8},{8,12},{12,16},{16,20},{20,24},{24,28},{28,32},{32,36}... | collective-permute-start | bytes 393224 | tf_op jit(solution)/shard_map/ppermute | solution.py:17
  54.3 0.1 reshape.373
  54.4 0.6 copy.121.refs_5_
  55.0 0.7 copy.122.refs_6_
  55.9 0.5 fusion.16
  56.4 1.7 %constant_dynamic-slice_fusion.1 = (bf16[4,64,1,128]{3,2,1,0:T(2,128)(2,1)S(1)}, bf16[4,64,1,128]{3,2,1,0:T(2,128)(2,1)S(1)}, bf16[4,64,1,128]{3,2,1,0:T(2,128)(...) fusion(bf16[8,64,1,128]{3,2,1,0:T(2,128)(2,1)S(1)} %get-tuple-e, ...), kind=kLoop, calls=%fused_computation.54 | loop fusion | bytes 1048608 | tf_op jit(solution)/shard_map/dynamic_slice | solution.py:150
  58.1 0.2 fusion.17
  58.6 0.5 fusion.18
  59.1 1.7 %constant_dynamic-slice_fusion.9 = (bf16[4,64,1,128]{3,2,1,0:T(2,128)(2,1)S(1)}, bf16[4,64,1,128]{3,2,1,0:T(2,128)(2,1)S(1)}, bf16[4,64,1,128]{3,2,1,0:T(2,128)(...) fusion(bf16[8,64,1,128]{3,2,1,0:T(2,128)(2,1)S(1)} %get-tuple-e, ...), kind=kLoop, calls=%fused_computation.62 | loop fusion | bytes 1048608 | tf_op jit(solution)/shard_map/dynamic_slice | solution.py:147
  60.8 0.2 fusion.19
  61.3 1.0 pad_maximum_fusion.1.refs_2_
  62.3 1.0 pad_maximum_fusion.refs_1_
  63.3 21.6 %all-gather.3.cloned.1.call-done = bf16[64,2,2,64,128]{4,3,2,1,0:T(8,128)(2,1)} async-done(((bf16[2,2,2,64,128]{4,3,2,1,0:T(8,128)(2,1)}), bf16[64,2,2,64,128]{4,3,2,1,0:T(8,128)(2,1)}) %all-gather.3.cloned.1.call-update) | async-done | bytes 4194320 | tf_op jit(solution)/shard_map/all_gather | solution.py:134
  84.9 3.2 %gather_fusion.4 = bf16[64,2,64,128]{3,2,1,0:T(8,128)(2,1)S(1)} fusion(bf16[32,2,2,2,64,128]{5,4,3,2,1,0:T(8,128)(2,1)} %bitcast.142, s32[64]{0:T(128)S(1)} %reshape.373), kind=kCustom, calls=%fused_computation.4 | custom fusion | bytes 4195072 | tf_op jit(solution)/shard_map/gather | solution.py:136
  88.1 1.5 %fusion.15 = (bf16[2,32,1,64,128]{4,3,2,1,0:T(8,128)(2,1)}, bf16[2,32,1,64,128]{4,3,2,1,0:T(8,128)(2,1)}) fusion(bf16[2,32,2,64,128]{4,3,2,1,0:T(8,128)(2,1)S(1)} %bitcast.131), kind=kLoop, calls=%fused_computation.108 | loop fusion | bytes 4194304 | tf_op jit(solution)/shard_map/slice | solution.py:138
  89.7 0.8 copy-done
  90.5 13.1 %shard_map.55 = bf16[256,1024]{1,0:T(8,128)(2,1)} custom-call(bf16[256,1024]{1,0:T(8,128)(2,1)} %bitcast.146, bf16[2,4,384,128]{3,2,1,0:T(8,128)(2,1)} %pad_maximum_fusion.refs_1_, bf16[2,4,384,128]{3,2,1,0:T(8,128)(2,1)} %pad_maximum_fusion.1.refs_2_, bf16[2,2048,128]{2,1,0:T(8,128)(2,1)} %bitcast.144, bf16[2,2048,128]{2,1,0:T(8,128)(2,1)} %bitcast.143, ...), custom_call_target="tpu_custom_call" | custom-call | flops 2550136832 | bytes 4718592 | tf_op jit(solution)/shard_map/pallas_call | solution.py:68
  (59 shorter events, 1.3 us)
Async XLA Ops:
  8.1 10.7 %all-to-all-start.1 = ((bf16[64,4,256]{2,0,1:T(8,128)(2,1)}), bf16[64,4,256]{2,0,1:T(8,128)(2,1)S(1)}, u32[]{:S(2)}, u32[]{:S(2)}) async-start(bf16[64,4,256]{2,0,1:T(8,128)(2,1)} %bitcast.130), calls=%async_computation.1 | async-start | bytes 262144 | tf_op jit(solution)/shard_map/all_to_all | solution.py:93
  18.8 8.7 %all-to-all-start.2 = ((bf16[64,4,256]{2,0,1:T(8,128)(2,1)}), bf16[64,4,256]{2,0,1:T(8,128)(2,1)S(1)}, u32[]{:S(2)}, u32[]{:S(2)}) async-start(bf16[64,4,256]{2,0,1:T(8,128)(2,1)} %bitcast.129), calls=%async_computation.2 | async-start | bytes 262144 | tf_op jit(solution)/shard_map/all_to_all | solution.py:94
  27.5 7.1 %copy-start.1 = (s32[8,4]{0,1:T(4,128)S(1)}, s32[8,4]{0,1:T(4,128)}, u32[]{:S(2)}) copy-start(s32[8,4]{0,1:T(4,128)} %param.8) | copy-start | bytes 388
  27.5 62.1 %all-to-all-start = ((bf16[64,4,1024]{2,0,1:T(8,128)(2,1)}), bf16[64,4,1024]{2,0,1:T(8,128)(2,1)S(1)}, u32[]{:S(2)}, u32[]{:S(2)}) async-start(bf16[64,4,1024]{2,0,1:T(8,128)(2,1)} %bitcast.128), calls=%async_computation | async-start | bytes 1048576 | tf_op jit(solution)/shard_map/all_to_all | solution.py:92
  31.1 53.8 %all-gather.3.cloned.1.call-start = ((), (), s32[]{:S(2)}) async-start(), calls=%async_computation.3 | async-start | bytes 4325376 | tf_op jit(solution)/shard_map/all_gather | solution.py:134
  35.7 20.0 %collective-permute-start.1 = (bf16[256,256]{1,0:T(8,128)(2,1)S(1)}, bf16[256,256]{1,0:T(8,128)(2,1)S(1)}, u32[]{:S(2)}, u32[]{:S(2)}) collective-permute-start(bf16[256,256]{1,0:T(8,128)(2,1)S(1)} %bitcast.140), channel_id=1, source_target_pairs={{0,4},{4,8},{8,12},{12,16},{16,20},{20,24},{24,28},{28,32},{32,36}... | collective-permute-start | bytes 393224 | tf_op jit(solution)/shard_map/ppermute | solution.py:17
  42.4 13.4 %collective-permute-start = (bf16[256,256]{1,0:T(8,128)(2,1)S(1)}, bf16[256,256]{1,0:T(8,128)(2,1)S(1)}, u32[]{:S(2)}, u32[]{:S(2)}) collective-permute-start(bf16[256,256]{1,0:T(8,128)(2,1)S(1)} %bitcast.137), channel_id=1, source_target_pairs={{0,4},{4,8},{8,12},{12,16},{16,20},{20,24},{24,28},{28,32},{32,36}... | collective-permute-start | bytes 393224 | tf_op jit(solution)/shard_map/ppermute | solution.py:17
  89.7 0.8 copy-start
Sparse Core Ops, SparseCore 0:
  34.8 50.0 all-gather.2

commit v3 on v2

--- a/solution.py
+++ b/solution.py
@@ -2,7 +2,7 @@
 import jax.numpy as jnp
 from jax import lax
 from jax.experimental import pallas as pl
-from jax.sharding import PartitionSpec as P
+from jax.sharding import Mesh, PartitionSpec as P
 
 HEAD_WIDTH = 128
 BLOCK_TOKENS = 64
@@ -86,19 +86,20 @@
 
 def local(queries, keys, values, slash, vertical):
     softmax_scale = HEAD_WIDTH ** (-0.5)
-    seq_index = lax.axis_index("seq")
+    core_index = lax.axis_index("core")
+    seq_index = lax.axis_index("chip") * lax.axis_size("core") + core_index
     head_index = lax.axis_index("head")
-    q_all, k_all, v_all = (
-        lax.all_to_all(queries, "head", split_axis=1, concat_axis=0, tiled=True),
-        lax.all_to_all(keys, "head", split_axis=1, concat_axis=0, tiled=True),
-        lax.all_to_all(values, "head", split_axis=1, concat_axis=0, tiled=True),
-    )
+    both = jnp.stack([keys, values], 1).reshape(keys.shape[0], 2, lax.axis_size("head"), -1)
+    both = lax.all_to_all(both, "head", split_axis=2, concat_axis=0, tiled=True)
+    k_all = both[:, 0].reshape(both.shape[0], -1)
+    v_all = both[:, 1].reshape(both.shape[0], -1)
+    q_all = lax.all_to_all(queries, "head", split_axis=1, concat_axis=0, tiled=True)
     rows = q_all.shape[0]
     nbd = rows // BLOCK_TOKENS
     kv_local = k_all.shape[1] // HEAD_WIDTH
     query_group = q_all.shape[1] // HEAD_WIDTH // kv_local
     width = EXTRA_DIAGONALS + 1
-    prev_k, prev_v = shifted((k_all, v_all), "seq", 1)
+    prev_k, prev_v = shifted((k_all, v_all), ("chip", "core"), 1)
     window_k = jnp.concatenate([prev_k, k_all], 0).reshape(
         2 * nbd, BLOCK_TOKENS, kv_local, HEAD_WIDTH
     )
@@ -131,9 +132,14 @@
                 1,
             )
         )
-    gathered = lax.all_gather(jnp.stack(pieces, 0), "seq", axis=0, tiled=False)
+    half = lax.all_gather(jnp.stack(pieces, 0), "chip", axis=0, tiled=False)
+    cores = lax.axis_size("core")
+    other = lax.ppermute(half, "core", [(c, cores - 1 - c) for c in range(cores)])
+    gathered = jnp.concatenate([half, other], 0)
+    chips = half.shape[0]
+    source = jnp.where(owner % cores == core_index, owner // cores, chips + owner // cores)
     heads_idx = jnp.arange(kv_local)[:, None]
-    fetched = gathered[owner, heads_idx, rank]
+    fetched = gathered[source, heads_idx, rank]
     vert_keys = fetched[:, :, 0].reshape(kv_local, listed * BLOCK_TOKENS, HEAD_WIDTH)
     vert_vals = fetched[:, :, 1].reshape(kv_local, listed * BLOCK_TOKENS, HEAD_WIDTH)
     qblocks = seq_index * nbd + jnp.arange(nbd, dtype=jnp.int32)
@@ -168,16 +174,19 @@
 
 
 def solution(mesh):
+    cores = 2
+    devices = mesh.devices.reshape(mesh.shape["seq"] // cores, cores, mesh.shape["head"])
+    split = Mesh(devices, ("chip", "core", "head"))
     return jax.shard_map(
         local,
-        mesh=mesh,
+        mesh=split,
         in_specs=(
-            P(("seq", "head"), None),
-            P(("seq", "head"), None),
-            P(("seq", "head"), None),
+            P(("chip", "core", "head"), None),
+            P(("chip", "core", "head"), None),
+            P(("chip", "core", "head"), None),
             P(),
             P(),
         ),
-        out_specs=P("seq", "head"),
+        out_specs=P(("chip", "core"), "head"),
         check_vma=False,
     )

time: 111 us -> 124 us (1.12)
  waiting for transfers between devices: 26.7 us -> 41.7 us
  other arithmetic: 3.53 us -> 6.01 us
  starting transfers between devices: 21 us -> 18.7 us
  local copies, waits for them, and re-layouts: 22.3 us -> 20.3 us
    all_gather x1, waiting for transfers between devices: 21.6 us -> 39 us  [local(): half = lax.all_gather(jnp.stack(pieces, 0), 'chip', axis=0, tiled=False)]
    all_to_all x2 -> x1, waiting for transfers between devices: 5.09 us -> 0.01 us  [local(): both = lax.all_to_all(both, 'head', split_axis=2, concat_axis=0, tiled=True)]
    all_to_all x2 -> x1, starting transfers between devices: 9.77 us -> 5.84 us  [local(): both = lax.all_to_all(both, 'head', split_axis=2, concat_axis=0, tiled=True)]
    all_to_all x2 -> x1, local copies, waits for them, and re-layouts: 3.13 us -> 0.02 us  [local(): both = lax.all_to_all(both, 'head', split_axis=2, concat_axis=0, tiled=True)]
    another operation x1 -> x6, local copies, waits for them, and re-layouts: 0.66 us -> 3.48 us  [the longest x3 2.75 us: local(): jnp.stack([keys, values], 1)]
    concatenate x1 -> x2, other arithmetic: 0.01 us -> 2.33 us  [the longest x1 2.3 us: local(): gathered = jnp.concatenate([half, other], 0)]
    ppermute x0 -> x1, starting transfers between devices: none -> 2.22 us  [local(): lax.ppermute(half, 'core', [(c, cores - 1 - c) for c in range(cores)])]
    ppermute x0 -> x1, waiting for transfers between devices: none -> 1.67 us  [local(): lax.ppermute(half, 'core', [(c, cores - 1 - c) for c in range(cores)])]
  transfers between devices with their start and end apart: 6 -> 6, of which waited for: 3 -> 3; matrix products, arithmetic and copies ran while one was open for 21% -> 18% of each run, Pallas kernels for 0% -> 0%
where the time goes in v3:
time: 124 us
  waiting for transfers between devices  41.7 us (34%)
  between operations  23.6 us (19%)
  local copies, waits for them, and re-layouts  20.3 us (16%)
  starting transfers between devices  18.7 us (15%)
  Pallas kernels  13.1 us (11%)
  other arithmetic  6.01 us (5%)
    all_gather x1, waiting for transfers between devices, local(): half = lax.all_gather(jnp.stack(pieces, 0), 'chip', axis=0, tiled=False)  39 us
    pallas_call x1, Pallas kernels, attend(): pl.pallas_call(kernel, grid=(kv_local, nbd), in_specs=[pl.BlockSpec((BLOC...  13.1 us
    ppermute x2, starting transfers between devices, shifted(): return lax.ppermute(value, axis, pairs)  6.44 us
    all_to_all x1, starting transfers between devices, local(): both = lax.all_to_all(both, 'head', split_axis=2, concat_axis=0, tiled=True)  5.84 us
    all_to_all x1, starting transfers between devices, local(): lax.all_to_all(queries, 'head', split_axis=1, concat_axis=0, tiled=True)  4.24 us
    gather x1, local copies, waits for them, and re-layouts, local(): fetched = gathered[source, heads_idx, rank]  3.2 us
    another operation x3, local copies, waits for them, and re-layouts, local(): jnp.stack([keys, values], 1)  2.75 us
  transfers between devices with their start and end apart: 6, of which 3 were waited for; matrix products, arithmetic and copies ran while one was open for 18% of the time, Pallas kernels for 0%

profile of v3, /device:TPU:1, one launch (start us, length us, event | category | flops | bytes accessed | tf_op | source)
XLA Modules:
  0.0 123.6 jit_solution(11419082150494457386)
XLA Ops:
  6.5 1.0 stack.128
  7.6 1.0 stack.129
  8.6 0.2 pad_maximum_fusion.3
  8.8 0.7 copy.84
  9.5 5.8 %all-to-all-start.1 = ((bf16[64,2,4,256]{3,0,1,2:T(8,128)(2,1)}), bf16[64,2,4,256]{3,0,1,2:T(8,128)(2,1)S(1)}, u32[]{:S(2)}, u32[]{:S(2)}) async-start(bf16[64,2,4,256]{3,0,1,2:T(8,128)(2,1)} %copy.84), calls=%async_computation.1 | async-start | bytes 524288 | tf_op jit(solution)/shard_map/all_to_all | solution.py:93
  15.4 0.6 fusion.23
  25.9 0.2 fusion.2
  26.1 0.7 and_select_fusion.3
  26.8 0.2 convert_reduce_fusion
  27.0 0.1 fusion.4
  27.2 0.1 reshape.362
  27.4 0.1 compare_reduce_fusion
  27.6 0.1 broadcast_in_dim.33
  27.7 0.1 stack.169
  27.8 0.1 broadcast_in_dim.34
  27.9 0.1 stack.170
  28.0 0.7 copy.96.refs_6_
  28.8 0.1 stack.166
  28.9 0.1 stack.167
  29.0 0.6 copy.95.refs_5_
  29.7 0.8 copy.153
  30.5 4.2 %all-to-all-start = ((bf16[64,4,1024]{2,0,1:T(8,128)(2,1)}), bf16[64,4,1024]{2,0,1:T(8,128)(2,1)S(1)}, u32[]{:S(2)}, u32[]{:S(2)}) async-start(bf16[64,4,1024]{2,0,1:T(8,128)(2,1)} %bitcast.133), calls=%async_computation | async-start | bytes 1048576 | tf_op jit(solution)/shard_map/all_to_all | solution.py:96
  34.9 0.2 fusion.21
  35.1 0.2 fusion.22
  35.3 0.6 gather_fusion
  35.9 0.6 gather_fusion.1
  36.5 0.6 gather_fusion.2
  37.0 0.6 gather_fusion.3
  37.6 4.5 %collective-permute-start.1 = (bf16[256,256]{1,0:T(8,128)(2,1)S(1)}, bf16[256,256]{1,0:T(8,128)(2,1)S(1)}, u32[]{:S(2)}, u32[]{:S(2)}) collective-permute-start(bf16[256,256]{1,0:T(8,128)(2,1)S(1)} %get-tuple-element.15), channel_id=1, source_target_pairs={{0,4},{4,8},{8,12},{12,16},{16,20},{20,24},{24,28},{28,32},{32,36}... | collective-permute-start | bytes 393224 | tf_op jit(solution)/shard_map/ppermute | solution.py:17
  42.1 1.9 %collective-permute-start = (bf16[256,256]{1,0:T(8,128)(2,1)S(1)}, bf16[256,256]{1,0:T(8,128)(2,1)S(1)}, u32[]{:S(2)}, u32[]{:S(2)}) collective-permute-start(bf16[256,256]{1,0:T(8,128)(2,1)S(1)} %get-tuple-element.14), channel_id=1, source_target_pairs={{0,4},{4,8},{8,12},{12,16},{16,20},{20,24},{24,28},{28,32},{32,36}... | collective-permute-start | bytes 393224 | tf_op jit(solution)/shard_map/ppermute | solution.py:17
  44.1 0.7 copy.92
  44.9 1.1 collective-permute-done
  46.1 0.5 fusion.17
  46.5 1.7 %constant_dynamic-slice_fusion.1 = (bf16[4,64,1,128]{3,2,1,0:T(2,128)(2,1)S(1)}, bf16[4,64,1,128]{3,2,1,0:T(2,128)(2,1)S(1)}, bf16[4,64,1,128]{3,2,1,0:T(2,128)(...) fusion(bf16[8,64,1,128]{3,2,1,0:T(2,128)(2,1)S(1)} %get-tuple-e, ...), kind=kLoop, calls=%fused_computation.54 | loop fusion | bytes 1048608 | tf_op jit(solution)/shard_map/dynamic_slice | solution.py:156
  48.2 0.2 fusion.18
  48.6 0.5 fusion.19
  49.1 1.2 constant_dynamic-slice_fusion.9
  50.3 0.2 fusion.20
  50.6 39.0 %all-gather.3.cloned.1.call-done = bf16[32,2,2,64,128]{4,3,2,1,0:T(8,128)(2,1)} async-done(((bf16[2,2,2,64,128]{4,3,2,1,0:T(8,128)(2,1)}), bf16[32,2,2,64,128]{4,3,2,1,0:T(8,128)(2,1)}) %all-gather.3.cloned.1.call-update) | async-done | bytes 2097168 | tf_op jit(solution)/shard_map/all_gather | solution.py:135
  89.5 2.2 %collective-permute-start.2 = (bf16[16,2,2,2,64,128]{5,4,3,2,1,0:T(8,128)(2,1)}, bf16[16,2,2,2,64,128]{5,4,3,2,1,0:T(8,128)(2,1)S(1)}, u32[]{:S(2)}, u32[]{:S(2)}) collective-permute-start(bf16[16,2,2,2,64,128]{5,4,3,2,1,0:T(8,128)(2,1)} %bitcast.135), channel_id=1, source_target_pairs={{0,4},{4,0},{1,5},{5,1},{2,6},{6,2},{3,7},{7,3},{8,12},{12,8},{9,1... | collective-permute-start | bytes 6291464 | tf_op jit(solution)/shard_map/ppermute | solution.py:137
  92.1 1.0 pad_maximum_fusion.2.refs_2_
  93.1 1.0 pad_maximum_fusion.1.refs_1_
  94.1 1.7 %collective-permute-done.2 = bf16[16,2,2,2,64,128]{5,4,3,2,1,0:T(8,128)(2,1)S(1)} collective-permute-done((bf16[16,2,2,2,64,128]{5,4,3,2,1,0:T(8,128)(2,1)}, bf16[16,2,2,2,64,128]{5,4,3,2,1,0:T(8,128)(2,1)S(1)}, u32[]{:S(2)}, u32[]{:S(2)}) %collective-permute-start.2) | collective-permute-done | bytes 2097184 | tf_op jit(solution)/shard_map/ppermute | solution.py:137
  95.8 2.3 %pad_maximum_fusion = bf16[32,2,2,2,64,128]{5,4,3,2,1,0:T(8,128)(2,1)} fusion(bf16[16,2,2,2,64,128]{5,4,3,2,1,0:T(8,128)(2,1)S(1)} %collective-permute-done.2, bf16[16,2,2,2,64,128]{5,4,3,2,1,0:T(8,128)(2,1)S(1)} %bitcast.136), kind=kLoop, calls=%fused_computation.5 | loop fusion | flops 2097152 | bytes 8388608 | tf_op jit(solution)/shard_map/concatenate | solution.py:138
  98.1 3.2 %gather_fusion.4 = bf16[64,2,64,128]{3,2,1,0:T(8,128)(2,1)S(1)} fusion(bf16[32,2,2,2,64,128]{5,4,3,2,1,0:T(8,128)(2,1)} %pad_maximum_fusion, s32[64]{0:T(128)S(1)} %reshape.362), kind=kCustom, calls=%fused_computation.4 | custom fusion | bytes 4195072 | tf_op jit(solution)/shard_map/gather | solution.py:142
  101.3 1.6 %fusion.15 = (bf16[2,32,1,64,128]{4,3,2,1,0:T(8,128)(2,1)}, bf16[2,32,1,64,128]{4,3,2,1,0:T(8,128)(2,1)}) fusion(bf16[2,32,2,64,128]{4,3,2,1,0:T(8,128)(2,1)S(1)} %bitcast.134), kind=kLoop, calls=%fused_computation.116 | loop fusion | bytes 4194304 | tf_op jit(solution)/shard_map/slice | solution.py:144
  102.8 0.8 copy-done.2
  103.6 13.1 %shard_map.55 = bf16[256,1024]{1,0:T(8,128)(2,1)} custom-call(bf16[256,1024]{1,0:T(8,128)(2,1)} %bitcast.145, bf16[2,4,384,128]{3,2,1,0:T(8,128)(2,1)} %pad_maximum_fusion.1.refs_1_, bf16[2,4,384,128]{3,2,1,0:T(8,128)(2,1)} %pad_maximum_fusion.2.refs_2_, bf16[2,2048,128]{2,1,0:T(8,128)(2,1)} %bitcast.143, bf16[2,2048,128]{2,1,0:T(8,128)(2,1)} %bitcast.142, ...), custom_call_target="tpu_custom_call" | custom-call | flops 2550136832 | bytes 4718592 | tf_op jit(solution)/shard_map/pallas_call | solution.py:68
  (68 shorter events, 1.5 us)
Async XLA Ops:
  6.5 8.8 %copy-start.3 = (s32[8,4]{0,1:T(4,128)S(1)}, s32[8,4]{0,1:T(4,128)}, u32[]{:S(2)}) copy-start(s32[8,4]{0,1:T(4,128)} %param.8) | copy-start | bytes 388
  6.5 23.1 %copy-start.1 = (bf16[64,4096]{1,0:T(8,128)(2,1)S(1)}, bf16[64,4096]{1,0:T(8,128)(2,1)}, u32[]{:S(2)}) copy-start(bf16[64,4096]{1,0:T(8,128)(2,1)} %param.5) | copy-start | bytes 1572868
  9.5 21.0 %all-to-all-start.1 = ((bf16[64,2,4,256]{3,0,1,2:T(8,128)(2,1)}), bf16[64,2,4,256]{3,0,1,2:T(8,128)(2,1)S(1)}, u32[]{:S(2)}, u32[]{:S(2)}) async-start(bf16[64,2,4,256]{3,0,1,2:T(8,128)(2,1)} %copy.84), calls=%async_computation.1 | async-start | bytes 524288 | tf_op jit(solution)/shard_map/all_to_all | solution.py:93
  30.5 72.3 %all-to-all-start = ((bf16[64,4,1024]{2,0,1:T(8,128)(2,1)}), bf16[64,4,1024]{2,0,1:T(8,128)(2,1)S(1)}, u32[]{:S(2)}, u32[]{:S(2)}) async-start(bf16[64,4,1024]{2,0,1:T(8,128)(2,1)} %bitcast.133), calls=%async_computation | async-start | bytes 1048576 | tf_op jit(solution)/shard_map/all_to_all | solution.py:96
  34.7 54.8 %all-gather.3.cloned.1.call-start = ((), (), s32[]{:S(2)}) async-start(), calls=%async_computation.2 | async-start | bytes 2228224 | tf_op jit(solution)/shard_map/all_gather | solution.py:135
  37.6 7.2 %collective-permute-start.1 = (bf16[256,256]{1,0:T(8,128)(2,1)S(1)}, bf16[256,256]{1,0:T(8,128)(2,1)S(1)}, u32[]{:S(2)}, u32[]{:S(2)}) collective-permute-start(bf16[256,256]{1,0:T(8,128)(2,1)S(1)} %get-tuple-element.15), channel_id=1, source_target_pairs={{0,4},{4,8},{8,12},{12,16},{16,20},{20,24},{24,28},{28,32},{32,36}... | collective-permute-start | bytes 393224 | tf_op jit(solution)/shard_map/ppermute | solution.py:17
  42.1 3.9 %collective-permute-start = (bf16[256,256]{1,0:T(8,128)(2,1)S(1)}, bf16[256,256]{1,0:T(8,128)(2,1)S(1)}, u32[]{:S(2)}, u32[]{:S(2)}) collective-permute-start(bf16[256,256]{1,0:T(8,128)(2,1)S(1)} %get-tuple-element.14), channel_id=1, source_target_pairs={{0,4},{4,8},{8,12},{12,16},{16,20},{20,24},{24,28},{28,32},{32,36}... | collective-permute-start | bytes 393224 | tf_op jit(solution)/shard_map/ppermute | solution.py:17
  89.5 6.2 %collective-permute-start.2 = (bf16[16,2,2,2,64,128]{5,4,3,2,1,0:T(8,128)(2,1)}, bf16[16,2,2,2,64,128]{5,4,3,2,1,0:T(8,128)(2,1)S(1)}, u32[]{:S(2)}, u32[]{:S(2)}) collective-permute-start(bf16[16,2,2,2,64,128]{5,4,3,2,1,0:T(8,128)(2,1)} %bitcast.135), channel_id=1, source_target_pairs={{0,4},{4,0},{1,5},{5,1},{2,6},{6,2},{3,7},{7,3},{8,12},{12,8},{9,1... | collective-permute-start | bytes 6291464 | tf_op jit(solution)/shard_map/ppermute | solution.py:137
  92.0 3.7 %copy-start = (bf16[32,2,2,64,128]{4,3,2,1,0:T(8,128)(2,1)S(1)}, bf16[32,2,2,64,128]{4,3,2,1,0:T(8,128)(2,1)}, u32[]{:S(2)}) copy-start(bf16[32,2,2,64,128]{4,3,2,1,0:T(8,128)(2,1)} %all-gather.3.cloned.1.call-done) | copy-start | bytes 6291460
  102.8 0.8 copy-start.2
Sparse Core Ops, SparseCore 0:
  44.9 44.5 all-gather.2

commit v4 on v3

--- a/solution.py
+++ b/solution.py
@@ -89,11 +89,22 @@
     core_index = lax.axis_index("core")
     seq_index = lax.axis_index("chip") * lax.axis_size("core") + core_index
     head_index = lax.axis_index("head")
-    both = jnp.stack([keys, values], 1).reshape(keys.shape[0], 2, lax.axis_size("head"), -1)
-    both = lax.all_to_all(both, "head", split_axis=2, concat_axis=0, tiled=True)
-    k_all = both[:, 0].reshape(both.shape[0], -1)
-    v_all = both[:, 1].reshape(both.shape[0], -1)
-    q_all = lax.all_to_all(queries, "head", split_axis=1, concat_axis=0, tiled=True)
+    heads = lax.axis_size("head")
+    tokens = queries.shape[0]
+    joined = jnp.concatenate(
+        [
+            queries.reshape(tokens, heads, -1),
+            keys.reshape(tokens, heads, -1),
+            values.reshape(tokens, heads, -1),
+        ],
+        2,
+    )
+    joined = lax.all_to_all(joined, "head", split_axis=1, concat_axis=0, tiled=True)
+    q_cols = queries.shape[1] // heads
+    k_cols = keys.shape[1] // heads
+    q_all = joined[:, 0, :q_cols]
+    k_all = joined[:, 0, q_cols : q_cols + k_cols]
+    v_all = joined[:, 0, q_cols + k_cols :]
     rows = q_all.shape[0]
     nbd = rows // BLOCK_TOKENS
     kv_local = k_all.shape[1] // HEAD_WIDTH
@@ -132,14 +143,9 @@
                 1,
             )
         )
-    half = lax.all_gather(jnp.stack(pieces, 0), "chip", axis=0, tiled=False)
-    cores = lax.axis_size("core")
-    other = lax.ppermute(half, "core", [(c, cores - 1 - c) for c in range(cores)])
-    gathered = jnp.concatenate([half, other], 0)
-    chips = half.shape[0]
-    source = jnp.where(owner % cores == core_index, owner // cores, chips + owner // cores)
+    gathered = lax.all_gather(jnp.stack(pieces, 0), ("chip", "core"), axis=0, tiled=False)
     heads_idx = jnp.arange(kv_local)[:, None]
-    fetched = gathered[source, heads_idx, rank]
+    fetched = gathered[owner, heads_idx, rank]
     vert_keys = fetched[:, :, 0].reshape(kv_local, listed * BLOCK_TOKENS, HEAD_WIDTH)
     vert_vals = fetched[:, :, 1].reshape(kv_local, listed * BLOCK_TOKENS, HEAD_WIDTH)
     qblocks = seq_index * nbd + jnp.arange(nbd, dtype=jnp.int32)

time: 124 us -> 106 us (0.85)
  waiting for transfers between devices: 41.7 us -> 34.2 us
  starting transfers between devices: 18.7 us -> 11.7 us
  local copies, waits for them, and re-layouts: 20.3 us -> 18.2 us
  other arithmetic: 6.01 us -> 4.49 us
    all_gather x1, waiting for transfers between devices: 39 us -> 33.2 us  [local(): lax.all_gather(jnp.stack(pieces, 0), ('chip', 'core'), axis=0, tiled=False)]
    all_to_all x2 -> x1, starting transfers between devices: 10.1 us -> 5.84 us  [local(): lax.all_to_all(joined, 'head', split_axis=1, concat_axis=0, tiled=True)]
    another operation x4 -> x1, local copies, waits for them, and re-layouts: 3.4 us -> 0.66 us  [local(): jnp.stack(pieces, 0)]
    ppermute x1 -> x0, starting transfers between devices: 2.22 us -> none  [local(): lax.ppermute(half, 'core', [(c, cores - 1 - c) for c in range(cores)])]
    reshape x0 -> x2, local copies, waits for them, and re-layouts: none -> 2.07 us  [the longest x1 1.08 us: local(): queries.reshape(tokens, heads, -1)]
    ppermute x1 -> x0, waiting for transfers between devices: 1.67 us -> none  [local(): lax.ppermute(half, 'core', [(c, cores - 1 - c) for c in range(cores)])]
    concatenate x2, other arithmetic: 2.33 us -> 0.98 us  [the longest x1 0.97 us: local(): jnp.concatenate([queries.reshape(tokens, heads, -1), keys.reshape(tokens,...]
  transfers between devices with their start and end apart: 6 -> 4, of which waited for: 3 -> 2; matrix products, arithmetic and copies ran while one was open for 18% -> 11% of each run, Pallas kernels for 0% -> 0%
where the time goes in v4:
time: 106 us
  waiting for transfers between devices  34.2 us (32%)
  between operations  24.1 us (23%)
  local copies, waits for them, and re-layouts  18.2 us (17%)
  Pallas kernels  13.1 us (12%)
  starting transfers between devices  11.7 us (11%)
  other arithmetic  4.49 us (4%)
    all_gather x1, waiting for transfers between devices, local(): lax.all_gather(jnp.stack(pieces, 0), ('chip', 'core'), axis=0, tiled=False)  33.2 us
    pallas_call x1, Pallas kernels, attend(): pl.pallas_call(kernel, grid=(kv_local, nbd), in_specs=[pl.BlockSpec((BLOC...  13.1 us
    ppermute x2, starting transfers between devices, shifted(): return lax.ppermute(value, axis, pairs)  5.87 us
    all_to_all x1, starting transfers between devices, local(): lax.all_to_all(joined, 'head', split_axis=1, concat_axis=0, tiled=True)  5.84 us
    gather x1, local copies, waits for them, and re-layouts, local(): fetched = gathered[owner, heads_idx, rank]  3.2 us
  transfers between devices with their start and end apart: 4, of which 2 were waited for; matrix products, arithmetic and copies ran while one was open for 11% of the time, Pallas kernels for 0%

profile of v4, /device:TPU:1, one launch (start us, length us, event | category | flops | bytes accessed | tf_op | source)
XLA Modules:
  0.0 105.8 jit_solution(7878189908006543767)
XLA Ops:
  6.5 1.1 %copy.211 = bf16[8,4,8,1024]{3,2,0,1:T(8,128)(2,1)S(1)} copy(bf16[8,4,8,1024]{3,2,1,0:T(8,128)(2,1)} %bitcast.186) | data formatting | bytes 1048576 | tf_op jit(solution)/shard_map/reshape | solution.py:96
  7.6 1.0 copy_bitcast_fusion.1
  8.6 1.0 pad_maximum_fusion
  9.6 5.8 %all-to-all-start = ((bf16[64,4,1536]{2,0,1:T(8,128)(2,1)}), bf16[64,4,1536]{2,0,1:T(8,128)(2,1)S(1)}, u32[]{:S(2)}, u32[]{:S(2)}) async-start(bf16[64,4,1536]{2,0,1:T(8,128)(2,1)} %pad_maximum_fusion), calls=%async_computation | async-start | bytes 1572864 | tf_op jit(solution)/shard_map/all_to_all | solution.py:102
  15.5 0.1 fusion.23
  15.6 0.2 fusion.20
  15.7 0.7 and_select_fusion.1
  16.5 0.2 convert_reduce_fusion
  16.7 0.1 subtract_compare_fusion.1
  16.7 0.7 fusion.41
  27.7 0.1 broadcast_in_dim.32
  27.7 0.1 stack.155
  27.9 0.1 stack.154
  28.0 0.1 reshape.366
  28.1 0.6 copy.109.refs_5_
  28.7 0.1 fusion.22
  29.0 0.2 fusion.40
  29.2 0.2 fusion.39
  29.5 0.6 gather_fusion.1
  30.0 0.6 gather_fusion
  30.6 0.6 gather_fusion.3
  31.2 0.6 gather_fusion.2
  31.8 0.7 copy.106
  32.6 0.1 compare_reduce_fusion
  32.6 0.1 not_and_fusion.1
  32.7 0.1 broadcast_in_dim.33
  32.8 0.1 stack.157
  32.9 0.1 broadcast_in_dim.34
  33.0 0.1 stack.158
  33.1 0.7 copy.110.refs_6_
  33.8 3.9 %collective-permute-start = (bf16[256,256]{1,0:T(8,128)(2,1)S(1)}, bf16[256,256]{1,0:T(8,128)(2,1)S(1)}, u32[]{:S(2)}, u32[]{:S(2)}) collective-permute-start(bf16[256,256]{1,0:T(8,128)(2,1)S(1)} %get-tuple-element.14), channel_id=1, source_target_pairs={{0,4},{4,8},{8,12},{12,16},{16,20},{20,24},{24,28},{28,32},{32,36}... | collective-permute-start | bytes 393224 | tf_op jit(solution)/shard_map/ppermute | solution.py:17
  37.8 1.9 %collective-permute-start.1 = (bf16[256,256]{1,0:T(8,128)(2,1)S(1)}, bf16[256,256]{1,0:T(8,128)(2,1)S(1)}, u32[]{:S(2)}, u32[]{:S(2)}) collective-permute-start(bf16[256,256]{1,0:T(8,128)(2,1)S(1)} %get-tuple-element.15), channel_id=1, source_target_pairs={{0,4},{4,8},{8,12},{12,16},{16,20},{20,24},{24,28},{28,32},{32,36}... | collective-permute-start | bytes 393224 | tf_op jit(solution)/shard_map/ppermute | solution.py:17
  39.7 0.9 slice_bitcast_fusion.refs_0_
  40.7 1.0 collective-permute-done.1
  41.7 0.4 fusion.35
  42.1 0.6 constant_dynamic-slice_fusion.5
  42.7 0.2 fusion.36
  43.0 0.5 fusion.37
  43.5 0.6 constant_dynamic-slice_fusion.13
  44.1 0.2 fusion.38
  44.4 0.6 constant_dynamic-slice_fusion.9
  45.2 0.6 constant_dynamic-slice_fusion.1
  45.9 1.0 pad_maximum_fusion.1.refs_1_
  46.9 1.0 pad_maximum_fusion.2.refs_2_
  47.9 33.2 %all-gather.3.cloned.1.call-done = bf16[64,2,2,64,128]{4,3,2,1,0:T(8,128)(2,1)} async-done(((bf16[2,2,2,64,128]{4,3,2,1,0:T(8,128)(2,1)}), bf16[64,2,2,64,128]{4,3,2,1,0:T(8,128)(2,1)}) %all-gather.3.cloned.1.call-update) | async-done | bytes 4194320 | tf_op jit(solution)/shard_map/all_gather | solution.py:146
  81.1 3.2 %gather_fusion.4 = bf16[64,2,64,128]{3,2,1,0:T(8,128)(2,1)S(1)} fusion(bf16[32,2,2,2,64,128]{5,4,3,2,1,0:T(8,128)(2,1)} %bitcast.183, s32[64]{0:T(128)S(1)} %reshape.366), kind=kCustom, calls=%fused_computation.4 | custom fusion | bytes 4195072 | tf_op jit(solution)/shard_map/gather | solution.py:148
  84.3 1.6 %fusion.33 = (bf16[2,32,1,64,128]{4,3,2,1,0:T(8,128)(2,1)}, bf16[2,32,1,64,128]{4,3,2,1,0:T(8,128)(2,1)}) fusion(bf16[2,32,2,64,128]{4,3,2,1,0:T(8,128)(2,1)S(1)} %bitcast.175), kind=kLoop, calls=%fused_computation.130 | loop fusion | bytes 4194304 | tf_op jit(solution)/shard_map/slice | solution.py:150
  85.8 13.1 %shard_map.55 = bf16[256,1024]{1,0:T(8,128)(2,1)} custom-call(bf16[256,1024]{1,0:T(8,128)(2,1)} %slice_bitcast_fusion.refs_0_, bf16[2,4,384,128]{3,2,1,0:T(8,128)(2,1)} %pad_maximum_fusion.1.refs_1_, bf16[2,4,384,128]{3,2,1,0:T(8,128)(2,1)} %pad_maximum_fusion.2.refs_2_, bf16[2,2048,128]{2,1,0:T(8,128)(2,1)} %bitcast.185, bf16[2,2048,128]{2,1,0:T(8,128)(2,1)} %bitcast.184, ...), custom_call_target="tpu_custom_call" | custom-call | flops 2550136832 | bytes 4718592 | tf_op jit(solution)/shard_map/pallas_call | solution.py:68
  (61 shorter events, 1.2 us)
Async XLA Ops:
  7.6 7.9 %copy-start = (s32[8,4]{0,1:T(4,128)S(1)}, s32[8,4]{0,1:T(4,128)}, u32[]{:S(2)}) copy-start(s32[8,4]{0,1:T(4,128)} %param.8) | copy-start | bytes 388
  9.6 19.3 %all-to-all-start = ((bf16[64,4,1536]{2,0,1:T(8,128)(2,1)}), bf16[64,4,1536]{2,0,1:T(8,128)(2,1)S(1)}, u32[]{:S(2)}, u32[]{:S(2)}) async-start(bf16[64,4,1536]{2,0,1:T(8,128)(2,1)} %pad_maximum_fusion), calls=%async_computation | async-start | bytes 1572864 | tf_op jit(solution)/shard_map/all_to_all | solution.py:102
  15.4 65.6 %all-gather.3.cloned.1.call-start = ((), (), s32[]{:S(2)}) async-start(), calls=%async_computation.1 | async-start | bytes 4325376 | tf_op jit(solution)/shard_map/all_gather | solution.py:146
  33.8 6.8 %collective-permute-start = (bf16[256,256]{1,0:T(8,128)(2,1)S(1)}, bf16[256,256]{1,0:T(8,128)(2,1)S(1)}, u32[]{:S(2)}, u32[]{:S(2)}) collective-permute-start(bf16[256,256]{1,0:T(8,128)(2,1)S(1)} %get-tuple-element.14), channel_id=1, source_target_pairs={{0,4},{4,8},{8,12},{12,16},{16,20},{20,24},{24,28},{28,32},{32,36}... | collective-permute-start | bytes 393224 | tf_op jit(solution)/shard_map/ppermute | solution.py:17
  37.8 3.9 %collective-permute-start.1 = (bf16[256,256]{1,0:T(8,128)(2,1)S(1)}, bf16[256,256]{1,0:T(8,128)(2,1)S(1)}, u32[]{:S(2)}, u32[]{:S(2)}) collective-permute-start(bf16[256,256]{1,0:T(8,128)(2,1)S(1)} %get-tuple-element.15), channel_id=1, source_target_pairs={{0,4},{4,8},{8,12},{12,16},{16,20},{20,24},{24,28},{28,32},{32,36}... | collective-permute-start | bytes 393224 | tf_op jit(solution)/shard_map/ppermute | solution.py:17
Sparse Core Ops, SparseCore 0:
  32.6 48.4 all-gather.2

commit v5 on v4

--- a/solution.py
+++ b/solution.py
@@ -90,25 +90,18 @@
     seq_index = lax.axis_index("chip") * lax.axis_size("core") + core_index
     head_index = lax.axis_index("head")
     heads = lax.axis_size("head")
-    tokens = queries.shape[0]
+    tokens = keys.shape[0]
     joined = jnp.concatenate(
-        [
-            queries.reshape(tokens, heads, -1),
-            keys.reshape(tokens, heads, -1),
-            values.reshape(tokens, heads, -1),
-        ],
-        2,
+        [keys.reshape(tokens, heads, -1), values.reshape(tokens, heads, -1)], 2
     )
     joined = lax.all_to_all(joined, "head", split_axis=1, concat_axis=0, tiled=True)
-    q_cols = queries.shape[1] // heads
     k_cols = keys.shape[1] // heads
-    q_all = joined[:, 0, :q_cols]
-    k_all = joined[:, 0, q_cols : q_cols + k_cols]
-    v_all = joined[:, 0, q_cols + k_cols :]
-    rows = q_all.shape[0]
+    k_all = joined[:, 0, :k_cols]
+    v_all = joined[:, 0, k_cols:]
+    rows = k_all.shape[0]
     nbd = rows // BLOCK_TOKENS
     kv_local = k_all.shape[1] // HEAD_WIDTH
-    query_group = q_all.shape[1] // HEAD_WIDTH // kv_local
+    query_group = queries.shape[1] // heads // HEAD_WIDTH // kv_local
     width = EXTRA_DIAGONALS + 1
     prev_k, prev_v = shifted((k_all, v_all), ("chip", "core"), 1)
     window_k = jnp.concatenate([prev_k, k_all], 0).reshape(
@@ -143,7 +136,9 @@
                 1,
             )
         )
-    gathered = lax.all_gather(jnp.stack(pieces, 0), ("chip", "core"), axis=0, tiled=False)
+    pieces, queries = lax.optimization_barrier((jnp.stack(pieces, 0), queries))
+    gathered = lax.all_gather(pieces, ("chip", "core"), axis=0, tiled=False)
+    q_all = lax.all_to_all(queries, "head", split_axis=1, concat_axis=0, tiled=True)
     heads_idx = jnp.arange(kv_local)[:, None]
     fetched = gathered[owner, heads_idx, rank]
     vert_keys = fetched[:, :, 0].reshape(kv_local, listed * BLOCK_TOKENS, HEAD_WIDTH)

time: 106 us -> 97.8 us (0.923)
  waiting for transfers between devices: 34.2 us -> 19.7 us
  starting transfers between devices: 11.7 us -> 16.3 us
  local copies, waits for them, and re-layouts: 18.2 us -> 20.8 us
    all_gather x1, waiting for transfers between devices: 33.2 us -> 15.2 us  [local(): gathered = lax.all_gather(pieces, ('chip', 'core'), axis=0, tiled=False)]
    all_to_all x1, waiting for transfers between devices: 0.01 us -> 4.46 us  [local(): lax.all_to_all(joined, 'head', split_axis=1, concat_axis=0, tiled=True)]
    all_to_all x0 -> x1, starting transfers between devices: none -> 3.47 us  [local(): lax.all_to_all(queries, 'head', split_axis=1, concat_axis=0, tiled=True)]
    ppermute x2, starting transfers between devices: 5.87 us -> 6.99 us  [shifted(): return lax.ppermute(value, axis, pairs)]
  transfers between devices with their start and end apart: 4 -> 5, of which waited for: 2 -> 2; matrix products, arithmetic and copies ran while one was open for 11% -> 18% of each run, Pallas kernels for 0% -> 0%
where the time goes in v5:
time: 97.8 us; the launch traced here: 97.3 us
  between operations  23.7 us (24%)
  local copies, waits for them, and re-layouts  20.8 us (21%)
  waiting for transfers between devices  19.7 us (20%)
  starting transfers between devices  16.3 us (17%)
  Pallas kernels  13.1 us (13%)
  other arithmetic  3.65 us (4%)
    all_gather x1, waiting for transfers between devices, local(): gathered = lax.all_gather(pieces, ('chip', 'core'), axis=0, tiled=False)  15.2 us
    pallas_call x1, Pallas kernels, attend(): pl.pallas_call(kernel, grid=(kv_local, nbd), in_specs=[pl.BlockSpec((BLOC...  13.1 us
    ppermute x2, starting transfers between devices, shifted(): return lax.ppermute(value, axis, pairs)  6.99 us
    all_to_all x1, starting transfers between devices, local(): lax.all_to_all(joined, 'head', split_axis=1, concat_axis=0, tiled=True)  5.84 us
    all_to_all x1, waiting for transfers between devices, local(): lax.all_to_all(joined, 'head', split_axis=1, concat_axis=0, tiled=True)  4.46 us
    all_to_all x1, starting transfers between devices, local(): lax.all_to_all(queries, 'head', split_axis=1, concat_axis=0, tiled=True)  3.47 us
    gather x1, local copies, waits for them, and re-layouts, local(): fetched = gathered[owner, heads_idx, rank]  3.2 us
  transfers between devices with their start and end apart: 5, of which 2 were waited for; matrix products, arithmetic and copies ran while one was open for 18% of the time, Pallas kernels for 0%

profile of v5, /device:TPU:1, one launch (start us, length us, event | category | flops | bytes accessed | tf_op | source)
XLA Modules:
  0.0 97.3 jit_solution(3619426259542139268)
XLA Ops:
  6.5 1.0 %reshape.329 = bf16[64,4,256]{2,1,0:T(4,128)(2,1)S(1)} reshape(bf16[64,1024]{1,0:T(8,128)(2,1)} %param.6) | data formatting | bytes 262144 | tf_op jit(solution)/shard_map/reshape | solution.py:95
  7.5 1.0 %reshape.330 = bf16[64,4,256]{2,1,0:T(4,128)(2,1)S(1)} reshape(bf16[64,1024]{1,0:T(8,128)(2,1)} %param.7) | data formatting | bytes 262144 | tf_op jit(solution)/shard_map/reshape | solution.py:95
  8.5 0.1 pad_maximum_fusion.2
  8.6 0.7 copy.81
  9.4 5.8 %all-to-all-start = ((bf16[64,4,512]{2,0,1:T(8,128)(2,1)}), bf16[64,4,512]{2,0,1:T(8,128)(2,1)S(1)}, u32[]{:S(2)}, u32[]{:S(2)}) async-start(bf16[64,4,512]{2,0,1:T(8,128)(2,1)} %copy.81), calls=%async_computation | async-start | bytes 524288 | tf_op jit(solution)/shard_map/all_to_all | solution.py:97
  15.2 0.7 and_select_fusion.1
  16.0 0.2 convert_reduce_fusion
  16.1 0.2 fusion.4
  16.3 4.5 %all-to-all-done = bf16[64,4,512]{2,0,1:T(8,128)(2,1)S(1)} async-done(((bf16[64,4,512]{2,0,1:T(8,128)(2,1)}), bf16[64,4,512]{2,0,1:T(8,128)(2,1)S(1)}, u32[]{:S(2)}, u32[]{:S(2)}) %all-to-all-start) | async-done | bytes 262176 | tf_op jit(solution)/shard_map/all_to_all | solution.py:97
  20.9 0.2 fusion.20
  21.1 0.2 fusion.21
  21.3 0.6 gather_fusion.2
  21.9 0.6 gather_fusion.3
  22.5 0.6 gather_fusion
  23.0 0.6 gather_fusion.1
  23.7 0.7 copy.89
  24.4 0.1 fusion.5
  24.4 0.2 fusion.2
  24.7 0.1 compare_reduce_fusion
  24.8 0.1 not_and_fusion.1
  24.9 0.1 broadcast_in_dim.33
  25.0 0.1 stack.157
  25.1 0.1 broadcast_in_dim.34
  25.2 0.1 stack.158
  25.3 0.1 subtract_compare_fusion.1
  25.4 5.1 %collective-permute-start.1 = (bf16[256,256]{1,0:T(8,128)(2,1)S(1)}, bf16[256,256]{1,0:T(8,128)(2,1)S(1)}, u32[]{:S(2)}, u32[]{:S(2)}) collective-permute-start(bf16[256,256]{1,0:T(8,128)(2,1)S(1)} %get-tuple-element.29), channel_id=1, source_target_pairs={{0,4},{4,8},{8,12},{12,16},{16,20},{20,24},{24,28},{28,32},{32,36}... | collective-permute-start | bytes 393224 | tf_op jit(solution)/shard_map/ppermute | solution.py:17
  30.5 0.6 fusion.22
  31.2 0.1 stack.155
  31.4 0.1 stack.154
  31.5 1.9 %collective-permute-start = (bf16[256,256]{1,0:T(8,128)(2,1)S(1)}, bf16[256,256]{1,0:T(8,128)(2,1)S(1)}, u32[]{:S(2)}, u32[]{:S(2)}) collective-permute-start(bf16[256,256]{1,0:T(8,128)(2,1)S(1)} %get-tuple-element.30), channel_id=1, source_target_pairs={{0,4},{4,8},{8,12},{12,16},{16,20},{20,24},{24,28},{28,32},{32,36}... | collective-permute-start | bytes 393224 | tf_op jit(solution)/shard_map/ppermute | solution.py:17
  43.3 0.1 reshape.365
  43.3 0.6 copy.92.refs_5_
  44.0 0.7 copy.93.refs_6_
  44.6 0.8 copy.150
  45.5 3.5 %all-to-all-start.1 = ((bf16[64,4,1024]{2,0,1:T(8,128)(2,1)}), bf16[64,4,1024]{2,0,1:T(8,128)(2,1)S(1)}, u32[]{:S(2)}, u32[]{:S(2)}) async-start(bf16[64,4,1024]{2,0,1:T(8,128)(2,1)} %bitcast.129), calls=%async_computation.1 | async-start | bytes 1048576 | tf_op jit(solution)/shard_map/all_to_all | solution.py:141
  49.2 0.5 fusion.16
  49.6 1.7 %constant_dynamic-slice_fusion = (bf16[4,64,1,128]{3,2,1,0:T(2,128)(2,1)S(1)}, bf16[4,64,1,128]{3,2,1,0:T(2,128)(2,1)S(1)}, bf16[4,64,1,128]{3,2,1,0:T(2,128)(2,...) fusion(bf16[8,64,1,128]{3,2,1,0:T(2,128)(2,1)S(1)} %get-tuple-e, ...), kind=kLoop, calls=%fused_computation.52 | loop fusion | bytes 1048608 | tf_op jit(solution)/shard_map/dynamic_slice | solution.py:157
  51.3 0.2 fusion.17
  51.9 0.5 fusion.18
  52.4 1.7 %constant_dynamic-slice_fusion.8 = (bf16[4,64,1,128]{3,2,1,0:T(2,128)(2,1)S(1)}, bf16[4,64,1,128]{3,2,1,0:T(2,128)(2,1)S(1)}, bf16[4,64,1,128]{3,2,1,0:T(2,128)(...) fusion(bf16[8,64,1,128]{3,2,1,0:T(2,128)(2,1)S(1)} %get-tuple-e, ...), kind=kLoop, calls=%fused_computation.60 | loop fusion | bytes 1048608 | tf_op jit(solution)/shard_map/dynamic_slice | solution.py:154
  54.1 0.2 fusion.19
  54.6 1.0 %pad_maximum_fusion.1.refs_2_ = bf16[2,4,384,128]{3,2,1,0:T(8,128)(2,1)} fusion(bf16[1,4,384,128]{3,2,1,0:T(8,128)(2,1)S(1)} %bitcast.131, bf16[1,4,384,128]{3,2,1,0:T(8,128)(2,1)S(1)} %bitcast.132), kind=kLoop, calls=%fused_computation.6 | loop fusion | flops 393216 | bytes 1572864 | tf_op jit(solution)/shard_map/stack | solution.py:171
  55.6 1.0 pad_maximum_fusion.refs_1_
  56.6 15.2 %all-gather.3.cloned.1.call-done = bf16[64,2,2,64,128]{4,3,2,1,0:T(8,128)(2,1)} async-done(((bf16[2,2,2,64,128]{4,3,2,1,0:T(8,128)(2,1)}), bf16[64,2,2,64,128]{4,3,2,1,0:T(8,128)(2,1)}) %all-gather.3.cloned.1.call-update) | async-done | bytes 4194320 | tf_op jit(solution)/shard_map/all_gather | solution.py:140
  71.7 3.2 %gather_fusion.4 = bf16[64,2,64,128]{3,2,1,0:T(8,128)(2,1)S(1)} fusion(bf16[32,2,2,2,64,128]{5,4,3,2,1,0:T(8,128)(2,1)} %bitcast.136, s32[64]{0:T(128)S(1)} %reshape.365), kind=kCustom, calls=%fused_computation.4 | custom fusion | bytes 4195072 | tf_op jit(solution)/shard_map/gather | solution.py:143
  74.9 1.5 %fusion.15 = (bf16[2,32,1,64,128]{4,3,2,1,0:T(8,128)(2,1)}, bf16[2,32,1,64,128]{4,3,2,1,0:T(8,128)(2,1)}) fusion(bf16[2,32,2,64,128]{4,3,2,1,0:T(8,128)(2,1)S(1)} %bitcast.130), kind=kLoop, calls=%fused_computation.109 | loop fusion | bytes 4194304 | tf_op jit(solution)/shard_map/slice | solution.py:145
  76.5 0.8 copy-done.1
  77.3 13.1 %shard_map.55 = bf16[256,1024]{1,0:T(8,128)(2,1)} custom-call(bf16[256,1024]{1,0:T(8,128)(2,1)} %bitcast.140, bf16[2,4,384,128]{3,2,1,0:T(8,128)(2,1)} %pad_maximum_fusion.refs_1_, bf16[2,4,384,128]{3,2,1,0:T(8,128)(2,1)} %pad_maximum_fusion.1.refs_2_, bf16[2,2048,128]{2,1,0:T(8,128)(2,1)} %bitcast.138, bf16[2,2048,128]{2,1,0:T(8,128)(2,1)} %bitcast.137, ...), custom_call_target="tpu_custom_call" | custom-call | flops 2550136832 | bytes 4718592 | tf_op jit(solution)/shard_map/pallas_call | solution.py:68
  (62 shorter events, 1.3 us)
Async XLA Ops:
  9.4 11.4 %all-to-all-start = ((bf16[64,4,512]{2,0,1:T(8,128)(2,1)}), bf16[64,4,512]{2,0,1:T(8,128)(2,1)S(1)}, u32[]{:S(2)}, u32[]{:S(2)}) async-start(bf16[64,4,512]{2,0,1:T(8,128)(2,1)} %copy.81), calls=%async_computation | async-start | bytes 524288 | tf_op jit(solution)/shard_map/all_to_all | solution.py:97
  15.2 56.5 %all-gather.3.cloned.1.call-start = ((), (), s32[]{:S(2)}) async-start(), calls=%async_computation.2 | async-start | bytes 4325376 | tf_op jit(solution)/shard_map/all_gather | solution.py:140
  20.8 3.6 %copy-start.2 = (s32[8,4]{0,1:T(4,128)S(1)}, s32[8,4]{0,1:T(4,128)}, u32[]{:S(2)}) copy-start(s32[8,4]{0,1:T(4,128)} %param.8) | copy-start | bytes 388
  20.8 23.8 %copy-start = (bf16[64,4096]{1,0:T(8,128)(2,1)S(1)}, bf16[64,4096]{1,0:T(8,128)(2,1)}, u32[]{:S(2)}) copy-start(bf16[64,4096]{1,0:T(8,128)(2,1)} %param.5) | copy-start | bytes 1572868
  25.4 23.6 %collective-permute-start.1 = (bf16[256,256]{1,0:T(8,128)(2,1)S(1)}, bf16[256,256]{1,0:T(8,128)(2,1)S(1)}, u32[]{:S(2)}, u32[]{:S(2)}) collective-permute-start(bf16[256,256]{1,0:T(8,128)(2,1)S(1)} %get-tuple-element.29), channel_id=1, source_target_pairs={{0,4},{4,8},{8,12},{12,16},{16,20},{20,24},{24,28},{28,32},{32,36}... | collective-permute-start | bytes 393224 | tf_op jit(solution)/shard_map/ppermute | solution.py:17
  31.5 17.6 %collective-permute-start = (bf16[256,256]{1,0:T(8,128)(2,1)S(1)}, bf16[256,256]{1,0:T(8,128)(2,1)S(1)}, u32[]{:S(2)}, u32[]{:S(2)}) collective-permute-start(bf16[256,256]{1,0:T(8,128)(2,1)S(1)} %get-tuple-element.30), channel_id=1, source_target_pairs={{0,4},{4,8},{8,12},{12,16},{16,20},{20,24},{24,28},{28,32},{32,36}... | collective-permute-start | bytes 393224 | tf_op jit(solution)/shard_map/ppermute | solution.py:17
  45.5 31.0 %all-to-all-start.1 = ((bf16[64,4,1024]{2,0,1:T(8,128)(2,1)}), bf16[64,4,1024]{2,0,1:T(8,128)(2,1)S(1)}, u32[]{:S(2)}, u32[]{:S(2)}) async-start(bf16[64,4,1024]{2,0,1:T(8,128)(2,1)} %bitcast.129), calls=%async_computation.1 | async-start | bytes 1048576 | tf_op jit(solution)/shard_map/all_to_all | solution.py:141
  76.5 0.8 copy-start.1
Sparse Core Ops, SparseCore 0:
  24.5 47.2 all-gather.2

commit v6 on v5

--- a/solution.py
+++ b/solution.py
@@ -137,7 +137,13 @@
             )
         )
     pieces, queries = lax.optimization_barrier((jnp.stack(pieces, 0), queries))
-    gathered = lax.all_gather(pieces, ("chip", "core"), axis=0, tiled=False)
+    chips = lax.axis_size("chip")
+    cores = lax.axis_size("core")
+    spread = jnp.broadcast_to(pieces[None], (chips,) + pieces.shape)
+    half = lax.all_to_all(spread, "chip", split_axis=0, concat_axis=0, tiled=True)
+    other = lax.ppermute(half, "core", [(c, cores - 1 - c) for c in range(cores)])
+    gathered = jnp.concatenate([half, other], 0)
+    owner = jnp.where(owner % cores == core_index, owner // cores, chips + owner // cores)
     q_all = lax.all_to_all(queries, "head", split_axis=1, concat_axis=0, tiled=True)
     heads_idx = jnp.arange(kv_local)[:, None]
     fetched = gathered[owner, heads_idx, rank]

time: 97.8 us -> 110 us (1.12)
  the two profiles are of different devices: /device:TPU:1 before, /device:TPU:39 now
where the time goes in v6:
time: 110 us; the launch traced here: 109 us
  starting transfers between devices  29.5 us (27%)
  local copies, waits for them, and re-layouts  29.2 us (27%)
  waiting for transfers between devices  19.9 us (18%)
  Pallas kernels  13.2 us (12%)
  between operations  10.6 us (10%)
  other arithmetic  6.9 us (6%)
    ppermute x2, waiting for transfers between devices, shifted(): return lax.ppermute(value, axis, pairs)  18.3 us
    pallas_call x1, Pallas kernels, attend(): pl.pallas_call(kernel, grid=(kv_local, nbd), in_specs=[pl.BlockSpec((BLOC...  13.2 us
    ppermute x2, starting transfers between devices, shifted(): return lax.ppermute(value, axis, pairs)  6.96 us
    ppermute x1, starting transfers between devices, local(): lax.ppermute(half, 'core', [(c, cores - 1 - c) for c in range(cores)])  6.77 us
    all_to_all x1, starting transfers between devices, local(): lax.all_to_all(spread, 'chip', split_axis=0, concat_axis=0, tiled=True)  6.7 us
    unnamed x36, local copies, waits for them, and re-layouts  5.36 us
    all_to_all x1, starting transfers between devices, local(): lax.all_to_all(joined, 'head', split_axis=1, concat_axis=0, tiled=True)  4.85 us
    all_to_all x1, starting transfers between devices, local(): lax.all_to_all(queries, 'head', split_axis=1, concat_axis=0, tiled=True)  4.24 us
  transfers between devices with their start and end apart: 6, of which 2 were waited for; matrix products, arithmetic and copies ran while one was open for 30% of the time, Pallas kernels for 0%

profile of v6, /device:TPU:39, one launch (start us, length us, event | category | flops | bytes accessed | tf_op | source)
XLA Modules:
  0.0 109.3 jit_solution(16096978387575682532)
XLA Ops:
  0.0 1.0 reshape.330
  1.0 1.0 reshape.331
  2.0 0.1 pad_maximum_fusion.3
  2.1 0.7 copy.82
  2.9 4.9 %all-to-all-start = ((bf16[64,4,512]{2,0,1:T(8,128)(2,1)}), bf16[64,4,512]{2,0,1:T(8,128)(2,1)S(1)}, u32[]{:S(2)}, u32[]{:S(2)}) async-start(bf16[64,4,512]{2,0,1:T(8,128)(2,1)} %copy.82), calls=%async_computation | async-start | bytes 524288 | tf_op jit(solution)/shard_map/all_to_all | solution.py:97
  7.8 0.7 fusion.22
  18.6 0.2 fusion.2
  18.8 0.7 and_select_fusion.3
  19.6 0.2 convert_reduce_fusion
  19.8 0.1 fusion.4
  20.8 0.7 copy.94.refs_6_
  21.8 0.6 copy.93.refs_5_
  22.4 0.7 slice_bitcast_fusion.2
  23.1 4.2 %collective-permute-start.1 = (bf16[256,256]{1,0:T(8,128)(2,1)S(1)}, bf16[256,256]{1,0:T(8,128)(2,1)S(1)}, u32[]{:S(2)}, u32[]{:S(2)}) collective-permute-start(bf16[256,256]{1,0:T(8,128)(2,1)S(1)} %get-tuple-element.29), channel_id=1, source_target_pairs={{0,4},{4,8},{8,12},{12,16},{16,20},{20,24},{24,28},{28,32},{32,36}... | collective-permute-start | bytes 393224 | tf_op jit(solution)/shard_map/ppermute | solution.py:17
  27.4 0.2 fusion.20
  27.6 0.2 fusion.21
  27.8 0.6 gather_fusion
  28.4 0.6 gather_fusion.1
  29.0 0.6 gather_fusion.2
  29.6 0.6 gather_fusion.3
  30.2 1.9 %broadcast_in_dim.31 = bf16[16,2,2,2,64,128]{5,4,3,2,1,0:T(8,128)(2,1)} broadcast(bf16[2,2,2,64,128]{4,3,2,1,0:T(8,128)(2,1)S(1)} %copy.90), dimensions={1,2,3,4,5} | broadcast | bytes 2228224 | tf_op jit(solution)/shard_map/broadcast_in_dim | solution.py:142
  32.1 6.7 %all-to-all-start.2 = ((bf16[16,2,2,2,64,128]{5,4,3,2,1,0:T(8,128)(2,1)}), bf16[16,2,2,2,64,128]{5,4,3,2,1,0:T(8,128)(2,1)S(1)}, u32[]{:S(2)}, u32[]{:S(2)}) async-start(bf16[16,2,2,2,64,128]{5,4,3,2,1,0:T(8,128)(2,1)} %broadcast_in_dim.31), calls=%async_computation.2 | async-start | bytes 4194304 | tf_op jit(solution)/shard_map/all_to_all | solution.py:143
  38.8 2.7 %collective-permute-start = (bf16[256,256]{1,0:T(8,128)(2,1)}, bf16[256,256]{1,0:T(8,128)(2,1)}, u32[]{:S(2)}, u32[]{:S(2)}) collective-permute-start(bf16[256,256]{1,0:T(8,128)(2,1)} %get-tuple-element.30), channel_id=1, source_target_pairs={{0,4},{4,8},{8,12},{12,16},{16,20},{20,24},{24,28},{28,32},{32,36}... | collective-permute-start | bytes 393224 | tf_op jit(solution)/shard_map/ppermute | solution.py:17
  41.5 0.8 copy.151
  42.4 0.5 fusion.16
  42.9 0.2 fusion.17
  43.1 2.1 %constant_dynamic-slice_fusion = (bf16[4,64,1,128]{3,2,1,0:T(2,128)(2,1)S(1)}, bf16[4,64,1,128]{3,2,1,0:T(2,128)(2,1)}, bf16[4,64,1,128]{3,2,1,0:T(2,128)(2,1)},...) fusion(bf16[8,64,1,128]{3,2,1,0:T(2,128)(2,1)S(1)} %get-tuple-e, ...), kind=kLoop, calls=%fused_computation.53 | loop fusion | bytes 1048608 | tf_op jit(solution)/shard_map/dynamic_slice | solution.py:163
  45.4 18.3 %collective-permute-done = bf16[256,256]{1,0:T(8,128)(2,1)} collective-permute-done((bf16[256,256]{1,0:T(8,128)(2,1)}, bf16[256,256]{1,0:T(8,128)(2,1)}, u32[]{:S(2)}, u32[]{:S(2)}) %collective-permute-start) | collective-permute-done | bytes 131104 | tf_op jit(solution)/shard_map/ppermute | solution.py:17
  63.7 1.0 pad_maximum_fusion.4
  64.8 0.5 fusion.18
  65.2 2.0 %constant_dynamic-slice_fusion.8 = (bf16[4,64,1,128]{3,2,1,0:T(2,128)(2,1)S(1)}, bf16[4,64,1,128]{3,2,1,0:T(2,128)(2,1)S(1)}, bf16[4,64,1,128]{3,2,1,0:T(2,128)(...) fusion(bf16[8,64,1,128]{3,2,1,0:T(2,128)(2,1)S(1)} %get-tuple-e, ...), kind=kLoop, calls=%fused_computation.61 | loop fusion | bytes 1048608 | tf_op jit(solution)/shard_map/dynamic_slice | solution.py:160
  67.4 0.2 fusion.19
  67.6 0.7 bitcast_dynamic-update-slice_fusion.12
  68.2 0.6 bitcast_dynamic-update-slice_fusion.16
  68.9 1.6 %all-to-all-done.2 = bf16[16,2,2,2,64,128]{5,4,3,2,1,0:T(8,128)(2,1)S(1)} async-done(((bf16[16,2,2,2,64,128]{5,4,3,2,1,0:T(8,128)(2,1)}), bf16[16,2,2,2,64,128]{5,4,3,2,1,0:T(8,128)(2,1)S(1)}, u32[]{:S(2)}, u32[]{:S(2)}) %all-to-all-start.2) | async-done | bytes 2097184 | tf_op jit(solution)/shard_map/all_to_all | solution.py:143
  70.5 4.2 %all-to-all-start.1 = ((bf16[64,4,1024]{2,0,1:T(8,128)(2,1)}), bf16[64,4,1024]{2,0,1:T(8,128)(2,1)}, u32[]{:S(2)}, u32[]{:S(2)}) async-start(bf16[64,4,1024]{2,0,1:T(8,128)(2,1)} %bitcast.128), calls=%async_computation.1 | async-start | bytes 1048576 | tf_op jit(solution)/shard_map/all_to_all | solution.py:147
  74.7 6.8 %collective-permute-start.2 = (bf16[16,2,2,2,64,128]{5,4,3,2,1,0:T(8,128)(2,1)S(1)}, bf16[16,2,2,2,64,128]{5,4,3,2,1,0:T(8,128)(2,1)S(1)}, u32[]{:S(2)}, u32[]{:S(2)}) collective-permute-start(bf16[16,2,2,2,64,128]{5,4,3,2,1,0:T(8,128)(2,1)S(1)} %all-to-all-done.2), channel_id=1, source_target_pairs={{0,4},{4,0},{1,5},{5,1},{2,6},{6,2},{3,7},{7,3},{8,12},{12,8},{9,1... | collective-permute-start | bytes 6291464 | tf_op jit(solution)/shard_map/ppermute | solution.py:144
  81.6 1.5 %bitcast_dynamic-update-slice_fusion.15 = bf16[4,6,64,128]{3,2,0,1:T(8,128)(2,1)} fusion(bf16[4,6,64,128]{3,2,0,1:T(8,128)(2,1)} %bitcast_dynamic-update-slice_fusion.16, bf16[4,64,1,128]{3,2,1,0:T(2,128)(2,1)} %get-tuple-element.76), kind=kLoop, calls=%fused_computation.34 | loop fusion | bytes 196608
  83.1 1.5 %bitcast_dynamic-update-slice_fusion.14 = bf16[4,6,64,128]{3,2,0,1:T(8,128)(2,1)} fusion(bf16[4,6,64,128]{3,2,0,1:T(8,128)(2,1)} %bitcast_dynamic-update-slice_fusion.15, bf16[4,64,1,128]{3,2,1,0:T(2,128)(2,1)} %get-tuple-element.77), kind=kLoop, calls=%fused_computation.33 | loop fusion | bytes 196608
  84.6 0.6 bitcast_dynamic-update-slice_fusion.13
  85.3 0.6 constant_dynamic-update-slice_fusion
  85.9 1.0 copy.84
  87.1 1.0 pad_maximum_fusion.2.refs_2_
  88.1 0.9 pad_maximum_fusion.1.refs_1_
  89.1 2.3 %pad_maximum_fusion = bf16[32,2,2,2,64,128]{5,4,3,2,1,0:T(8,128)(2,1)} fusion(bf16[16,2,2,2,64,128]{5,4,3,2,1,0:T(8,128)(2,1)S(1)} %collective-permute-done.2, bf16[16,2,2,2,64,128]{5,4,3,2,1,0:T(8,128)(2,1)S(1)} %all-to-all-done.2), kind=kLoop, calls=%fused_computation.5 | loop fusion | flops 2097152 | bytes 8388608 | tf_op jit(solution)/shard_map/concatenate | solution.py:145
  91.4 3.2 %gather_fusion.4 = bf16[64,2,64,128]{3,2,1,0:T(8,128)(2,1)S(1)} fusion(bf16[32,2,2,2,64,128]{5,4,3,2,1,0:T(8,128)(2,1)} %pad_maximum_fusion, s32[64]{0:T(128)S(1)} %reshape.366), kind=kCustom, calls=%fused_computation.4 | custom fusion | bytes 4195072 | tf_op jit(solution)/shard_map/gather | solution.py:149
  94.6 1.6 %fusion.15 = (bf16[2,32,1,64,128]{4,3,2,1,0:T(8,128)(2,1)}, bf16[2,32,1,64,128]{4,3,2,1,0:T(8,128)(2,1)}) fusion(bf16[2,32,2,64,128]{4,3,2,1,0:T(8,128)(2,1)S(1)} %bitcast.129), kind=kLoop, calls=%fused_computation.116 | loop fusion | bytes 4194304 | tf_op jit(solution)/shard_map/slice | solution.py:151
  96.1 13.2 %shard_map.55 = bf16[256,1024]{1,0:T(8,128)(2,1)} custom-call(bf16[256,1024]{1,0:T(8,128)(2,1)} %bitcast.16.refs_0_, bf16[2,4,384,128]{3,2,1,0:T(8,128)(2,1)} %pad_maximum_fusion.1.refs_1_, bf16[2,4,384,128]{3,2,1,0:T(8,128)(2,1)} %pad_maximum_fusion.2.refs_2_, bf16[2,2048,128]{2,1,0:T(8,128)(2,1)} %bitcast.136, bf16[2,2048,128]{2,1,0:T(8,128)(2,1)} %bitcast.135, ...), custom_call_target="tpu_custom_call" | custom-call | flops 2550136832 | bytes 4718592 | tf_op jit(solution)/shard_map/pallas_call | solution.py:68
  (75 shorter events, 2.0 us)
Async XLA Ops:
  0.0 7.7 %copy-start.7 = (s32[8,4]{0,1:T(4,128)S(1)}, s32[8,4]{0,1:T(4,128)}, u32[]{:S(2)}) copy-start(s32[8,4]{0,1:T(4,128)} %param.8) | copy-start | bytes 388
  2.9 19.6 %all-to-all-start = ((bf16[64,4,512]{2,0,1:T(8,128)(2,1)}), bf16[64,4,512]{2,0,1:T(8,128)(2,1)S(1)}, u32[]{:S(2)}, u32[]{:S(2)}) async-start(bf16[64,4,512]{2,0,1:T(8,128)(2,1)} %copy.82), calls=%async_computation | async-start | bytes 524288 | tf_op jit(solution)/shard_map/all_to_all | solution.py:97
  23.1 19.2 %collective-permute-start.1 = (bf16[256,256]{1,0:T(8,128)(2,1)S(1)}, bf16[256,256]{1,0:T(8,128)(2,1)S(1)}, u32[]{:S(2)}, u32[]{:S(2)}) collective-permute-start(bf16[256,256]{1,0:T(8,128)(2,1)S(1)} %get-tuple-element.29), channel_id=1, source_target_pairs={{0,4},{4,8},{8,12},{12,16},{16,20},{20,24},{24,28},{28,32},{32,36}... | collective-permute-start | bytes 393224 | tf_op jit(solution)/shard_map/ppermute | solution.py:17
  32.1 9.4 %copy-start.6 = (bf16[64,4096]{1,0:T(8,128)(2,1)S(1)}, bf16[64,4096]{1,0:T(8,128)(2,1)}, u32[]{:S(2)}) copy-start(bf16[64,4096]{1,0:T(8,128)(2,1)} %param.5) | copy-start | bytes 1572868
  32.1 38.4 %all-to-all-start.2 = ((bf16[16,2,2,2,64,128]{5,4,3,2,1,0:T(8,128)(2,1)}), bf16[16,2,2,2,64,128]{5,4,3,2,1,0:T(8,128)(2,1)S(1)}, u32[]{:S(2)}, u32[]{:S(2)}) async-start(bf16[16,2,2,2,64,128]{5,4,3,2,1,0:T(8,128)(2,1)} %broadcast_in_dim.31), calls=%async_computation.2 | async-start | bytes 4194304 | tf_op jit(solution)/shard_map/all_to_all | solution.py:143
  38.8 24.9 %collective-permute-start = (bf16[256,256]{1,0:T(8,128)(2,1)}, bf16[256,256]{1,0:T(8,128)(2,1)}, u32[]{:S(2)}, u32[]{:S(2)}) collective-permute-start(bf16[256,256]{1,0:T(8,128)(2,1)} %get-tuple-element.30), channel_id=1, source_target_pairs={{0,4},{4,8},{8,12},{12,16},{16,20},{20,24},{24,28},{28,32},{32,36}... | collective-permute-start | bytes 393224 | tf_op jit(solution)/shard_map/ppermute | solution.py:17
  64.7 2.5 %copy-start.5 = (bf16[4,64,1,128]{3,2,1,0:T(2,128)(2,1)S(1)}, bf16[4,64,1,128]{3,2,1,0:T(2,128)(2,1)}, u32[]{:S(2)}) copy-start(bf16[4,64,1,128]{3,2,1,0:T(2,128)(2,1)} %get-tuple-element.28) | copy-start | bytes 196612
  64.7 2.5 %copy-start.4 = (bf16[4,64,1,128]{3,2,1,0:T(2,128)(2,1)S(1)}, bf16[4,64,1,128]{3,2,1,0:T(2,128)(2,1)}, u32[]{:S(2)}) copy-start(bf16[4,64,1,128]{3,2,1,0:T(2,128)(2,1)} %get-tuple-element.27) | copy-start | bytes 196612
  64.7 2.6 %copy-start.3 = (bf16[4,64,1,128]{3,2,1,0:T(2,128)(2,1)S(1)}, bf16[4,64,1,128]{3,2,1,0:T(2,128)(2,1)}, u32[]{:S(2)}) copy-start(bf16[4,64,1,128]{3,2,1,0:T(2,128)(2,1)} %get-tuple-element.26) | copy-start | bytes 196612
  70.5 25.7 %all-to-all-start.1 = ((bf16[64,4,1024]{2,0,1:T(8,128)(2,1)}), bf16[64,4,1024]{2,0,1:T(8,128)(2,1)}, u32[]{:S(2)}, u32[]{:S(2)}) async-start(bf16[64,4,1024]{2,0,1:T(8,128)(2,1)} %bitcast.128), calls=%async_computation.1 | async-start | bytes 1048576 | tf_op jit(solution)/shard_map/all_to_all | solution.py:147
  74.7 9.9 %copy-start.2 = (bf16[4,64,1,128]{3,2,1,0:T(2,128)(2,1)S(1)}, bf16[4,64,1,128]{3,2,1,0:T(2,128)(2,1)}, u32[]{:S(2)}) copy-start(bf16[4,64,1,128]{3,2,1,0:T(2,128)(2,1)} %get-tuple-element.78) | copy-start | bytes 196612
  74.7 12.2 %copy-start.1 = (bf16[4,64,1,128]{3,2,1,0:T(2,128)(2,1)S(1)}, bf16[4,64,1,128]{3,2,1,0:T(2,128)(2,1)}, u32[]{:S(2)}) copy-start(bf16[4,64,1,128]{3,2,1,0:T(2,128)(2,1)} %get-tuple-element.44) | copy-start | bytes 196612
  74.7 12.3 %copy-start = (bf16[4,64,1,128]{3,2,1,0:T(2,128)(2,1)S(1)}, bf16[4,64,1,128]{3,2,1,0:T(2,128)(2,1)}, u32[]{:S(2)}) copy-start(bf16[4,64,1,128]{3,2,1,0:T(2,128)(2,1)} %get-tuple-element.43) | copy-start | bytes 196612
  74.7 14.3 %collective-permute-start.2 = (bf16[16,2,2,2,64,128]{5,4,3,2,1,0:T(8,128)(2,1)S(1)}, bf16[16,2,2,2,64,128]{5,4,3,2,1,0:T(8,128)(2,1)S(1)}, u32[]{:S(2)}, u32[]{:S(2)}) collective-permute-start(bf16[16,2,2,2,64,128]{5,4,3,2,1,0:T(8,128)(2,1)S(1)} %all-to-all-done.2), channel_id=1, source_target_pairs={{0,4},{4,0},{1,5},{5,1},{2,6},{6,2},{3,7},{7,3},{8,12},{12,8},{9,1... | collective-permute-start | bytes 6291464 | tf_op jit(solution)/shard_map/ppermute | solution.py:144

commit v7 on v5

--- a/solution.py
+++ b/solution.py
@@ -137,12 +137,39 @@
             )
         )
     pieces, queries = lax.optimization_barrier((jnp.stack(pieces, 0), queries))
-    gathered = lax.all_gather(pieces, ("chip", "core"), axis=0, tiled=False)
+    chips = lax.axis_size("chip")
+    cores = lax.axis_size("core")
+    side = int(round(chips ** 0.5))
+    chip_index = lax.axis_index("chip")
+    swap = [(c, cores - 1 - c) for c in range(cores)]
+    mine = lax.dynamic_index_in_dim(pieces, core_index, 2, keepdims=False)
+    sent = lax.dynamic_index_in_dim(pieces, cores - 1 - core_index, 2, keepdims=False)
+    stage = jnp.stack([mine, lax.ppermute(sent, "core", swap)], 0)
     q_all = lax.all_to_all(queries, "head", split_axis=1, concat_axis=0, tiled=True)
+    for stride in (1, side):
+        moved = [stage]
+        for step in range(1, side):
+            pairs = []
+            for chip in range(chips):
+                row, col = chip // side, chip % side
+                if stride == 1:
+                    pairs.append((chip, row * side + (col + step) % side))
+                else:
+                    pairs.append((chip, ((row + step) % side) * side + col))
+            moved.append(lax.ppermute(stage, "chip", pairs))
+        stage = jnp.stack(moved, 0)
+    partner = lax.ppermute(stage, "core", swap)
+    keys_src = jnp.where(core_index == 0, stage, partner)
+    vals_src = jnp.where(core_index == 0, partner, stage)
+    owner_chip = owner // cores
+    owner_core = owner % cores
+    dy = (chip_index // side - owner_chip // side) % side
+    dx = (chip_index % side - owner_chip % side) % side
     heads_idx = jnp.arange(kv_local)[:, None]
-    fetched = gathered[owner, heads_idx, rank]
-    vert_keys = fetched[:, :, 0].reshape(kv_local, listed * BLOCK_TOKENS, HEAD_WIDTH)
-    vert_vals = fetched[:, :, 1].reshape(kv_local, listed * BLOCK_TOKENS, HEAD_WIDTH)
+    vert_keys = keys_src[dy, dx, owner_core, heads_idx, rank]
+    vert_vals = vals_src[dy, dx, cores - 1 - owner_core, heads_idx, rank]
+    vert_keys = vert_keys.reshape(kv_local, listed * BLOCK_TOKENS, HEAD_WIDTH)
+    vert_vals = vert_vals.reshape(kv_local, listed * BLOCK_TOKENS, HEAD_WIDTH)
     qblocks = seq_index * nbd + jnp.arange(nbd, dtype=jnp.int32)
     pad = jnp.zeros((nbd, SLASH_SLOTS - width, BLOCK_TOKENS, HEAD_WIDTH), k_all.dtype)
     slash_k, slash_v, slash_ok, vert_ok = [], [], [], []

time: 97.8 us -> 104 us (1.063)
  between operations: 23.7 us -> 10.1 us
  starting transfers between devices: 16.3 us -> 28 us
  waiting for transfers between devices: 19.7 us -> 25.8 us
  other arithmetic: 3.65 us -> 5.56 us
    ppermute x0 -> x8, waiting for transfers between devices: none -> 23.5 us  [the longest x6 22 us: local(): moved.append(lax.ppermute(stage, 'chip', pairs))]
    all_gather x1 -> x0, waiting for transfers between devices: 15.2 us -> none  [local(): gathered = lax.all_gather(pieces, ('chip', 'core'), axis=0, tiled=False)]
    ppermute x0 -> x8, starting transfers between devices: none -> 13.3 us  [the longest x6 9.35 us: local(): moved.append(lax.ppermute(stage, 'chip', pairs))]
    gather x1 -> x2, local copies, waits for them, and re-layouts: 3.2 us -> 5.48 us  [the longest x1 3.52 us: local(): vert_vals = vals_src[dy, dx, cores - 1 - owner_core, heads_idx, rank]]
    all_to_all x1, waiting for transfers between devices: 4.46 us -> 2.33 us  [local(): lax.all_to_all(joined, 'head', split_axis=1, concat_axis=0, tiled=True)]
    ppermute x2, starting transfers between devices: 6.99 us -> 5.4 us  [shifted(): return lax.ppermute(value, axis, pairs)]
    slice x1 -> x0, local copies, waits for them, and re-layouts: 1.54 us -> none  [local(): fetched[:, :, 1].reshape(kv_local, listed * BLOCK_TOKENS, HEAD_WIDTH)]
    select_n x0 -> x1, other arithmetic: none -> 1.53 us  [local(): vals_src = jnp.where(core_index == 0, partner, stage)]
  transfers between devices with their start and end apart: 5 -> 12, of which waited for: 2 -> 6; matrix products, arithmetic and copies ran while one was open for 18% -> 19% of each run, Pallas kernels for 0% -> 0%
where the time goes in v7:
time: 104 us; the launch traced here: 103 us
  starting transfers between devices  28 us (27%)
  waiting for transfers between devices  25.8 us (25%)
  local copies, waits for them, and re-layouts  20.4 us (20%)
  Pallas kernels  13.1 us (13%)
  between operations  10.1 us (10%)
  other arithmetic  5.56 us (5%)
    ppermute x6, waiting for transfers between devices, local(): moved.append(lax.ppermute(stage, 'chip', pairs))  22 us
    pallas_call x1, Pallas kernels, attend(): pl.pallas_call(kernel, grid=(kv_local, nbd), in_specs=[pl.BlockSpec((BLOC...  13.1 us
    ppermute x6, starting transfers between devices, local(): moved.append(lax.ppermute(stage, 'chip', pairs))  9.35 us
    all_to_all x1, starting transfers between devices, local(): lax.all_to_all(joined, 'head', split_axis=1, concat_axis=0, tiled=True)  5.84 us
    ppermute x2, starting transfers between devices, shifted(): return lax.ppermute(value, axis, pairs)  5.4 us
    gather x1, local copies, waits for them, and re-layouts, local(): vert_vals = vals_src[dy, dx, cores - 1 - owner_core, heads_idx, rank]  3.52 us
    all_to_all x1, starting transfers between devices, local(): lax.all_to_all(queries, 'head', split_axis=1, concat_axis=0, tiled=True)  3.47 us
    all_to_all x1, waiting for transfers between devices, local(): lax.all_to_all(joined, 'head', split_axis=1, concat_axis=0, tiled=True)  2.33 us
  transfers between devices with their start and end apart: 12, of which 6 were waited for; matrix products, arithmetic and copies ran while one was open for 19% of the time, Pallas kernels for 0%

profile of v7, /device:TPU:1, one launch (start us, length us, event | category | flops | bytes accessed | tf_op | source)
XLA Modules:
  0.0 103.1 jit_solution(18445625278892244421)
XLA Ops:
  0.0 1.0 reshape.336
  1.0 1.0 reshape.337
  2.1 0.7 copy.66
  2.9 5.8 %all-to-all-start = ((bf16[64,4,512]{2,0,1:T(8,128)(2,1)}), bf16[64,4,512]{2,0,1:T(8,128)(2,1)S(1)}, u32[]{:S(2)}, u32[]{:S(2)}) async-start(bf16[64,4,512]{2,0,1:T(8,128)(2,1)} %copy.66), calls=%async_computation | async-start | bytes 524288 | tf_op jit(solution)/shard_map/all_to_all | solution.py:97
  8.7 0.7 and_select_fusion.7
  9.5 0.7 fusion.35
  10.2 0.2 fusion.2
  10.4 0.2 convert_reduce_fusion
  11.9 2.3 %all-to-all-done = bf16[64,4,512]{2,0,1:T(8,128)(2,1)S(1)} async-done(((bf16[64,4,512]{2,0,1:T(8,128)(2,1)}), bf16[64,4,512]{2,0,1:T(8,128)(2,1)S(1)}, u32[]{:S(2)}, u32[]{:S(2)}) %all-to-all-start) | async-done | bytes 262176 | tf_op jit(solution)/shard_map/all_to_all | solution.py:97
  14.3 0.2 fusion.33
  14.6 0.2 fusion.34
  14.8 0.6 gather_fusion
  15.4 0.6 gather_fusion.1
  15.9 0.6 gather_fusion.2
  16.5 0.6 gather_fusion.3
  17.2 2.2 %collective-permute-start.2 = (bf16[2,2,64,128]{3,2,1,0:T(8,128)(2,1)S(1)}, bf16[2,2,64,128]{3,2,1,0:T(8,128)(2,1)S(1)}, u32[]{:S(2)}, u32[]{:S(2)}) collective-permute-start(bf16[2,2,64,128]{3,2,1,0:T(8,128)(2,1)S(1)} %get-tuple-element.52), channel_id=1, source_target_pairs={{0,4},{4,0},{1,5},{5,1},{2,6},{6,2},{3,7},{7,3},{8,12},{12,8},{9,1... | collective-permute-start | bytes 196616 | tf_op jit(solution)/shard_map/ppermute | solution.py:147
  19.3 3.0 %collective-permute-start.1 = (bf16[256,256]{1,0:T(8,128)(2,1)S(1)}, bf16[256,256]{1,0:T(8,128)(2,1)S(1)}, u32[]{:S(2)}, u32[]{:S(2)}) collective-permute-start(bf16[256,256]{1,0:T(8,128)(2,1)S(1)} %get-tuple-element.33), channel_id=1, source_target_pairs={{0,4},{4,8},{8,12},{12,16},{16,20},{20,24},{24,28},{28,32},{32,36}... | collective-permute-start | bytes 393224 | tf_op jit(solution)/shard_map/ppermute | solution.py:17
  32.1 0.7 copy.75.refs_6_
  32.8 0.6 copy.74.refs_5_
  33.4 2.4 %collective-permute-start = (bf16[256,256]{1,0:T(8,128)(2,1)S(1)}, bf16[256,256]{1,0:T(8,128)(2,1)S(1)}, u32[]{:S(2)}, u32[]{:S(2)}) collective-permute-start(bf16[256,256]{1,0:T(8,128)(2,1)S(1)} %get-tuple-element.34), channel_id=1, source_target_pairs={{0,4},{4,8},{8,12},{12,16},{16,20},{20,24},{24,28},{28,32},{32,36}... | collective-permute-start | bytes 393224 | tf_op jit(solution)/shard_map/ppermute | solution.py:17
  35.8 0.8 copy.130
  36.7 3.5 %all-to-all-start.1 = ((bf16[64,4,1024]{2,0,1:T(8,128)(2,1)}), bf16[64,4,1024]{2,0,1:T(8,128)(2,1)S(1)}, u32[]{:S(2)}, u32[]{:S(2)}) async-start(bf16[64,4,1024]{2,0,1:T(8,128)(2,1)} %bitcast.146), calls=%async_computation.1 | async-start | bytes 1048576 | tf_op jit(solution)/shard_map/all_to_all | solution.py:148
  40.2 1.3 %collective-permute-start.3 = (bf16[2,2,2,64,128]{4,3,2,1,0:T(8,128)(2,1)S(1)}, bf16[2,2,2,64,128]{4,3,2,1,0:T(8,128)(2,1)S(1)}, u32[]{:S(2)}, u32[]{:S(2)}) collective-permute-start(bf16[2,2,2,64,128]{4,3,2,1,0:T(8,128)(2,1)S(1)} %get-tuple-element.50), channel_id=1, source_target_pairs={{0,8},{8,16},{16,24},{24,0},{32,40},{40,48},{48,56},{56,32},{64,72... | collective-permute-start | bytes 393224 | tf_op jit(solution)/shard_map/ppermute | solution.py:159
  41.5 2.5 %collective-permute-start.4 = (bf16[2,2,2,64,128]{4,3,2,1,0:T(8,128)(2,1)S(1)}, bf16[2,2,2,64,128]{4,3,2,1,0:T(8,128)(2,1)S(1)}, u32[]{:S(2)}, u32[]{:S(2)}) collective-permute-start(bf16[2,2,2,64,128]{4,3,2,1,0:T(8,128)(2,1)S(1)} %get-tuple-element.50), channel_id=1, source_target_pairs={{0,16},{8,24},{16,0},{24,8},{32,48},{40,56},{48,32},{56,40},{64,80... | collective-permute-start | bytes 393224 | tf_op jit(solution)/shard_map/ppermute | solution.py:159
  43.9 0.9 collective-permute-start.5
  44.9 0.5 fusion.29
  45.3 0.2 fusion.30
  45.7 0.5 fusion.31
  46.1 0.2 fusion.32
  46.4 1.7 %constant_dynamic-slice_fusion = (bf16[4,64,1,128]{3,2,1,0:T(2,128)(2,1)S(1)}, bf16[4,64,1,128]{3,2,1,0:T(2,128)(2,1)S(1)}, bf16[4,64,1,128]{3,2,1,0:T(2,128)(2,...) fusion(bf16[8,64,1,128]{3,2,1,0:T(2,128)(2,1)S(1)} %get-tuple-e, ...), kind=kLoop, calls=%fused_computation.58 | loop fusion | bytes 1048608 | tf_op jit(solution)/shard_map/dynamic_slice | solution.py:184
  48.3 1.1 %constant_dynamic-slice_fusion.8 = (bf16[4,64,1,128]{3,2,1,0:T(2,128)(2,1)S(1)}, bf16[4,64,1,128]{3,2,1,0:T(2,128)(2,1)S(1)}, bf16[4,64,1,128]{3,2,1,0:T(2,128)(...) fusion(bf16[8,64,1,128]{3,2,1,0:T(2,128)(2,1)S(1)} %get-tuple-e, ...), kind=kLoop, calls=%fused_computation.66 | loop fusion | bytes 1048608 | tf_op jit(solution)/shard_map/dynamic_slice | solution.py:181
  49.4 0.9 collective-permute-done.4
  50.4 1.4 %collective-permute-start.6 = (bf16[4,2,2,2,64,128]{5,4,3,2,1,0:T(8,128)(2,1)S(1)}, bf16[4,2,2,2,64,128]{5,4,3,2,1,0:T(8,128)(2,1)S(1)}, u32[]{:S(2)}, u32[]{:S(2)}) collective-permute-start(bf16[4,2,2,2,64,128]{5,4,3,2,1,0:T(8,128)(2,1)S(1)} %get-tuple-element.20), channel_id=1, source_target_pairs={{0,32},{8,40},{16,48},{24,56},{32,64},{40,72},{48,80},{56,88},{64,... | collective-permute-start | bytes 1572872 | tf_op jit(solution)/shard_map/ppermute | solution.py:159
  51.7 1.9 %collective-permute-start.7 = (bf16[4,2,2,2,64,128]{5,4,3,2,1,0:T(8,128)(2,1)S(1)}, bf16[4,2,2,2,64,128]{5,4,3,2,1,0:T(8,128)(2,1)S(1)}, u32[]{:S(2)}, u32[]{:S(2)}) collective-permute-start(bf16[4,2,2,2,64,128]{5,4,3,2,1,0:T(8,128)(2,1)S(1)} %get-tuple-element.20), channel_id=1, source_target_pairs={{0,64},{8,72},{16,80},{24,88},{32,96},{40,104},{48,112},{56,120},{... | collective-permute-start | bytes 1572872 | tf_op jit(solution)/shard_map/ppermute | solution.py:159
  53.7 1.5 %collective-permute-start.8 = (bf16[4,2,2,2,64,128]{5,4,3,2,1,0:T(8,128)(2,1)S(1)}, bf16[4,2,2,2,64,128]{5,4,3,2,1,0:T(8,128)(2,1)S(1)}, u32[]{:S(2)}, u32[]{:S(2)}) collective-permute-start(bf16[4,2,2,2,64,128]{5,4,3,2,1,0:T(8,128)(2,1)S(1)} %get-tuple-element.20), channel_id=1, source_target_pairs={{0,96},{8,104},{16,112},{24,120},{32,0},{40,8},{48,16},{56,24},{64... | collective-permute-start | bytes 1572872 | tf_op jit(solution)/shard_map/ppermute | solution.py:159
  55.2 9.0 %collective-permute-done.6 = bf16[4,2,2,2,64,128]{5,4,3,2,1,0:T(8,128)(2,1)S(1)} collective-permute-done((bf16[4,2,2,2,64,128]{5,4,3,2,1,0:T(8,128)(2,1)S(1)}, bf16[4,2,2,2,64,128]{5,4,3,2,1,0:T(8,128)(2,1)S(1)}, u32[]{:S(2)}, u32[]{:S(2)}) %collective-permute-start.6) | collective-permute-done | bytes 524320 | tf_op jit(solution)/shard_map/ppermute | solution.py:159
  64.3 11.5 %collective-permute-done.7 = bf16[4,2,2,2,64,128]{5,4,3,2,1,0:T(8,128)(2,1)S(1)} collective-permute-done((bf16[4,2,2,2,64,128]{5,4,3,2,1,0:T(8,128)(2,1)S(1)}, bf16[4,2,2,2,64,128]{5,4,3,2,1,0:T(8,128)(2,1)S(1)}, u32[]{:S(2)}, u32[]{:S(2)}) %collective-permute-start.7) | collective-permute-done | bytes 524320 | tf_op jit(solution)/shard_map/ppermute | solution.py:159
  75.8 0.5 collective-permute-done.8
  76.3 0.3 pad_maximum_fusion
  76.6 1.8 %collective-permute-start.9 = (bf16[4,4,2,2,2,64,128]{6,5,4,3,2,1,0:T(8,128)(2,1)S(1)}, bf16[4,4,2,2,2,64,128]{6,5,4,3,2,1,0:T(8,128)(2,1)S(1)}, u32[]{:S(2)}, u32[]{:S(2)}) collective-permute-start(bf16[4,4,2,2,2,64,128]{6,5,4,3,2,1,0:T(8,128)(2,1)S(1)} %pad_maximum_fusion), channel_id=1, source_target_pairs={{0,4},{4,0},{1,5},{5,1},{2,6},{6,2},{3,7},{7,3},{8,12},{12,8},{9,1... | collective-permute-start | bytes 6291464 | tf_op jit(solution)/shard_map/ppermute | solution.py:161
  78.8 1.0 pad_maximum_fusion.2.refs_2_
  79.7 1.0 pad_maximum_fusion.1.refs_1_
  80.7 1.5 %collective-permute-done.9 = bf16[4,4,2,2,2,64,128]{6,5,4,3,2,1,0:T(8,128)(2,1)S(1)} collective-permute-done((bf16[4,4,2,2,2,64,128]{6,5,4,3,2,1,0:T(8,128)(2,1)S(1)}, bf16[4,4,2,2,2,64,128]{6,5,4,3,2,1,0:T(8,128)(2,1)S(1)}, u32[]{:S(2)}, u32[]{:S(2)}) %collective-permute-start.9) | collective-permute-done | bytes 2097184 | tf_op jit(solution)/shard_map/ppermute | solution.py:161
  82.2 1.5 %broadcast_select_fusion = (bf16[4,4,2,2,2,64,128]{6,5,4,3,2,1,0:T(8,128)(2,1)}, bf16[4,4,2,2,2,64,128]{6,5,4,3,2,1,0:T(8,128)(2,1)S(1)}) fusion(bf16[4,4,2,2,2,64,128]{6,5,4,3,2,1,0:T(8,128)(2,1)S(1)} %collective-permute-done.9, pred[]{:T(512)S(6)} %eq.78, bf16[1,4,2,2,2,64,128]{6,5,4,3,2,1,0:T(8,128)(2,1)S(1)} %bitcast.152, ...), kind=kLoop, calls=%fused_computation.7 | loop fusion | flops 5242880 | bytes 8388609 | tf_op jit(solution)/shard_map/jit(_where)/select_n | solution.py:163
  83.7 3.5 %gather_fusion.5 = bf16[64,64,128]{2,1,0:T(8,128)(2,1)} fusion(bf16[4,4,2,2,2,64,128]{6,5,4,3,2,1,0:T(8,128)(2,1)} %get-tuple-element.17, s32[64]{0:T(128)S(1)} %reshape.380), kind=kCustom, calls=%fused_computation.5 | custom fusion | bytes 2098432 | tf_op jit(solution)/shard_map/gather | solution.py:170
  87.2 2.0 %gather_fusion.4 = bf16[64,64,128]{2,1,0:T(8,128)(2,1)} fusion(bf16[4,4,2,2,2,64,128]{6,5,4,3,2,1,0:T(8,128)(2,1)S(1)} %get-tuple-element.18, s32[64]{0:T(128)S(1)} %reshape.374), kind=kCustom, calls=%fused_computation.4 | custom fusion | bytes 2098432 | tf_op jit(solution)/shard_map/gather | solution.py:169
  89.2 0.8 copy-done.1
  90.0 13.1 %shard_map.55 = bf16[256,1024]{1,0:T(8,128)(2,1)} custom-call(bf16[256,1024]{1,0:T(8,128)(2,1)} %bitcast.161, bf16[2,4,384,128]{3,2,1,0:T(8,128)(2,1)} %pad_maximum_fusion.1.refs_1_, bf16[2,4,384,128]{3,2,1,0:T(8,128)(2,1)} %pad_maximum_fusion.2.refs_2_, bf16[2,2048,128]{2,1,0:T(8,128)(2,1)} %bitcast.159, bf16[2,2048,128]{2,1,0:T(8,128)(2,1)} %bitcast.158, ...), custom_call_target="tpu_custom_call" | custom-call | flops 2550136832 | bytes 4718592 | tf_op jit(solution)/shard_map/pallas_call | solution.py:68
  (81 shorter events, 2.7 us)
Async XLA Ops:
  0.0 9.5 %copy-start.2 = (s32[8,4]{0,1:T(4,128)S(1)}, s32[8,4]{0,1:T(4,128)}, u32[]{:S(2)}) copy-start(s32[8,4]{0,1:T(4,128)} %param.8) | copy-start | bytes 388
  2.9 11.4 %all-to-all-start = ((bf16[64,4,512]{2,0,1:T(8,128)(2,1)}), bf16[64,4,512]{2,0,1:T(8,128)(2,1)S(1)}, u32[]{:S(2)}, u32[]{:S(2)}) async-start(bf16[64,4,512]{2,0,1:T(8,128)(2,1)} %copy.66), calls=%async_computation | async-start | bytes 524288 | tf_op jit(solution)/shard_map/all_to_all | solution.py:97
  14.3 21.6 %copy-start = (bf16[64,4096]{1,0:T(8,128)(2,1)S(1)}, bf16[64,4096]{1,0:T(8,128)(2,1)}, u32[]{:S(2)}) copy-start(bf16[64,4096]{1,0:T(8,128)(2,1)} %param.5) | copy-start | bytes 1572868
  17.2 23.0 %collective-permute-start.2 = (bf16[2,2,64,128]{3,2,1,0:T(8,128)(2,1)S(1)}, bf16[2,2,64,128]{3,2,1,0:T(8,128)(2,1)S(1)}, u32[]{:S(2)}, u32[]{:S(2)}) collective-permute-start(bf16[2,2,64,128]{3,2,1,0:T(8,128)(2,1)S(1)} %get-tuple-element.52), channel_id=1, source_target_pairs={{0,4},{4,0},{1,5},{5,1},{2,6},{6,2},{3,7},{7,3},{8,12},{12,8},{9,1... | collective-permute-start | bytes 196616 | tf_op jit(solution)/shard_map/ppermute | solution.py:147
  19.3 25.5 %collective-permute-start.1 = (bf16[256,256]{1,0:T(8,128)(2,1)S(1)}, bf16[256,256]{1,0:T(8,128)(2,1)S(1)}, u32[]{:S(2)}, u32[]{:S(2)}) collective-permute-start(bf16[256,256]{1,0:T(8,128)(2,1)S(1)} %get-tuple-element.33), channel_id=1, source_target_pairs={{0,4},{4,8},{8,12},{12,16},{16,20},{20,24},{24,28},{28,32},{32,36}... | collective-permute-start | bytes 393224 | tf_op jit(solution)/shard_map/ppermute | solution.py:17
  33.4 12.1 %collective-permute-start = (bf16[256,256]{1,0:T(8,128)(2,1)S(1)}, bf16[256,256]{1,0:T(8,128)(2,1)S(1)}, u32[]{:S(2)}, u32[]{:S(2)}) collective-permute-start(bf16[256,256]{1,0:T(8,128)(2,1)S(1)} %get-tuple-element.34), channel_id=1, source_target_pairs={{0,4},{4,8},{8,12},{12,16},{16,20},{20,24},{24,28},{28,32},{32,36}... | collective-permute-start | bytes 393224 | tf_op jit(solution)/shard_map/ppermute | solution.py:17
  36.7 52.5 %all-to-all-start.1 = ((bf16[64,4,1024]{2,0,1:T(8,128)(2,1)}), bf16[64,4,1024]{2,0,1:T(8,128)(2,1)S(1)}, u32[]{:S(2)}, u32[]{:S(2)}) async-start(bf16[64,4,1024]{2,0,1:T(8,128)(2,1)} %bitcast.146), calls=%async_computation.1 | async-start | bytes 1048576 | tf_op jit(solution)/shard_map/all_to_all | solution.py:148
  40.2 9.2 %collective-permute-start.3 = (bf16[2,2,2,64,128]{4,3,2,1,0:T(8,128)(2,1)S(1)}, bf16[2,2,2,64,128]{4,3,2,1,0:T(8,128)(2,1)S(1)}, u32[]{:S(2)}, u32[]{:S(2)}) collective-permute-start(bf16[2,2,2,64,128]{4,3,2,1,0:T(8,128)(2,1)S(1)} %get-tuple-element.50), channel_id=1, source_target_pairs={{0,8},{8,16},{16,24},{24,0},{32,40},{40,48},{48,56},{56,32},{64,72... | collective-permute-start | bytes 393224 | tf_op jit(solution)/shard_map/ppermute | solution.py:159
  41.5 8.8 %collective-permute-start.4 = (bf16[2,2,2,64,128]{4,3,2,1,0:T(8,128)(2,1)S(1)}, bf16[2,2,2,64,128]{4,3,2,1,0:T(8,128)(2,1)S(1)}, u32[]{:S(2)}, u32[]{:S(2)}) collective-permute-start(bf16[2,2,2,64,128]{4,3,2,1,0:T(8,128)(2,1)S(1)} %get-tuple-element.50), channel_id=1, source_target_pairs={{0,16},{8,24},{16,0},{24,8},{32,48},{40,56},{48,32},{56,40},{64,80... | collective-permute-start | bytes 393224 | tf_op jit(solution)/shard_map/ppermute | solution.py:159
  43.9 6.4 %collective-permute-start.5 = (bf16[2,2,2,64,128]{4,3,2,1,0:T(8,128)(2,1)S(1)}, bf16[2,2,2,64,128]{4,3,2,1,0:T(8,128)(2,1)S(1)}, u32[]{:S(2)}, u32[]{:S(2)}) collective-permute-start(bf16[2,2,2,64,128]{4,3,2,1,0:T(8,128)(2,1)S(1)} %get-tuple-element.50), channel_id=1, source_target_pairs={{0,24},{8,0},{16,8},{24,16},{32,56},{40,32},{48,40},{56,48},{64,88... | collective-permute-start | bytes 393224 | tf_op jit(solution)/shard_map/ppermute | solution.py:159
  50.4 13.9 %collective-permute-start.6 = (bf16[4,2,2,2,64,128]{5,4,3,2,1,0:T(8,128)(2,1)S(1)}, bf16[4,2,2,2,64,128]{5,4,3,2,1,0:T(8,128)(2,1)S(1)}, u32[]{:S(2)}, u32[]{:S(2)}) collective-permute-start(bf16[4,2,2,2,64,128]{5,4,3,2,1,0:T(8,128)(2,1)S(1)} %get-tuple-element.20), channel_id=1, source_target_pairs={{0,32},{8,40},{16,48},{24,56},{32,64},{40,72},{48,80},{56,88},{64,... | collective-permute-start | bytes 1572872 | tf_op jit(solution)/shard_map/ppermute | solution.py:159
  51.7 24.0 %collective-permute-start.7 = (bf16[4,2,2,2,64,128]{5,4,3,2,1,0:T(8,128)(2,1)S(1)}, bf16[4,2,2,2,64,128]{5,4,3,2,1,0:T(8,128)(2,1)S(1)}, u32[]{:S(2)}, u32[]{:S(2)}) collective-permute-start(bf16[4,2,2,2,64,128]{5,4,3,2,1,0:T(8,128)(2,1)S(1)} %get-tuple-element.20), channel_id=1, source_target_pairs={{0,64},{8,72},{16,80},{24,88},{32,96},{40,104},{48,112},{56,120},{... | collective-permute-start | bytes 1572872 | tf_op jit(solution)/shard_map/ppermute | solution.py:159
  53.7 22.6 %collective-permute-start.8 = (bf16[4,2,2,2,64,128]{5,4,3,2,1,0:T(8,128)(2,1)S(1)}, bf16[4,2,2,2,64,128]{5,4,3,2,1,0:T(8,128)(2,1)S(1)}, u32[]{:S(2)}, u32[]{:S(2)}) collective-permute-start(bf16[4,2,2,2,64,128]{5,4,3,2,1,0:T(8,128)(2,1)S(1)} %get-tuple-element.20), channel_id=1, source_target_pairs={{0,96},{8,104},{16,112},{24,120},{32,0},{40,8},{48,16},{56,24},{64... | collective-permute-start | bytes 1572872 | tf_op jit(solution)/shard_map/ppermute | solution.py:159
  76.6 5.6 %collective-permute-start.9 = (bf16[4,4,2,2,2,64,128]{6,5,4,3,2,1,0:T(8,128)(2,1)S(1)}, bf16[4,4,2,2,2,64,128]{6,5,4,3,2,1,0:T(8,128)(2,1)S(1)}, u32[]{:S(2)}, u32[]{:S(2)}) collective-permute-start(bf16[4,4,2,2,2,64,128]{6,5,4,3,2,1,0:T(8,128)(2,1)S(1)} %pad_maximum_fusion), channel_id=1, source_target_pairs={{0,4},{4,0},{1,5},{5,1},{2,6},{6,2},{3,7},{7,3},{8,12},{12,8},{9,1... | collective-permute-start | bytes 6291464 | tf_op jit(solution)/shard_map/ppermute | solution.py:161
  89.2 0.8 copy-start.1

commit v8 on v7

--- a/solution.py
+++ b/solution.py
@@ -2,6 +2,7 @@
 import jax.numpy as jnp
 from jax import lax
 from jax.experimental import pallas as pl
+from jax.experimental.pallas import tpu as pltpu
 from jax.sharding import Mesh, PartitionSpec as P
 
 HEAD_WIDTH = 128
@@ -17,16 +18,29 @@
     return lax.ppermute(value, axis, pairs)
 
 
-def attend_kernel(q_ref, ks_ref, vs_ref, kv_ref, vv_ref, ms_ref, mv_ref, o_ref, *, group, scale):
+def attend_kernel(
+    off_ref, q_ref, wk_ref, wv_ref, kv_ref, vv_ref, ms_ref, mv_ref, o_ref, *, group, scale, nbd
+):
+    g = pl.program_id(0)
+    i = pl.program_id(1)
     rows = BLOCK_TOKENS * group
+    picked_k, picked_v = [], []
+    for j in range(EXTRA_DIAGONALS + 1):
+        block = jnp.clip(nbd + i - off_ref[g, j], 0, 2 * nbd - 1)
+        start = pl.multiple_of(block * BLOCK_TOKENS, BLOCK_TOKENS)
+        picked_k.append(wk_ref[pl.ds(start, BLOCK_TOKENS), :])
+        picked_v.append(wv_ref[pl.ds(start, BLOCK_TOKENS), :])
+    pad = jnp.zeros(
+        ((SLASH_SLOTS - EXTRA_DIAGONALS - 1) * BLOCK_TOKENS, HEAD_WIDTH), wk_ref.dtype
+    )
+    ks = jnp.concatenate(picked_k + [pad], 0)
+    vs = jnp.concatenate(picked_v + [pad], 0)
     q = q_ref[...]
     q_stack = jnp.concatenate(
         [q[:, h * HEAD_WIDTH : (h + 1) * HEAD_WIDTH] for h in range(group)], axis=0
     )
     nt = (((1,), (1,)), ((), ()))
-    s_slash = (
-        lax.dot_general(q_stack, ks_ref[0, 0], nt, preferred_element_type=jnp.float32) * scale
-    )
+    s_slash = lax.dot_general(q_stack, ks, nt, preferred_element_type=jnp.float32) * scale
     s_vert = lax.dot_general(q_stack, kv_ref[0], nt, preferred_element_type=jnp.float32) * scale
     width = s_slash.shape[1]
     row = jnp.bitwise_and(lax.broadcasted_iota(jnp.int32, (rows, width), 0), BLOCK_TOKENS - 1)
@@ -40,7 +54,7 @@
     w_slash = jnp.exp(s_slash - top)
     w_vert = jnp.exp(s_vert - top)
     total = jnp.sum(w_slash, axis=1, keepdims=True) + jnp.sum(w_vert, axis=1, keepdims=True)
-    acc = jnp.dot(w_slash.astype(jnp.bfloat16), vs_ref[0, 0], preferred_element_type=jnp.float32)
+    acc = jnp.dot(w_slash.astype(jnp.bfloat16), vs, preferred_element_type=jnp.float32)
     acc = acc + jnp.dot(
         w_vert.astype(jnp.bfloat16), vv_ref[0], preferred_element_type=jnp.float32
     )
@@ -51,10 +65,11 @@
         ]
 
 
-def attend(q_all, ks, vs, kv, vv, ms, mv, group, scale):
-    kv_local, nbd = ks.shape[0], ks.shape[1]
-    slash_rows = ks.shape[2]
+def attend(offsets, q_all, win_k, win_v, kv, vv, ms, mv, group, scale):
+    kv_local, nbd = ms.shape[0], ms.shape[1]
+    slash_rows = ms.shape[3]
     vert_rows = kv.shape[1]
+    window_rows = win_k.shape[0]
     cols = group * HEAD_WIDTH
     rows = BLOCK_TOKENS * group
     steps = kv_local * nbd
@@ -62,26 +77,30 @@
     cost = pl.CostEstimate(
         flops=flops,
         transcendentals=steps * rows * (slash_rows + vert_rows),
-        bytes_accessed=2 * (2 * q_all.size + ks.size + vs.size + kv.size + vv.size),
-    )
-    kernel = lambda *refs: attend_kernel(*refs, group=group, scale=scale)
+        bytes_accessed=2 * (2 * q_all.size + win_k.size + win_v.size + kv.size + vv.size),
+    )
+    kernel = lambda *refs: attend_kernel(*refs, group=group, scale=scale, nbd=nbd)
+    grid_spec = pltpu.PrefetchScalarGridSpec(
+        num_scalar_prefetch=1,
+        grid=(kv_local, nbd),
+        in_specs=[
+            pl.BlockSpec((BLOCK_TOKENS, cols), lambda g, i, off: (i, g)),
+            pl.BlockSpec((window_rows, HEAD_WIDTH), lambda g, i, off: (0, g)),
+            pl.BlockSpec((window_rows, HEAD_WIDTH), lambda g, i, off: (0, g)),
+            pl.BlockSpec((1, vert_rows, HEAD_WIDTH), lambda g, i, off: (g, 0, 0)),
+            pl.BlockSpec((1, vert_rows, HEAD_WIDTH), lambda g, i, off: (g, 0, 0)),
+            pl.BlockSpec((1, 1, 1, slash_rows), lambda g, i, off: (g, i, 0, 0)),
+            pl.BlockSpec((1, 1, 1, vert_rows), lambda g, i, off: (g, i, 0, 0)),
+        ],
+        out_specs=pl.BlockSpec((BLOCK_TOKENS, cols), lambda g, i, off: (i, g)),
+    )
     return pl.pallas_call(
         kernel,
-        grid=(kv_local, nbd),
-        in_specs=[
-            pl.BlockSpec((BLOCK_TOKENS, cols), lambda g, i: (i, g)),
-            pl.BlockSpec((1, 1, slash_rows, HEAD_WIDTH), lambda g, i: (g, i, 0, 0)),
-            pl.BlockSpec((1, 1, slash_rows, HEAD_WIDTH), lambda g, i: (g, i, 0, 0)),
-            pl.BlockSpec((1, vert_rows, HEAD_WIDTH), lambda g, i: (g, 0, 0)),
-            pl.BlockSpec((1, vert_rows, HEAD_WIDTH), lambda g, i: (g, 0, 0)),
-            pl.BlockSpec((1, 1, 1, slash_rows), lambda g, i: (g, i, 0, 0)),
-            pl.BlockSpec((1, 1, 1, vert_rows), lambda g, i: (g, i, 0, 0)),
-        ],
-        out_specs=pl.BlockSpec((BLOCK_TOKENS, cols), lambda g, i: (i, g)),
+        grid_spec=grid_spec,
         out_shape=jax.ShapeDtypeStruct(q_all.shape, q_all.dtype),
         cost_estimate=cost,
         interpret=INTERPRET,
-    )(q_all, ks, vs, kv, vv, ms, mv)
+    )(offsets, q_all, win_k, win_v, kv, vv, ms, mv)
 
 
 def local(queries, keys, values, slash, vertical):
@@ -104,12 +123,8 @@
     query_group = queries.shape[1] // heads // HEAD_WIDTH // kv_local
     width = EXTRA_DIAGONALS + 1
     prev_k, prev_v = shifted((k_all, v_all), ("chip", "core"), 1)
-    window_k = jnp.concatenate([prev_k, k_all], 0).reshape(
-        2 * nbd, BLOCK_TOKENS, kv_local, HEAD_WIDTH
-    )
-    window_v = jnp.concatenate([prev_v, v_all], 0).reshape(
-        2 * nbd, BLOCK_TOKENS, kv_local, HEAD_WIDTH
-    )
+    window_k = jnp.concatenate([prev_k, k_all], 0)
+    window_v = jnp.concatenate([prev_v, v_all], 0)
     own_k = k_all.reshape(nbd, BLOCK_TOKENS, kv_local, HEAD_WIDTH)
     own_v = v_all.reshape(nbd, BLOCK_TOKENS, kv_local, HEAD_WIDTH)
     first_head = head_index * kv_local
@@ -158,33 +173,20 @@
                     pairs.append((chip, ((row + step) % side) * side + col))
             moved.append(lax.ppermute(stage, "chip", pairs))
         stage = jnp.stack(moved, 0)
-    partner = lax.ppermute(stage, "core", swap)
-    keys_src = jnp.where(core_index == 0, stage, partner)
-    vals_src = jnp.where(core_index == 0, partner, stage)
     owner_chip = owner // cores
     owner_core = owner % cores
     dy = (chip_index // side - owner_chip // side) % side
     dx = (chip_index % side - owner_chip % side) % side
     heads_idx = jnp.arange(kv_local)[:, None]
-    vert_keys = keys_src[dy, dx, owner_core, heads_idx, rank]
-    vert_vals = vals_src[dy, dx, cores - 1 - owner_core, heads_idx, rank]
-    vert_keys = vert_keys.reshape(kv_local, listed * BLOCK_TOKENS, HEAD_WIDTH)
-    vert_vals = vert_vals.reshape(kv_local, listed * BLOCK_TOKENS, HEAD_WIDTH)
+    part = stage[dy, dx, (owner_core + core_index) % cores, heads_idx, rank]
+    part = part.reshape(kv_local, listed * BLOCK_TOKENS, HEAD_WIDTH)
+    other = lax.ppermute(part, "core", swap)
+    vert_keys = jnp.where(core_index == 0, part, other)
+    vert_vals = jnp.where(core_index == 0, other, part)
     qblocks = seq_index * nbd + jnp.arange(nbd, dtype=jnp.int32)
-    pad = jnp.zeros((nbd, SLASH_SLOTS - width, BLOCK_TOKENS, HEAD_WIDTH), k_all.dtype)
-    slash_k, slash_v, slash_ok, vert_ok = [], [], [], []
+    slash_ok, vert_ok = [], []
     for group_member in range(kv_local):
         offset = diagonal_offsets[group_member]
-        slab_k = window_k[:, :, group_member]
-        slab_v = window_v[:, :, group_member]
-        picked_k = jnp.stack(
-            [lax.dynamic_slice_in_dim(slab_k, nbd - offset[j], nbd, 0) for j in range(width)], 1
-        )
-        picked_v = jnp.stack(
-            [lax.dynamic_slice_in_dim(slab_v, nbd - offset[j], nbd, 0) for j in range(width)], 1
-        )
-        slash_k.append(jnp.concatenate([picked_k, pad], 1))
-        slash_v.append(jnp.concatenate([picked_v, pad], 1))
         block_ok = qblocks[:, None] - offset[None, :] >= 0
         block_ok = jnp.concatenate(
             [block_ok, jnp.zeros((nbd, SLASH_SLOTS - width), jnp.bool_)], 1
@@ -194,11 +196,12 @@
         hit = jnp.any(dist[:, :, None] == offset[None, None, :], axis=2)
         ok = (dist > 0) & jnp.logical_not(hit)
         vert_ok.append(jnp.repeat(ok, BLOCK_TOKENS, axis=1))
-    ks = jnp.stack(slash_k, 0).reshape(kv_local, nbd, SLASH_SLOTS * BLOCK_TOKENS, HEAD_WIDTH)
-    vs = jnp.stack(slash_v, 0).reshape(kv_local, nbd, SLASH_SLOTS * BLOCK_TOKENS, HEAD_WIDTH)
     ms = jnp.stack(slash_ok, 0).astype(jnp.int32)[:, :, None, :]
     mv = jnp.stack(vert_ok, 0).astype(jnp.int32)[:, :, None, :]
-    return attend(q_all, ks, vs, vert_keys, vert_vals, ms, mv, query_group, softmax_scale)
+    return attend(
+        diagonal_offsets, q_all, window_k, window_v, vert_keys, vert_vals, ms, mv,
+        query_group, softmax_scale,
+    )
 
 
 def solution(mesh):

time: 104 us -> 96.7 us (0.930)
  waiting for transfers between devices: 25.8 us -> 37.4 us
  local copies, waits for them, and re-layouts: 20.4 us -> 10.4 us
  between operations: 10.1 us -> 0.29 us
    all_to_all x1, waiting for transfers between devices: 0.01 us -> 6.57 us  [local(): lax.all_to_all(queries, 'head', split_axis=1, concat_axis=0, tiled=True)]
    gather x2 -> x1, local copies, waits for them, and re-layouts: 5.48 us -> 1 us  [local(): part = stage[dy, dx, (owner_core + core_index) % cores, heads_idx, rank]]
    ppermute x6, waiting for transfers between devices: 22 us -> 25.7 us  [local(): moved.append(lax.ppermute(stage, 'chip', pairs))]
    dynamic_slice x4 -> x1, local copies, waits for them, and re-layouts: 3.16 us -> 0.07 us  [local(): local_slash = lax.dynamic_slice_in_dim(slash, first_head, kv_local, 0) + 1]
    all_to_all x1, waiting for transfers between devices: 2.33 us -> 4.38 us  [local(): lax.all_to_all(joined, 'head', split_axis=1, concat_axis=0, tiled=True)]
    another operation x2 -> x0, other arithmetic: 1.92 us -> none  [the longest x1 0.96 us: local(): jnp.stack(slash_v, 0)]
    slice x4 -> x0, local copies, waits for them, and re-layouts: 1.77 us -> none  [the longest x1 0.65 us: local(): offset[j]]
    ppermute x1, waiting for transfers between devices: 1.49 us -> 0.01 us  [local(): other = lax.ppermute(part, 'core', swap)]
  transfers between devices with their start and end apart: 12 -> 12, of which waited for: 6 -> 7; matrix products, arithmetic and copies ran while one was open for 19% -> 10% of each run, Pallas kernels for 0% -> 0%
where the time goes in v8:
time: 96.7 us; the launch traced here: 96.3 us
  waiting for transfers between devices  37.4 us (39%)
  starting transfers between devices  28.8 us (30%)
  Pallas kernels  13.9 us (14%)
  local copies, waits for them, and re-layouts  10.4 us (11%)
  other arithmetic  5.5 us (6%)
    ppermute x6, waiting for transfers between devices, local(): moved.append(lax.ppermute(stage, 'chip', pairs))  25.7 us
    pallas_call x1, Pallas kernels, attend(): pl.pallas_call(kernel, grid_spec=grid_spec, out_shape=jax.ShapeDtypeStruc...  13.9 us
    ppermute x6, starting transfers between devices, local(): moved.append(lax.ppermute(stage, 'chip', pairs))  9.94 us
    all_to_all x1, waiting for transfers between devices, local(): lax.all_to_all(queries, 'head', split_axis=1, concat_axis=0, tiled=True)  6.57 us
    all_to_all x1, starting transfers between devices, local(): lax.all_to_all(joined, 'head', split_axis=1, concat_axis=0, tiled=True)  5.84 us
    ppermute x2, starting transfers between devices, shifted(): return lax.ppermute(value, axis, pairs)  5.3 us
    all_to_all x1, waiting for transfers between devices, local(): lax.all_to_all(joined, 'head', split_axis=1, concat_axis=0, tiled=True)  4.38 us
    all_to_all x1, starting transfers between devices, local(): lax.all_to_all(queries, 'head', split_axis=1, concat_axis=0, tiled=True)  3.47 us
  transfers between devices with their start and end apart: 12, of which 7 were waited for; matrix products, arithmetic and copies ran while one was open for 10% of the time, Pallas kernels for 0%

profile of v8, /device:TPU:1, one launch (start us, length us, event | category | flops | bytes accessed | tf_op | source)
XLA Modules:
  0.0 96.3 jit_solution(17348425301253520756)
XLA Ops:
  0.0 1.0 %copy_bitcast_fusion.1 = (bf16[64,4,256]{2,0,1:T(8,128)(2,1)S(1)}, bf16[64,4,256]{2,0,1:T(8,128)(2,1)S(1)}) fusion(bf16[8,4,8,256]{3,2,1,0:T(8,128)(2,1)} %bitcast.108, bf16[8,4,8,256]{3,2,1,0:T(8,128)(2,1)} %bitcast.109), kind=kLoop, calls=%fused_computation.13 | loop fusion | bytes 524288 | tf_op jit(solution)/shard_map/reshape | solution.py:114
  1.0 0.7 pad_maximum_fusion.2
  1.7 5.8 %all-to-all-start = ((bf16[64,4,512]{2,0,1:T(8,128)(2,1)}), bf16[64,4,512]{2,0,1:T(8,128)(2,1)S(1)}, u32[]{:S(2)}, u32[]{:S(2)}) async-start(bf16[64,4,512]{2,0,1:T(8,128)(2,1)} %pad_maximum_fusion.2), calls=%async_computation | async-start | bytes 524288 | tf_op jit(solution)/shard_map/all_to_all | solution.py:116
  7.6 0.7 and_select_fusion.8
  8.3 0.2 convert_reduce_fusion
  8.5 0.2 fusion
  8.8 4.4 %all-to-all-done = bf16[64,4,512]{2,0,1:T(8,128)(2,1)S(1)} async-done(((bf16[64,4,512]{2,0,1:T(8,128)(2,1)}), bf16[64,4,512]{2,0,1:T(8,128)(2,1)S(1)}, u32[]{:S(2)}, u32[]{:S(2)}) %all-to-all-start) | async-done | bytes 262176 | tf_op jit(solution)/shard_map/all_to_all | solution.py:116
  13.2 0.2 fusion.22
  13.5 0.2 fusion.21
  13.7 0.6 gather_fusion.1
  14.2 0.6 gather_fusion
  14.8 0.6 gather_fusion.2
  15.4 0.6 gather_fusion.3
  16.0 2.2 %collective-permute-start.2 = (bf16[2,2,64,128]{3,2,1,0:T(8,128)(2,1)S(1)}, bf16[2,2,64,128]{3,2,1,0:T(8,128)(2,1)S(1)}, u32[]{:S(2)}, u32[]{:S(2)}) collective-permute-start(bf16[2,2,64,128]{3,2,1,0:T(8,128)(2,1)S(1)} %get-tuple-element.24), channel_id=1, source_target_pairs={{0,4},{4,0},{1,5},{5,1},{2,6},{6,2},{3,7},{7,3},{8,12},{12,8},{9,1... | collective-permute-start | bytes 196616 | tf_op jit(solution)/shard_map/ppermute | solution.py:162
  18.3 0.1 copy.52
  18.4 0.7 collective-permute-done.2
  19.1 1.3 %collective-permute-start.3 = (bf16[2,2,2,64,128]{4,3,2,1,0:T(8,128)(2,1)S(1)}, bf16[2,2,2,64,128]{4,3,2,1,0:T(8,128)(2,1)S(1)}, u32[]{:S(2)}, u32[]{:S(2)}) collective-permute-start(bf16[2,2,2,64,128]{4,3,2,1,0:T(8,128)(2,1)S(1)} %get-tuple-element.22), channel_id=1, source_target_pairs={{0,8},{8,16},{16,24},{24,0},{32,40},{40,48},{48,56},{56,32},{64,72... | collective-permute-start | bytes 393224 | tf_op jit(solution)/shard_map/ppermute | solution.py:174
  20.4 2.5 %collective-permute-start.4 = (bf16[2,2,2,64,128]{4,3,2,1,0:T(8,128)(2,1)S(1)}, bf16[2,2,2,64,128]{4,3,2,1,0:T(8,128)(2,1)S(1)}, u32[]{:S(2)}, u32[]{:S(2)}) collective-permute-start(bf16[2,2,2,64,128]{4,3,2,1,0:T(8,128)(2,1)S(1)} %get-tuple-element.22), channel_id=1, source_target_pairs={{0,16},{8,24},{16,0},{24,8},{32,48},{40,56},{48,32},{56,40},{64,80... | collective-permute-start | bytes 393224 | tf_op jit(solution)/shard_map/ppermute | solution.py:174
  22.9 1.2 %collective-permute-start.5 = (bf16[2,2,2,64,128]{4,3,2,1,0:T(8,128)(2,1)S(1)}, bf16[2,2,2,64,128]{4,3,2,1,0:T(8,128)(2,1)S(1)}, u32[]{:S(2)}, u32[]{:S(2)}) collective-permute-start(bf16[2,2,2,64,128]{4,3,2,1,0:T(8,128)(2,1)S(1)} %get-tuple-element.22), channel_id=1, source_target_pairs={{0,24},{8,0},{16,8},{24,16},{32,56},{40,32},{48,40},{56,48},{64,88... | collective-permute-start | bytes 393224 | tf_op jit(solution)/shard_map/ppermute | solution.py:174
  24.2 0.9 collective-permute-done.3
  25.1 3.8 %collective-permute-done.4 = bf16[2,2,2,64,128]{4,3,2,1,0:T(8,128)(2,1)S(1)} collective-permute-done((bf16[2,2,2,64,128]{4,3,2,1,0:T(8,128)(2,1)S(1)}, bf16[2,2,2,64,128]{4,3,2,1,0:T(8,128)(2,1)S(1)}, u32[]{:S(2)}, u32[]{:S(2)}) %collective-permute-start.4) | collective-permute-done | bytes 131104 | tf_op jit(solution)/shard_map/ppermute | solution.py:174
  28.9 0.1 fusion.20
  29.0 1.4 %collective-permute-start.6 = (bf16[4,2,2,2,64,128]{5,4,3,2,1,0:T(8,128)(2,1)S(1)}, bf16[4,2,2,2,64,128]{5,4,3,2,1,0:T(8,128)(2,1)S(1)}, u32[]{:S(2)}, u32[]{:S(2)}) collective-permute-start(bf16[4,2,2,2,64,128]{5,4,3,2,1,0:T(8,128)(2,1)S(1)} %get-tuple-element.16), channel_id=1, source_target_pairs={{0,32},{8,40},{16,48},{24,56},{32,64},{40,72},{48,80},{56,88},{64,... | collective-permute-start | bytes 1572872 | tf_op jit(solution)/shard_map/ppermute | solution.py:174
  30.4 2.6 %collective-permute-start.7 = (bf16[4,2,2,2,64,128]{5,4,3,2,1,0:T(8,128)(2,1)S(1)}, bf16[4,2,2,2,64,128]{5,4,3,2,1,0:T(8,128)(2,1)S(1)}, u32[]{:S(2)}, u32[]{:S(2)}) collective-permute-start(bf16[4,2,2,2,64,128]{5,4,3,2,1,0:T(8,128)(2,1)S(1)} %get-tuple-element.16), channel_id=1, source_target_pairs={{0,64},{8,72},{16,80},{24,88},{32,96},{40,104},{48,112},{56,120},{... | collective-permute-start | bytes 1572872 | tf_op jit(solution)/shard_map/ppermute | solution.py:174
  33.0 1.1 %collective-permute-start.8 = (bf16[4,2,2,2,64,128]{5,4,3,2,1,0:T(8,128)(2,1)S(1)}, bf16[4,2,2,2,64,128]{5,4,3,2,1,0:T(8,128)(2,1)S(1)}, u32[]{:S(2)}, u32[]{:S(2)}) collective-permute-start(bf16[4,2,2,2,64,128]{5,4,3,2,1,0:T(8,128)(2,1)S(1)} %get-tuple-element.16), channel_id=1, source_target_pairs={{0,96},{8,104},{16,112},{24,120},{32,0},{40,8},{48,16},{56,24},{64... | collective-permute-start | bytes 1572872 | tf_op jit(solution)/shard_map/ppermute | solution.py:174
  34.1 8.5 %collective-permute-done.6 = bf16[4,2,2,2,64,128]{5,4,3,2,1,0:T(8,128)(2,1)S(1)} collective-permute-done((bf16[4,2,2,2,64,128]{5,4,3,2,1,0:T(8,128)(2,1)S(1)}, bf16[4,2,2,2,64,128]{5,4,3,2,1,0:T(8,128)(2,1)S(1)}, u32[]{:S(2)}, u32[]{:S(2)}) %collective-permute-start.6) | collective-permute-done | bytes 524320 | tf_op jit(solution)/shard_map/ppermute | solution.py:174
  42.7 12.4 %collective-permute-done.7 = bf16[4,2,2,2,64,128]{5,4,3,2,1,0:T(8,128)(2,1)S(1)} collective-permute-done((bf16[4,2,2,2,64,128]{5,4,3,2,1,0:T(8,128)(2,1)S(1)}, bf16[4,2,2,2,64,128]{5,4,3,2,1,0:T(8,128)(2,1)S(1)}, u32[]{:S(2)}, u32[]{:S(2)}) %collective-permute-start.7) | collective-permute-done | bytes 524320 | tf_op jit(solution)/shard_map/ppermute | solution.py:174
  55.1 0.3 pad_maximum_fusion
  55.3 1.0 %gather_fusion.4 = bf16[64,64,128]{2,1,0:T(8,128)(2,1)S(1)} fusion(bf16[4,4,2,2,2,64,128]{6,5,4,3,2,1,0:T(8,128)(2,1)S(1)} %pad_maximum_fusion, s32[64]{0:T(128)S(1)} %reshape.260), kind=kCustom, calls=%fused_computation.4 | custom fusion | bytes 2098432 | tf_op jit(solution)/shard_map/gather | solution.py:181
  56.3 2.1 %collective-permute-start.9 = (bf16[2,2048,128]{2,1,0:T(8,128)(2,1)S(1)}, bf16[2,2048,128]{2,1,0:T(8,128)(2,1)S(1)}, u32[]{:S(2)}, u32[]{:S(2)}) collective-permute-start(bf16[2,2048,128]{2,1,0:T(8,128)(2,1)S(1)} %bitcast.89), channel_id=1, source_target_pairs={{0,4},{4,0},{1,5},{5,1},{2,6},{6,2},{3,7},{7,3},{8,12},{12,8},{9,1... | collective-permute-start | bytes 3145736 | tf_op jit(solution)/shard_map/ppermute | solution.py:183
  58.6 0.1 broadcast_in_dim.36
  58.7 0.1 stack.105
  58.9 0.1 stack.106
  59.0 2.9 %collective-permute-start = (bf16[256,256]{1,0:T(8,128)(2,1)S(1)}, bf16[256,256]{1,0:T(8,128)(2,1)S(1)}, u32[]{:S(2)}, u32[]{:S(2)}) collective-permute-start(bf16[256,256]{1,0:T(8,128)(2,1)S(1)} %get-tuple-element.18), channel_id=1, source_target_pairs={{0,4},{4,8},{8,12},{12,16},{16,20},{20,24},{24,28},{28,32},{32,36}... | collective-permute-start | bytes 393224 | tf_op jit(solution)/shard_map/ppermute | solution.py:18
  62.1 0.1 stack.102
  62.3 0.1 stack.103
  62.4 2.4 %collective-permute-start.1 = (bf16[256,256]{1,0:T(8,128)(2,1)S(1)}, bf16[256,256]{1,0:T(8,128)(2,1)S(1)}, u32[]{:S(2)}, u32[]{:S(2)}) collective-permute-start(bf16[256,256]{1,0:T(8,128)(2,1)S(1)} %get-tuple-element.17), channel_id=1, source_target_pairs={{0,4},{4,8},{8,12},{12,16},{16,20},{20,24},{24,28},{28,32},{32,36}... | collective-permute-start | bytes 393224 | tf_op jit(solution)/shard_map/ppermute | solution.py:18
  64.8 0.6 concatenate.35.refs_0_
  65.4 0.7 copy.51.refs_7_
  66.1 0.6 copy.50.refs_6_
  66.7 1.9 %copy.67 = bf16[8,4,8,1024]{3,2,0,1:T(8,128)(2,1)} copy(bf16[8,4,8,1024]{3,2,1,0:T(8,128)(2,1)} %bitcast.92) | data formatting | bytes 1048576 | tf_op jit(solution)/shard_map/all_to_all | solution.py:163
  68.6 3.5 %all-to-all-start.1 = ((bf16[64,4,1024]{2,0,1:T(8,128)(2,1)}), bf16[64,4,1024]{2,0,1:T(8,128)(2,1)S(1)}, u32[]{:S(2)}, u32[]{:S(2)}) async-start(bf16[64,4,1024]{2,0,1:T(8,128)(2,1)} %bitcast.83), calls=%async_computation.1 | async-start | bytes 1048576 | tf_op jit(solution)/shard_map/all_to_all | solution.py:163
  72.1 0.7 pad_maximum_fusion.3.refs_2_
  72.8 0.7 pad_maximum_fusion.4.refs_3_
  73.6 1.5 %broadcast_select_fusion = (bf16[2,2048,128]{2,1,0:T(8,128)(2,1)}, bf16[2,2048,128]{2,1,0:T(8,128)(2,1)}) fusion(bf16[2,2048,128]{2,1,0:T(8,128)(2,1)S(1)} %collective-permute-done.9, pred[]{:T(512)S(6)} %eq.79, bf16[2,2048,128]{2,1,0:T(8,128)(2,1)S(1)} %bitcast.90), kind=kLoop, calls=%fused_computation.6 | loop fusion | flops 1048576 | bytes 4194305 | tf_op jit(solution)/shard_map/jit(_where)/select_n | solution.py:185
  75.0 6.6 %all-to-all-done.1 = bf16[64,4,1024]{2,0,1:T(8,128)(2,1)S(1)} async-done(((bf16[64,4,1024]{2,0,1:T(8,128)(2,1)}), bf16[64,4,1024]{2,0,1:T(8,128)(2,1)S(1)}, u32[]{:S(2)}, u32[]{:S(2)}) %all-to-all-start.1) | async-done | bytes 524320 | tf_op jit(solution)/shard_map/all_to_all | solution.py:163
  81.6 0.8 copy-done.1
  82.4 13.9 %shard_map.55 = bf16[256,1024]{1,0:T(8,128)(2,1)} custom-call(s32[2,5]{1,0:T(2,128)} %concatenate.35.refs_0_, bf16[256,1024]{1,0:T(8,128)(2,1)} %bitcast.93, bf16[512,256]{1,0:T(8,128)(2,1)} %pad_maximum_fusion.3.refs_2_, bf16[512,256]{1,0:T(8,128)(2,1)} %pad_maximum_fusion.4.refs_3_, bf16[2,2048,128]{2,1,0:T(8,128)(2,1)} %get-tuple-element.14.refs_4_, ...), custom_call_target="tpu_custom_call" | custom-call | flops 2550136832 | bytes 3670016 | tf_op jit(solution)/shard_map/pallas_call | solution.py:97
  (42 shorter events, 1.2 us)
Async XLA Ops:
  0.0 18.2 %copy-start = (s32[8,4]{0,1:T(4,128)S(1)}, s32[8,4]{0,1:T(4,128)}, u32[]{:S(2)}) copy-start(s32[8,4]{0,1:T(4,128)} %param.8) | copy-start | bytes 388
  1.7 11.4 %all-to-all-start = ((bf16[64,4,512]{2,0,1:T(8,128)(2,1)}), bf16[64,4,512]{2,0,1:T(8,128)(2,1)S(1)}, u32[]{:S(2)}, u32[]{:S(2)}) async-start(bf16[64,4,512]{2,0,1:T(8,128)(2,1)} %pad_maximum_fusion.2), calls=%async_computation | async-start | bytes 524288 | tf_op jit(solution)/shard_map/all_to_all | solution.py:116
  16.0 3.1 %collective-permute-start.2 = (bf16[2,2,64,128]{3,2,1,0:T(8,128)(2,1)S(1)}, bf16[2,2,64,128]{3,2,1,0:T(8,128)(2,1)S(1)}, u32[]{:S(2)}, u32[]{:S(2)}) collective-permute-start(bf16[2,2,64,128]{3,2,1,0:T(8,128)(2,1)S(1)} %get-tuple-element.24), channel_id=1, source_target_pairs={{0,4},{4,0},{1,5},{5,1},{2,6},{6,2},{3,7},{7,3},{8,12},{12,8},{9,1... | collective-permute-start | bytes 196616 | tf_op jit(solution)/shard_map/ppermute | solution.py:162
  19.1 6.0 %collective-permute-start.3 = (bf16[2,2,2,64,128]{4,3,2,1,0:T(8,128)(2,1)S(1)}, bf16[2,2,2,64,128]{4,3,2,1,0:T(8,128)(2,1)S(1)}, u32[]{:S(2)}, u32[]{:S(2)}) collective-permute-start(bf16[2,2,2,64,128]{4,3,2,1,0:T(8,128)(2,1)S(1)} %get-tuple-element.22), channel_id=1, source_target_pairs={{0,8},{8,16},{16,24},{24,0},{32,40},{40,48},{48,56},{56,32},{64,72... | collective-permute-start | bytes 393224 | tf_op jit(solution)/shard_map/ppermute | solution.py:174
  20.4 8.5 %collective-permute-start.4 = (bf16[2,2,2,64,128]{4,3,2,1,0:T(8,128)(2,1)S(1)}, bf16[2,2,2,64,128]{4,3,2,1,0:T(8,128)(2,1)S(1)}, u32[]{:S(2)}, u32[]{:S(2)}) collective-permute-start(bf16[2,2,2,64,128]{4,3,2,1,0:T(8,128)(2,1)S(1)} %get-tuple-element.22), channel_id=1, source_target_pairs={{0,16},{8,24},{16,0},{24,8},{32,48},{40,56},{48,32},{56,40},{64,80... | collective-permute-start | bytes 393224 | tf_op jit(solution)/shard_map/ppermute | solution.py:174
  22.9 6.0 %collective-permute-start.5 = (bf16[2,2,2,64,128]{4,3,2,1,0:T(8,128)(2,1)S(1)}, bf16[2,2,2,64,128]{4,3,2,1,0:T(8,128)(2,1)S(1)}, u32[]{:S(2)}, u32[]{:S(2)}) collective-permute-start(bf16[2,2,2,64,128]{4,3,2,1,0:T(8,128)(2,1)S(1)} %get-tuple-element.22), channel_id=1, source_target_pairs={{0,24},{8,0},{16,8},{24,16},{32,56},{40,32},{48,40},{56,48},{64,88... | collective-permute-start | bytes 393224 | tf_op jit(solution)/shard_map/ppermute | solution.py:174
  29.0 13.7 %collective-permute-start.6 = (bf16[4,2,2,2,64,128]{5,4,3,2,1,0:T(8,128)(2,1)S(1)}, bf16[4,2,2,2,64,128]{5,4,3,2,1,0:T(8,128)(2,1)S(1)}, u32[]{:S(2)}, u32[]{:S(2)}) collective-permute-start(bf16[4,2,2,2,64,128]{5,4,3,2,1,0:T(8,128)(2,1)S(1)} %get-tuple-element.16), channel_id=1, source_target_pairs={{0,32},{8,40},{16,48},{24,56},{32,64},{40,72},{48,80},{56,88},{64,... | collective-permute-start | bytes 1572872 | tf_op jit(solution)/shard_map/ppermute | solution.py:174
  30.4 24.7 %collective-permute-start.7 = (bf16[4,2,2,2,64,128]{5,4,3,2,1,0:T(8,128)(2,1)S(1)}, bf16[4,2,2,2,64,128]{5,4,3,2,1,0:T(8,128)(2,1)S(1)}, u32[]{:S(2)}, u32[]{:S(2)}) collective-permute-start(bf16[4,2,2,2,64,128]{5,4,3,2,1,0:T(8,128)(2,1)S(1)} %get-tuple-element.16), channel_id=1, source_target_pairs={{0,64},{8,72},{16,80},{24,88},{32,96},{40,104},{48,112},{56,120},{... | collective-permute-start | bytes 1572872 | tf_op jit(solution)/shard_map/ppermute | solution.py:174
  33.0 22.1 %collective-permute-start.8 = (bf16[4,2,2,2,64,128]{5,4,3,2,1,0:T(8,128)(2,1)S(1)}, bf16[4,2,2,2,64,128]{5,4,3,2,1,0:T(8,128)(2,1)S(1)}, u32[]{:S(2)}, u32[]{:S(2)}) collective-permute-start(bf16[4,2,2,2,64,128]{5,4,3,2,1,0:T(8,128)(2,1)S(1)} %get-tuple-element.16), channel_id=1, source_target_pairs={{0,96},{8,104},{16,112},{24,120},{32,0},{40,8},{48,16},{56,24},{64... | collective-permute-start | bytes 1572872 | tf_op jit(solution)/shard_map/ppermute | solution.py:174
  56.3 17.2 %collective-permute-start.9 = (bf16[2,2048,128]{2,1,0:T(8,128)(2,1)S(1)}, bf16[2,2048,128]{2,1,0:T(8,128)(2,1)S(1)}, u32[]{:S(2)}, u32[]{:S(2)}) collective-permute-start(bf16[2,2048,128]{2,1,0:T(8,128)(2,1)S(1)} %bitcast.89), channel_id=1, source_target_pairs={{0,4},{4,0},{1,5},{5,1},{2,6},{6,2},{3,7},{7,3},{8,12},{12,8},{9,1... | collective-permute-start | bytes 3145736 | tf_op jit(solution)/shard_map/ppermute | solution.py:183
  59.0 13.1 %collective-permute-start = (bf16[256,256]{1,0:T(8,128)(2,1)S(1)}, bf16[256,256]{1,0:T(8,128)(2,1)S(1)}, u32[]{:S(2)}, u32[]{:S(2)}) collective-permute-start(bf16[256,256]{1,0:T(8,128)(2,1)S(1)} %get-tuple-element.18), channel_id=1, source_target_pairs={{0,4},{4,8},{8,12},{12,16},{16,20},{20,24},{24,28},{28,32},{32,36}... | collective-permute-start | bytes 393224 | tf_op jit(solution)/shard_map/ppermute | solution.py:18
  62.4 10.5 %collective-permute-start.1 = (bf16[256,256]{1,0:T(8,128)(2,1)S(1)}, bf16[256,256]{1,0:T(8,128)(2,1)S(1)}, u32[]{:S(2)}, u32[]{:S(2)}) collective-permute-start(bf16[256,256]{1,0:T(8,128)(2,1)S(1)} %get-tuple-element.17), channel_id=1, source_target_pairs={{0,4},{4,8},{8,12},{12,16},{16,20},{20,24},{24,28},{28,32},{32,36}... | collective-permute-start | bytes 393224 | tf_op jit(solution)/shard_map/ppermute | solution.py:18
  68.6 13.0 %all-to-all-start.1 = ((bf16[64,4,1024]{2,0,1:T(8,128)(2,1)}), bf16[64,4,1024]{2,0,1:T(8,128)(2,1)S(1)}, u32[]{:S(2)}, u32[]{:S(2)}) async-start(bf16[64,4,1024]{2,0,1:T(8,128)(2,1)} %bitcast.83), calls=%async_computation.1 | async-start | bytes 1048576 | tf_op jit(solution)/shard_map/all_to_all | solution.py:163
  81.6 0.8 copy-start.1

commit v9 on v8

--- a/solution.py
+++ b/solution.py
@@ -123,8 +123,6 @@
     query_group = queries.shape[1] // heads // HEAD_WIDTH // kv_local
     width = EXTRA_DIAGONALS + 1
     prev_k, prev_v = shifted((k_all, v_all), ("chip", "core"), 1)
-    window_k = jnp.concatenate([prev_k, k_all], 0)
-    window_v = jnp.concatenate([prev_v, v_all], 0)
     own_k = k_all.reshape(nbd, BLOCK_TOKENS, kv_local, HEAD_WIDTH)
     own_v = v_all.reshape(nbd, BLOCK_TOKENS, kv_local, HEAD_WIDTH)
     first_head = head_index * kv_local
@@ -173,6 +171,8 @@
                     pairs.append((chip, ((row + step) % side) * side + col))
             moved.append(lax.ppermute(stage, "chip", pairs))
         stage = jnp.stack(moved, 0)
+        if stride == 1:
+            stage, q_all, prev_k, prev_v = lax.optimization_barrier((stage, q_all, prev_k, prev_v))
     owner_chip = owner // cores
     owner_core = owner % cores
     dy = (chip_index // side - owner_chip // side) % side
@@ -183,6 +183,8 @@
     other = lax.ppermute(part, "core", swap)
     vert_keys = jnp.where(core_index == 0, part, other)
     vert_vals = jnp.where(core_index == 0, other, part)
+    window_k = jnp.concatenate([prev_k, k_all], 0)
+    window_v = jnp.concatenate([prev_v, v_all], 0)
     qblocks = seq_index * nbd + jnp.arange(nbd, dtype=jnp.int32)
     slash_ok, vert_ok = [], []
     for group_member in range(kv_local):

time: 96.7 us -> 88.3 us (0.913)
  waiting for transfers between devices: 37.4 us -> 25.3 us
  other arithmetic: 5.5 us -> 9.02 us
  starting transfers between devices: 28.8 us -> 30.1 us
  local copies, waits for them, and re-layouts: 10.4 us -> 9.24 us
    all_to_all x1, waiting for transfers between devices: 6.57 us -> 0.01 us  [local(): lax.all_to_all(queries, 'head', split_axis=1, concat_axis=0, tiled=True)]
    ppermute x6, waiting for transfers between devices: 25.7 us -> 19.9 us  [local(): moved.append(lax.ppermute(stage, 'chip', pairs))]
    ppermute x1, starting transfers between devices: 2.11 us -> 3.85 us  [local(): other = lax.ppermute(part, 'core', swap)]
    ppermute x2, waiting for transfers between devices: 0.01 us -> 1.08 us  [shifted(): return lax.ppermute(value, axis, pairs)]
    all_to_all x1, local copies, waits for them, and re-layouts: 1.87 us -> 0.83 us  [local(): lax.all_to_all(queries, 'head', split_axis=1, concat_axis=0, tiled=True)]
  transfers between devices with their start and end apart: 12 -> 12, of which waited for: 7 -> 5; matrix products, arithmetic and copies ran while one was open for 10% -> 12% of each run, Pallas kernels for 0% -> 0%
where the time goes in v9:
time: 88.3 us; the launch traced here: 87.9 us
  starting transfers between devices  30.1 us (34%)
  waiting for transfers between devices  25.3 us (29%)
  Pallas kernels  13.9 us (16%)
  local copies, waits for them, and re-layouts  9.24 us (10%)
  other arithmetic  9.02 us (10%)
    ppermute x6, waiting for transfers between devices, local(): moved.append(lax.ppermute(stage, 'chip', pairs))  19.9 us
    pallas_call x1, Pallas kernels, attend(): pl.pallas_call(kernel, grid_spec=grid_spec, out_shape=jax.ShapeDtypeStruc...  13.9 us
    ppermute x6, starting transfers between devices, local(): moved.append(lax.ppermute(stage, 'chip', pairs))  9.87 us
    all_to_all x1, starting transfers between devices, local(): lax.all_to_all(joined, 'head', split_axis=1, concat_axis=0, tiled=True)  5.84 us
    ppermute x2, starting transfers between devices, shifted(): return lax.ppermute(value, axis, pairs)  4.88 us
    all_to_all x1, waiting for transfers between devices, local(): lax.all_to_all(joined, 'head', split_axis=1, concat_axis=0, tiled=True)  4.38 us
    ppermute x1, starting transfers between devices, local(): other = lax.ppermute(part, 'core', swap)  3.85 us
    all_to_all x1, starting transfers between devices, local(): lax.all_to_all(queries, 'head', split_axis=1, concat_axis=0, tiled=True)  3.47 us
  transfers between devices with their start and end apart: 12, of which 5 were waited for; matrix products, arithmetic and copies ran while one was open for 12% of the time, Pallas kernels for 0%

profile of v9, /device:TPU:1, one launch (start us, length us, event | category | flops | bytes accessed | tf_op | source)
XLA Modules:
  0.0 87.9 jit_solution(1155460444196184769)
XLA Ops:
  0.0 1.0 %copy_bitcast_fusion.1 = (bf16[64,4,256]{2,0,1:T(8,128)(2,1)S(1)}, bf16[64,4,256]{2,0,1:T(8,128)(2,1)S(1)}) fusion(bf16[8,4,8,256]{3,2,1,0:T(8,128)(2,1)} %bitcast.105, bf16[8,4,8,256]{3,2,1,0:T(8,128)(2,1)} %bitcast.106), kind=kLoop, calls=%fused_computation.13 | loop fusion | bytes 524288 | tf_op jit(solution)/shard_map/reshape | solution.py:114
  1.0 0.7 pad_maximum_fusion.2
  1.7 5.8 %all-to-all-start = ((bf16[64,4,512]{2,0,1:T(8,128)(2,1)}), bf16[64,4,512]{2,0,1:T(8,128)(2,1)S(1)}, u32[]{:S(2)}, u32[]{:S(2)}) async-start(bf16[64,4,512]{2,0,1:T(8,128)(2,1)} %pad_maximum_fusion.2), calls=%async_computation | async-start | bytes 524288 | tf_op jit(solution)/shard_map/all_to_all | solution.py:116
  7.6 0.7 and_select_fusion.8
  8.3 0.2 convert_reduce_fusion
  8.5 0.2 fusion
  8.8 4.4 %all-to-all-done = bf16[64,4,512]{2,0,1:T(8,128)(2,1)S(1)} async-done(((bf16[64,4,512]{2,0,1:T(8,128)(2,1)}), bf16[64,4,512]{2,0,1:T(8,128)(2,1)S(1)}, u32[]{:S(2)}, u32[]{:S(2)}) %all-to-all-start) | async-done | bytes 262176 | tf_op jit(solution)/shard_map/all_to_all | solution.py:116
  13.2 0.2 fusion.21
  13.5 0.2 fusion.20
  13.7 0.6 gather_fusion.1
  14.2 0.6 gather_fusion
  14.8 0.6 gather_fusion.2
  15.4 0.6 gather_fusion.3
  16.0 2.2 %collective-permute-start = (bf16[2,2,64,128]{3,2,1,0:T(8,128)(2,1)S(1)}, bf16[2,2,64,128]{3,2,1,0:T(8,128)(2,1)S(1)}, u32[]{:S(2)}, u32[]{:S(2)}) collective-permute-start(bf16[2,2,64,128]{3,2,1,0:T(8,128)(2,1)S(1)} %get-tuple-element.30), channel_id=1, source_target_pairs={{0,4},{4,0},{1,5},{5,1},{2,6},{6,2},{3,7},{7,3},{8,12},{12,8},{9,1... | collective-permute-start | bytes 196616 | tf_op jit(solution)/shard_map/ppermute | solution.py:160
  18.3 0.1 copy.52
  18.4 0.8 copy.67
  19.2 3.5 %all-to-all-start.1 = ((bf16[64,4,1024]{2,0,1:T(8,128)(2,1)}), bf16[64,4,1024]{2,0,1:T(8,128)(2,1)S(1)}, u32[]{:S(2)}, u32[]{:S(2)}) async-start(bf16[64,4,1024]{2,0,1:T(8,128)(2,1)} %bitcast.82), calls=%async_computation.1 | async-start | bytes 1048576 | tf_op jit(solution)/shard_map/all_to_all | solution.py:161
  22.7 1.3 %collective-permute-start.1 = (bf16[2,2,2,64,128]{4,3,2,1,0:T(8,128)(2,1)S(1)}, bf16[2,2,2,64,128]{4,3,2,1,0:T(8,128)(2,1)S(1)}, u32[]{:S(2)}, u32[]{:S(2)}) collective-permute-start(bf16[2,2,2,64,128]{4,3,2,1,0:T(8,128)(2,1)S(1)} %get-tuple-element.28), channel_id=1, source_target_pairs={{0,8},{8,16},{16,24},{24,0},{32,40},{40,48},{48,56},{56,32},{64,72... | collective-permute-start | bytes 393224 | tf_op jit(solution)/shard_map/ppermute | solution.py:172
  24.0 2.5 %collective-permute-start.2 = (bf16[2,2,2,64,128]{4,3,2,1,0:T(8,128)(2,1)S(1)}, bf16[2,2,2,64,128]{4,3,2,1,0:T(8,128)(2,1)S(1)}, u32[]{:S(2)}, u32[]{:S(2)}) collective-permute-start(bf16[2,2,2,64,128]{4,3,2,1,0:T(8,128)(2,1)S(1)} %get-tuple-element.28), channel_id=1, source_target_pairs={{0,16},{8,24},{16,0},{24,8},{32,48},{40,56},{48,32},{56,40},{64,80... | collective-permute-start | bytes 393224 | tf_op jit(solution)/shard_map/ppermute | solution.py:172
  26.5 1.2 %collective-permute-start.3 = (bf16[2,2,2,64,128]{4,3,2,1,0:T(8,128)(2,1)S(1)}, bf16[2,2,2,64,128]{4,3,2,1,0:T(8,128)(2,1)S(1)}, u32[]{:S(2)}, u32[]{:S(2)}) collective-permute-start(bf16[2,2,2,64,128]{4,3,2,1,0:T(8,128)(2,1)S(1)} %get-tuple-element.28), channel_id=1, source_target_pairs={{0,24},{8,0},{16,8},{24,16},{32,56},{40,32},{48,40},{56,48},{64,88... | collective-permute-start | bytes 393224 | tf_op jit(solution)/shard_map/ppermute | solution.py:172
  27.6 3.0 %collective-permute-start.4 = (bf16[256,256]{1,0:T(8,128)(2,1)S(1)}, bf16[256,256]{1,0:T(8,128)(2,1)S(1)}, u32[]{:S(2)}, u32[]{:S(2)}) collective-permute-start(bf16[256,256]{1,0:T(8,128)(2,1)S(1)} %get-tuple-element.24), channel_id=1, source_target_pairs={{0,4},{4,8},{8,12},{12,16},{16,20},{20,24},{24,28},{28,32},{32,36}... | collective-permute-start | bytes 393224 | tf_op jit(solution)/shard_map/ppermute | solution.py:18
  30.6 1.9 %collective-permute-start.5 = (bf16[256,256]{1,0:T(8,128)(2,1)S(1)}, bf16[256,256]{1,0:T(8,128)(2,1)S(1)}, u32[]{:S(2)}, u32[]{:S(2)}) collective-permute-start(bf16[256,256]{1,0:T(8,128)(2,1)S(1)} %get-tuple-element.23), channel_id=1, source_target_pairs={{0,4},{4,8},{8,12},{12,16},{16,20},{20,24},{24,28},{28,32},{32,36}... | collective-permute-start | bytes 393224 | tf_op jit(solution)/shard_map/ppermute | solution.py:18
  32.5 0.7 slice_bitcast_fusion.3
  33.4 1.1 %collective-permute-done.5 = bf16[256,256]{1,0:T(8,128)(2,1)S(1)} collective-permute-done((bf16[256,256]{1,0:T(8,128)(2,1)S(1)}, bf16[256,256]{1,0:T(8,128)(2,1)S(1)}, u32[]{:S(2)}, u32[]{:S(2)}) %collective-permute-start.5) | collective-permute-done | bytes 131104 | tf_op jit(solution)/shard_map/ppermute | solution.py:18
  34.4 1.3 %collective-permute-start.6 = (bf16[4,2,2,2,64,128]{5,4,3,2,1,0:T(8,128)(2,1)S(1)}, bf16[4,2,2,2,64,128]{5,4,3,2,1,0:T(8,128)(2,1)S(1)}, u32[]{:S(2)}, u32[]{:S(2)}) collective-permute-start(bf16[4,2,2,2,64,128]{5,4,3,2,1,0:T(8,128)(2,1)S(1)} %pad_maximum_fusion.1), channel_id=1, source_target_pairs={{0,32},{8,40},{16,48},{24,56},{32,64},{40,72},{48,80},{56,88},{64,... | collective-permute-start | bytes 1572872 | tf_op jit(solution)/shard_map/ppermute | solution.py:172
  35.7 2.6 %collective-permute-start.7 = (bf16[4,2,2,2,64,128]{5,4,3,2,1,0:T(8,128)(2,1)S(1)}, bf16[4,2,2,2,64,128]{5,4,3,2,1,0:T(8,128)(2,1)S(1)}, u32[]{:S(2)}, u32[]{:S(2)}) collective-permute-start(bf16[4,2,2,2,64,128]{5,4,3,2,1,0:T(8,128)(2,1)S(1)} %pad_maximum_fusion.1), channel_id=1, source_target_pairs={{0,64},{8,72},{16,80},{24,88},{32,96},{40,104},{48,112},{56,120},{... | collective-permute-start | bytes 1572872 | tf_op jit(solution)/shard_map/ppermute | solution.py:172
  38.4 1.1 %collective-permute-start.8 = (bf16[4,2,2,2,64,128]{5,4,3,2,1,0:T(8,128)(2,1)S(1)}, bf16[4,2,2,2,64,128]{5,4,3,2,1,0:T(8,128)(2,1)S(1)}, u32[]{:S(2)}, u32[]{:S(2)}) collective-permute-start(bf16[4,2,2,2,64,128]{5,4,3,2,1,0:T(8,128)(2,1)S(1)} %pad_maximum_fusion.1), channel_id=1, source_target_pairs={{0,96},{8,104},{16,112},{24,120},{32,0},{40,8},{48,16},{56,24},{64... | collective-permute-start | bytes 1572872 | tf_op jit(solution)/shard_map/ppermute | solution.py:172
  39.5 0.6 broadcast_subtract_fusion.1
  40.1 4.9 %collective-permute-done.6 = bf16[4,2,2,2,64,128]{5,4,3,2,1,0:T(8,128)(2,1)S(1)} collective-permute-done((bf16[4,2,2,2,64,128]{5,4,3,2,1,0:T(8,128)(2,1)S(1)}, bf16[4,2,2,2,64,128]{5,4,3,2,1,0:T(8,128)(2,1)S(1)}, u32[]{:S(2)}, u32[]{:S(2)}) %collective-permute-start.6) | collective-permute-done | bytes 524320 | tf_op jit(solution)/shard_map/ppermute | solution.py:172
  45.0 14.6 %collective-permute-done.7 = bf16[4,2,2,2,64,128]{5,4,3,2,1,0:T(8,128)(2,1)S(1)} collective-permute-done((bf16[4,2,2,2,64,128]{5,4,3,2,1,0:T(8,128)(2,1)S(1)}, bf16[4,2,2,2,64,128]{5,4,3,2,1,0:T(8,128)(2,1)S(1)}, u32[]{:S(2)}, u32[]{:S(2)}) %collective-permute-start.7) | collective-permute-done | bytes 524320 | tf_op jit(solution)/shard_map/ppermute | solution.py:172
  59.6 0.4 collective-permute-done.8
  60.0 0.3 pad_maximum_fusion
  60.3 1.0 %gather_fusion.4 = bf16[64,64,128]{2,1,0:T(8,128)(2,1)S(1)} fusion(bf16[4,4,2,2,2,64,128]{6,5,4,3,2,1,0:T(8,128)(2,1)S(1)} %pad_maximum_fusion, s32[64]{0:T(128)S(1)} %reshape.260), kind=kCustom, calls=%fused_computation.4 | custom fusion | bytes 2098432 | tf_op jit(solution)/shard_map/gather | solution.py:181
  61.3 3.9 %collective-permute-start.9 = (bf16[2,2048,128]{2,1,0:T(8,128)(2,1)S(1)}, bf16[2,2048,128]{2,1,0:T(8,128)(2,1)S(1)}, u32[]{:S(2)}, u32[]{:S(2)}) collective-permute-start(bf16[2,2048,128]{2,1,0:T(8,128)(2,1)S(1)} %bitcast.88), channel_id=1, source_target_pairs={{0,4},{4,0},{1,5},{5,1},{2,6},{6,2},{3,7},{7,3},{8,12},{12,8},{9,1... | collective-permute-start | bytes 3145736 | tf_op jit(solution)/shard_map/ppermute | solution.py:183
  65.1 0.8 compare_reduce_fusion
  65.9 0.7 concatenate.35.refs_0_
  66.6 0.8 not_and_fusion.1
  67.4 0.1 stack.105
  67.6 0.1 stack.106
  67.7 0.7 copy.51.refs_7_
  68.4 0.8 subtract_compare_fusion.1
  69.3 0.1 stack.102
  69.5 0.1 stack.103
  69.6 0.6 copy.50.refs_6_
  70.2 1.6 %pad_maximum_fusion.4.refs_3_ = bf16[512,256]{1,0:T(8,128)(2,1)} fusion(bf16[256,256]{1,0:T(8,128)(2,1)S(1)} %get-tuple-element.23, bf16[256,256]{1,0:T(8,128)(2,1)} %copy-done.3), kind=kLoop, calls=%fused_computation.12 | loop fusion | flops 524288 | bytes 524288 | tf_op jit(solution)/shard_map/concatenate | solution.py:187
  71.8 0.7 pad_maximum_fusion.3.refs_2_
  72.5 1.5 %broadcast_select_fusion = (bf16[2,2048,128]{2,1,0:T(8,128)(2,1)}, bf16[2,2048,128]{2,1,0:T(8,128)(2,1)}) fusion(bf16[2,2048,128]{2,1,0:T(8,128)(2,1)S(1)} %collective-permute-done.9, pred[]{:T(512)S(6)} %eq.79, bf16[2,2048,128]{2,1,0:T(8,128)(2,1)S(1)} %bitcast.89), kind=kLoop, calls=%fused_computation.6 | loop fusion | flops 1048576 | bytes 4194305 | tf_op jit(solution)/shard_map/jit(_where)/select_n | solution.py:185
  74.0 13.9 %shard_map.55 = bf16[256,1024]{1,0:T(8,128)(2,1)} custom-call(s32[2,5]{1,0:T(2,128)} %concatenate.35.refs_0_, bf16[256,1024]{1,0:T(8,128)(2,1)} %bitcast.93, bf16[512,256]{1,0:T(8,128)(2,1)} %pad_maximum_fusion.3.refs_2_, bf16[512,256]{1,0:T(8,128)(2,1)} %pad_maximum_fusion.4.refs_3_, bf16[2,2048,128]{2,1,0:T(8,128)(2,1)} %get-tuple-element.22.refs_4_, ...), custom_call_target="tpu_custom_call" | custom-call | flops 2550136832 | bytes 3670016 | tf_op jit(solution)/shard_map/pallas_call | solution.py:97
  (52 shorter events, 0.9 us)
Async XLA Ops:
  0.0 18.2 %copy-start = (s32[8,4]{0,1:T(4,128)S(1)}, s32[8,4]{0,1:T(4,128)}, u32[]{:S(2)}) copy-start(s32[8,4]{0,1:T(4,128)} %param.8) | copy-start | bytes 388
  1.7 11.4 %all-to-all-start = ((bf16[64,4,512]{2,0,1:T(8,128)(2,1)}), bf16[64,4,512]{2,0,1:T(8,128)(2,1)S(1)}, u32[]{:S(2)}, u32[]{:S(2)}) async-start(bf16[64,4,512]{2,0,1:T(8,128)(2,1)} %pad_maximum_fusion.2), calls=%async_computation | async-start | bytes 524288 | tf_op jit(solution)/shard_map/all_to_all | solution.py:116
  13.1 5.2 %copy-start.1 = (bf16[64,4096]{1,0:T(8,128)(2,1)S(1)}, bf16[64,4096]{1,0:T(8,128)(2,1)}, u32[]{:S(2)}) copy-start(bf16[64,4096]{1,0:T(8,128)(2,1)} %param.5) | copy-start | bytes 1572868
  16.0 6.6 %collective-permute-start = (bf16[2,2,64,128]{3,2,1,0:T(8,128)(2,1)S(1)}, bf16[2,2,64,128]{3,2,1,0:T(8,128)(2,1)S(1)}, u32[]{:S(2)}, u32[]{:S(2)}) collective-permute-start(bf16[2,2,64,128]{3,2,1,0:T(8,128)(2,1)S(1)} %get-tuple-element.30), channel_id=1, source_target_pairs={{0,4},{4,0},{1,5},{5,1},{2,6},{6,2},{3,7},{7,3},{8,12},{12,8},{9,1... | collective-permute-start | bytes 196616 | tf_op jit(solution)/shard_map/ppermute | solution.py:160
  19.2 15.2 %all-to-all-start.1 = ((bf16[64,4,1024]{2,0,1:T(8,128)(2,1)}), bf16[64,4,1024]{2,0,1:T(8,128)(2,1)S(1)}, u32[]{:S(2)}, u32[]{:S(2)}) async-start(bf16[64,4,1024]{2,0,1:T(8,128)(2,1)} %bitcast.82), calls=%async_computation.1 | async-start | bytes 1048576 | tf_op jit(solution)/shard_map/all_to_all | solution.py:161
  22.7 10.5 %collective-permute-start.1 = (bf16[2,2,2,64,128]{4,3,2,1,0:T(8,128)(2,1)S(1)}, bf16[2,2,2,64,128]{4,3,2,1,0:T(8,128)(2,1)S(1)}, u32[]{:S(2)}, u32[]{:S(2)}) collective-permute-start(bf16[2,2,2,64,128]{4,3,2,1,0:T(8,128)(2,1)S(1)} %get-tuple-element.28), channel_id=1, source_target_pairs={{0,8},{8,16},{16,24},{24,0},{32,40},{40,48},{48,56},{56,32},{64,72... | collective-permute-start | bytes 393224 | tf_op jit(solution)/shard_map/ppermute | solution.py:172
  24.0 9.3 %collective-permute-start.2 = (bf16[2,2,2,64,128]{4,3,2,1,0:T(8,128)(2,1)S(1)}, bf16[2,2,2,64,128]{4,3,2,1,0:T(8,128)(2,1)S(1)}, u32[]{:S(2)}, u32[]{:S(2)}) collective-permute-start(bf16[2,2,2,64,128]{4,3,2,1,0:T(8,128)(2,1)S(1)} %get-tuple-element.28), channel_id=1, source_target_pairs={{0,16},{8,24},{16,0},{24,8},{32,48},{40,56},{48,32},{56,40},{64,80... | collective-permute-start | bytes 393224 | tf_op jit(solution)/shard_map/ppermute | solution.py:172
  26.5 6.8 %collective-permute-start.3 = (bf16[2,2,2,64,128]{4,3,2,1,0:T(8,128)(2,1)S(1)}, bf16[2,2,2,64,128]{4,3,2,1,0:T(8,128)(2,1)S(1)}, u32[]{:S(2)}, u32[]{:S(2)}) collective-permute-start(bf16[2,2,2,64,128]{4,3,2,1,0:T(8,128)(2,1)S(1)} %get-tuple-element.28), channel_id=1, source_target_pairs={{0,24},{8,0},{16,8},{24,16},{32,56},{40,32},{48,40},{56,48},{64,88... | collective-permute-start | bytes 393224 | tf_op jit(solution)/shard_map/ppermute | solution.py:172
  27.6 5.7 %collective-permute-start.4 = (bf16[256,256]{1,0:T(8,128)(2,1)S(1)}, bf16[256,256]{1,0:T(8,128)(2,1)S(1)}, u32[]{:S(2)}, u32[]{:S(2)}) collective-permute-start(bf16[256,256]{1,0:T(8,128)(2,1)S(1)} %get-tuple-element.24), channel_id=1, source_target_pairs={{0,4},{4,8},{8,12},{12,16},{16,20},{20,24},{24,28},{28,32},{32,36}... | collective-permute-start | bytes 393224 | tf_op jit(solution)/shard_map/ppermute | solution.py:18
  30.6 3.9 %collective-permute-start.5 = (bf16[256,256]{1,0:T(8,128)(2,1)S(1)}, bf16[256,256]{1,0:T(8,128)(2,1)S(1)}, u32[]{:S(2)}, u32[]{:S(2)}) collective-permute-start(bf16[256,256]{1,0:T(8,128)(2,1)S(1)} %get-tuple-element.23), channel_id=1, source_target_pairs={{0,4},{4,8},{8,12},{12,16},{16,20},{20,24},{24,28},{28,32},{32,36}... | collective-permute-start | bytes 393224 | tf_op jit(solution)/shard_map/ppermute | solution.py:18
  34.4 25.5 %copy-start.3 = (bf16[256,256]{1,0:T(8,128)(2,1)}, bf16[256,256]{1,0:T(8,128)(2,1)S(1)}, u32[]{:S(2)}) copy-start(bf16[256,256]{1,0:T(8,128)(2,1)S(1)} %collective-permute-done.5) | copy-start | bytes 393220
  34.4 25.5 %copy-start.2 = (bf16[64,4,1024]{2,0,1:T(8,128)(2,1)}, bf16[64,4,1024]{2,0,1:T(8,128)(2,1)S(1)}, u32[]{:S(2)}) copy-start(bf16[64,4,1024]{2,0,1:T(8,128)(2,1)S(1)} %all-to-all-done.1) | copy-start | bytes 1572868
  34.4 10.6 %collective-permute-start.6 = (bf16[4,2,2,2,64,128]{5,4,3,2,1,0:T(8,128)(2,1)S(1)}, bf16[4,2,2,2,64,128]{5,4,3,2,1,0:T(8,128)(2,1)S(1)}, u32[]{:S(2)}, u32[]{:S(2)}) collective-permute-start(bf16[4,2,2,2,64,128]{5,4,3,2,1,0:T(8,128)(2,1)S(1)} %pad_maximum_fusion.1), channel_id=1, source_target_pairs={{0,32},{8,40},{16,48},{24,56},{32,64},{40,72},{48,80},{56,88},{64,... | collective-permute-start | bytes 1572872 | tf_op jit(solution)/shard_map/ppermute | solution.py:172
  35.7 23.8 %collective-permute-start.7 = (bf16[4,2,2,2,64,128]{5,4,3,2,1,0:T(8,128)(2,1)S(1)}, bf16[4,2,2,2,64,128]{5,4,3,2,1,0:T(8,128)(2,1)S(1)}, u32[]{:S(2)}, u32[]{:S(2)}) collective-permute-start(bf16[4,2,2,2,64,128]{5,4,3,2,1,0:T(8,128)(2,1)S(1)} %pad_maximum_fusion.1), channel_id=1, source_target_pairs={{0,64},{8,72},{16,80},{24,88},{32,96},{40,104},{48,112},{56,120},{... | collective-permute-start | bytes 1572872 | tf_op jit(solution)/shard_map/ppermute | solution.py:172
  38.4 21.6 %collective-permute-start.8 = (bf16[4,2,2,2,64,128]{5,4,3,2,1,0:T(8,128)(2,1)S(1)}, bf16[4,2,2,2,64,128]{5,4,3,2,1,0:T(8,128)(2,1)S(1)}, u32[]{:S(2)}, u32[]{:S(2)}) collective-permute-start(bf16[4,2,2,2,64,128]{5,4,3,2,1,0:T(8,128)(2,1)S(1)} %pad_maximum_fusion.1), channel_id=1, source_target_pairs={{0,96},{8,104},{16,112},{24,120},{32,0},{40,8},{48,16},{56,24},{64... | collective-permute-start | bytes 1572872 | tf_op jit(solution)/shard_map/ppermute | solution.py:172
  39.4 20.5 %copy-start.4 = (s32[4]{0:T(128)}, s32[4]{0:T(128)S(1)}, u32[]{:S(2)}) copy-start(s32[4]{0:T(128)S(1)} %iota_add_fusion) | copy-start | bytes 52
  39.4 20.5 %copy-start.5 = (s32[32]{0:T(128)}, s32[32]{0:T(128)S(1)}, u32[]{:S(2)}) copy-start(s32[32]{0:T(128)S(1)} %get-tuple-element.35) | copy-start | bytes 388
  39.5 20.5 %copy-start.6 = (s32[32]{0:T(128)}, s32[32]{0:T(128)S(1)}, u32[]{:S(2)}) copy-start(s32[32]{0:T(128)S(1)} %get-tuple-element.36) | copy-start | bytes 388
  61.3 11.3 %collective-permute-start.9 = (bf16[2,2048,128]{2,1,0:T(8,128)(2,1)S(1)}, bf16[2,2048,128]{2,1,0:T(8,128)(2,1)S(1)}, u32[]{:S(2)}, u32[]{:S(2)}) collective-permute-start(bf16[2,2048,128]{2,1,0:T(8,128)(2,1)S(1)} %bitcast.88), channel_id=1, source_target_pairs={{0,4},{4,0},{1,5},{5,1},{2,6},{6,2},{3,7},{7,3},{8,12},{12,8},{9,1... | collective-permute-start | bytes 3145736 | tf_op jit(solution)/shard_map/ppermute | solution.py:183

commit v10 on v9

--- a/solution.py
+++ b/solution.py
@@ -101,6 +101,28 @@
         cost_estimate=cost,
         interpret=INTERPRET,
     )(offsets, q_all, win_k, win_v, kv, vv, ms, mv)
+
+
+def side_inputs(prev_k, prev_v, k_all, v_all, diagonal_offsets, local_vert, seq_index, nbd):
+    kv_local, width = diagonal_offsets.shape
+    window_k = jnp.concatenate([prev_k, k_all], 0)
+    window_v = jnp.concatenate([prev_v, v_all], 0)
+    qblocks = seq_index * nbd + jnp.arange(nbd, dtype=jnp.int32)
+    slash_ok, vert_ok = [], []
+    for group_member in range(kv_local):
+        offset = diagonal_offsets[group_member]
+        block_ok = qblocks[:, None] - offset[None, :] >= 0
+        block_ok = jnp.concatenate(
+            [block_ok, jnp.zeros((nbd, SLASH_SLOTS - width), jnp.bool_)], 1
+        )
+        slash_ok.append(jnp.repeat(block_ok, BLOCK_TOKENS, axis=1))
+        dist = qblocks[:, None] - local_vert[group_member][None, :]
+        hit = jnp.any(dist[:, :, None] == offset[None, None, :], axis=2)
+        ok = (dist > 0) & jnp.logical_not(hit)
+        vert_ok.append(jnp.repeat(ok, BLOCK_TOKENS, axis=1))
+    ms = jnp.stack(slash_ok, 0).astype(jnp.int32)[:, :, None, :]
+    mv = jnp.stack(vert_ok, 0).astype(jnp.int32)[:, :, None, :]
+    return window_k, window_v, ms, mv
 
 
 def local(queries, keys, values, slash, vertical):
@@ -172,7 +194,16 @@
             moved.append(lax.ppermute(stage, "chip", pairs))
         stage = jnp.stack(moved, 0)
         if stride == 1:
-            stage, q_all, prev_k, prev_v = lax.optimization_barrier((stage, q_all, prev_k, prev_v))
+            stage, q_all, prev_k, prev_v, diagonal_offsets, local_vert = lax.optimization_barrier(
+                (stage, q_all, prev_k, prev_v, diagonal_offsets, local_vert)
+            )
+            window_k, window_v, ms, mv = side_inputs(
+                prev_k, prev_v, k_all, v_all, diagonal_offsets, local_vert, seq_index, nbd
+            )
+        else:
+            stage, window_k, window_v, ms, mv = lax.optimization_barrier(
+                (stage, window_k, window_v, ms, mv)
+            )
     owner_chip = owner // cores
     owner_core = owner % cores
     dy = (chip_index // side - owner_chip // side) % side
@@ -183,23 +214,6 @@
     other = lax.ppermute(part, "core", swap)
     vert_keys = jnp.where(core_index == 0, part, other)
     vert_vals = jnp.where(core_index == 0, other, part)
-    window_k = jnp.concatenate([prev_k, k_all], 0)
-    window_v = jnp.concatenate([prev_v, v_all], 0)
-    qblocks = seq_index * nbd + jnp.arange(nbd, dtype=jnp.int32)
-    slash_ok, vert_ok = [], []
-    for group_member in range(kv_local):
-        offset = diagonal_offsets[group_member]
-        block_ok = qblocks[:, None] - offset[None, :] >= 0
-        block_ok = jnp.concatenate(
-            [block_ok, jnp.zeros((nbd, SLASH_SLOTS - width), jnp.bool_)], 1
-        )
-        slash_ok.append(jnp.repeat(block_ok, BLOCK_TOKENS, axis=1))
-        dist = qblocks[:, None] - local_vert[group_member][None, :]
-        hit = jnp.any(dist[:, :, None] == offset[None, None, :], axis=2)
-        ok = (dist > 0) & jnp.logical_not(hit)
-        vert_ok.append(jnp.repeat(ok, BLOCK_TOKENS, axis=1))
-    ms = jnp.stack(slash_ok, 0).astype(jnp.int32)[:, :, None, :]
-    mv = jnp.stack(vert_ok, 0).astype(jnp.int32)[:, :, None, :]
     return attend(
         diagonal_offsets, q_all, window_k, window_v, vert_keys, vert_vals, ms, mv,
         query_group, softmax_scale,

time: 88.3 us -> 85.9 us (0.973)
  waiting for transfers between devices: 25.3 us -> 30.7 us
  starting transfers between devices: 30.1 us -> 25.7 us
  local copies, waits for them, and re-layouts: 9.24 us -> 6.68 us
    ppermute x6, waiting for transfers between devices: 19.9 us -> 24 us  [local(): moved.append(lax.ppermute(stage, 'chip', pairs))]
    ppermute x1, starting transfers between devices: 3.85 us -> 0.57 us  [local(): other = lax.ppermute(part, 'core', swap)]
    ppermute x6, starting transfers between devices: 9.87 us -> 7.52 us  [local(): moved.append(lax.ppermute(stage, 'chip', pairs))]
    ppermute x1, waiting for transfers between devices: 0.01 us -> 2.29 us  [local(): other = lax.ppermute(part, 'core', swap)]
    another operation x3, other arithmetic: 0.35 us -> 1.71 us  [local(): stage = jnp.stack(moved, 0)]
    convert_element_type x2 -> x0, local copies, waits for them, and re-layouts: 1.3 us -> none  [the longest x1 0.69 us: local(): mv = jnp.stack(vert_ok, 0).astype(jnp.int32)[:, :, None, :]]
    convert_element_type x2, other arithmetic: 0.03 us -> 1.28 us  [the longest x1 0.67 us: side_inputs(): mv = jnp.stack(vert_ok, 0).astype(jnp.int32)[:, :, None, :]]
    ppermute x2, starting transfers between devices: 4.88 us -> 6.09 us  [shifted(): return lax.ppermute(value, axis, pairs)]
  transfers between devices with their start and end apart: 12 -> 12, of which waited for: 5 -> 6; matrix products, arithmetic and copies ran while one was open for 12% -> 7% of each run, Pallas kernels for 0% -> 0%
where the time goes in v10:
time: 85.9 us; the launch traced here: 85.5 us
  waiting for transfers between devices  30.7 us (36%)
  starting transfers between devices  25.7 us (30%)
  Pallas kernels  13.9 us (16%)
  other arithmetic  8.21 us (10%)
  local copies, waits for them, and re-layouts  6.68 us (8%)
    ppermute x6, waiting for transfers between devices, local(): moved.append(lax.ppermute(stage, 'chip', pairs))  24 us
    pallas_call x1, Pallas kernels, attend(): pl.pallas_call(kernel, grid_spec=grid_spec, out_shape=jax.ShapeDtypeStruc...  13.9 us
    ppermute x6, starting transfers between devices, local(): moved.append(lax.ppermute(stage, 'chip', pairs))  7.52 us
    ppermute x2, starting transfers between devices, shifted(): return lax.ppermute(value, axis, pairs)  6.09 us
    all_to_all x1, starting transfers between devices, local(): lax.all_to_all(joined, 'head', split_axis=1, concat_axis=0, tiled=True)  5.84 us
    all_to_all x1, waiting for transfers between devices, local(): lax.all_to_all(joined, 'head', split_axis=1, concat_axis=0, tiled=True)  4.38 us
    all_to_all x1, starting transfers between devices, local(): lax.all_to_all(queries, 'head', split_axis=1, concat_axis=0, tiled=True)  3.47 us
    ppermute x1, waiting for transfers between devices, local(): other = lax.ppermute(part, 'core', swap)  2.29 us
  transfers between devices with their start and end apart: 12, of which 6 were waited for; matrix products, arithmetic and copies ran while one was open for 7% of the time, Pallas kernels for 0%

profile of v10, /device:TPU:1, one launch (start us, length us, event | category | flops | bytes accessed | tf_op | source)
XLA Modules:
  0.0 85.5 jit_solution(5246958252583093416)
XLA Ops:
  0.0 1.0 %copy_bitcast_fusion.1 = (bf16[64,4,256]{2,0,1:T(8,128)(2,1)S(1)}, bf16[64,4,256]{2,0,1:T(8,128)(2,1)S(1)}) fusion(bf16[8,4,8,256]{3,2,1,0:T(8,128)(2,1)} %bitcast.102, bf16[8,4,8,256]{3,2,1,0:T(8,128)(2,1)} %bitcast.103), kind=kLoop, calls=%fused_computation.14 | loop fusion | bytes 524288 | tf_op jit(solution)/shard_map/reshape | solution.py:136
  1.0 0.7 pad_maximum_fusion.2
  1.7 5.8 %all-to-all-start = ((bf16[64,4,512]{2,0,1:T(8,128)(2,1)}), bf16[64,4,512]{2,0,1:T(8,128)(2,1)S(1)}, u32[]{:S(2)}, u32[]{:S(2)}) async-start(bf16[64,4,512]{2,0,1:T(8,128)(2,1)} %pad_maximum_fusion.2), calls=%async_computation | async-start | bytes 524288 | tf_op jit(solution)/shard_map/all_to_all | solution.py:138
  7.6 0.7 and_select_fusion.8
  8.3 0.2 convert_reduce_fusion
  8.5 0.2 fusion
  8.8 4.4 %all-to-all-done = bf16[64,4,512]{2,0,1:T(8,128)(2,1)S(1)} async-done(((bf16[64,4,512]{2,0,1:T(8,128)(2,1)}), bf16[64,4,512]{2,0,1:T(8,128)(2,1)S(1)}, u32[]{:S(2)}, u32[]{:S(2)}) %all-to-all-start) | async-done | bytes 262176 | tf_op jit(solution)/shard_map/all_to_all | solution.py:138
  13.2 0.2 fusion.21
  13.5 0.2 fusion.20
  13.7 0.6 gather_fusion.3
  14.2 0.6 gather_fusion.2
  14.8 0.6 gather_fusion.1
  15.4 0.6 gather_fusion
  16.0 2.2 %collective-permute-start = (bf16[2,2,64,128]{3,2,1,0:T(8,128)(2,1)S(1)}, bf16[2,2,64,128]{3,2,1,0:T(8,128)(2,1)S(1)}, u32[]{:S(2)}, u32[]{:S(2)}) collective-permute-start(bf16[2,2,64,128]{3,2,1,0:T(8,128)(2,1)S(1)} %get-tuple-element.44), channel_id=1, source_target_pairs={{0,4},{4,0},{1,5},{5,1},{2,6},{6,2},{3,7},{7,3},{8,12},{12,8},{9,1... | collective-permute-start | bytes 196616 | tf_op jit(solution)/shard_map/ppermute | solution.py:182
  18.3 0.1 copy.46
  18.4 0.8 copy.59
  19.2 3.5 %all-to-all-start.1 = ((bf16[64,4,1024]{2,0,1:T(8,128)(2,1)}), bf16[64,4,1024]{2,0,1:T(8,128)(2,1)S(1)}, u32[]{:S(2)}, u32[]{:S(2)}) async-start(bf16[64,4,1024]{2,0,1:T(8,128)(2,1)} %bitcast.82), calls=%async_computation.1 | async-start | bytes 1048576 | tf_op jit(solution)/shard_map/all_to_all | solution.py:183
  22.7 2.5 %collective-permute-start.3 = (bf16[2,2,2,64,128]{4,3,2,1,0:T(8,128)(2,1)S(1)}, bf16[2,2,2,64,128]{4,3,2,1,0:T(8,128)(2,1)S(1)}, u32[]{:S(2)}, u32[]{:S(2)}) collective-permute-start(bf16[2,2,2,64,128]{4,3,2,1,0:T(8,128)(2,1)S(1)} %get-tuple-element.42), channel_id=1, source_target_pairs={{0,24},{8,0},{16,8},{24,16},{32,56},{40,32},{48,40},{56,48},{64,88... | collective-permute-start | bytes 393224 | tf_op jit(solution)/shard_map/ppermute | solution.py:194
  25.3 0.5 collective-permute-start.2
  25.8 0.6 collective-permute-start.1
  26.4 4.2 %collective-permute-start.4 = (bf16[256,256]{1,0:T(8,128)(2,1)S(1)}, bf16[256,256]{1,0:T(8,128)(2,1)S(1)}, u32[]{:S(2)}, u32[]{:S(2)}) collective-permute-start(bf16[256,256]{1,0:T(8,128)(2,1)S(1)} %get-tuple-element.38), channel_id=1, source_target_pairs={{0,4},{4,8},{8,12},{12,16},{16,20},{20,24},{24,28},{28,32},{32,36}... | collective-permute-start | bytes 393224 | tf_op jit(solution)/shard_map/ppermute | solution.py:18
  30.6 1.9 %collective-permute-start.5 = (bf16[256,256]{1,0:T(8,128)(2,1)S(1)}, bf16[256,256]{1,0:T(8,128)(2,1)S(1)}, u32[]{:S(2)}, u32[]{:S(2)}) collective-permute-start(bf16[256,256]{1,0:T(8,128)(2,1)S(1)} %get-tuple-element.37), channel_id=1, source_target_pairs={{0,4},{4,8},{8,12},{12,16},{16,20},{20,24},{24,28},{28,32},{32,36}... | collective-permute-start | bytes 393224 | tf_op jit(solution)/shard_map/ppermute | solution.py:18
  32.6 0.1 reshape.260
  32.7 2.3 %collective-permute-done.1 = bf16[2,2,2,64,128]{4,3,2,1,0:T(8,128)(2,1)S(1)} collective-permute-done((bf16[2,2,2,64,128]{4,3,2,1,0:T(8,128)(2,1)S(1)}, bf16[2,2,2,64,128]{4,3,2,1,0:T(8,128)(2,1)S(1)}, u32[]{:S(2)}, u32[]{:S(2)}) %collective-permute-start.1) | collective-permute-done | bytes 131104 | tf_op jit(solution)/shard_map/ppermute | solution.py:194
  35.1 2.8 %collective-permute-start.8 = (bf16[4,2,2,2,64,128]{5,4,3,2,1,0:T(8,128)(2,1)S(1)}, bf16[4,2,2,2,64,128]{5,4,3,2,1,0:T(8,128)(2,1)}, u32[]{:S(2)}, u32[]{:S(2)}) collective-permute-start(bf16[4,2,2,2,64,128]{5,4,3,2,1,0:T(8,128)(2,1)S(1)} %pad_maximum_fusion.1), channel_id=1, source_target_pairs={{0,96},{8,104},{16,112},{24,120},{32,0},{40,8},{48,16},{56,24},{64... | collective-permute-start | bytes 1572872 | tf_op jit(solution)/shard_map/ppermute | solution.py:194
  37.9 0.3 collective-permute-start.7
  38.3 0.7 collective-permute-start.6
  39.0 0.7 pad_maximum_fusion.3.refs_2_
  39.9 0.1 stack.103
  40.1 0.1 stack.102
  40.2 0.6 copy_convert_fusion.1.refs_6_
  40.8 0.1 compare_reduce_fusion.1
  40.9 0.1 compare_reduce_fusion
  41.1 0.1 broadcast_in_dim.33
  41.2 0.1 stack.106
  41.3 0.1 broadcast_in_dim.32
  41.4 0.1 stack.105
  41.5 0.7 pad_maximum_fusion.4.refs_3_
  42.2 0.7 copy_convert_fusion.refs_7_
  42.9 3.3 %collective-permute-done.8 = bf16[4,2,2,2,64,128]{5,4,3,2,1,0:T(8,128)(2,1)} collective-permute-done((bf16[4,2,2,2,64,128]{5,4,3,2,1,0:T(8,128)(2,1)S(1)}, bf16[4,2,2,2,64,128]{5,4,3,2,1,0:T(8,128)(2,1)}, u32[]{:S(2)}, u32[]{:S(2)}) %collective-permute-start.8) | collective-permute-done | bytes 524320 | tf_op jit(solution)/shard_map/ppermute | solution.py:194
  46.2 3.3 %collective-permute-done.7 = bf16[4,2,2,2,64,128]{5,4,3,2,1,0:T(8,128)(2,1)} collective-permute-done((bf16[4,2,2,2,64,128]{5,4,3,2,1,0:T(8,128)(2,1)S(1)}, bf16[4,2,2,2,64,128]{5,4,3,2,1,0:T(8,128)(2,1)}, u32[]{:S(2)}, u32[]{:S(2)}) %collective-permute-start.7) | collective-permute-done | bytes 524320 | tf_op jit(solution)/shard_map/ppermute | solution.py:194
  49.5 15.1 %collective-permute-done.6 = bf16[4,2,2,2,64,128]{5,4,3,2,1,0:T(8,128)(2,1)} collective-permute-done((bf16[4,2,2,2,64,128]{5,4,3,2,1,0:T(8,128)(2,1)S(1)}, bf16[4,2,2,2,64,128]{5,4,3,2,1,0:T(8,128)(2,1)}, u32[]{:S(2)}, u32[]{:S(2)}) %collective-permute-start.6) | collective-permute-done | bytes 524320 | tf_op jit(solution)/shard_map/ppermute | solution.py:194
  64.6 1.6 %pad_maximum_fusion = bf16[4,4,2,2,2,64,128]{6,5,4,3,2,1,0:T(8,128)(2,1)S(1)} fusion(bf16[1,4,2,2,2,64,128]{6,5,4,3,2,1,0:T(8,128)(2,1)} %bitcast.33, bf16[1,4,2,2,2,64,128]{6,5,4,3,2,1,0:T(8,128)(2,1)} %bitcast.32, bf16[1,4,2,2,2,64,128]{6,5,4,3,2,1,0:T(8,128)(2,1)} %bitcast.31, bf16[1,4,2,2,2,64,128]{6,5,4,3,2,1,0:T(8,128)(2,1)S(1)} %bitcast.90), kind=kLoop, calls=%fused_computation.5 | loop fusion | flops 3145728 | bytes 4194304 | tf_op jit(solution)/shard_map/stack | solution.py:195
  66.3 1.0 %gather_fusion.4 = bf16[64,64,128]{2,1,0:T(8,128)(2,1)S(1)} fusion(bf16[4,4,2,2,2,64,128]{6,5,4,3,2,1,0:T(8,128)(2,1)S(1)} %pad_maximum_fusion, s32[64]{0:T(128)S(1)} %reshape.260), kind=kCustom, calls=%fused_computation.4 | custom fusion | bytes 2098432 | tf_op jit(solution)/shard_map/gather | solution.py:212
  67.3 0.6 collective-permute-start.9
  67.8 2.3 %collective-permute-done.9 = bf16[2,2048,128]{2,1,0:T(8,128)(2,1)S(1)} collective-permute-done((bf16[2,2048,128]{2,1,0:T(8,128)(2,1)S(1)}, bf16[2,2048,128]{2,1,0:T(8,128)(2,1)S(1)}, u32[]{:S(2)}, u32[]{:S(2)}) %collective-permute-start.9) | collective-permute-done | bytes 1048608 | tf_op jit(solution)/shard_map/ppermute | solution.py:214
  70.1 1.5 %broadcast_select_fusion = (bf16[2,2048,128]{2,1,0:T(8,128)(2,1)}, bf16[2,2048,128]{2,1,0:T(8,128)(2,1)}) fusion(bf16[2,2048,128]{2,1,0:T(8,128)(2,1)S(1)} %collective-permute-done.9, pred[]{:T(512)S(6)} %eq.85, bf16[2,2048,128]{2,1,0:T(8,128)(2,1)S(1)} %bitcast.89), kind=kLoop, calls=%fused_computation.6 | loop fusion | flops 1048576 | bytes 4194305 | tf_op jit(solution)/shard_map/jit(_where)/select_n | solution.py:216
  71.6 13.9 %shard_map.55 = bf16[256,1024]{1,0:T(8,128)(2,1)} custom-call(s32[2,5]{1,0:T(2,128)} %copy-done.3, bf16[256,1024]{1,0:T(8,128)(2,1)} %bitcast.93, bf16[512,256]{1,0:T(8,128)(2,1)} %pad_maximum_fusion.3.refs_2_, bf16[512,256]{1,0:T(8,128)(2,1)} %pad_maximum_fusion.4.refs_3_, bf16[2,2048,128]{2,1,0:T(8,128)(2,1)} %get-tuple-element.36.refs_4_, ...), custom_call_target="tpu_custom_call" | custom-call | flops 2550136832 | bytes 3670016 | tf_op jit(solution)/shard_map/pallas_call | solution.py:97
  (47 shorter events, 1.0 us)
Async XLA Ops:
  0.0 18.2 %copy-start = (s32[8,4]{0,1:T(4,128)S(1)}, s32[8,4]{0,1:T(4,128)}, u32[]{:S(2)}) copy-start(s32[8,4]{0,1:T(4,128)} %param.8) | copy-start | bytes 388
  1.7 11.4 %all-to-all-start = ((bf16[64,4,512]{2,0,1:T(8,128)(2,1)}), bf16[64,4,512]{2,0,1:T(8,128)(2,1)S(1)}, u32[]{:S(2)}, u32[]{:S(2)}) async-start(bf16[64,4,512]{2,0,1:T(8,128)(2,1)} %pad_maximum_fusion.2), calls=%async_computation | async-start | bytes 524288 | tf_op jit(solution)/shard_map/all_to_all | solution.py:138
  13.1 5.2 %copy-start.1 = (bf16[64,4096]{1,0:T(8,128)(2,1)S(1)}, bf16[64,4096]{1,0:T(8,128)(2,1)}, u32[]{:S(2)}) copy-start(bf16[64,4096]{1,0:T(8,128)(2,1)} %param.5) | copy-start | bytes 1572868
  16.0 6.6 %collective-permute-start = (bf16[2,2,64,128]{3,2,1,0:T(8,128)(2,1)S(1)}, bf16[2,2,64,128]{3,2,1,0:T(8,128)(2,1)S(1)}, u32[]{:S(2)}, u32[]{:S(2)}) collective-permute-start(bf16[2,2,64,128]{3,2,1,0:T(8,128)(2,1)S(1)} %get-tuple-element.44), channel_id=1, source_target_pairs={{0,4},{4,0},{1,5},{5,1},{2,6},{6,2},{3,7},{7,3},{8,12},{12,8},{9,1... | collective-permute-start | bytes 196616 | tf_op jit(solution)/shard_map/ppermute | solution.py:182
  19.2 15.9 %all-to-all-start.1 = ((bf16[64,4,1024]{2,0,1:T(8,128)(2,1)}), bf16[64,4,1024]{2,0,1:T(8,128)(2,1)S(1)}, u32[]{:S(2)}, u32[]{:S(2)}) async-start(bf16[64,4,1024]{2,0,1:T(8,128)(2,1)} %bitcast.82), calls=%async_computation.1 | async-start | bytes 1048576 | tf_op jit(solution)/shard_map/all_to_all | solution.py:183
  22.7 10.0 %collective-permute-start.3 = (bf16[2,2,2,64,128]{4,3,2,1,0:T(8,128)(2,1)S(1)}, bf16[2,2,2,64,128]{4,3,2,1,0:T(8,128)(2,1)S(1)}, u32[]{:S(2)}, u32[]{:S(2)}) collective-permute-start(bf16[2,2,2,64,128]{4,3,2,1,0:T(8,128)(2,1)S(1)} %get-tuple-element.42), channel_id=1, source_target_pairs={{0,24},{8,0},{16,8},{24,16},{32,56},{40,32},{48,40},{56,48},{64,88... | collective-permute-start | bytes 393224 | tf_op jit(solution)/shard_map/ppermute | solution.py:194
  25.3 7.4 %collective-permute-start.2 = (bf16[2,2,2,64,128]{4,3,2,1,0:T(8,128)(2,1)S(1)}, bf16[2,2,2,64,128]{4,3,2,1,0:T(8,128)(2,1)S(1)}, u32[]{:S(2)}, u32[]{:S(2)}) collective-permute-start(bf16[2,2,2,64,128]{4,3,2,1,0:T(8,128)(2,1)S(1)} %get-tuple-element.42), channel_id=1, source_target_pairs={{0,16},{8,24},{16,0},{24,8},{32,48},{40,56},{48,32},{56,40},{64,80... | collective-permute-start | bytes 393224 | tf_op jit(solution)/shard_map/ppermute | solution.py:194
  25.8 9.2 %collective-permute-start.1 = (bf16[2,2,2,64,128]{4,3,2,1,0:T(8,128)(2,1)S(1)}, bf16[2,2,2,64,128]{4,3,2,1,0:T(8,128)(2,1)S(1)}, u32[]{:S(2)}, u32[]{:S(2)}) collective-permute-start(bf16[2,2,2,64,128]{4,3,2,1,0:T(8,128)(2,1)S(1)} %get-tuple-element.42), channel_id=1, source_target_pairs={{0,8},{8,16},{16,24},{24,0},{32,40},{40,48},{48,56},{56,32},{64,72... | collective-permute-start | bytes 393224 | tf_op jit(solution)/shard_map/ppermute | solution.py:194
  26.4 8.7 %collective-permute-start.4 = (bf16[256,256]{1,0:T(8,128)(2,1)S(1)}, bf16[256,256]{1,0:T(8,128)(2,1)S(1)}, u32[]{:S(2)}, u32[]{:S(2)}) collective-permute-start(bf16[256,256]{1,0:T(8,128)(2,1)S(1)} %get-tuple-element.38), channel_id=1, source_target_pairs={{0,4},{4,8},{8,12},{12,16},{16,20},{20,24},{24,28},{28,32},{32,36}... | collective-permute-start | bytes 393224 | tf_op jit(solution)/shard_map/ppermute | solution.py:18
  30.6 4.5 %collective-permute-start.5 = (bf16[256,256]{1,0:T(8,128)(2,1)S(1)}, bf16[256,256]{1,0:T(8,128)(2,1)S(1)}, u32[]{:S(2)}, u32[]{:S(2)}) collective-permute-start(bf16[256,256]{1,0:T(8,128)(2,1)S(1)} %get-tuple-element.37), channel_id=1, source_target_pairs={{0,4},{4,8},{8,12},{12,16},{16,20},{20,24},{24,28},{28,32},{32,36}... | collective-permute-start | bytes 393224 | tf_op jit(solution)/shard_map/ppermute | solution.py:18
  32.6 33.6 %copy-start.3 = (s32[2,5]{1,0:T(2,128)}, s32[2,5]{1,0:T(2,128)S(1)}, u32[]{:S(2)}) copy-start(s32[2,5]{1,0:T(2,128)S(1)} %concatenate.36.refs_0_) | copy-start | bytes 124
  35.1 29.5 %copy-start.2 = (bf16[64,4,1024]{2,0,1:T(8,128)(2,1)}, bf16[64,4,1024]{2,0,1:T(8,128)(2,1)S(1)}, u32[]{:S(2)}) copy-start(bf16[64,4,1024]{2,0,1:T(8,128)(2,1)S(1)} %all-to-all-done.1) | copy-start | bytes 1572868
  35.1 11.1 %collective-permute-start.8 = (bf16[4,2,2,2,64,128]{5,4,3,2,1,0:T(8,128)(2,1)S(1)}, bf16[4,2,2,2,64,128]{5,4,3,2,1,0:T(8,128)(2,1)}, u32[]{:S(2)}, u32[]{:S(2)}) collective-permute-start(bf16[4,2,2,2,64,128]{5,4,3,2,1,0:T(8,128)(2,1)S(1)} %pad_maximum_fusion.1), channel_id=1, source_target_pairs={{0,96},{8,104},{16,112},{24,120},{32,0},{40,8},{48,16},{56,24},{64... | collective-permute-start | bytes 1572872 | tf_op jit(solution)/shard_map/ppermute | solution.py:194
  37.9 11.6 %collective-permute-start.7 = (bf16[4,2,2,2,64,128]{5,4,3,2,1,0:T(8,128)(2,1)S(1)}, bf16[4,2,2,2,64,128]{5,4,3,2,1,0:T(8,128)(2,1)}, u32[]{:S(2)}, u32[]{:S(2)}) collective-permute-start(bf16[4,2,2,2,64,128]{5,4,3,2,1,0:T(8,128)(2,1)S(1)} %pad_maximum_fusion.1), channel_id=1, source_target_pairs={{0,64},{8,72},{16,80},{24,88},{32,96},{40,104},{48,112},{56,120},{... | collective-permute-start | bytes 1572872 | tf_op jit(solution)/shard_map/ppermute | solution.py:194
  38.3 26.3 %collective-permute-start.6 = (bf16[4,2,2,2,64,128]{5,4,3,2,1,0:T(8,128)(2,1)S(1)}, bf16[4,2,2,2,64,128]{5,4,3,2,1,0:T(8,128)(2,1)}, u32[]{:S(2)}, u32[]{:S(2)}) collective-permute-start(bf16[4,2,2,2,64,128]{5,4,3,2,1,0:T(8,128)(2,1)S(1)} %pad_maximum_fusion.1), channel_id=1, source_target_pairs={{0,32},{8,40},{16,48},{24,56},{32,64},{40,72},{48,80},{56,88},{64,... | collective-permute-start | bytes 1572872 | tf_op jit(solution)/shard_map/ppermute | solution.py:194
  67.3 2.9 %collective-permute-start.9 = (bf16[2,2048,128]{2,1,0:T(8,128)(2,1)S(1)}, bf16[2,2048,128]{2,1,0:T(8,128)(2,1)S(1)}, u32[]{:S(2)}, u32[]{:S(2)}) collective-permute-start(bf16[2,2048,128]{2,1,0:T(8,128)(2,1)S(1)} %bitcast.88), channel_id=1, source_target_pairs={{0,4},{4,0},{1,5},{5,1},{2,6},{6,2},{3,7},{7,3},{8,12},{12,8},{9,1... | collective-permute-start | bytes 3145736 | tf_op jit(solution)/shard_map/ppermute | solution.py:214

commit v11 on v10

--- a/solution.py
+++ b/solution.py
@@ -175,6 +175,7 @@
     chips = lax.axis_size("chip")
     cores = lax.axis_size("core")
     side = int(round(chips ** 0.5))
+    assert side == 4 and side * side == chips
     chip_index = lax.axis_index("chip")
     swap = [(c, cores - 1 - c) for c in range(cores)]
     mine = lax.dynamic_index_in_dim(pieces, core_index, 2, keepdims=False)
@@ -182,8 +183,7 @@
     stage = jnp.stack([mine, lax.ppermute(sent, "core", swap)], 0)
     q_all = lax.all_to_all(queries, "head", split_axis=1, concat_axis=0, tiled=True)
     for stride in (1, side):
-        moved = [stage]
-        for step in range(1, side):
+        def shift(value, step):
             pairs = []
             for chip in range(chips):
                 row, col = chip // side, chip % side
@@ -191,8 +191,19 @@
                     pairs.append((chip, row * side + (col + step) % side))
                 else:
                     pairs.append((chip, ((row + step) % side) * side + col))
-            moved.append(lax.ppermute(stage, "chip", pairs))
-        stage = jnp.stack(moved, 0)
+            return lax.ppermute(value, "chip", pairs)
+
+        split = stage.ndim - 4
+        ahead = shift(stage, 1)
+        behind = shift(stage, side - 1)
+        far = jnp.concatenate(
+            [
+                shift(lax.index_in_dim(ahead, 0, split), 1),
+                shift(lax.index_in_dim(behind, 1, split), side - 1),
+            ],
+            split,
+        )
+        stage = jnp.stack([stage, ahead, far, behind], 0)
         if stride == 1:
             stage, q_all, prev_k, prev_v, diagonal_offsets, local_vert = lax.optimization_barrier(
                 (stage, q_all, prev_k, prev_v, diagonal_offsets, local_vert)

time: 85.9 us -> 88.3 us (1.028)
  starting transfers between devices: 25.7 us -> 35.7 us
  waiting for transfers between devices: 30.7 us -> 22.2 us
    ppermute x6 -> x8, waiting for transfers between devices: 24 us -> 13.9 us  [shift(): return lax.ppermute(value, 'chip', pairs)]
    ppermute x1, starting transfers between devices: 0.57 us -> 8.1 us  [local(): other = lax.ppermute(part, 'core', swap)]
    ppermute x6 -> x8, starting transfers between devices: 7.52 us -> 12 us  [shift(): return lax.ppermute(value, 'chip', pairs)]
    ppermute x2, starting transfers between devices: 6.09 us -> 4.11 us  [shifted(): return lax.ppermute(value, axis, pairs)]
    ppermute x2, waiting for transfers between devices: 0.01 us -> 1.65 us  [shifted(): return lax.ppermute(value, axis, pairs)]
  transfers between devices with their start and end apart: 12 -> 14, of which waited for: 6 -> 8; matrix products, arithmetic and copies ran while one was open for 7% -> 7% of each run, Pallas kernels for 0% -> 0%
where the time goes in v11:
time: 88.3 us; the launch traced here: 87.7 us
  starting transfers between devices  35.7 us (40%)
  waiting for transfers between devices  22.2 us (25%)
  Pallas kernels  13.9 us (16%)
  other arithmetic  8 us (9%)
  local copies, waits for them, and re-layouts  7.52 us (9%)
    pallas_call x1, Pallas kernels, attend(): pl.pallas_call(kernel, grid_spec=grid_spec, out_shape=jax.ShapeDtypeStruc...  13.9 us
    ppermute x8, waiting for transfers between devices, shift(): return lax.ppermute(value, 'chip', pairs)  13.9 us
    ppermute x8, starting transfers between devices, shift(): return lax.ppermute(value, 'chip', pairs)  12 us
    ppermute x1, starting transfers between devices, local(): other = lax.ppermute(part, 'core', swap)  8.1 us
    all_to_all x1, starting transfers between devices, local(): lax.all_to_all(joined, 'head', split_axis=1, concat_axis=0, tiled=True)  5.84 us
    all_to_all x1, waiting for transfers between devices, local(): lax.all_to_all(joined, 'head', split_axis=1, concat_axis=0, tiled=True)  4.38 us
    ppermute x2, starting transfers between devices, shifted(): return lax.ppermute(value, axis, pairs)  4.11 us
    all_to_all x1, starting transfers between devices, local(): lax.all_to_all(queries, 'head', split_axis=1, concat_axis=0, tiled=True)  3.47 us
  transfers between devices with their start and end apart: 14, of which 8 were waited for; matrix products, arithmetic and copies ran while one was open for 7% of the time, Pallas kernels for 0%

profile of v11, /device:TPU:1, one launch (start us, length us, event | category | flops | bytes accessed | tf_op | source)
XLA Modules:
  0.0 87.7 jit_solution(5391939499356257353)
XLA Ops:
  0.0 1.0 %copy_bitcast_fusion.1 = (bf16[64,4,256]{2,0,1:T(8,128)(2,1)S(1)}, bf16[64,4,256]{2,0,1:T(8,128)(2,1)S(1)}) fusion(bf16[8,4,8,256]{3,2,1,0:T(8,128)(2,1)} %bitcast.108, bf16[8,4,8,256]{3,2,1,0:T(8,128)(2,1)} %bitcast.109), kind=kLoop, calls=%fused_computation.15 | loop fusion | bytes 524288 | tf_op jit(solution)/shard_map/reshape | solution.py:136
  1.0 0.7 pad_maximum_fusion.2
  1.7 5.8 %all-to-all-start = ((bf16[64,4,512]{2,0,1:T(8,128)(2,1)}), bf16[64,4,512]{2,0,1:T(8,128)(2,1)S(1)}, u32[]{:S(2)}, u32[]{:S(2)}) async-start(bf16[64,4,512]{2,0,1:T(8,128)(2,1)} %pad_maximum_fusion.2), calls=%async_computation | async-start | bytes 524288 | tf_op jit(solution)/shard_map/all_to_all | solution.py:138
  7.6 0.7 and_select_fusion.8
  8.3 0.2 convert_reduce_fusion
  8.5 0.2 fusion
  8.8 4.4 %all-to-all-done = bf16[64,4,512]{2,0,1:T(8,128)(2,1)S(1)} async-done(((bf16[64,4,512]{2,0,1:T(8,128)(2,1)}), bf16[64,4,512]{2,0,1:T(8,128)(2,1)S(1)}, u32[]{:S(2)}, u32[]{:S(2)}) %all-to-all-start) | async-done | bytes 262176 | tf_op jit(solution)/shard_map/all_to_all | solution.py:138
  13.2 0.2 fusion.21
  13.5 0.2 fusion.20
  13.7 0.6 gather_fusion.3
  14.2 0.6 gather_fusion.2
  14.8 0.6 gather_fusion.1
  15.4 0.6 gather_fusion
  16.0 2.2 %collective-permute-start = (bf16[2,2,64,128]{3,2,1,0:T(8,128)(2,1)S(1)}, bf16[2,2,64,128]{3,2,1,0:T(8,128)(2,1)S(1)}, u32[]{:S(2)}, u32[]{:S(2)}) collective-permute-start(bf16[2,2,64,128]{3,2,1,0:T(8,128)(2,1)S(1)} %get-tuple-element.44), channel_id=1, source_target_pairs={{0,4},{4,0},{1,5},{5,1},{2,6},{6,2},{3,7},{7,3},{8,12},{12,8},{9,1... | collective-permute-start | bytes 196616 | tf_op jit(solution)/shard_map/ppermute | solution.py:183
  18.3 0.1 copy.46
  18.4 0.8 copy.59
  19.2 3.5 %all-to-all-start.1 = ((bf16[64,4,1024]{2,0,1:T(8,128)(2,1)}), bf16[64,4,1024]{2,0,1:T(8,128)(2,1)S(1)}, u32[]{:S(2)}, u32[]{:S(2)}) async-start(bf16[64,4,1024]{2,0,1:T(8,128)(2,1)} %bitcast.84), calls=%async_computation.1 | async-start | bytes 1048576 | tf_op jit(solution)/shard_map/all_to_all | solution.py:184
  22.7 2.5 %collective-permute-start.3 = (bf16[2,2,2,64,128]{4,3,2,1,0:T(8,128)(2,1)S(1)}, bf16[2,2,2,64,128]{4,3,2,1,0:T(8,128)(2,1)S(1)}, u32[]{:S(2)}, u32[]{:S(2)}) collective-permute-start(bf16[2,2,2,64,128]{4,3,2,1,0:T(8,128)(2,1)S(1)} %get-tuple-element.42), channel_id=1, source_target_pairs={{0,24},{8,0},{16,8},{24,16},{32,56},{40,32},{48,40},{56,48},{64,88... | collective-permute-start | bytes 393224 | tf_op jit(solution)/shard_map/ppermute | solution.py:194
  25.4 0.1 reshape.260
  25.4 2.7 %collective-permute-done.3 = bf16[2,2,2,64,128]{4,3,2,1,0:T(8,128)(2,1)S(1)} collective-permute-done((bf16[2,2,2,64,128]{4,3,2,1,0:T(8,128)(2,1)S(1)}, bf16[2,2,2,64,128]{4,3,2,1,0:T(8,128)(2,1)S(1)}, u32[]{:S(2)}, u32[]{:S(2)}) %collective-permute-start.3) | collective-permute-done | bytes 131104 | tf_op jit(solution)/shard_map/ppermute | solution.py:194
  28.1 3.4 %collective-permute-start.4 = (bf16[2,1,2,64,128]{4,3,2,1,0:T(8,128)(2,1)S(1)}, bf16[2,1,2,64,128]{4,3,2,1,0:T(8,128)(2,1)S(1)}, u32[]{:S(2)}, u32[]{:S(2)}) collective-permute-start(bf16[2,1,2,64,128]{4,3,2,1,0:T(8,128)(2,1)S(1)} %slice.86), channel_id=1, source_target_pairs={{0,24},{8,0},{16,8},{24,16},{32,56},{40,32},{48,40},{56,48},{64,88... | collective-permute-start | bytes 196616 | tf_op jit(solution)/shard_map/ppermute | solution.py:194
  31.6 2.2 %collective-permute-start.5 = (bf16[256,256]{1,0:T(8,128)(2,1)S(1)}, bf16[256,256]{1,0:T(8,128)(2,1)S(1)}, u32[]{:S(2)}, u32[]{:S(2)}) collective-permute-start(bf16[256,256]{1,0:T(8,128)(2,1)S(1)} %get-tuple-element.38), channel_id=1, source_target_pairs={{0,4},{4,8},{8,12},{12,16},{16,20},{20,24},{24,28},{28,32},{32,36}... | collective-permute-start | bytes 393224 | tf_op jit(solution)/shard_map/ppermute | solution.py:18
  33.8 1.9 %collective-permute-start.6 = (bf16[256,256]{1,0:T(8,128)(2,1)S(1)}, bf16[256,256]{1,0:T(8,128)(2,1)S(1)}, u32[]{:S(2)}, u32[]{:S(2)}) collective-permute-start(bf16[256,256]{1,0:T(8,128)(2,1)S(1)} %get-tuple-element.37), channel_id=1, source_target_pairs={{0,4},{4,8},{8,12},{12,16},{16,20},{20,24},{24,28},{28,32},{32,36}... | collective-permute-start | bytes 393224 | tf_op jit(solution)/shard_map/ppermute | solution.py:18
  35.8 0.2 collective-permute-done.2
  36.0 1.6 %collective-permute-done.6 = bf16[256,256]{1,0:T(8,128)(2,1)S(1)} collective-permute-done((bf16[256,256]{1,0:T(8,128)(2,1)S(1)}, bf16[256,256]{1,0:T(8,128)(2,1)S(1)}, u32[]{:S(2)}, u32[]{:S(2)}) %collective-permute-start.6) | collective-permute-done | bytes 131104 | tf_op jit(solution)/shard_map/ppermute | solution.py:18
  37.7 0.8 copy-done.3
  38.5 2.7 %collective-permute-start.9 = (bf16[4,2,2,2,64,128]{5,4,3,2,1,0:T(8,128)(2,1)S(1)}, bf16[4,2,2,2,64,128]{5,4,3,2,1,0:T(8,128)(2,1)S(1)}, u32[]{:S(2)}, u32[]{:S(2)}) collective-permute-start(bf16[4,2,2,2,64,128]{5,4,3,2,1,0:T(8,128)(2,1)S(1)} %pad_maximum_fusion.1), channel_id=1, source_target_pairs={{0,96},{8,104},{16,112},{24,120},{32,0},{40,8},{48,16},{56,24},{64... | collective-permute-start | bytes 1572872 | tf_op jit(solution)/shard_map/ppermute | solution.py:194
  41.2 0.7 pad_maximum_fusion.3.refs_2_
  42.1 0.1 stack.103
  42.3 0.1 stack.102
  42.5 0.1 compare_reduce_fusion.1
  42.6 0.1 compare_reduce_fusion
  42.7 0.1 broadcast_in_dim.33
  42.8 0.1 stack.106
  43.0 0.1 stack.105
  43.1 0.7 pad_maximum_fusion.4.refs_3_
  43.9 0.7 copy_convert_fusion.refs_7_
  44.5 2.8 %collective-permute-done.9 = bf16[4,2,2,2,64,128]{5,4,3,2,1,0:T(8,128)(2,1)S(1)} collective-permute-done((bf16[4,2,2,2,64,128]{5,4,3,2,1,0:T(8,128)(2,1)S(1)}, bf16[4,2,2,2,64,128]{5,4,3,2,1,0:T(8,128)(2,1)S(1)}, u32[]{:S(2)}, u32[]{:S(2)}) %collective-permute-start.9) | collective-permute-done | bytes 524320 | tf_op jit(solution)/shard_map/ppermute | solution.py:194
  47.4 3.2 %collective-permute-start.10 = (bf16[4,2,1,2,64,128]{5,4,3,2,1,0:T(8,128)(2,1)S(1)}, bf16[4,2,1,2,64,128]{5,4,3,2,1,0:T(8,128)(2,1)S(1)}, u32[]{:S(2)}, u32[]{:S(2)}) collective-permute-start(bf16[4,2,1,2,64,128]{5,4,3,2,1,0:T(8,128)(2,1)S(1)} %slice.88), channel_id=1, source_target_pairs={{0,96},{8,104},{16,112},{24,120},{32,0},{40,8},{48,16},{56,24},{64... | collective-permute-start | bytes 786440 | tf_op jit(solution)/shard_map/ppermute | solution.py:194
  50.7 0.6 copy_convert_fusion.1.refs_6_
  51.3 4.8 %collective-permute-done.10 = bf16[4,2,1,2,64,128]{5,4,3,2,1,0:T(8,128)(2,1)S(1)} collective-permute-done((bf16[4,2,1,2,64,128]{5,4,3,2,1,0:T(8,128)(2,1)S(1)}, bf16[4,2,1,2,64,128]{5,4,3,2,1,0:T(8,128)(2,1)S(1)}, u32[]{:S(2)}, u32[]{:S(2)}) %collective-permute-start.10) | collective-permute-done | bytes 262176 | tf_op jit(solution)/shard_map/ppermute | solution.py:194
  56.1 3.4 %collective-permute-done.8 = bf16[4,2,1,2,64,128]{5,4,3,2,1,0:T(8,128)(2,1)S(1)} collective-permute-done((bf16[4,2,1,2,64,128]{5,4,3,2,1,0:T(8,128)(2,1)S(1)}, bf16[4,2,1,2,64,128]{5,4,3,2,1,0:T(8,128)(2,1)S(1)}, u32[]{:S(2)}, u32[]{:S(2)}) %collective-permute-start.8) | collective-permute-done | bytes 262176 | tf_op jit(solution)/shard_map/ppermute | solution.py:194
  59.6 1.3 %pad_maximum_fusion = bf16[4,4,2,2,2,64,128]{6,5,4,3,2,1,0:T(8,128)(2,1)S(1)} fusion(bf16[1,4,2,2,2,64,128]{6,5,4,3,2,1,0:T(8,128)(2,1)S(1)} %bitcast.93, bf16[1,4,2,2,2,64,128]{6,5,4,3,2,1,0:T(8,128)(2,1)S(1)} %maximum_bitcast_fusion, bf16[1,4,2,2,2,64,128]{6,5,4,3,2,1,0:T(8,128)(2,1)} %bitcast.94, bf16[1,4,2,2,2,64,128]{6,5,4,3,2,1,0:T(8,128)(2,1)S(1)} %bitcast.92), kind=kLoop, calls=%fused_computation.5 | loop fusion | flops 3145728 | bytes 4194304 | tf_op jit(solution)/shard_map/stack | solution.py:206
  60.9 1.0 %gather_fusion.4 = bf16[64,64,128]{2,1,0:T(8,128)(2,1)S(1)} fusion(bf16[4,4,2,2,2,64,128]{6,5,4,3,2,1,0:T(8,128)(2,1)S(1)} %pad_maximum_fusion, s32[64]{0:T(128)S(1)} %reshape.260), kind=kCustom, calls=%fused_computation.4 | custom fusion | bytes 2098432 | tf_op jit(solution)/shard_map/gather | solution.py:223
  61.9 8.1 %collective-permute-start.11 = (bf16[2,2048,128]{2,1,0:T(8,128)(2,1)S(1)}, bf16[2,2048,128]{2,1,0:T(8,128)(2,1)S(1)}, u32[]{:S(2)}, u32[]{:S(2)}) collective-permute-start(bf16[2,2048,128]{2,1,0:T(8,128)(2,1)S(1)} %bitcast.90), channel_id=1, source_target_pairs={{0,4},{4,0},{1,5},{5,1},{2,6},{6,2},{3,7},{7,3},{8,12},{12,8},{9,1... | collective-permute-start | bytes 3145736 | tf_op jit(solution)/shard_map/ppermute | solution.py:225
  70.0 2.3 %collective-permute-done.11 = bf16[2,2048,128]{2,1,0:T(8,128)(2,1)S(1)} collective-permute-done((bf16[2,2048,128]{2,1,0:T(8,128)(2,1)S(1)}, bf16[2,2048,128]{2,1,0:T(8,128)(2,1)S(1)}, u32[]{:S(2)}, u32[]{:S(2)}) %collective-permute-start.11) | collective-permute-done | bytes 1048608 | tf_op jit(solution)/shard_map/ppermute | solution.py:225
  72.3 1.5 %broadcast_select_fusion = (bf16[2,2048,128]{2,1,0:T(8,128)(2,1)}, bf16[2,2048,128]{2,1,0:T(8,128)(2,1)}) fusion(bf16[2,2048,128]{2,1,0:T(8,128)(2,1)S(1)} %collective-permute-done.11, pred[]{:T(512)S(6)} %eq.85, bf16[2,2048,128]{2,1,0:T(8,128)(2,1)S(1)} %bitcast.91), kind=kLoop, calls=%fused_computation.6 | loop fusion | flops 1048576 | bytes 4194305 | tf_op jit(solution)/shard_map/jit(_where)/select_n | solution.py:227
  73.8 13.9 %shard_map.55 = bf16[256,1024]{1,0:T(8,128)(2,1)} custom-call(s32[2,5]{1,0:T(2,128)} %copy-done.4, bf16[256,1024]{1,0:T(8,128)(2,1)} %bitcast.97, bf16[512,256]{1,0:T(8,128)(2,1)} %pad_maximum_fusion.3.refs_2_, bf16[512,256]{1,0:T(8,128)(2,1)} %pad_maximum_fusion.4.refs_3_, bf16[2,2048,128]{2,1,0:T(8,128)(2,1)} %get-tuple-element.36.refs_4_, ...), custom_call_target="tpu_custom_call" | custom-call | flops 2550136832 | bytes 3670016 | tf_op jit(solution)/shard_map/pallas_call | solution.py:97
  (59 shorter events, 1.3 us)
Async XLA Ops:
  0.0 18.2 %copy-start = (s32[8,4]{0,1:T(4,128)S(1)}, s32[8,4]{0,1:T(4,128)}, u32[]{:S(2)}) copy-start(s32[8,4]{0,1:T(4,128)} %param.8) | copy-start | bytes 388
  1.7 11.4 %all-to-all-start = ((bf16[64,4,512]{2,0,1:T(8,128)(2,1)}), bf16[64,4,512]{2,0,1:T(8,128)(2,1)S(1)}, u32[]{:S(2)}, u32[]{:S(2)}) async-start(bf16[64,4,512]{2,0,1:T(8,128)(2,1)} %pad_maximum_fusion.2), calls=%async_computation | async-start | bytes 524288 | tf_op jit(solution)/shard_map/all_to_all | solution.py:138
  13.1 5.2 %copy-start.2 = (bf16[64,4096]{1,0:T(8,128)(2,1)S(1)}, bf16[64,4096]{1,0:T(8,128)(2,1)}, u32[]{:S(2)}) copy-start(bf16[64,4096]{1,0:T(8,128)(2,1)} %param.5) | copy-start | bytes 1572868
  16.0 6.6 %collective-permute-start = (bf16[2,2,64,128]{3,2,1,0:T(8,128)(2,1)S(1)}, bf16[2,2,64,128]{3,2,1,0:T(8,128)(2,1)S(1)}, u32[]{:S(2)}, u32[]{:S(2)}) collective-permute-start(bf16[2,2,64,128]{3,2,1,0:T(8,128)(2,1)S(1)} %get-tuple-element.44), channel_id=1, source_target_pairs={{0,4},{4,0},{1,5},{5,1},{2,6},{6,2},{3,7},{7,3},{8,12},{12,8},{9,1... | collective-permute-start | bytes 196616 | tf_op jit(solution)/shard_map/ppermute | solution.py:183
  19.2 18.5 %all-to-all-start.1 = ((bf16[64,4,1024]{2,0,1:T(8,128)(2,1)}), bf16[64,4,1024]{2,0,1:T(8,128)(2,1)S(1)}, u32[]{:S(2)}, u32[]{:S(2)}) async-start(bf16[64,4,1024]{2,0,1:T(8,128)(2,1)} %bitcast.84), calls=%async_computation.1 | async-start | bytes 1048576 | tf_op jit(solution)/shard_map/all_to_all | solution.py:184
  22.7 5.4 %collective-permute-start.3 = (bf16[2,2,2,64,128]{4,3,2,1,0:T(8,128)(2,1)S(1)}, bf16[2,2,2,64,128]{4,3,2,1,0:T(8,128)(2,1)S(1)}, u32[]{:S(2)}, u32[]{:S(2)}) collective-permute-start(bf16[2,2,2,64,128]{4,3,2,1,0:T(8,128)(2,1)S(1)} %get-tuple-element.42), channel_id=1, source_target_pairs={{0,24},{8,0},{16,8},{24,16},{32,56},{40,32},{48,40},{56,48},{64,88... | collective-permute-start | bytes 393224 | tf_op jit(solution)/shard_map/ppermute | solution.py:194
  25.3 6.2 %collective-permute-start.1 = (bf16[2,2,2,64,128]{4,3,2,1,0:T(8,128)(2,1)S(1)}, bf16[2,2,2,64,128]{4,3,2,1,0:T(8,128)(2,1)S(1)}, u32[]{:S(2)}, u32[]{:S(2)}) collective-permute-start(bf16[2,2,2,64,128]{4,3,2,1,0:T(8,128)(2,1)S(1)} %get-tuple-element.42), channel_id=1, source_target_pairs={{0,8},{8,16},{16,24},{24,0},{32,40},{40,48},{48,56},{56,32},{64,72... | collective-permute-start | bytes 393224 | tf_op jit(solution)/shard_map/ppermute | solution.py:194
  25.4 34.2 %copy-start.4 = (s32[2,5]{1,0:T(2,128)}, s32[2,5]{1,0:T(2,128)S(1)}, u32[]{:S(2)}) copy-start(s32[2,5]{1,0:T(2,128)S(1)} %concatenate.43.refs_0_) | copy-start | bytes 124
  28.1 7.6 %collective-permute-start.4 = (bf16[2,1,2,64,128]{4,3,2,1,0:T(8,128)(2,1)S(1)}, bf16[2,1,2,64,128]{4,3,2,1,0:T(8,128)(2,1)S(1)}, u32[]{:S(2)}, u32[]{:S(2)}) collective-permute-start(bf16[2,1,2,64,128]{4,3,2,1,0:T(8,128)(2,1)S(1)} %slice.86), channel_id=1, source_target_pairs={{0,24},{8,0},{16,8},{24,16},{32,56},{40,32},{48,40},{56,48},{64,88... | collective-permute-start | bytes 196616 | tf_op jit(solution)/shard_map/ppermute | solution.py:194
  31.5 4.4 %collective-permute-start.2 = (bf16[2,1,2,64,128]{4,3,2,1,0:T(8,128)(2,1)S(1)}, bf16[2,1,2,64,128]{4,3,2,1,0:T(8,128)(2,1)S(1)}, u32[]{:S(2)}, u32[]{:S(2)}) collective-permute-start(bf16[2,1,2,64,128]{4,3,2,1,0:T(8,128)(2,1)S(1)} %slice.85), channel_id=1, source_target_pairs={{0,8},{8,16},{16,24},{24,0},{32,40},{40,48},{48,56},{56,32},{64,72... | collective-permute-start | bytes 196616 | tf_op jit(solution)/shard_map/ppermute | solution.py:194
  31.6 4.4 %collective-permute-start.5 = (bf16[256,256]{1,0:T(8,128)(2,1)S(1)}, bf16[256,256]{1,0:T(8,128)(2,1)S(1)}, u32[]{:S(2)}, u32[]{:S(2)}) collective-permute-start(bf16[256,256]{1,0:T(8,128)(2,1)S(1)} %get-tuple-element.38), channel_id=1, source_target_pairs={{0,4},{4,8},{8,12},{12,16},{16,20},{20,24},{24,28},{28,32},{32,36}... | collective-permute-start | bytes 393224 | tf_op jit(solution)/shard_map/ppermute | solution.py:18
  33.8 3.9 %collective-permute-start.6 = (bf16[256,256]{1,0:T(8,128)(2,1)S(1)}, bf16[256,256]{1,0:T(8,128)(2,1)S(1)}, u32[]{:S(2)}, u32[]{:S(2)}) collective-permute-start(bf16[256,256]{1,0:T(8,128)(2,1)S(1)} %get-tuple-element.37), channel_id=1, source_target_pairs={{0,4},{4,8},{8,12},{12,16},{16,20},{20,24},{24,28},{28,32},{32,36}... | collective-permute-start | bytes 393224 | tf_op jit(solution)/shard_map/ppermute | solution.py:18
  37.7 0.8 copy-start.3
  38.5 8.9 %collective-permute-start.9 = (bf16[4,2,2,2,64,128]{5,4,3,2,1,0:T(8,128)(2,1)S(1)}, bf16[4,2,2,2,64,128]{5,4,3,2,1,0:T(8,128)(2,1)S(1)}, u32[]{:S(2)}, u32[]{:S(2)}) collective-permute-start(bf16[4,2,2,2,64,128]{5,4,3,2,1,0:T(8,128)(2,1)S(1)} %pad_maximum_fusion.1), channel_id=1, source_target_pairs={{0,96},{8,104},{16,112},{24,120},{32,0},{40,8},{48,16},{56,24},{64... | collective-permute-start | bytes 1572872 | tf_op jit(solution)/shard_map/ppermute | solution.py:194
  41.2 9.3 %collective-permute-start.7 = (bf16[4,2,2,2,64,128]{5,4,3,2,1,0:T(8,128)(2,1)S(1)}, bf16[4,2,2,2,64,128]{5,4,3,2,1,0:T(8,128)(2,1)S(1)}, u32[]{:S(2)}, u32[]{:S(2)}) collective-permute-start(bf16[4,2,2,2,64,128]{5,4,3,2,1,0:T(8,128)(2,1)S(1)} %pad_maximum_fusion.1), channel_id=1, source_target_pairs={{0,32},{8,40},{16,48},{24,56},{32,64},{40,72},{48,80},{56,88},{64,... | collective-permute-start | bytes 1572872 | tf_op jit(solution)/shard_map/ppermute | solution.py:194
  47.4 8.8 %collective-permute-start.10 = (bf16[4,2,1,2,64,128]{5,4,3,2,1,0:T(8,128)(2,1)S(1)}, bf16[4,2,1,2,64,128]{5,4,3,2,1,0:T(8,128)(2,1)S(1)}, u32[]{:S(2)}, u32[]{:S(2)}) collective-permute-start(bf16[4,2,1,2,64,128]{5,4,3,2,1,0:T(8,128)(2,1)S(1)} %slice.88), channel_id=1, source_target_pairs={{0,96},{8,104},{16,112},{24,120},{32,0},{40,8},{48,16},{56,24},{64... | collective-permute-start | bytes 786440 | tf_op jit(solution)/shard_map/ppermute | solution.py:194
  50.6 9.1 %copy-start.1 = (bf16[4,2,2,2,64,128]{5,4,3,2,1,0:T(8,128)(2,1)}, bf16[4,2,2,2,64,128]{5,4,3,2,1,0:T(8,128)(2,1)S(1)}, u32[]{:S(2)}) copy-start(bf16[4,2,2,2,64,128]{5,4,3,2,1,0:T(8,128)(2,1)S(1)} %collective-permute-done.7) | copy-start | bytes 1572868
  50.6 9.0 %collective-permute-start.8 = (bf16[4,2,1,2,64,128]{5,4,3,2,1,0:T(8,128)(2,1)S(1)}, bf16[4,2,1,2,64,128]{5,4,3,2,1,0:T(8,128)(2,1)S(1)}, u32[]{:S(2)}, u32[]{:S(2)}) collective-permute-start(bf16[4,2,1,2,64,128]{5,4,3,2,1,0:T(8,128)(2,1)S(1)} %slice.87), channel_id=1, source_target_pairs={{0,32},{8,40},{16,48},{24,56},{32,64},{40,72},{48,80},{56,88},{64,... | collective-permute-start | bytes 786440 | tf_op jit(solution)/shard_map/ppermute | solution.py:194
  61.9 10.4 %collective-permute-start.11 = (bf16[2,2048,128]{2,1,0:T(8,128)(2,1)S(1)}, bf16[2,2048,128]{2,1,0:T(8,128)(2,1)S(1)}, u32[]{:S(2)}, u32[]{:S(2)}) collective-permute-start(bf16[2,2048,128]{2,1,0:T(8,128)(2,1)S(1)} %bitcast.90), channel_id=1, source_target_pairs={{0,4},{4,0},{1,5},{5,1},{2,6},{6,2},{3,7},{7,3},{8,12},{12,8},{9,1... | collective-permute-start | bytes 3145736 | tf_op jit(solution)/shard_map/ppermute | solution.py:225

commit v12 on v10

--- a/solution.py
+++ b/solution.py
@@ -160,25 +160,15 @@
     slots = 2
     mine = (owner == seq_index)[:, None, :] & (rank[:, None, :] == jnp.arange(slots)[None, :, None])
     pick = jnp.sum(jnp.where(mine, inner[:, None, :], 0), axis=2)
-    pieces = []
-    for group_member in range(kv_local):
-        pieces.append(
-            jnp.stack(
-                [
-                    own_k[:, :, group_member][pick[group_member]],
-                    own_v[:, :, group_member][pick[group_member]],
-                ],
-                1,
-            )
-        )
-    pieces, queries = lax.optimization_barrier((jnp.stack(pieces, 0), queries))
+    pieces, queries = lax.optimization_barrier((pick, queries))
     chips = lax.axis_size("chip")
     cores = lax.axis_size("core")
     side = int(round(chips ** 0.5))
     chip_index = lax.axis_index("chip")
     swap = [(c, cores - 1 - c) for c in range(cores)]
-    mine = lax.dynamic_index_in_dim(pieces, core_index, 2, keepdims=False)
-    sent = lax.dynamic_index_in_dim(pieces, cores - 1 - core_index, 2, keepdims=False)
+    heads_col = jnp.arange(kv_local)[:, None]
+    mine = jnp.where(core_index == 0, own_k, own_v)[pieces, :, heads_col]
+    sent = jnp.where(core_index == 0, own_v, own_k)[pieces, :, heads_col]
     stage = jnp.stack([mine, lax.ppermute(sent, "core", swap)], 0)
     q_all = lax.all_to_all(queries, "head", split_axis=1, concat_axis=0, tiled=True)
     for stride in (1, side):

time: 85.9 us -> 83.6 us (0.973)
  waiting for transfers between devices: 30.7 us -> 28.5 us
    all_to_all x1, waiting for transfers between devices: 4.38 us -> 2.46 us  [local(): lax.all_to_all(joined, 'head', split_axis=1, concat_axis=0, tiled=True)]
    gather x4 -> x2, local copies, waits for them, and re-layouts: 2.24 us -> 1.14 us  [the longest x1 0.57 us: local(): sent = jnp.where(core_index == 0, own_v, own_k)[pieces, :, heads_col]]
    all_to_all x1, local copies, waits for them, and re-layouts: 0.83 us -> 1.88 us  [local(): lax.all_to_all(queries, 'head', split_axis=1, concat_axis=0, tiled=True)]
  transfers between devices with their start and end apart: 12 -> 12, of which waited for: 6 -> 7; matrix products, arithmetic and copies ran while one was open for 7% -> 10% of each run, Pallas kernels for 0% -> 0%
where the time goes in v12:
time: 83.6 us; the launch traced here: 83.1 us
  waiting for transfers between devices  28.5 us (34%)
  starting transfers between devices  26 us (31%)
  Pallas kernels  13.9 us (17%)
  other arithmetic  8.23 us (10%)
  local copies, waits for them, and re-layouts  6.27 us (8%)
    ppermute x6, waiting for transfers between devices, local(): moved.append(lax.ppermute(stage, 'chip', pairs))  23.7 us
    pallas_call x1, Pallas kernels, attend(): pl.pallas_call(kernel, grid_spec=grid_spec, out_shape=jax.ShapeDtypeStruc...  13.9 us
    ppermute x6, starting transfers between devices, local(): moved.append(lax.ppermute(stage, 'chip', pairs))  7.52 us
    ppermute x2, starting transfers between devices, shifted(): return lax.ppermute(value, axis, pairs)  6.42 us
    all_to_all x1, starting transfers between devices, local(): lax.all_to_all(joined, 'head', split_axis=1, concat_axis=0, tiled=True)  5.84 us
    all_to_all x1, starting transfers between devices, local(): lax.all_to_all(queries, 'head', split_axis=1, concat_axis=0, tiled=True)  3.47 us
    all_to_all x1, waiting for transfers between devices, local(): lax.all_to_all(joined, 'head', split_axis=1, concat_axis=0, tiled=True)  2.46 us
    ppermute x1, waiting for transfers between devices, local(): other = lax.ppermute(part, 'core', swap)  2.29 us
  transfers between devices with their start and end apart: 12, of which 7 were waited for; matrix products, arithmetic and copies ran while one was open for 10% of the time, Pallas kernels for 0%

profile of v12, /device:TPU:1, one launch (start us, length us, event | category | flops | bytes accessed | tf_op | source)
XLA Modules:
  0.0 83.1 jit_solution(2288644960224453492)
XLA Ops:
  0.0 1.0 %copy_bitcast_fusion.1 = (bf16[64,4,256]{2,0,1:T(8,128)(2,1)S(1)}, bf16[64,4,256]{2,0,1:T(8,128)(2,1)S(1)}) fusion(bf16[8,4,8,256]{3,2,1,0:T(8,128)(2,1)} %bitcast.71, bf16[8,4,8,256]{3,2,1,0:T(8,128)(2,1)} %bitcast.72), kind=kLoop, calls=%fused_computation.12 | loop fusion | bytes 524288 | tf_op jit(solution)/shard_map/reshape | solution.py:136
  1.0 0.7 pad_maximum_fusion.2
  1.7 5.8 %all-to-all-start = ((bf16[64,4,512]{2,0,1:T(8,128)(2,1)}), bf16[64,4,512]{2,0,1:T(8,128)(2,1)S(1)}, u32[]{:S(2)}, u32[]{:S(2)}) async-start(bf16[64,4,512]{2,0,1:T(8,128)(2,1)} %pad_maximum_fusion.2), calls=%async_computation | async-start | bytes 524288 | tf_op jit(solution)/shard_map/all_to_all | solution.py:138
  7.6 0.7 and_select_fusion.8
  8.3 0.2 convert_reduce_fusion
  8.5 0.2 fusion
  8.7 0.1 reshape.175
  8.7 1.9 %copy.45 = bf16[8,4,8,1024]{3,2,0,1:T(8,128)(2,1)} copy(bf16[8,4,8,1024]{3,2,1,0:T(8,128)(2,1)} %bitcast.68) | data formatting | bytes 1048576 | tf_op jit(solution)/shard_map/all_to_all | solution.py:173
  10.7 2.5 %all-to-all-done = bf16[64,4,512]{2,0,1:T(8,128)(2,1)S(1)} async-done(((bf16[64,4,512]{2,0,1:T(8,128)(2,1)}), bf16[64,4,512]{2,0,1:T(8,128)(2,1)S(1)}, u32[]{:S(2)}, u32[]{:S(2)}) %all-to-all-start) | async-done | bytes 262176 | tf_op jit(solution)/shard_map/all_to_all | solution.py:138
  13.1 3.5 %all-to-all-start.1 = ((bf16[64,4,1024]{2,0,1:T(8,128)(2,1)}), bf16[64,4,1024]{2,0,1:T(8,128)(2,1)S(1)}, u32[]{:S(2)}, u32[]{:S(2)}) async-start(bf16[64,4,1024]{2,0,1:T(8,128)(2,1)} %bitcast.62), calls=%async_computation.1 | async-start | bytes 1048576 | tf_op jit(solution)/shard_map/all_to_all | solution.py:173
  16.7 0.6 gather_fusion.1
  17.3 2.2 %collective-permute-start = (bf16[2,2,64,128]{3,2,1,0:T(8,128)(2,1)S(1)}, bf16[2,2,64,128]{3,2,1,0:T(8,128)(2,1)S(1)}, u32[]{:S(2)}, u32[]{:S(2)}) collective-permute-start(bf16[2,2,64,128]{3,2,1,0:T(8,128)(2,1)S(1)} %bitcast.76), channel_id=1, source_target_pairs={{0,4},{4,0},{1,5},{5,1},{2,6},{6,2},{3,7},{7,3},{8,12},{12,8},{9,1... | collective-permute-start | bytes 196616 | tf_op jit(solution)/shard_map/ppermute | solution.py:172
  19.5 0.1 copy.36
  19.7 0.6 gather_fusion
  20.3 0.1 collective-permute-done
  20.4 2.5 %collective-permute-start.3 = (bf16[2,2,2,64,128]{4,3,2,1,0:T(8,128)(2,1)S(1)}, bf16[2,2,2,64,128]{4,3,2,1,0:T(8,128)(2,1)S(1)}, u32[]{:S(2)}, u32[]{:S(2)}) collective-permute-start(bf16[2,2,2,64,128]{4,3,2,1,0:T(8,128)(2,1)S(1)} %get-tuple-element.42), channel_id=1, source_target_pairs={{0,24},{8,0},{16,8},{24,16},{32,56},{40,32},{48,40},{56,48},{64,88... | collective-permute-start | bytes 393224 | tf_op jit(solution)/shard_map/ppermute | solution.py:184
  22.9 0.5 collective-permute-start.2
  23.4 0.6 collective-permute-start.1
  24.0 4.5 %collective-permute-start.4 = (bf16[256,256]{1,0:T(8,128)(2,1)S(1)}, bf16[256,256]{1,0:T(8,128)(2,1)S(1)}, u32[]{:S(2)}, u32[]{:S(2)}) collective-permute-start(bf16[256,256]{1,0:T(8,128)(2,1)S(1)} %get-tuple-element.40), channel_id=1, source_target_pairs={{0,4},{4,8},{8,12},{12,16},{16,20},{20,24},{24,28},{28,32},{32,36}... | collective-permute-start | bytes 393224 | tf_op jit(solution)/shard_map/ppermute | solution.py:18
  28.6 1.9 %collective-permute-start.5 = (bf16[256,256]{1,0:T(8,128)(2,1)S(1)}, bf16[256,256]{1,0:T(8,128)(2,1)S(1)}, u32[]{:S(2)}, u32[]{:S(2)}) collective-permute-start(bf16[256,256]{1,0:T(8,128)(2,1)S(1)} %get-tuple-element.37), channel_id=1, source_target_pairs={{0,4},{4,8},{8,12},{12,16},{16,20},{20,24},{24,28},{28,32},{32,36}... | collective-permute-start | bytes 393224 | tf_op jit(solution)/shard_map/ppermute | solution.py:18
  30.6 0.1 reshape.187
  30.7 2.0 %collective-permute-done.1 = bf16[2,2,2,64,128]{4,3,2,1,0:T(8,128)(2,1)S(1)} collective-permute-done((bf16[2,2,2,64,128]{4,3,2,1,0:T(8,128)(2,1)S(1)}, bf16[2,2,2,64,128]{4,3,2,1,0:T(8,128)(2,1)S(1)}, u32[]{:S(2)}, u32[]{:S(2)}) %collective-permute-start.1) | collective-permute-done | bytes 131104 | tf_op jit(solution)/shard_map/ppermute | solution.py:184
  32.8 2.8 %collective-permute-start.8 = (bf16[4,2,2,2,64,128]{5,4,3,2,1,0:T(8,128)(2,1)S(1)}, bf16[4,2,2,2,64,128]{5,4,3,2,1,0:T(8,128)(2,1)}, u32[]{:S(2)}, u32[]{:S(2)}) collective-permute-start(bf16[4,2,2,2,64,128]{5,4,3,2,1,0:T(8,128)(2,1)S(1)} %pad_maximum_fusion.1), channel_id=1, source_target_pairs={{0,96},{8,104},{16,112},{24,120},{32,0},{40,8},{48,16},{56,24},{64... | collective-permute-start | bytes 1572872 | tf_op jit(solution)/shard_map/ppermute | solution.py:184
  35.6 0.3 collective-permute-start.7
  35.9 0.7 collective-permute-start.6
  36.6 0.7 pad_maximum_fusion.3.refs_2_
  37.4 0.1 broadcast_in_dim.37
  37.5 0.1 stack.67
  37.6 0.1 broadcast_in_dim.36
  37.7 0.1 stack.66
  37.8 0.6 copy_convert_fusion.1.refs_6_
  38.5 0.1 compare_reduce_fusion.1
  38.6 0.1 compare_reduce_fusion
  38.7 0.1 broadcast_in_dim.39
  38.8 0.1 stack.70
  38.9 0.1 broadcast_in_dim.38
  39.0 0.1 stack.69
  39.2 0.7 pad_maximum_fusion.4.refs_3_
  39.9 0.7 copy_convert_fusion.refs_7_
  40.6 3.3 %collective-permute-done.8 = bf16[4,2,2,2,64,128]{5,4,3,2,1,0:T(8,128)(2,1)} collective-permute-done((bf16[4,2,2,2,64,128]{5,4,3,2,1,0:T(8,128)(2,1)S(1)}, bf16[4,2,2,2,64,128]{5,4,3,2,1,0:T(8,128)(2,1)}, u32[]{:S(2)}, u32[]{:S(2)}) %collective-permute-start.8) | collective-permute-done | bytes 524320 | tf_op jit(solution)/shard_map/ppermute | solution.py:184
  43.9 3.3 %collective-permute-done.7 = bf16[4,2,2,2,64,128]{5,4,3,2,1,0:T(8,128)(2,1)} collective-permute-done((bf16[4,2,2,2,64,128]{5,4,3,2,1,0:T(8,128)(2,1)S(1)}, bf16[4,2,2,2,64,128]{5,4,3,2,1,0:T(8,128)(2,1)}, u32[]{:S(2)}, u32[]{:S(2)}) %collective-permute-start.7) | collective-permute-done | bytes 524320 | tf_op jit(solution)/shard_map/ppermute | solution.py:184
  47.2 15.1 %collective-permute-done.6 = bf16[4,2,2,2,64,128]{5,4,3,2,1,0:T(8,128)(2,1)} collective-permute-done((bf16[4,2,2,2,64,128]{5,4,3,2,1,0:T(8,128)(2,1)S(1)}, bf16[4,2,2,2,64,128]{5,4,3,2,1,0:T(8,128)(2,1)}, u32[]{:S(2)}, u32[]{:S(2)}) %collective-permute-start.6) | collective-permute-done | bytes 524320 | tf_op jit(solution)/shard_map/ppermute | solution.py:184
  62.3 1.6 %pad_maximum_fusion = bf16[4,4,2,2,2,64,128]{6,5,4,3,2,1,0:T(8,128)(2,1)S(1)} fusion(bf16[1,4,2,2,2,64,128]{6,5,4,3,2,1,0:T(8,128)(2,1)} %bitcast.20, bf16[1,4,2,2,2,64,128]{6,5,4,3,2,1,0:T(8,128)(2,1)} %bitcast.19, bf16[1,4,2,2,2,64,128]{6,5,4,3,2,1,0:T(8,128)(2,1)} %bitcast.18, bf16[1,4,2,2,2,64,128]{6,5,4,3,2,1,0:T(8,128)(2,1)S(1)} %bitcast.66), kind=kLoop, calls=%fused_computation.3 | loop fusion | flops 3145728 | bytes 4194304 | tf_op jit(solution)/shard_map/stack | solution.py:185
  63.9 1.0 %gather_fusion.2 = bf16[64,64,128]{2,1,0:T(8,128)(2,1)S(1)} fusion(bf16[4,4,2,2,2,64,128]{6,5,4,3,2,1,0:T(8,128)(2,1)S(1)} %pad_maximum_fusion, s32[64]{0:T(128)S(1)} %reshape.187), kind=kCustom, calls=%fused_computation.2 | custom fusion | bytes 2098432 | tf_op jit(solution)/shard_map/gather | solution.py:202
  64.9 0.6 collective-permute-start.9
  65.5 2.3 %collective-permute-done.9 = bf16[2,2048,128]{2,1,0:T(8,128)(2,1)S(1)} collective-permute-done((bf16[2,2048,128]{2,1,0:T(8,128)(2,1)S(1)}, bf16[2,2048,128]{2,1,0:T(8,128)(2,1)S(1)}, u32[]{:S(2)}, u32[]{:S(2)}) %collective-permute-start.9) | collective-permute-done | bytes 1048608 | tf_op jit(solution)/shard_map/ppermute | solution.py:204
  67.8 1.5 %broadcast_select_fusion = (bf16[2,2048,128]{2,1,0:T(8,128)(2,1)}, bf16[2,2048,128]{2,1,0:T(8,128)(2,1)}) fusion(bf16[2,2048,128]{2,1,0:T(8,128)(2,1)S(1)} %collective-permute-done.9, pred[]{:T(512)S(6)} %eq.73, bf16[2,2048,128]{2,1,0:T(8,128)(2,1)S(1)} %bitcast.65), kind=kLoop, calls=%fused_computation.4 | loop fusion | flops 1048576 | bytes 4194305 | tf_op jit(solution)/shard_map/jit(_where)/select_n | solution.py:206
  69.2 13.9 %shard_map.55 = bf16[256,1024]{1,0:T(8,128)(2,1)} custom-call(s32[2,5]{1,0:T(2,128)} %copy-done.2, bf16[256,1024]{1,0:T(8,128)(2,1)} %bitcast.69, bf16[512,256]{1,0:T(8,128)(2,1)} %pad_maximum_fusion.3.refs_2_, bf16[512,256]{1,0:T(8,128)(2,1)} %pad_maximum_fusion.4.refs_3_, bf16[2,2048,128]{2,1,0:T(8,128)(2,1)} %get-tuple-element.36.refs_4_, ...), custom_call_target="tpu_custom_call" | custom-call | flops 2550136832 | bytes 3670016 | tf_op jit(solution)/shard_map/pallas_call | solution.py:97
  (35 shorter events, 0.8 us)
Async XLA Ops:
  0.0 19.4 %copy-start = (s32[8,4]{0,1:T(4,128)S(1)}, s32[8,4]{0,1:T(4,128)}, u32[]{:S(2)}) copy-start(s32[8,4]{0,1:T(4,128)} %param.8) | copy-start | bytes 388
  1.7 11.4 %all-to-all-start = ((bf16[64,4,512]{2,0,1:T(8,128)(2,1)}), bf16[64,4,512]{2,0,1:T(8,128)(2,1)S(1)}, u32[]{:S(2)}, u32[]{:S(2)}) async-start(bf16[64,4,512]{2,0,1:T(8,128)(2,1)} %pad_maximum_fusion.2), calls=%async_computation | async-start | bytes 524288 | tf_op jit(solution)/shard_map/all_to_all | solution.py:138
  13.1 19.6 %all-to-all-start.1 = ((bf16[64,4,1024]{2,0,1:T(8,128)(2,1)}), bf16[64,4,1024]{2,0,1:T(8,128)(2,1)S(1)}, u32[]{:S(2)}, u32[]{:S(2)}) async-start(bf16[64,4,1024]{2,0,1:T(8,128)(2,1)} %bitcast.62), calls=%async_computation.1 | async-start | bytes 1048576 | tf_op jit(solution)/shard_map/all_to_all | solution.py:173
  17.3 3.1 %collective-permute-start = (bf16[2,2,64,128]{3,2,1,0:T(8,128)(2,1)S(1)}, bf16[2,2,64,128]{3,2,1,0:T(8,128)(2,1)S(1)}, u32[]{:S(2)}, u32[]{:S(2)}) collective-permute-start(bf16[2,2,64,128]{3,2,1,0:T(8,128)(2,1)S(1)} %bitcast.76), channel_id=1, source_target_pairs={{0,4},{4,0},{1,5},{5,1},{2,6},{6,2},{3,7},{7,3},{8,12},{12,8},{9,1... | collective-permute-start | bytes 196616 | tf_op jit(solution)/shard_map/ppermute | solution.py:172
  20.4 10.3 %collective-permute-start.3 = (bf16[2,2,2,64,128]{4,3,2,1,0:T(8,128)(2,1)S(1)}, bf16[2,2,2,64,128]{4,3,2,1,0:T(8,128)(2,1)S(1)}, u32[]{:S(2)}, u32[]{:S(2)}) collective-permute-start(bf16[2,2,2,64,128]{4,3,2,1,0:T(8,128)(2,1)S(1)} %get-tuple-element.42), channel_id=1, source_target_pairs={{0,24},{8,0},{16,8},{24,16},{32,56},{40,32},{48,40},{56,48},{64,88... | collective-permute-start | bytes 393224 | tf_op jit(solution)/shard_map/ppermute | solution.py:184
  22.9 7.7 %collective-permute-start.2 = (bf16[2,2,2,64,128]{4,3,2,1,0:T(8,128)(2,1)S(1)}, bf16[2,2,2,64,128]{4,3,2,1,0:T(8,128)(2,1)S(1)}, u32[]{:S(2)}, u32[]{:S(2)}) collective-permute-start(bf16[2,2,2,64,128]{4,3,2,1,0:T(8,128)(2,1)S(1)} %get-tuple-element.42), channel_id=1, source_target_pairs={{0,16},{8,24},{16,0},{24,8},{32,48},{40,56},{48,32},{56,40},{64,80... | collective-permute-start | bytes 393224 | tf_op jit(solution)/shard_map/ppermute | solution.py:184
  23.4 9.2 %collective-permute-start.1 = (bf16[2,2,2,64,128]{4,3,2,1,0:T(8,128)(2,1)S(1)}, bf16[2,2,2,64,128]{4,3,2,1,0:T(8,128)(2,1)S(1)}, u32[]{:S(2)}, u32[]{:S(2)}) collective-permute-start(bf16[2,2,2,64,128]{4,3,2,1,0:T(8,128)(2,1)S(1)} %get-tuple-element.42), channel_id=1, source_target_pairs={{0,8},{8,16},{16,24},{24,0},{32,40},{40,48},{48,56},{56,32},{64,72... | collective-permute-start | bytes 393224 | tf_op jit(solution)/shard_map/ppermute | solution.py:184
  24.0 8.7 %collective-permute-start.4 = (bf16[256,256]{1,0:T(8,128)(2,1)S(1)}, bf16[256,256]{1,0:T(8,128)(2,1)S(1)}, u32[]{:S(2)}, u32[]{:S(2)}) collective-permute-start(bf16[256,256]{1,0:T(8,128)(2,1)S(1)} %get-tuple-element.40), channel_id=1, source_target_pairs={{0,4},{4,8},{8,12},{12,16},{16,20},{20,24},{24,28},{28,32},{32,36}... | collective-permute-start | bytes 393224 | tf_op jit(solution)/shard_map/ppermute | solution.py:18
  28.6 4.2 %collective-permute-start.5 = (bf16[256,256]{1,0:T(8,128)(2,1)S(1)}, bf16[256,256]{1,0:T(8,128)(2,1)S(1)}, u32[]{:S(2)}, u32[]{:S(2)}) collective-permute-start(bf16[256,256]{1,0:T(8,128)(2,1)S(1)} %get-tuple-element.37), channel_id=1, source_target_pairs={{0,4},{4,8},{8,12},{12,16},{16,20},{20,24},{24,28},{28,32},{32,36}... | collective-permute-start | bytes 393224 | tf_op jit(solution)/shard_map/ppermute | solution.py:18
  30.6 33.3 %copy-start.2 = (s32[2,5]{1,0:T(2,128)}, s32[2,5]{1,0:T(2,128)S(1)}, u32[]{:S(2)}) copy-start(s32[2,5]{1,0:T(2,128)S(1)} %concatenate.41.refs_0_) | copy-start | bytes 124
  32.8 29.5 %copy-start.1 = (bf16[64,4,1024]{2,0,1:T(8,128)(2,1)}, bf16[64,4,1024]{2,0,1:T(8,128)(2,1)S(1)}, u32[]{:S(2)}) copy-start(bf16[64,4,1024]{2,0,1:T(8,128)(2,1)S(1)} %all-to-all-done.1) | copy-start | bytes 1572868
  32.8 11.1 %collective-permute-start.8 = (bf16[4,2,2,2,64,128]{5,4,3,2,1,0:T(8,128)(2,1)S(1)}, bf16[4,2,2,2,64,128]{5,4,3,2,1,0:T(8,128)(2,1)}, u32[]{:S(2)}, u32[]{:S(2)}) collective-permute-start(bf16[4,2,2,2,64,128]{5,4,3,2,1,0:T(8,128)(2,1)S(1)} %pad_maximum_fusion.1), channel_id=1, source_target_pairs={{0,96},{8,104},{16,112},{24,120},{32,0},{40,8},{48,16},{56,24},{64... | collective-permute-start | bytes 1572872 | tf_op jit(solution)/shard_map/ppermute | solution.py:184
  35.6 11.6 %collective-permute-start.7 = (bf16[4,2,2,2,64,128]{5,4,3,2,1,0:T(8,128)(2,1)S(1)}, bf16[4,2,2,2,64,128]{5,4,3,2,1,0:T(8,128)(2,1)}, u32[]{:S(2)}, u32[]{:S(2)}) collective-permute-start(bf16[4,2,2,2,64,128]{5,4,3,2,1,0:T(8,128)(2,1)S(1)} %pad_maximum_fusion.1), channel_id=1, source_target_pairs={{0,64},{8,72},{16,80},{24,88},{32,96},{40,104},{48,112},{56,120},{... | collective-permute-start | bytes 1572872 | tf_op jit(solution)/shard_map/ppermute | solution.py:184
  35.9 26.3 %collective-permute-start.6 = (bf16[4,2,2,2,64,128]{5,4,3,2,1,0:T(8,128)(2,1)S(1)}, bf16[4,2,2,2,64,128]{5,4,3,2,1,0:T(8,128)(2,1)}, u32[]{:S(2)}, u32[]{:S(2)}) collective-permute-start(bf16[4,2,2,2,64,128]{5,4,3,2,1,0:T(8,128)(2,1)S(1)} %pad_maximum_fusion.1), channel_id=1, source_target_pairs={{0,32},{8,40},{16,48},{24,56},{32,64},{40,72},{48,80},{56,88},{64,... | collective-permute-start | bytes 1572872 | tf_op jit(solution)/shard_map/ppermute | solution.py:184
  64.9 2.9 %collective-permute-start.9 = (bf16[2,2048,128]{2,1,0:T(8,128)(2,1)S(1)}, bf16[2,2048,128]{2,1,0:T(8,128)(2,1)S(1)}, u32[]{:S(2)}, u32[]{:S(2)}) collective-permute-start(bf16[2,2048,128]{2,1,0:T(8,128)(2,1)S(1)} %bitcast.64), channel_id=1, source_target_pairs={{0,4},{4,0},{1,5},{5,1},{2,6},{6,2},{3,7},{7,3},{8,12},{12,8},{9,1... | collective-permute-start | bytes 3145736 | tf_op jit(solution)/shard_map/ppermute | solution.py:204

commit v13 on v12

--- a/solution.py
+++ b/solution.py
@@ -171,35 +171,45 @@
     sent = jnp.where(core_index == 0, own_v, own_k)[pieces, :, heads_col]
     stage = jnp.stack([mine, lax.ppermute(sent, "core", swap)], 0)
     q_all = lax.all_to_all(queries, "head", split_axis=1, concat_axis=0, tiled=True)
-    for stride in (1, side):
-        moved = [stage]
-        for step in range(1, side):
-            pairs = []
-            for chip in range(chips):
-                row, col = chip // side, chip % side
-                if stride == 1:
-                    pairs.append((chip, row * side + (col + step) % side))
-                else:
-                    pairs.append((chip, ((row + step) % side) * side + col))
-            moved.append(lax.ppermute(stage, "chip", pairs))
-        stage = jnp.stack(moved, 0)
-        if stride == 1:
-            stage, q_all, prev_k, prev_v, diagonal_offsets, local_vert = lax.optimization_barrier(
-                (stage, q_all, prev_k, prev_v, diagonal_offsets, local_vert)
-            )
-            window_k, window_v, ms, mv = side_inputs(
-                prev_k, prev_v, k_all, v_all, diagonal_offsets, local_vert, seq_index, nbd
-            )
-        else:
-            stage, window_k, window_v, ms, mv = lax.optimization_barrier(
-                (stage, window_k, window_v, ms, mv)
-            )
+    def shift(value, stride, step):
+        pairs = []
+        for chip in range(chips):
+            row, col = chip // side, chip % side
+            if stride == 1:
+                pairs.append((chip, row * side + (col + step) % side))
+            else:
+                pairs.append((chip, ((row + step) % side) * side + col))
+        return lax.ppermute(value, "chip", pairs)
+
+    def ring(value, stride):
+        return jnp.stack([value] + [shift(value, stride, s) for s in range(1, side)], 0)
+
+    across = ring(lax.index_in_dim(stage, 0, 1), 1)
+    down = ring(lax.index_in_dim(stage, 1, 1), side)
+    across, down, q_all, prev_k, prev_v, diagonal_offsets, local_vert = lax.optimization_barrier(
+        (across, down, q_all, prev_k, prev_v, diagonal_offsets, local_vert)
+    )
+    window_k, window_v, ms, mv = side_inputs(
+        prev_k, prev_v, k_all, v_all, diagonal_offsets, local_vert, seq_index, nbd
+    )
+    across = ring(across, side)
+    down = ring(down, 1)
+    across, down, window_k, window_v, ms, mv = lax.optimization_barrier(
+        (across, down, window_k, window_v, ms, mv)
+    )
     owner_chip = owner // cores
     owner_core = owner % cores
     dy = (chip_index // side - owner_chip // side) % side
     dx = (chip_index % side - owner_chip % side) % side
     heads_idx = jnp.arange(kv_local)[:, None]
-    part = stage[dy, dx, (owner_core + core_index) % cores, heads_idx, rank]
+    dc = (owner_core + core_index) % cores
+    part = jnp.stack(
+        [
+            across[dy[0], dx[0], dc[0], 0, rank[0]],
+            down[dx[1], dy[1], dc[1], 0, rank[1]],
+        ],
+        0,
+    )
     part = part.reshape(kv_local, listed * BLOCK_TOKENS, HEAD_WIDTH)
     other = lax.ppermute(part, "core", swap)
     vert_keys = jnp.where(core_index == 0, part, other)

time: 83.6 us -> 81.2 us (0.971)
  waiting for transfers between devices: 28.5 us -> 18 us
  starting transfers between devices: 26 us -> 34.9 us
    ppermute x6 -> x12, waiting for transfers between devices: 23.7 us -> 12.2 us  [shift(): return lax.ppermute(value, 'chip', pairs)]
    ppermute x6 -> x12, starting transfers between devices: 7.52 us -> 12.9 us  [shift(): return lax.ppermute(value, 'chip', pairs)]
    ppermute x1, starting transfers between devices: 0.57 us -> 4.44 us  [local(): other = lax.ppermute(part, 'core', swap)]
    all_to_all x1, local copies, waits for them, and re-layouts: 1.88 us -> 0.84 us  [local(): lax.all_to_all(queries, 'head', split_axis=1, concat_axis=0, tiled=True)]
    another operation x3 -> x6, other arithmetic: 1.71 us -> 1.39 us  [the longest x4 1.28 us: ring(): jnp.stack([value] + [shift(value, stride, s) for s in range(1, side)], 0)]
  transfers between devices with their start and end apart: 12 -> 18, of which waited for: 7 -> 8; matrix products, arithmetic and copies ran while one was open for 10% -> 10% of each run, Pallas kernels for 0% -> 0%
where the time goes in v13:
time: 81.2 us; the launch traced here: 80.8 us
  starting transfers between devices  34.9 us (43%)
  waiting for transfers between devices  18 us (22%)
  Pallas kernels  13.9 us (17%)
  other arithmetic  8.08 us (10%)
  local copies, waits for them, and re-layouts  5.64 us (7%)
    pallas_call x1, Pallas kernels, attend(): pl.pallas_call(kernel, grid_spec=grid_spec, out_shape=jax.ShapeDtypeStruc...  13.9 us
    ppermute x12, starting transfers between devices, shift(): return lax.ppermute(value, 'chip', pairs)  12.9 us
    ppermute x12, waiting for transfers between devices, shift(): return lax.ppermute(value, 'chip', pairs)  12.2 us
    ppermute x2, starting transfers between devices, shifted(): return lax.ppermute(value, axis, pairs)  6.11 us
    all_to_all x1, starting transfers between devices, local(): lax.all_to_all(joined, 'head', split_axis=1, concat_axis=0, tiled=True)  5.84 us
    ppermute x1, starting transfers between devices, local(): other = lax.ppermute(part, 'core', swap)  4.44 us
    all_to_all x1, starting transfers between devices, local(): lax.all_to_all(queries, 'head', split_axis=1, concat_axis=0, tiled=True)  3.47 us
    all_to_all x1, waiting for transfers between devices, local(): lax.all_to_all(joined, 'head', split_axis=1, concat_axis=0, tiled=True)  3.27 us
  transfers between devices with their start and end apart: 18, of which 8 were waited for; matrix products, arithmetic and copies ran while one was open for 10% of the time, Pallas kernels for 0%

profile of v13, /device:TPU:1, one launch (start us, length us, event | category | flops | bytes accessed | tf_op | source)
XLA Modules:
  0.0 80.8 jit_solution(818482192075872395)
XLA Ops:
  0.0 1.0 %copy_bitcast_fusion.1 = (bf16[64,4,256]{2,0,1:T(8,128)(2,1)S(1)}, bf16[64,4,256]{2,0,1:T(8,128)(2,1)S(1)}) fusion(bf16[8,4,8,256]{3,2,1,0:T(8,128)(2,1)} %bitcast.133, bf16[8,4,8,256]{3,2,1,0:T(8,128)(2,1)} %bitcast.134), kind=kLoop, calls=%fused_computation.16 | loop fusion | bytes 524288 | tf_op jit(solution)/shard_map/reshape | solution.py:136
  1.0 0.7 pad_maximum_fusion.3
  1.8 5.8 %all-to-all-start = ((bf16[64,4,512]{2,0,1:T(8,128)(2,1)}), bf16[64,4,512]{2,0,1:T(8,128)(2,1)S(1)}, u32[]{:S(2)}, u32[]{:S(2)}) async-start(bf16[64,4,512]{2,0,1:T(8,128)(2,1)} %pad_maximum_fusion.3), calls=%async_computation | async-start | bytes 524288 | tf_op jit(solution)/shard_map/all_to_all | solution.py:138
  7.7 0.1 copy.74
  7.8 0.7 and_select_fusion.3
  8.6 0.2 convert_reduce_fusion
  8.7 0.2 fusion.1
  9.0 0.8 %copy.83 = bf16[8,4,8,1024]{3,2,0,1:T(8,128)(2,1)} copy(bf16[8,4,8,1024]{3,2,1,0:T(8,128)(2,1)S(1)} %bitcast.123) | data formatting | bytes 1048576 | tf_op jit(solution)/shard_map/all_to_all | solution.py:173
  9.9 3.3 %all-to-all-done = bf16[64,4,512]{2,0,1:T(8,128)(2,1)S(1)} async-done(((bf16[64,4,512]{2,0,1:T(8,128)(2,1)}), bf16[64,4,512]{2,0,1:T(8,128)(2,1)S(1)}, u32[]{:S(2)}, u32[]{:S(2)}) %all-to-all-start) | async-done | bytes 262176 | tf_op jit(solution)/shard_map/all_to_all | solution.py:138
  13.2 3.5 %all-to-all-start.1 = ((bf16[64,4,1024]{2,0,1:T(8,128)(2,1)}), bf16[64,4,1024]{2,0,1:T(8,128)(2,1)S(1)}, u32[]{:S(2)}, u32[]{:S(2)}) async-start(bf16[64,4,1024]{2,0,1:T(8,128)(2,1)} %bitcast.112), calls=%async_computation.1 | async-start | bytes 1048576 | tf_op jit(solution)/shard_map/all_to_all | solution.py:173
  16.7 0.6 gather_fusion.1
  17.3 2.2 %collective-permute-start = (bf16[2,2,64,128]{3,2,1,0:T(8,128)(2,1)S(1)}, bf16[2,2,64,128]{3,2,1,0:T(8,128)(2,1)S(1)}, u32[]{:S(2)}, u32[]{:S(2)}) collective-permute-start(bf16[2,2,64,128]{3,2,1,0:T(8,128)(2,1)S(1)} %bitcast.135), channel_id=1, source_target_pairs={{0,4},{4,0},{1,5},{5,1},{2,6},{6,2},{3,7},{7,3},{8,12},{12,8},{9,1... | collective-permute-start | bytes 196616 | tf_op jit(solution)/shard_map/ppermute | solution.py:172
  19.6 0.6 gather_fusion
  20.2 0.2 collective-permute-done
  20.4 3.0 %collective-permute-start.5 = (bf16[2,1,2,64,128]{4,3,2,0,1:T(8,128)(2,1)S(1)}, bf16[2,1,2,64,128]{4,3,2,0,1:T(8,128)(2,1)S(1)}, u32[]{:S(2)}, u32[]{:S(2)}) collective-permute-start(bf16[2,1,2,64,128]{4,3,2,0,1:T(8,128)(2,1)S(1)} %get-tuple-element.45), channel_id=1, source_target_pairs={{0,64},{8,72},{16,80},{24,88},{32,96},{40,104},{48,112},{56,120},{... | collective-permute-start | bytes 196616 | tf_op jit(solution)/shard_map/ppermute | solution.py:182
  23.4 0.4 collective-permute-start.4
  23.8 2.3 %collective-permute-start.6 = (bf16[2,1,2,64,128]{4,3,2,0,1:T(8,128)(2,1)S(1)}, bf16[2,1,2,64,128]{4,3,2,0,1:T(8,128)(2,1)S(1)}, u32[]{:S(2)}, u32[]{:S(2)}) collective-permute-start(bf16[2,1,2,64,128]{4,3,2,0,1:T(8,128)(2,1)S(1)} %get-tuple-element.45), channel_id=1, source_target_pairs={{0,96},{8,104},{16,112},{24,120},{32,0},{40,8},{48,16},{56,24},{64... | collective-permute-start | bytes 196616 | tf_op jit(solution)/shard_map/ppermute | solution.py:182
  26.1 4.2 %collective-permute-start.8 = (bf16[256,256]{1,0:T(8,128)(2,1)S(1)}, bf16[256,256]{1,0:T(8,128)(2,1)S(1)}, u32[]{:S(2)}, u32[]{:S(2)}) collective-permute-start(bf16[256,256]{1,0:T(8,128)(2,1)S(1)} %get-tuple-element.41), channel_id=1, source_target_pairs={{0,4},{4,8},{8,12},{12,16},{16,20},{20,24},{24,28},{28,32},{32,36}... | collective-permute-start | bytes 393224 | tf_op jit(solution)/shard_map/ppermute | solution.py:18
  30.3 1.9 %collective-permute-start.7 = (bf16[256,256]{1,0:T(8,128)(2,1)S(1)}, bf16[256,256]{1,0:T(8,128)(2,1)S(1)}, u32[]{:S(2)}, u32[]{:S(2)}) collective-permute-start(bf16[256,256]{1,0:T(8,128)(2,1)S(1)} %get-tuple-element.44), channel_id=1, source_target_pairs={{0,4},{4,8},{8,12},{12,16},{16,20},{20,24},{24,28},{28,32},{32,36}... | collective-permute-start | bytes 393224 | tf_op jit(solution)/shard_map/ppermute | solution.py:18
  32.2 0.4 collective-permute-start.3
  32.6 2.6 %collective-permute-start.2 = (bf16[2,1,2,64,128]{4,3,2,0,1:T(8,128)(2,1)S(1)}, bf16[2,1,2,64,128]{4,3,2,0,1:T(8,128)(2,1)S(1)}, u32[]{:S(2)}, u32[]{:S(2)}) collective-permute-start(bf16[2,1,2,64,128]{4,3,2,0,1:T(8,128)(2,1)S(1)} %get-tuple-element.46), channel_id=1, source_target_pairs={{0,16},{8,24},{16,0},{24,8},{32,48},{40,56},{48,32},{56,40},{64,80... | collective-permute-start | bytes 196616 | tf_op jit(solution)/shard_map/ppermute | solution.py:182
  35.3 0.3 collective-permute-start.1
  35.6 2.0 %collective-permute-done.2 = bf16[2,1,2,64,128]{4,3,2,0,1:T(8,128)(2,1)S(1)} collective-permute-done((bf16[2,1,2,64,128]{4,3,2,0,1:T(8,128)(2,1)S(1)}, bf16[2,1,2,64,128]{4,3,2,0,1:T(8,128)(2,1)S(1)}, u32[]{:S(2)}, u32[]{:S(2)}) %collective-permute-start.2) | collective-permute-done | bytes 65568 | tf_op jit(solution)/shard_map/ppermute | solution.py:182
  37.7 2.3 %collective-permute-done.1 = bf16[2,1,2,64,128]{4,3,2,0,1:T(8,128)(2,1)S(1)} collective-permute-done((bf16[2,1,2,64,128]{4,3,2,0,1:T(8,128)(2,1)S(1)}, bf16[2,1,2,64,128]{4,3,2,0,1:T(8,128)(2,1)S(1)}, u32[]{:S(2)}, u32[]{:S(2)}) %collective-permute-start.1) | collective-permute-done | bytes 65568 | tf_op jit(solution)/shard_map/ppermute | solution.py:182
  40.2 0.7 collective-permute-start.12
  40.9 2.0 %collective-permute-start.14 = (bf16[4,2,1,2,64,128]{5,4,3,1,2,0:T(8,128)(2,1)S(1)}, bf16[4,2,1,2,64,128]{5,4,3,1,2,0:T(8,128)(2,1)S(1)}, u32[]{:S(2)}, u32[]{:S(2)}) collective-permute-start(bf16[4,2,1,2,64,128]{5,4,3,1,2,0:T(8,128)(2,1)S(1)} %pad_maximum_fusion.5), channel_id=1, source_target_pairs={{0,24},{8,0},{16,8},{24,16},{32,56},{40,32},{48,40},{56,48},{64,88... | collective-permute-start | bytes 786440 | tf_op jit(solution)/shard_map/ppermute | solution.py:182
  42.9 1.0 %collective-permute-start.10 = (bf16[4,2,1,2,64,128]{5,4,3,1,0,2:T(8,128)(2,1)S(1)}, bf16[4,2,1,2,64,128]{5,4,3,1,0,2:T(8,128)(2,1)}, u32[]{:S(2)}, u32[]{:S(2)}) collective-permute-start(bf16[4,2,1,2,64,128]{5,4,3,1,0,2:T(8,128)(2,1)S(1)} %pad_maximum_fusion.4), channel_id=1, source_target_pairs={{0,64},{8,72},{16,80},{24,88},{32,96},{40,104},{48,112},{56,120},{... | collective-permute-start | bytes 786440 | tf_op jit(solution)/shard_map/ppermute | solution.py:182
  44.1 0.1 stack.116
  44.3 0.1 stack.115
  44.7 0.1 broadcast_in_dim.30
  44.8 0.1 stack.118
  45.0 0.1 stack.119
  45.1 0.7 copy_convert_fusion.refs_7_
  45.8 0.6 copy_convert_fusion.1.refs_6_
  46.4 1.4 %collective-permute-done.13 = bf16[4,2,1,2,64,128]{5,4,3,1,0,2:T(8,128)(2,1)S(1)} collective-permute-done((bf16[4,2,1,2,64,128]{5,4,3,1,0,2:T(8,128)(2,1)S(1)}, bf16[4,2,1,2,64,128]{5,4,3,1,0,2:T(8,128)(2,1)S(1)}, u32[]{:S(2)}, u32[]{:S(2)}) %collective-permute-start.13) | collective-permute-done | bytes 262176 | tf_op jit(solution)/shard_map/ppermute | solution.py:182
  47.8 0.7 pad_maximum_fusion.6.refs_2_
  48.6 0.7 pad_maximum_fusion.7.refs_3_
  49.3 5.8 %collective-permute-done.12 = bf16[4,2,1,2,64,128]{5,4,3,1,0,2:T(8,128)(2,1)S(1)} collective-permute-done((bf16[4,2,1,2,64,128]{5,4,3,1,0,2:T(8,128)(2,1)S(1)}, bf16[4,2,1,2,64,128]{5,4,3,1,0,2:T(8,128)(2,1)S(1)}, u32[]{:S(2)}, u32[]{:S(2)}) %collective-permute-start.12) | collective-permute-done | bytes 262176 | tf_op jit(solution)/shard_map/ppermute | solution.py:182
  55.1 0.1 pad_maximum_fusion.1
  55.3 0.6 collective-permute-done.9
  55.9 1.1 %pad_maximum_fusion = bf16[4,4,2,1,2,64,128]{6,5,4,3,2,1,0:T(8,128)(2,1)S(1)} fusion(bf16[1,4,2,1,2,64,128]{6,5,4,3,2,1,0:T(8,128)(2,1)S(1)} %bitcast.128, bf16[1,4,2,1,2,64,128]{6,5,4,3,2,1,0:T(8,128)(2,1)} %bitcast.30, bf16[1,4,2,1,2,64,128]{6,5,4,3,2,1,0:T(8,128)(2,1)S(1)} %bitcast.132, bf16[1,4,2,1,2,64,128]{6,5,4,3,2,1,0:T(8,128)(2,1)S(1)} %bitcast.122), kind=kLoop, calls=%fused_computation.4 | loop fusion | flops 1572864 | bytes 2097152 | tf_op jit(solution)/shard_map/stack | solution.py:185
  57.0 0.7 gather_fusion.2
  57.7 0.7 gather_fusion.3
  58.4 0.1 pad_maximum_fusion.2
  58.5 4.4 %collective-permute-start.15 = (bf16[2,2048,128]{2,1,0:T(8,128)(2,1)S(1)}, bf16[2,2048,128]{2,1,0:T(8,128)(2,1)S(1)}, u32[]{:S(2)}, u32[]{:S(2)}) collective-permute-start(bf16[2,2048,128]{2,1,0:T(8,128)(2,1)S(1)} %pad_maximum_fusion.2), channel_id=1, source_target_pairs={{0,4},{4,0},{1,5},{5,1},{2,6},{6,2},{3,7},{7,3},{8,12},{12,8},{9,1... | collective-permute-start | bytes 3145736 | tf_op jit(solution)/shard_map/ppermute | solution.py:214
  63.0 2.3 %collective-permute-done.15 = bf16[2,2048,128]{2,1,0:T(8,128)(2,1)S(1)} collective-permute-done((bf16[2,2048,128]{2,1,0:T(8,128)(2,1)S(1)}, bf16[2,2048,128]{2,1,0:T(8,128)(2,1)S(1)}, u32[]{:S(2)}, u32[]{:S(2)}) %collective-permute-start.15) | collective-permute-done | bytes 1048608 | tf_op jit(solution)/shard_map/ppermute | solution.py:214
  65.3 1.6 %broadcast_select_fusion = (bf16[2,2048,128]{2,1,0:T(8,128)(2,1)}, bf16[2,2048,128]{2,1,0:T(8,128)(2,1)}) fusion(bf16[2,2048,128]{2,1,0:T(8,128)(2,1)S(1)} %collective-permute-done.15, pred[]{:T(512)S(6)} %eq.73, bf16[1,2048,128]{2,1,0:T(8,128)(2,1)S(1)} %bitcast.116, bf16[1,2048,128]{2,1,0:T(8,128)(2,1)S(1)} %bitcast.114), kind=kLoop, calls=%fused_computation.7 | loop fusion | flops 1572864 | bytes 4194305 | tf_op jit(solution)/shard_map/jit(_where)/select_n | solution.py:216
  66.9 13.9 %shard_map.55 = bf16[256,1024]{1,0:T(8,128)(2,1)} custom-call(s32[2,5]{1,0:T(2,128)} %copy-done.3, bf16[256,1024]{1,0:T(8,128)(2,1)} %bitcast.124, bf16[512,256]{1,0:T(8,128)(2,1)} %pad_maximum_fusion.6.refs_2_, bf16[512,256]{1,0:T(8,128)(2,1)} %pad_maximum_fusion.7.refs_3_, bf16[2,2048,128]{2,1,0:T(8,128)(2,1)} %get-tuple-element.40.refs_4_, ...), custom_call_target="tpu_custom_call" | custom-call | flops 2550136832 | bytes 3670016 | tf_op jit(solution)/shard_map/pallas_call | solution.py:97
  (54 shorter events, 1.4 us)
Async XLA Ops:
  0.0 7.6 %copy-start = (s32[8,4]{0,1:T(4,128)S(1)}, s32[8,4]{0,1:T(4,128)}, u32[]{:S(2)}) copy-start(s32[8,4]{0,1:T(4,128)} %param.8) | copy-start | bytes 388
  1.0 8.0 %copy-start.1 = (bf16[64,4096]{1,0:T(8,128)(2,1)S(1)}, bf16[64,4096]{1,0:T(8,128)(2,1)}, u32[]{:S(2)}) copy-start(bf16[64,4096]{1,0:T(8,128)(2,1)} %param.5) | copy-start | bytes 1572868
  1.8 11.4 %all-to-all-start = ((bf16[64,4,512]{2,0,1:T(8,128)(2,1)}), bf16[64,4,512]{2,0,1:T(8,128)(2,1)S(1)}, u32[]{:S(2)}, u32[]{:S(2)}) async-start(bf16[64,4,512]{2,0,1:T(8,128)(2,1)} %pad_maximum_fusion.3), calls=%async_computation | async-start | bytes 524288 | tf_op jit(solution)/shard_map/all_to_all | solution.py:138
  13.2 26.9 %all-to-all-start.1 = ((bf16[64,4,1024]{2,0,1:T(8,128)(2,1)}), bf16[64,4,1024]{2,0,1:T(8,128)(2,1)S(1)}, u32[]{:S(2)}, u32[]{:S(2)}) async-start(bf16[64,4,1024]{2,0,1:T(8,128)(2,1)} %bitcast.112), calls=%async_computation.1 | async-start | bytes 1048576 | tf_op jit(solution)/shard_map/all_to_all | solution.py:173
  17.3 3.1 %collective-permute-start = (bf16[2,2,64,128]{3,2,1,0:T(8,128)(2,1)S(1)}, bf16[2,2,64,128]{3,2,1,0:T(8,128)(2,1)S(1)}, u32[]{:S(2)}, u32[]{:S(2)}) collective-permute-start(bf16[2,2,64,128]{3,2,1,0:T(8,128)(2,1)S(1)} %bitcast.135), channel_id=1, source_target_pairs={{0,4},{4,0},{1,5},{5,1},{2,6},{6,2},{3,7},{7,3},{8,12},{12,8},{9,1... | collective-permute-start | bytes 196616 | tf_op jit(solution)/shard_map/ppermute | solution.py:172
  19.6 24.4 %copy-start.3 = (s32[2,5]{1,0:T(2,128)}, s32[2,5]{1,0:T(2,128)S(1)}, u32[]{:S(2)}) copy-start(s32[2,5]{1,0:T(2,128)S(1)} %concatenate.45.refs_0_) | copy-start | bytes 124
  20.4 11.8 %collective-permute-start.5 = (bf16[2,1,2,64,128]{4,3,2,0,1:T(8,128)(2,1)S(1)}, bf16[2,1,2,64,128]{4,3,2,0,1:T(8,128)(2,1)S(1)}, u32[]{:S(2)}, u32[]{:S(2)}) collective-permute-start(bf16[2,1,2,64,128]{4,3,2,0,1:T(8,128)(2,1)S(1)} %get-tuple-element.45), channel_id=1, source_target_pairs={{0,64},{8,72},{16,80},{24,88},{32,96},{40,104},{48,112},{56,120},{... | collective-permute-start | bytes 196616 | tf_op jit(solution)/shard_map/ppermute | solution.py:182
  23.4 9.3 %collective-permute-start.4 = (bf16[2,1,2,64,128]{4,3,2,0,1:T(8,128)(2,1)S(1)}, bf16[2,1,2,64,128]{4,3,2,0,1:T(8,128)(2,1)S(1)}, u32[]{:S(2)}, u32[]{:S(2)}) collective-permute-start(bf16[2,1,2,64,128]{4,3,2,0,1:T(8,128)(2,1)S(1)} %get-tuple-element.45), channel_id=1, source_target_pairs={{0,32},{8,40},{16,48},{24,56},{32,64},{40,72},{48,80},{56,88},{64,... | collective-permute-start | bytes 196616 | tf_op jit(solution)/shard_map/ppermute | solution.py:182
  23.8 11.5 %collective-permute-start.6 = (bf16[2,1,2,64,128]{4,3,2,0,1:T(8,128)(2,1)S(1)}, bf16[2,1,2,64,128]{4,3,2,0,1:T(8,128)(2,1)S(1)}, u32[]{:S(2)}, u32[]{:S(2)}) collective-permute-start(bf16[2,1,2,64,128]{4,3,2,0,1:T(8,128)(2,1)S(1)} %get-tuple-element.45), channel_id=1, source_target_pairs={{0,96},{8,104},{16,112},{24,120},{32,0},{40,8},{48,16},{56,24},{64... | collective-permute-start | bytes 196616 | tf_op jit(solution)/shard_map/ppermute | solution.py:182
  26.1 14.0 %collective-permute-start.8 = (bf16[256,256]{1,0:T(8,128)(2,1)S(1)}, bf16[256,256]{1,0:T(8,128)(2,1)S(1)}, u32[]{:S(2)}, u32[]{:S(2)}) collective-permute-start(bf16[256,256]{1,0:T(8,128)(2,1)S(1)} %get-tuple-element.41), channel_id=1, source_target_pairs={{0,4},{4,8},{8,12},{12,16},{16,20},{20,24},{24,28},{28,32},{32,36}... | collective-permute-start | bytes 393224 | tf_op jit(solution)/shard_map/ppermute | solution.py:18
  30.3 9.8 %collective-permute-start.7 = (bf16[256,256]{1,0:T(8,128)(2,1)S(1)}, bf16[256,256]{1,0:T(8,128)(2,1)S(1)}, u32[]{:S(2)}, u32[]{:S(2)}) collective-permute-start(bf16[256,256]{1,0:T(8,128)(2,1)S(1)} %get-tuple-element.44), channel_id=1, source_target_pairs={{0,4},{4,8},{8,12},{12,16},{16,20},{20,24},{24,28},{28,32},{32,36}... | collective-permute-start | bytes 393224 | tf_op jit(solution)/shard_map/ppermute | solution.py:18
  32.2 3.4 %collective-permute-start.3 = (bf16[2,1,2,64,128]{4,3,2,0,1:T(8,128)(2,1)S(1)}, bf16[2,1,2,64,128]{4,3,2,0,1:T(8,128)(2,1)S(1)}, u32[]{:S(2)}, u32[]{:S(2)}) collective-permute-start(bf16[2,1,2,64,128]{4,3,2,0,1:T(8,128)(2,1)S(1)} %get-tuple-element.46), channel_id=1, source_target_pairs={{0,24},{8,0},{16,8},{24,16},{32,56},{40,32},{48,40},{56,48},{64,88... | collective-permute-start | bytes 196616 | tf_op jit(solution)/shard_map/ppermute | solution.py:182
  32.6 5.0 %collective-permute-start.2 = (bf16[2,1,2,64,128]{4,3,2,0,1:T(8,128)(2,1)S(1)}, bf16[2,1,2,64,128]{4,3,2,0,1:T(8,128)(2,1)S(1)}, u32[]{:S(2)}, u32[]{:S(2)}) collective-permute-start(bf16[2,1,2,64,128]{4,3,2,0,1:T(8,128)(2,1)S(1)} %get-tuple-element.46), channel_id=1, source_target_pairs={{0,16},{8,24},{16,0},{24,8},{32,48},{40,56},{48,32},{56,40},{64,80... | collective-permute-start | bytes 196616 | tf_op jit(solution)/shard_map/ppermute | solution.py:182
  35.3 4.7 %collective-permute-start.1 = (bf16[2,1,2,64,128]{4,3,2,0,1:T(8,128)(2,1)S(1)}, bf16[2,1,2,64,128]{4,3,2,0,1:T(8,128)(2,1)S(1)}, u32[]{:S(2)}, u32[]{:S(2)}) collective-permute-start(bf16[2,1,2,64,128]{4,3,2,0,1:T(8,128)(2,1)S(1)} %get-tuple-element.46), channel_id=1, source_target_pairs={{0,8},{8,16},{16,24},{24,0},{32,40},{40,48},{48,56},{56,32},{64,72... | collective-permute-start | bytes 196616 | tf_op jit(solution)/shard_map/ppermute | solution.py:182
  40.1 9.2 %copy-start.2 = (bf16[64,4,1024]{2,0,1:T(8,128)(2,1)}, bf16[64,4,1024]{2,0,1:T(8,128)(2,1)S(1)}, u32[]{:S(2)}) copy-start(bf16[64,4,1024]{2,0,1:T(8,128)(2,1)S(1)} %all-to-all-done.1) | copy-start | bytes 1572868
  40.1 7.7 %collective-permute-start.13 = (bf16[4,2,1,2,64,128]{5,4,3,1,0,2:T(8,128)(2,1)S(1)}, bf16[4,2,1,2,64,128]{5,4,3,1,0,2:T(8,128)(2,1)S(1)}, u32[]{:S(2)}, u32[]{:S(2)}) collective-permute-start(bf16[4,2,1,2,64,128]{5,4,3,1,0,2:T(8,128)(2,1)S(1)} %bitcast.119), channel_id=1, source_target_pairs={{0,16},{8,24},{16,0},{24,8},{32,48},{40,56},{48,32},{56,40},{64,80... | collective-permute-start | bytes 786440 | tf_op jit(solution)/shard_map/ppermute | solution.py:182
  40.2 14.9 %collective-permute-start.12 = (bf16[4,2,1,2,64,128]{5,4,3,1,0,2:T(8,128)(2,1)S(1)}, bf16[4,2,1,2,64,128]{5,4,3,1,0,2:T(8,128)(2,1)S(1)}, u32[]{:S(2)}, u32[]{:S(2)}) collective-permute-start(bf16[4,2,1,2,64,128]{5,4,3,1,0,2:T(8,128)(2,1)S(1)} %bitcast.120), channel_id=1, source_target_pairs={{0,8},{8,16},{16,24},{24,0},{32,40},{40,48},{48,56},{56,32},{64,72... | collective-permute-start | bytes 786440 | tf_op jit(solution)/shard_map/ppermute | solution.py:182
  40.9 14.2 %collective-permute-start.14 = (bf16[4,2,1,2,64,128]{5,4,3,1,2,0:T(8,128)(2,1)S(1)}, bf16[4,2,1,2,64,128]{5,4,3,1,2,0:T(8,128)(2,1)S(1)}, u32[]{:S(2)}, u32[]{:S(2)}) collective-permute-start(bf16[4,2,1,2,64,128]{5,4,3,1,2,0:T(8,128)(2,1)S(1)} %pad_maximum_fusion.5), channel_id=1, source_target_pairs={{0,24},{8,0},{16,8},{24,16},{32,56},{40,32},{48,40},{56,48},{64,88... | collective-permute-start | bytes 786440 | tf_op jit(solution)/shard_map/ppermute | solution.py:182
  42.9 12.3 %collective-permute-start.11 = (bf16[4,2,1,2,64,128]{5,4,3,1,0,2:T(8,128)(2,1)S(1)}, bf16[4,2,1,2,64,128]{5,4,3,1,0,2:T(8,128)(2,1)S(1)}, u32[]{:S(2)}, u32[]{:S(2)}) collective-permute-start(bf16[4,2,1,2,64,128]{5,4,3,1,0,2:T(8,128)(2,1)S(1)} %pad_maximum_fusion.4), channel_id=1, source_target_pairs={{0,96},{8,104},{16,112},{24,120},{32,0},{40,8},{48,16},{56,24},{64... | collective-permute-start | bytes 786440 | tf_op jit(solution)/shard_map/ppermute | solution.py:182
  42.9 12.3 %collective-permute-start.10 = (bf16[4,2,1,2,64,128]{5,4,3,1,0,2:T(8,128)(2,1)S(1)}, bf16[4,2,1,2,64,128]{5,4,3,1,0,2:T(8,128)(2,1)}, u32[]{:S(2)}, u32[]{:S(2)}) collective-permute-start(bf16[4,2,1,2,64,128]{5,4,3,1,0,2:T(8,128)(2,1)S(1)} %pad_maximum_fusion.4), channel_id=1, source_target_pairs={{0,64},{8,72},{16,80},{24,88},{32,96},{40,104},{48,112},{56,120},{... | collective-permute-start | bytes 786440 | tf_op jit(solution)/shard_map/ppermute | solution.py:182
  47.8 8.0 %collective-permute-start.9 = (bf16[4,2,1,2,64,128]{5,4,3,1,0,2:T(8,128)(2,1)S(1)}, bf16[4,2,1,2,64,128]{5,4,3,1,0,2:T(8,128)(2,1)S(1)}, u32[]{:S(2)}, u32[]{:S(2)}) collective-permute-start(bf16[4,2,1,2,64,128]{5,4,3,1,0,2:T(8,128)(2,1)S(1)} %pad_maximum_fusion.4), channel_id=1, source_target_pairs={{0,32},{8,40},{16,48},{24,56},{32,64},{40,72},{48,80},{56,88},{64,... | collective-permute-start | bytes 786440 | tf_op jit(solution)/shard_map/ppermute | solution.py:182
  58.5 6.7 %collective-permute-start.15 = (bf16[2,2048,128]{2,1,0:T(8,128)(2,1)S(1)}, bf16[2,2048,128]{2,1,0:T(8,128)(2,1)S(1)}, u32[]{:S(2)}, u32[]{:S(2)}) collective-permute-start(bf16[2,2048,128]{2,1,0:T(8,128)(2,1)S(1)} %pad_maximum_fusion.2), channel_id=1, source_target_pairs={{0,4},{4,0},{1,5},{5,1},{2,6},{6,2},{3,7},{7,3},{8,12},{12,8},{9,1... | collective-permute-start | bytes 3145736 | tf_op jit(solution)/shard_map/ppermute | solution.py:214

commit v14 on v13

--- a/solution.py
+++ b/solution.py
@@ -170,7 +170,6 @@
     mine = jnp.where(core_index == 0, own_k, own_v)[pieces, :, heads_col]
     sent = jnp.where(core_index == 0, own_v, own_k)[pieces, :, heads_col]
     stage = jnp.stack([mine, lax.ppermute(sent, "core", swap)], 0)
-    q_all = lax.all_to_all(queries, "head", split_axis=1, concat_axis=0, tiled=True)
     def shift(value, stride, step):
         pairs = []
         for chip in range(chips):
@@ -186,16 +185,17 @@
 
     across = ring(lax.index_in_dim(stage, 0, 1), 1)
     down = ring(lax.index_in_dim(stage, 1, 1), side)
-    across, down, q_all, prev_k, prev_v, diagonal_offsets, local_vert = lax.optimization_barrier(
-        (across, down, q_all, prev_k, prev_v, diagonal_offsets, local_vert)
-    )
+    across, down, queries, prev_k, prev_v, diagonal_offsets, local_vert = lax.optimization_barrier(
+        (across, down, queries, prev_k, prev_v, diagonal_offsets, local_vert)
+    )
+    q_all = lax.all_to_all(queries, "head", split_axis=1, concat_axis=0, tiled=True)
     window_k, window_v, ms, mv = side_inputs(
         prev_k, prev_v, k_all, v_all, diagonal_offsets, local_vert, seq_index, nbd
     )
     across = ring(across, side)
     down = ring(down, 1)
-    across, down, window_k, window_v, ms, mv = lax.optimization_barrier(
-        (across, down, window_k, window_v, ms, mv)
+    across, down, window_k, window_v, ms, mv, q_all = lax.optimization_barrier(
+        (across, down, window_k, window_v, ms, mv, q_all)
     )
     owner_chip = owner // cores
     owner_core = owner % cores

time: 81.2 us -> 82.7 us (1.018)
  starting transfers between devices: 34.9 us -> 37.2 us
    ppermute x12, waiting for transfers between devices: 12.2 us -> 7.21 us  [shift(): return lax.ppermute(value, 'chip', pairs)]
    all_to_all x1, waiting for transfers between devices: 0.01 us -> 3.5 us  [local(): lax.all_to_all(queries, 'head', split_axis=1, concat_axis=0, tiled=True)]
    ppermute x1, starting transfers between devices: 4.44 us -> 6.04 us  [local(): other = lax.ppermute(part, 'core', swap)]
    all_to_all x1, waiting for transfers between devices: 3.27 us -> 4.11 us  [local(): lax.all_to_all(joined, 'head', split_axis=1, concat_axis=0, tiled=True)]
  transfers between devices with their start and end apart: 18 -> 18, of which waited for: 8 -> 9; matrix products, arithmetic and copies ran while one was open for 10% -> 10% of each run, Pallas kernels for 0% -> 0%
where the time goes in v14:
time: 82.7 us; the launch traced here: 82.4 us
  starting transfers between devices  37.2 us (45%)
  waiting for transfers between devices  17.3 us (21%)
  Pallas kernels  13.9 us (17%)
  other arithmetic  7.94 us (10%)
  local copies, waits for them, and re-layouts  5.72 us (7%)
    pallas_call x1, Pallas kernels, attend(): pl.pallas_call(kernel, grid_spec=grid_spec, out_shape=jax.ShapeDtypeStruc...  13.9 us
    ppermute x12, starting transfers between devices, shift(): return lax.ppermute(value, 'chip', pairs)  12.9 us
    ppermute x12, waiting for transfers between devices, shift(): return lax.ppermute(value, 'chip', pairs)  7.21 us
    ppermute x2, starting transfers between devices, shifted(): return lax.ppermute(value, axis, pairs)  6.11 us
    ppermute x1, starting transfers between devices, local(): other = lax.ppermute(part, 'core', swap)  6.04 us
    all_to_all x1, starting transfers between devices, local(): lax.all_to_all(joined, 'head', split_axis=1, concat_axis=0, tiled=True)  5.84 us
    all_to_all x1, starting transfers between devices, local(): lax.all_to_all(queries, 'head', split_axis=1, concat_axis=0, tiled=True)  4.15 us
    all_to_all x1, waiting for transfers between devices, local(): lax.all_to_all(joined, 'head', split_axis=1, concat_axis=0, tiled=True)  4.11 us
  transfers between devices with their start and end apart: 18, of which 9 were waited for; matrix products, arithmetic and copies ran while one was open for 10% of the time, Pallas kernels for 0%

profile of v14, /device:TPU:1, one launch (start us, length us, event | category | flops | bytes accessed | tf_op | source)
XLA Modules:
  0.0 82.4 jit_solution(16446456459969518086)
XLA Ops:
  0.0 1.0 %copy_bitcast_fusion.1 = (bf16[64,4,256]{2,0,1:T(8,128)(2,1)S(1)}, bf16[64,4,256]{2,0,1:T(8,128)(2,1)S(1)}) fusion(bf16[8,4,8,256]{3,2,1,0:T(8,128)(2,1)} %bitcast.133, bf16[8,4,8,256]{3,2,1,0:T(8,128)(2,1)} %bitcast.134), kind=kLoop, calls=%fused_computation.16 | loop fusion | bytes 524288 | tf_op jit(solution)/shard_map/reshape | solution.py:136
  1.0 0.7 pad_maximum_fusion.3
  1.7 5.8 %all-to-all-start = ((bf16[64,4,512]{2,0,1:T(8,128)(2,1)}), bf16[64,4,512]{2,0,1:T(8,128)(2,1)S(1)}, u32[]{:S(2)}, u32[]{:S(2)}) async-start(bf16[64,4,512]{2,0,1:T(8,128)(2,1)} %pad_maximum_fusion.3), calls=%async_computation | async-start | bytes 524288 | tf_op jit(solution)/shard_map/all_to_all | solution.py:138
  7.7 0.1 copy.74
  7.8 0.7 and_select_fusion.3
  8.5 0.2 convert_reduce_fusion
  8.7 0.2 fusion.1
  9.0 4.1 %all-to-all-done = bf16[64,4,512]{2,0,1:T(8,128)(2,1)S(1)} async-done(((bf16[64,4,512]{2,0,1:T(8,128)(2,1)}), bf16[64,4,512]{2,0,1:T(8,128)(2,1)S(1)}, u32[]{:S(2)}, u32[]{:S(2)}) %all-to-all-start) | async-done | bytes 262176 | tf_op jit(solution)/shard_map/all_to_all | solution.py:138
  13.2 0.6 gather_fusion.1
  13.8 2.2 %collective-permute-start = (bf16[2,2,64,128]{3,2,1,0:T(8,128)(2,1)S(1)}, bf16[2,2,64,128]{3,2,1,0:T(8,128)(2,1)S(1)}, u32[]{:S(2)}, u32[]{:S(2)}) collective-permute-start(bf16[2,2,64,128]{3,2,1,0:T(8,128)(2,1)S(1)} %bitcast.135), channel_id=1, source_target_pairs={{0,4},{4,0},{1,5},{5,1},{2,6},{6,2},{3,7},{7,3},{8,12},{12,8},{9,1... | collective-permute-start | bytes 196616 | tf_op jit(solution)/shard_map/ppermute | solution.py:172
  16.1 0.6 gather_fusion
  16.7 0.2 collective-permute-done
  16.9 3.0 %collective-permute-start.5 = (bf16[2,1,2,64,128]{4,3,2,0,1:T(8,128)(2,1)S(1)}, bf16[2,1,2,64,128]{4,3,2,0,1:T(8,128)(2,1)S(1)}, u32[]{:S(2)}, u32[]{:S(2)}) collective-permute-start(bf16[2,1,2,64,128]{4,3,2,0,1:T(8,128)(2,1)S(1)} %get-tuple-element.47), channel_id=1, source_target_pairs={{0,64},{8,72},{16,80},{24,88},{32,96},{40,104},{48,112},{56,120},{... | collective-permute-start | bytes 196616 | tf_op jit(solution)/shard_map/ppermute | solution.py:181
  19.9 0.4 collective-permute-start.4
  20.3 2.3 %collective-permute-start.6 = (bf16[2,1,2,64,128]{4,3,2,0,1:T(8,128)(2,1)S(1)}, bf16[2,1,2,64,128]{4,3,2,0,1:T(8,128)(2,1)S(1)}, u32[]{:S(2)}, u32[]{:S(2)}) collective-permute-start(bf16[2,1,2,64,128]{4,3,2,0,1:T(8,128)(2,1)S(1)} %get-tuple-element.47), channel_id=1, source_target_pairs={{0,96},{8,104},{16,112},{24,120},{32,0},{40,8},{48,16},{56,24},{64... | collective-permute-start | bytes 196616 | tf_op jit(solution)/shard_map/ppermute | solution.py:181
  22.6 4.2 %collective-permute-start.8 = (bf16[256,256]{1,0:T(8,128)(2,1)S(1)}, bf16[256,256]{1,0:T(8,128)(2,1)S(1)}, u32[]{:S(2)}, u32[]{:S(2)}) collective-permute-start(bf16[256,256]{1,0:T(8,128)(2,1)S(1)} %get-tuple-element.43), channel_id=1, source_target_pairs={{0,4},{4,8},{8,12},{12,16},{16,20},{20,24},{24,28},{28,32},{32,36}... | collective-permute-start | bytes 393224 | tf_op jit(solution)/shard_map/ppermute | solution.py:18
  26.8 1.9 %collective-permute-start.7 = (bf16[256,256]{1,0:T(8,128)(2,1)S(1)}, bf16[256,256]{1,0:T(8,128)(2,1)S(1)}, u32[]{:S(2)}, u32[]{:S(2)}) collective-permute-start(bf16[256,256]{1,0:T(8,128)(2,1)S(1)} %get-tuple-element.46), channel_id=1, source_target_pairs={{0,4},{4,8},{8,12},{12,16},{16,20},{20,24},{24,28},{28,32},{32,36}... | collective-permute-start | bytes 393224 | tf_op jit(solution)/shard_map/ppermute | solution.py:18
  28.7 0.4 collective-permute-start.3
  29.1 2.6 %collective-permute-start.2 = (bf16[2,1,2,64,128]{4,3,2,0,1:T(8,128)(2,1)S(1)}, bf16[2,1,2,64,128]{4,3,2,0,1:T(8,128)(2,1)S(1)}, u32[]{:S(2)}, u32[]{:S(2)}) collective-permute-start(bf16[2,1,2,64,128]{4,3,2,0,1:T(8,128)(2,1)S(1)} %get-tuple-element.48), channel_id=1, source_target_pairs={{0,16},{8,24},{16,0},{24,8},{32,48},{40,56},{48,32},{56,40},{64,80... | collective-permute-start | bytes 196616 | tf_op jit(solution)/shard_map/ppermute | solution.py:181
  31.8 0.3 collective-permute-start.1
  32.1 2.0 %collective-permute-done.2 = bf16[2,1,2,64,128]{4,3,2,0,1:T(8,128)(2,1)S(1)} collective-permute-done((bf16[2,1,2,64,128]{4,3,2,0,1:T(8,128)(2,1)S(1)}, bf16[2,1,2,64,128]{4,3,2,0,1:T(8,128)(2,1)S(1)}, u32[]{:S(2)}, u32[]{:S(2)}) %collective-permute-start.2) | collective-permute-done | bytes 65568 | tf_op jit(solution)/shard_map/ppermute | solution.py:181
  34.2 2.3 %collective-permute-done.1 = bf16[2,1,2,64,128]{4,3,2,0,1:T(8,128)(2,1)S(1)} collective-permute-done((bf16[2,1,2,64,128]{4,3,2,0,1:T(8,128)(2,1)S(1)}, bf16[2,1,2,64,128]{4,3,2,0,1:T(8,128)(2,1)S(1)}, u32[]{:S(2)}, u32[]{:S(2)}) %collective-permute-start.1) | collective-permute-done | bytes 65568 | tf_op jit(solution)/shard_map/ppermute | solution.py:181
  36.7 0.7 collective-permute-start.12
  37.4 2.0 %collective-permute-start.14 = (bf16[4,2,1,2,64,128]{5,4,3,1,2,0:T(8,128)(2,1)S(1)}, bf16[4,2,1,2,64,128]{5,4,3,1,2,0:T(8,128)(2,1)S(1)}, u32[]{:S(2)}, u32[]{:S(2)}) collective-permute-start(bf16[4,2,1,2,64,128]{5,4,3,1,2,0:T(8,128)(2,1)S(1)} %pad_maximum_fusion.5), channel_id=1, source_target_pairs={{0,24},{8,0},{16,8},{24,16},{32,56},{40,32},{48,40},{56,48},{64,88... | collective-permute-start | bytes 786440 | tf_op jit(solution)/shard_map/ppermute | solution.py:181
  39.4 1.0 %collective-permute-start.10 = (bf16[4,2,1,2,64,128]{5,4,3,1,0,2:T(8,128)(2,1)S(1)}, bf16[4,2,1,2,64,128]{5,4,3,1,0,2:T(8,128)(2,1)S(1)}, u32[]{:S(2)}, u32[]{:S(2)}) collective-permute-start(bf16[4,2,1,2,64,128]{5,4,3,1,0,2:T(8,128)(2,1)S(1)} %pad_maximum_fusion.4), channel_id=1, source_target_pairs={{0,64},{8,72},{16,80},{24,88},{32,96},{40,104},{48,112},{56,120},{... | collective-permute-start | bytes 786440 | tf_op jit(solution)/shard_map/ppermute | solution.py:181
  40.6 0.1 stack.116
  41.3 0.1 stack.118
  41.5 0.1 stack.119
  41.6 0.7 copy_convert_fusion.refs_7_
  42.3 0.6 copy_convert_fusion.1.refs_6_
  42.9 1.4 %collective-permute-done.13 = bf16[4,2,1,2,64,128]{5,4,3,1,0,2:T(8,128)(2,1)S(1)} collective-permute-done((bf16[4,2,1,2,64,128]{5,4,3,1,0,2:T(8,128)(2,1)S(1)}, bf16[4,2,1,2,64,128]{5,4,3,1,0,2:T(8,128)(2,1)S(1)}, u32[]{:S(2)}, u32[]{:S(2)}) %collective-permute-start.13) | collective-permute-done | bytes 262176 | tf_op jit(solution)/shard_map/ppermute | solution.py:181
  44.3 0.7 pad_maximum_fusion.6.refs_2_
  45.1 0.8 %copy.83 = bf16[8,4,8,1024]{3,2,0,1:T(8,128)(2,1)} copy(bf16[8,4,8,1024]{3,2,1,0:T(8,128)(2,1)S(1)} %bitcast.123) | data formatting | bytes 1048576 | tf_op jit(solution)/shard_map/all_to_all | solution.py:191
  45.9 4.2 %all-to-all-start.1 = ((bf16[64,4,1024]{2,0,1:T(8,128)(2,1)}), bf16[64,4,1024]{2,0,1:T(8,128)(2,1)}, u32[]{:S(2)}, u32[]{:S(2)}) async-start(bf16[64,4,1024]{2,0,1:T(8,128)(2,1)} %bitcast.112), calls=%async_computation.1 | async-start | bytes 1048576 | tf_op jit(solution)/shard_map/all_to_all | solution.py:191
  50.1 0.7 pad_maximum_fusion.7.refs_3_
  50.8 0.8 collective-permute-done.12
  51.6 0.1 pad_maximum_fusion.1
  51.8 0.6 collective-permute-done.9
  52.4 0.1 copy-done.2
  52.5 1.1 %pad_maximum_fusion = bf16[4,4,2,1,2,64,128]{6,5,4,3,2,1,0:T(8,128)(2,1)S(1)} fusion(bf16[1,4,2,1,2,64,128]{6,5,4,3,2,1,0:T(8,128)(2,1)S(1)} %bitcast.127, bf16[1,4,2,1,2,64,128]{6,5,4,3,2,1,0:T(8,128)(2,1)} %bitcast.129, bf16[1,4,2,1,2,64,128]{6,5,4,3,2,1,0:T(8,128)(2,1)S(1)} %bitcast.132, bf16[1,4,2,1,2,64,128]{6,5,4,3,2,1,0:T(8,128)(2,1)S(1)} %bitcast.122), kind=kLoop, calls=%fused_computation.4 | loop fusion | flops 1572864 | bytes 2097152 | tf_op jit(solution)/shard_map/stack | solution.py:184
  53.5 3.5 %all-to-all-done.1 = bf16[64,4,1024]{2,0,1:T(8,128)(2,1)} async-done(((bf16[64,4,1024]{2,0,1:T(8,128)(2,1)}), bf16[64,4,1024]{2,0,1:T(8,128)(2,1)}, u32[]{:S(2)}, u32[]{:S(2)}) %all-to-all-start.1) | async-done | bytes 524320 | tf_op jit(solution)/shard_map/all_to_all | solution.py:191
  57.0 0.7 gather_fusion.2
  57.8 0.7 gather_fusion.3
  58.5 0.1 pad_maximum_fusion.2
  58.6 6.0 %collective-permute-start.15 = (bf16[2,2048,128]{2,1,0:T(8,128)(2,1)S(1)}, bf16[2,2048,128]{2,1,0:T(8,128)(2,1)S(1)}, u32[]{:S(2)}, u32[]{:S(2)}) collective-permute-start(bf16[2,2048,128]{2,1,0:T(8,128)(2,1)S(1)} %pad_maximum_fusion.2), channel_id=1, source_target_pairs={{0,4},{4,0},{1,5},{5,1},{2,6},{6,2},{3,7},{7,3},{8,12},{12,8},{9,1... | collective-permute-start | bytes 3145736 | tf_op jit(solution)/shard_map/ppermute | solution.py:214
  64.7 2.3 %collective-permute-done.15 = bf16[2,2048,128]{2,1,0:T(8,128)(2,1)S(1)} collective-permute-done((bf16[2,2048,128]{2,1,0:T(8,128)(2,1)S(1)}, bf16[2,2048,128]{2,1,0:T(8,128)(2,1)S(1)}, u32[]{:S(2)}, u32[]{:S(2)}) %collective-permute-start.15) | collective-permute-done | bytes 1048608 | tf_op jit(solution)/shard_map/ppermute | solution.py:214
  67.0 1.5 %broadcast_select_fusion = (bf16[2,2048,128]{2,1,0:T(8,128)(2,1)}, bf16[2,2048,128]{2,1,0:T(8,128)(2,1)}) fusion(bf16[2,2048,128]{2,1,0:T(8,128)(2,1)S(1)} %collective-permute-done.15, pred[]{:T(512)S(6)} %eq.73, bf16[1,2048,128]{2,1,0:T(8,128)(2,1)S(1)} %bitcast.116, bf16[1,2048,128]{2,1,0:T(8,128)(2,1)S(1)} %bitcast.114), kind=kLoop, calls=%fused_computation.7 | loop fusion | flops 1572864 | bytes 4194305 | tf_op jit(solution)/shard_map/jit(_where)/select_n | solution.py:216
  68.4 13.9 %shard_map.55 = bf16[256,1024]{1,0:T(8,128)(2,1)} custom-call(s32[2,5]{1,0:T(2,128)} %copy-done.3, bf16[256,1024]{1,0:T(8,128)(2,1)} %bitcast.40.refs_1_, bf16[512,256]{1,0:T(8,128)(2,1)} %pad_maximum_fusion.6.refs_2_, bf16[512,256]{1,0:T(8,128)(2,1)} %pad_maximum_fusion.7.refs_3_, bf16[2,2048,128]{2,1,0:T(8,128)(2,1)} %get-tuple-element.42.refs_4_, ...), custom_call_target="tpu_custom_call" | custom-call | flops 2550136832 | bytes 3670016 | tf_op jit(solution)/shard_map/pallas_call | solution.py:97
  (54 shorter events, 1.5 us)
Async XLA Ops:
  0.0 7.6 %copy-start = (s32[8,4]{0,1:T(4,128)S(1)}, s32[8,4]{0,1:T(4,128)}, u32[]{:S(2)}) copy-start(s32[8,4]{0,1:T(4,128)} %param.8) | copy-start | bytes 388
  1.7 11.4 %all-to-all-start = ((bf16[64,4,512]{2,0,1:T(8,128)(2,1)}), bf16[64,4,512]{2,0,1:T(8,128)(2,1)S(1)}, u32[]{:S(2)}, u32[]{:S(2)}) async-start(bf16[64,4,512]{2,0,1:T(8,128)(2,1)} %pad_maximum_fusion.3), calls=%async_computation | async-start | bytes 524288 | tf_op jit(solution)/shard_map/all_to_all | solution.py:138
  13.8 3.1 %collective-permute-start = (bf16[2,2,64,128]{3,2,1,0:T(8,128)(2,1)S(1)}, bf16[2,2,64,128]{3,2,1,0:T(8,128)(2,1)S(1)}, u32[]{:S(2)}, u32[]{:S(2)}) collective-permute-start(bf16[2,2,64,128]{3,2,1,0:T(8,128)(2,1)S(1)} %bitcast.135), channel_id=1, source_target_pairs={{0,4},{4,0},{1,5},{5,1},{2,6},{6,2},{3,7},{7,3},{8,12},{12,8},{9,1... | collective-permute-start | bytes 196616 | tf_op jit(solution)/shard_map/ppermute | solution.py:172
  16.0 24.4 %copy-start.3 = (s32[2,5]{1,0:T(2,128)}, s32[2,5]{1,0:T(2,128)S(1)}, u32[]{:S(2)}) copy-start(s32[2,5]{1,0:T(2,128)S(1)} %concatenate.45.refs_0_) | copy-start | bytes 124
  16.9 11.8 %collective-permute-start.5 = (bf16[2,1,2,64,128]{4,3,2,0,1:T(8,128)(2,1)S(1)}, bf16[2,1,2,64,128]{4,3,2,0,1:T(8,128)(2,1)S(1)}, u32[]{:S(2)}, u32[]{:S(2)}) collective-permute-start(bf16[2,1,2,64,128]{4,3,2,0,1:T(8,128)(2,1)S(1)} %get-tuple-element.47), channel_id=1, source_target_pairs={{0,64},{8,72},{16,80},{24,88},{32,96},{40,104},{48,112},{56,120},{... | collective-permute-start | bytes 196616 | tf_op jit(solution)/shard_map/ppermute | solution.py:181
  19.9 9.3 %collective-permute-start.4 = (bf16[2,1,2,64,128]{4,3,2,0,1:T(8,128)(2,1)S(1)}, bf16[2,1,2,64,128]{4,3,2,0,1:T(8,128)(2,1)S(1)}, u32[]{:S(2)}, u32[]{:S(2)}) collective-permute-start(bf16[2,1,2,64,128]{4,3,2,0,1:T(8,128)(2,1)S(1)} %get-tuple-element.47), channel_id=1, source_target_pairs={{0,32},{8,40},{16,48},{24,56},{32,64},{40,72},{48,80},{56,88},{64,... | collective-permute-start | bytes 196616 | tf_op jit(solution)/shard_map/ppermute | solution.py:181
  20.3 11.5 %collective-permute-start.6 = (bf16[2,1,2,64,128]{4,3,2,0,1:T(8,128)(2,1)S(1)}, bf16[2,1,2,64,128]{4,3,2,0,1:T(8,128)(2,1)S(1)}, u32[]{:S(2)}, u32[]{:S(2)}) collective-permute-start(bf16[2,1,2,64,128]{4,3,2,0,1:T(8,128)(2,1)S(1)} %get-tuple-element.47), channel_id=1, source_target_pairs={{0,96},{8,104},{16,112},{24,120},{32,0},{40,8},{48,16},{56,24},{64... | collective-permute-start | bytes 196616 | tf_op jit(solution)/shard_map/ppermute | solution.py:181
  22.6 14.0 %collective-permute-start.8 = (bf16[256,256]{1,0:T(8,128)(2,1)S(1)}, bf16[256,256]{1,0:T(8,128)(2,1)S(1)}, u32[]{:S(2)}, u32[]{:S(2)}) collective-permute-start(bf16[256,256]{1,0:T(8,128)(2,1)S(1)} %get-tuple-element.43), channel_id=1, source_target_pairs={{0,4},{4,8},{8,12},{12,16},{16,20},{20,24},{24,28},{28,32},{32,36}... | collective-permute-start | bytes 393224 | tf_op jit(solution)/shard_map/ppermute | solution.py:18
  26.8 9.8 %collective-permute-start.7 = (bf16[256,256]{1,0:T(8,128)(2,1)S(1)}, bf16[256,256]{1,0:T(8,128)(2,1)S(1)}, u32[]{:S(2)}, u32[]{:S(2)}) collective-permute-start(bf16[256,256]{1,0:T(8,128)(2,1)S(1)} %get-tuple-element.46), channel_id=1, source_target_pairs={{0,4},{4,8},{8,12},{12,16},{16,20},{20,24},{24,28},{28,32},{32,36}... | collective-permute-start | bytes 393224 | tf_op jit(solution)/shard_map/ppermute | solution.py:18
  28.7 3.4 %collective-permute-start.3 = (bf16[2,1,2,64,128]{4,3,2,0,1:T(8,128)(2,1)S(1)}, bf16[2,1,2,64,128]{4,3,2,0,1:T(8,128)(2,1)S(1)}, u32[]{:S(2)}, u32[]{:S(2)}) collective-permute-start(bf16[2,1,2,64,128]{4,3,2,0,1:T(8,128)(2,1)S(1)} %get-tuple-element.48), channel_id=1, source_target_pairs={{0,24},{8,0},{16,8},{24,16},{32,56},{40,32},{48,40},{56,48},{64,88... | collective-permute-start | bytes 196616 | tf_op jit(solution)/shard_map/ppermute | solution.py:181
  29.1 5.0 %collective-permute-start.2 = (bf16[2,1,2,64,128]{4,3,2,0,1:T(8,128)(2,1)S(1)}, bf16[2,1,2,64,128]{4,3,2,0,1:T(8,128)(2,1)S(1)}, u32[]{:S(2)}, u32[]{:S(2)}) collective-permute-start(bf16[2,1,2,64,128]{4,3,2,0,1:T(8,128)(2,1)S(1)} %get-tuple-element.48), channel_id=1, source_target_pairs={{0,16},{8,24},{16,0},{24,8},{32,48},{40,56},{48,32},{56,40},{64,80... | collective-permute-start | bytes 196616 | tf_op jit(solution)/shard_map/ppermute | solution.py:181
  31.8 4.7 %collective-permute-start.1 = (bf16[2,1,2,64,128]{4,3,2,0,1:T(8,128)(2,1)S(1)}, bf16[2,1,2,64,128]{4,3,2,0,1:T(8,128)(2,1)S(1)}, u32[]{:S(2)}, u32[]{:S(2)}) collective-permute-start(bf16[2,1,2,64,128]{4,3,2,0,1:T(8,128)(2,1)S(1)} %get-tuple-element.48), channel_id=1, source_target_pairs={{0,8},{8,16},{16,24},{24,0},{32,40},{40,48},{48,56},{56,32},{64,72... | collective-permute-start | bytes 196616 | tf_op jit(solution)/shard_map/ppermute | solution.py:181
  36.5 8.5 %copy-start.1 = (bf16[64,4096]{1,0:T(8,128)(2,1)S(1)}, bf16[64,4096]{1,0:T(8,128)(2,1)}, u32[]{:S(2)}) copy-start(bf16[64,4096]{1,0:T(8,128)(2,1)} %param.5) | copy-start | bytes 1572868
  36.6 7.7 %collective-permute-start.13 = (bf16[4,2,1,2,64,128]{5,4,3,1,0,2:T(8,128)(2,1)S(1)}, bf16[4,2,1,2,64,128]{5,4,3,1,0,2:T(8,128)(2,1)S(1)}, u32[]{:S(2)}, u32[]{:S(2)}) collective-permute-start(bf16[4,2,1,2,64,128]{5,4,3,1,0,2:T(8,128)(2,1)S(1)} %bitcast.119), channel_id=1, source_target_pairs={{0,16},{8,24},{16,0},{24,8},{32,48},{40,56},{48,32},{56,40},{64,80... | collective-permute-start | bytes 786440 | tf_op jit(solution)/shard_map/ppermute | solution.py:181
  36.7 14.9 %collective-permute-start.12 = (bf16[4,2,1,2,64,128]{5,4,3,1,0,2:T(8,128)(2,1)S(1)}, bf16[4,2,1,2,64,128]{5,4,3,1,0,2:T(8,128)(2,1)S(1)}, u32[]{:S(2)}, u32[]{:S(2)}) collective-permute-start(bf16[4,2,1,2,64,128]{5,4,3,1,0,2:T(8,128)(2,1)S(1)} %bitcast.120), channel_id=1, source_target_pairs={{0,8},{8,16},{16,24},{24,0},{32,40},{40,48},{48,56},{56,32},{64,72... | collective-permute-start | bytes 786440 | tf_op jit(solution)/shard_map/ppermute | solution.py:181
  37.4 14.2 %collective-permute-start.14 = (bf16[4,2,1,2,64,128]{5,4,3,1,2,0:T(8,128)(2,1)S(1)}, bf16[4,2,1,2,64,128]{5,4,3,1,2,0:T(8,128)(2,1)S(1)}, u32[]{:S(2)}, u32[]{:S(2)}) collective-permute-start(bf16[4,2,1,2,64,128]{5,4,3,1,2,0:T(8,128)(2,1)S(1)} %pad_maximum_fusion.5), channel_id=1, source_target_pairs={{0,24},{8,0},{16,8},{24,16},{32,56},{40,32},{48,40},{56,48},{64,88... | collective-permute-start | bytes 786440 | tf_op jit(solution)/shard_map/ppermute | solution.py:181
  39.4 12.3 %collective-permute-start.11 = (bf16[4,2,1,2,64,128]{5,4,3,1,0,2:T(8,128)(2,1)S(1)}, bf16[4,2,1,2,64,128]{5,4,3,1,0,2:T(8,128)(2,1)S(1)}, u32[]{:S(2)}, u32[]{:S(2)}) collective-permute-start(bf16[4,2,1,2,64,128]{5,4,3,1,0,2:T(8,128)(2,1)S(1)} %pad_maximum_fusion.4), channel_id=1, source_target_pairs={{0,96},{8,104},{16,112},{24,120},{32,0},{40,8},{48,16},{56,24},{64... | collective-permute-start | bytes 786440 | tf_op jit(solution)/shard_map/ppermute | solution.py:181
  39.4 12.3 %collective-permute-start.10 = (bf16[4,2,1,2,64,128]{5,4,3,1,0,2:T(8,128)(2,1)S(1)}, bf16[4,2,1,2,64,128]{5,4,3,1,0,2:T(8,128)(2,1)S(1)}, u32[]{:S(2)}, u32[]{:S(2)}) collective-permute-start(bf16[4,2,1,2,64,128]{5,4,3,1,0,2:T(8,128)(2,1)S(1)} %pad_maximum_fusion.4), channel_id=1, source_target_pairs={{0,64},{8,72},{16,80},{24,88},{32,96},{40,104},{48,112},{56,120},{... | collective-permute-start | bytes 786440 | tf_op jit(solution)/shard_map/ppermute | solution.py:181
  44.3 8.0 %collective-permute-start.9 = (bf16[4,2,1,2,64,128]{5,4,3,1,0,2:T(8,128)(2,1)S(1)}, bf16[4,2,1,2,64,128]{5,4,3,1,0,2:T(8,128)(2,1)S(1)}, u32[]{:S(2)}, u32[]{:S(2)}) collective-permute-start(bf16[4,2,1,2,64,128]{5,4,3,1,0,2:T(8,128)(2,1)S(1)} %pad_maximum_fusion.4), channel_id=1, source_target_pairs={{0,32},{8,40},{16,48},{24,56},{32,64},{40,72},{48,80},{56,88},{64,... | collective-permute-start | bytes 786440 | tf_op jit(solution)/shard_map/ppermute | solution.py:181
  45.9 11.2 %all-to-all-start.1 = ((bf16[64,4,1024]{2,0,1:T(8,128)(2,1)}), bf16[64,4,1024]{2,0,1:T(8,128)(2,1)}, u32[]{:S(2)}, u32[]{:S(2)}) async-start(bf16[64,4,1024]{2,0,1:T(8,128)(2,1)} %bitcast.112), calls=%async_computation.1 | async-start | bytes 1048576 | tf_op jit(solution)/shard_map/all_to_all | solution.py:191
  51.7 0.7 copy-start.2
  58.6 8.3 %collective-permute-start.15 = (bf16[2,2048,128]{2,1,0:T(8,128)(2,1)S(1)}, bf16[2,2048,128]{2,1,0:T(8,128)(2,1)S(1)}, u32[]{:S(2)}, u32[]{:S(2)}) collective-permute-start(bf16[2,2048,128]{2,1,0:T(8,128)(2,1)S(1)} %pad_maximum_fusion.2), channel_id=1, source_target_pairs={{0,4},{4,0},{1,5},{5,1},{2,6},{6,2},{3,7},{7,3},{8,12},{12,8},{9,1... | collective-permute-start | bytes 3145736 | tf_op jit(solution)/shard_map/ppermute | solution.py:214

commit v15 on v13

--- a/solution.py
+++ b/solution.py
@@ -9,6 +9,7 @@
 BLOCK_TOKENS = 64
 EXTRA_DIAGONALS = 4
 SLASH_SLOTS = 6
+LOG2_E = 1.4426950408889634
 INTERPRET = False
 
 
@@ -40,8 +41,8 @@
         [q[:, h * HEAD_WIDTH : (h + 1) * HEAD_WIDTH] for h in range(group)], axis=0
     )
     nt = (((1,), (1,)), ((), ()))
-    s_slash = lax.dot_general(q_stack, ks, nt, preferred_element_type=jnp.float32) * scale
-    s_vert = lax.dot_general(q_stack, kv_ref[0], nt, preferred_element_type=jnp.float32) * scale
+    s_slash = lax.dot_general(q_stack, ks, nt, preferred_element_type=jnp.float32)
+    s_vert = lax.dot_general(q_stack, kv_ref[0], nt, preferred_element_type=jnp.float32)
     width = s_slash.shape[1]
     row = jnp.bitwise_and(lax.broadcasted_iota(jnp.int32, (rows, width), 0), BLOCK_TOKENS - 1)
     col = lax.broadcasted_iota(jnp.int32, (rows, width), 1)
@@ -51,8 +52,9 @@
     top = jnp.maximum(
         jnp.max(s_slash, axis=1, keepdims=True), jnp.max(s_vert, axis=1, keepdims=True)
     )
-    w_slash = jnp.exp(s_slash - top)
-    w_vert = jnp.exp(s_vert - top)
+    rate = scale * LOG2_E
+    w_slash = jnp.exp2((s_slash - top) * rate)
+    w_vert = jnp.exp2((s_vert - top) * rate)
     total = jnp.sum(w_slash, axis=1, keepdims=True) + jnp.sum(w_vert, axis=1, keepdims=True)
     acc = jnp.dot(w_slash.astype(jnp.bfloat16), vs, preferred_element_type=jnp.float32)
     acc = acc + jnp.dot(

time: 81.2 us -> 80.9 us (level)
  no operation moved by 1% of the time
where the time goes in v15:
time: 80.9 us; the launch traced here: 80.5 us
  starting transfers between devices  34.9 us (43%)
  waiting for transfers between devices  18 us (22%)
  Pallas kernels  13.6 us (17%)
  other arithmetic  8.08 us (10%)
  local copies, waits for them, and re-layouts  5.64 us (7%)
    pallas_call x1, Pallas kernels, attend(): pl.pallas_call(kernel, grid_spec=grid_spec, out_shape=jax.ShapeDtypeStruc...  13.6 us
    ppermute x12, starting transfers between devices, shift(): return lax.ppermute(value, 'chip', pairs)  12.9 us
    ppermute x12, waiting for transfers between devices, shift(): return lax.ppermute(value, 'chip', pairs)  12.2 us
    ppermute x2, starting transfers between devices, shifted(): return lax.ppermute(value, axis, pairs)  6.11 us
    all_to_all x1, starting transfers between devices, local(): lax.all_to_all(joined, 'head', split_axis=1, concat_axis=0, tiled=True)  5.84 us
    ppermute x1, starting transfers between devices, local(): other = lax.ppermute(part, 'core', swap)  4.44 us
    all_to_all x1, starting transfers between devices, local(): lax.all_to_all(queries, 'head', split_axis=1, concat_axis=0, tiled=True)  3.47 us
    all_to_all x1, waiting for transfers between devices, local(): lax.all_to_all(joined, 'head', split_axis=1, concat_axis=0, tiled=True)  3.27 us
  transfers between devices with their start and end apart: 18, of which 8 were waited for; matrix products, arithmetic and copies ran while one was open for 10% of the time, Pallas kernels for 0%

profile of v15, /device:TPU:1, one launch (start us, length us, event | category | flops | bytes accessed | tf_op | source)
XLA Modules:
  0.0 80.5 jit_solution(6151773143577235814)
XLA Ops:
  0.0 1.0 %copy_bitcast_fusion.1 = (bf16[64,4,256]{2,0,1:T(8,128)(2,1)S(1)}, bf16[64,4,256]{2,0,1:T(8,128)(2,1)S(1)}) fusion(bf16[8,4,8,256]{3,2,1,0:T(8,128)(2,1)} %bitcast.133, bf16[8,4,8,256]{3,2,1,0:T(8,128)(2,1)} %bitcast.134), kind=kLoop, calls=%fused_computation.16 | loop fusion | bytes 524288 | tf_op jit(solution)/shard_map/reshape | solution.py:138
  1.0 0.7 pad_maximum_fusion.3
  1.8 5.8 %all-to-all-start = ((bf16[64,4,512]{2,0,1:T(8,128)(2,1)}), bf16[64,4,512]{2,0,1:T(8,128)(2,1)S(1)}, u32[]{:S(2)}, u32[]{:S(2)}) async-start(bf16[64,4,512]{2,0,1:T(8,128)(2,1)} %pad_maximum_fusion.3), calls=%async_computation | async-start | bytes 524288 | tf_op jit(solution)/shard_map/all_to_all | solution.py:140
  7.7 0.1 copy.74
  7.8 0.7 and_select_fusion.3
  8.6 0.2 convert_reduce_fusion
  8.7 0.2 fusion.1
  9.0 0.8 %copy.83 = bf16[8,4,8,1024]{3,2,0,1:T(8,128)(2,1)} copy(bf16[8,4,8,1024]{3,2,1,0:T(8,128)(2,1)S(1)} %bitcast.123) | data formatting | bytes 1048576 | tf_op jit(solution)/shard_map/all_to_all | solution.py:175
  9.9 3.3 %all-to-all-done = bf16[64,4,512]{2,0,1:T(8,128)(2,1)S(1)} async-done(((bf16[64,4,512]{2,0,1:T(8,128)(2,1)}), bf16[64,4,512]{2,0,1:T(8,128)(2,1)S(1)}, u32[]{:S(2)}, u32[]{:S(2)}) %all-to-all-start) | async-done | bytes 262176 | tf_op jit(solution)/shard_map/all_to_all | solution.py:140
  13.2 3.5 %all-to-all-start.1 = ((bf16[64,4,1024]{2,0,1:T(8,128)(2,1)}), bf16[64,4,1024]{2,0,1:T(8,128)(2,1)S(1)}, u32[]{:S(2)}, u32[]{:S(2)}) async-start(bf16[64,4,1024]{2,0,1:T(8,128)(2,1)} %bitcast.112), calls=%async_computation.1 | async-start | bytes 1048576 | tf_op jit(solution)/shard_map/all_to_all | solution.py:175
  16.7 0.6 gather_fusion.1
  17.3 2.2 %collective-permute-start = (bf16[2,2,64,128]{3,2,1,0:T(8,128)(2,1)S(1)}, bf16[2,2,64,128]{3,2,1,0:T(8,128)(2,1)S(1)}, u32[]{:S(2)}, u32[]{:S(2)}) collective-permute-start(bf16[2,2,64,128]{3,2,1,0:T(8,128)(2,1)S(1)} %bitcast.135), channel_id=1, source_target_pairs={{0,4},{4,0},{1,5},{5,1},{2,6},{6,2},{3,7},{7,3},{8,12},{12,8},{9,1... | collective-permute-start | bytes 196616 | tf_op jit(solution)/shard_map/ppermute | solution.py:174
  19.6 0.6 gather_fusion
  20.2 0.2 collective-permute-done
  20.4 3.0 %collective-permute-start.5 = (bf16[2,1,2,64,128]{4,3,2,0,1:T(8,128)(2,1)S(1)}, bf16[2,1,2,64,128]{4,3,2,0,1:T(8,128)(2,1)S(1)}, u32[]{:S(2)}, u32[]{:S(2)}) collective-permute-start(bf16[2,1,2,64,128]{4,3,2,0,1:T(8,128)(2,1)S(1)} %get-tuple-element.45), channel_id=1, source_target_pairs={{0,64},{8,72},{16,80},{24,88},{32,96},{40,104},{48,112},{56,120},{... | collective-permute-start | bytes 196616 | tf_op jit(solution)/shard_map/ppermute | solution.py:184
  23.4 0.4 collective-permute-start.4
  23.8 2.3 %collective-permute-start.6 = (bf16[2,1,2,64,128]{4,3,2,0,1:T(8,128)(2,1)S(1)}, bf16[2,1,2,64,128]{4,3,2,0,1:T(8,128)(2,1)S(1)}, u32[]{:S(2)}, u32[]{:S(2)}) collective-permute-start(bf16[2,1,2,64,128]{4,3,2,0,1:T(8,128)(2,1)S(1)} %get-tuple-element.45), channel_id=1, source_target_pairs={{0,96},{8,104},{16,112},{24,120},{32,0},{40,8},{48,16},{56,24},{64... | collective-permute-start | bytes 196616 | tf_op jit(solution)/shard_map/ppermute | solution.py:184
  26.1 4.2 %collective-permute-start.8 = (bf16[256,256]{1,0:T(8,128)(2,1)S(1)}, bf16[256,256]{1,0:T(8,128)(2,1)S(1)}, u32[]{:S(2)}, u32[]{:S(2)}) collective-permute-start(bf16[256,256]{1,0:T(8,128)(2,1)S(1)} %get-tuple-element.41), channel_id=1, source_target_pairs={{0,4},{4,8},{8,12},{12,16},{16,20},{20,24},{24,28},{28,32},{32,36}... | collective-permute-start | bytes 393224 | tf_op jit(solution)/shard_map/ppermute | solution.py:19
  30.3 1.9 %collective-permute-start.7 = (bf16[256,256]{1,0:T(8,128)(2,1)S(1)}, bf16[256,256]{1,0:T(8,128)(2,1)S(1)}, u32[]{:S(2)}, u32[]{:S(2)}) collective-permute-start(bf16[256,256]{1,0:T(8,128)(2,1)S(1)} %get-tuple-element.44), channel_id=1, source_target_pairs={{0,4},{4,8},{8,12},{12,16},{16,20},{20,24},{24,28},{28,32},{32,36}... | collective-permute-start | bytes 393224 | tf_op jit(solution)/shard_map/ppermute | solution.py:19
  32.2 0.4 collective-permute-start.3
  32.6 2.6 %collective-permute-start.2 = (bf16[2,1,2,64,128]{4,3,2,0,1:T(8,128)(2,1)S(1)}, bf16[2,1,2,64,128]{4,3,2,0,1:T(8,128)(2,1)S(1)}, u32[]{:S(2)}, u32[]{:S(2)}) collective-permute-start(bf16[2,1,2,64,128]{4,3,2,0,1:T(8,128)(2,1)S(1)} %get-tuple-element.46), channel_id=1, source_target_pairs={{0,16},{8,24},{16,0},{24,8},{32,48},{40,56},{48,32},{56,40},{64,80... | collective-permute-start | bytes 196616 | tf_op jit(solution)/shard_map/ppermute | solution.py:184
  35.3 0.3 collective-permute-start.1
  35.6 2.0 %collective-permute-done.2 = bf16[2,1,2,64,128]{4,3,2,0,1:T(8,128)(2,1)S(1)} collective-permute-done((bf16[2,1,2,64,128]{4,3,2,0,1:T(8,128)(2,1)S(1)}, bf16[2,1,2,64,128]{4,3,2,0,1:T(8,128)(2,1)S(1)}, u32[]{:S(2)}, u32[]{:S(2)}) %collective-permute-start.2) | collective-permute-done | bytes 65568 | tf_op jit(solution)/shard_map/ppermute | solution.py:184
  37.7 2.3 %collective-permute-done.1 = bf16[2,1,2,64,128]{4,3,2,0,1:T(8,128)(2,1)S(1)} collective-permute-done((bf16[2,1,2,64,128]{4,3,2,0,1:T(8,128)(2,1)S(1)}, bf16[2,1,2,64,128]{4,3,2,0,1:T(8,128)(2,1)S(1)}, u32[]{:S(2)}, u32[]{:S(2)}) %collective-permute-start.1) | collective-permute-done | bytes 65568 | tf_op jit(solution)/shard_map/ppermute | solution.py:184
  40.2 0.7 collective-permute-start.12
  40.9 2.0 %collective-permute-start.14 = (bf16[4,2,1,2,64,128]{5,4,3,1,2,0:T(8,128)(2,1)S(1)}, bf16[4,2,1,2,64,128]{5,4,3,1,2,0:T(8,128)(2,1)S(1)}, u32[]{:S(2)}, u32[]{:S(2)}) collective-permute-start(bf16[4,2,1,2,64,128]{5,4,3,1,2,0:T(8,128)(2,1)S(1)} %pad_maximum_fusion.5), channel_id=1, source_target_pairs={{0,24},{8,0},{16,8},{24,16},{32,56},{40,32},{48,40},{56,48},{64,88... | collective-permute-start | bytes 786440 | tf_op jit(solution)/shard_map/ppermute | solution.py:184
  42.9 1.0 %collective-permute-start.10 = (bf16[4,2,1,2,64,128]{5,4,3,1,0,2:T(8,128)(2,1)S(1)}, bf16[4,2,1,2,64,128]{5,4,3,1,0,2:T(8,128)(2,1)}, u32[]{:S(2)}, u32[]{:S(2)}) collective-permute-start(bf16[4,2,1,2,64,128]{5,4,3,1,0,2:T(8,128)(2,1)S(1)} %pad_maximum_fusion.4), channel_id=1, source_target_pairs={{0,64},{8,72},{16,80},{24,88},{32,96},{40,104},{48,112},{56,120},{... | collective-permute-start | bytes 786440 | tf_op jit(solution)/shard_map/ppermute | solution.py:184
  44.1 0.1 stack.116
  44.3 0.1 stack.115
  44.7 0.1 broadcast_in_dim.30
  44.8 0.1 stack.118
  45.0 0.1 stack.119
  45.1 0.7 copy_convert_fusion.refs_7_
  45.8 0.6 copy_convert_fusion.1.refs_6_
  46.4 1.4 %collective-permute-done.13 = bf16[4,2,1,2,64,128]{5,4,3,1,0,2:T(8,128)(2,1)S(1)} collective-permute-done((bf16[4,2,1,2,64,128]{5,4,3,1,0,2:T(8,128)(2,1)S(1)}, bf16[4,2,1,2,64,128]{5,4,3,1,0,2:T(8,128)(2,1)S(1)}, u32[]{:S(2)}, u32[]{:S(2)}) %collective-permute-start.13) | collective-permute-done | bytes 262176 | tf_op jit(solution)/shard_map/ppermute | solution.py:184
  47.8 0.7 pad_maximum_fusion.6.refs_2_
  48.6 0.7 pad_maximum_fusion.7.refs_3_
  49.3 5.8 %collective-permute-done.12 = bf16[4,2,1,2,64,128]{5,4,3,1,0,2:T(8,128)(2,1)S(1)} collective-permute-done((bf16[4,2,1,2,64,128]{5,4,3,1,0,2:T(8,128)(2,1)S(1)}, bf16[4,2,1,2,64,128]{5,4,3,1,0,2:T(8,128)(2,1)S(1)}, u32[]{:S(2)}, u32[]{:S(2)}) %collective-permute-start.12) | collective-permute-done | bytes 262176 | tf_op jit(solution)/shard_map/ppermute | solution.py:184
  55.1 0.1 pad_maximum_fusion.1
  55.3 0.6 collective-permute-done.9
  55.9 1.1 %pad_maximum_fusion = bf16[4,4,2,1,2,64,128]{6,5,4,3,2,1,0:T(8,128)(2,1)S(1)} fusion(bf16[1,4,2,1,2,64,128]{6,5,4,3,2,1,0:T(8,128)(2,1)S(1)} %bitcast.128, bf16[1,4,2,1,2,64,128]{6,5,4,3,2,1,0:T(8,128)(2,1)} %bitcast.30, bf16[1,4,2,1,2,64,128]{6,5,4,3,2,1,0:T(8,128)(2,1)S(1)} %bitcast.132, bf16[1,4,2,1,2,64,128]{6,5,4,3,2,1,0:T(8,128)(2,1)S(1)} %bitcast.122), kind=kLoop, calls=%fused_computation.4 | loop fusion | flops 1572864 | bytes 2097152 | tf_op jit(solution)/shard_map/stack | solution.py:187
  57.0 0.7 gather_fusion.2
  57.7 0.7 gather_fusion.3
  58.4 0.1 pad_maximum_fusion.2
  58.5 4.4 %collective-permute-start.15 = (bf16[2,2048,128]{2,1,0:T(8,128)(2,1)S(1)}, bf16[2,2048,128]{2,1,0:T(8,128)(2,1)S(1)}, u32[]{:S(2)}, u32[]{:S(2)}) collective-permute-start(bf16[2,2048,128]{2,1,0:T(8,128)(2,1)S(1)} %pad_maximum_fusion.2), channel_id=1, source_target_pairs={{0,4},{4,0},{1,5},{5,1},{2,6},{6,2},{3,7},{7,3},{8,12},{12,8},{9,1... | collective-permute-start | bytes 3145736 | tf_op jit(solution)/shard_map/ppermute | solution.py:216
  63.0 2.3 %collective-permute-done.15 = bf16[2,2048,128]{2,1,0:T(8,128)(2,1)S(1)} collective-permute-done((bf16[2,2048,128]{2,1,0:T(8,128)(2,1)S(1)}, bf16[2,2048,128]{2,1,0:T(8,128)(2,1)S(1)}, u32[]{:S(2)}, u32[]{:S(2)}) %collective-permute-start.15) | collective-permute-done | bytes 1048608 | tf_op jit(solution)/shard_map/ppermute | solution.py:216
  65.3 1.6 %broadcast_select_fusion = (bf16[2,2048,128]{2,1,0:T(8,128)(2,1)}, bf16[2,2048,128]{2,1,0:T(8,128)(2,1)}) fusion(bf16[2,2048,128]{2,1,0:T(8,128)(2,1)S(1)} %collective-permute-done.15, pred[]{:T(512)S(6)} %eq.73, bf16[1,2048,128]{2,1,0:T(8,128)(2,1)S(1)} %bitcast.116, bf16[1,2048,128]{2,1,0:T(8,128)(2,1)S(1)} %bitcast.114), kind=kLoop, calls=%fused_computation.7 | loop fusion | flops 1572864 | bytes 4194305 | tf_op jit(solution)/shard_map/jit(_where)/select_n | solution.py:218
  66.9 13.6 %shard_map.55 = bf16[256,1024]{1,0:T(8,128)(2,1)} custom-call(s32[2,5]{1,0:T(2,128)} %copy-done.3, bf16[256,1024]{1,0:T(8,128)(2,1)} %bitcast.124, bf16[512,256]{1,0:T(8,128)(2,1)} %pad_maximum_fusion.6.refs_2_, bf16[512,256]{1,0:T(8,128)(2,1)} %pad_maximum_fusion.7.refs_3_, bf16[2,2048,128]{2,1,0:T(8,128)(2,1)} %get-tuple-element.40.refs_4_, ...), custom_call_target="tpu_custom_call" | custom-call | flops 2550136832 | bytes 3670016 | tf_op jit(solution)/shard_map/pallas_call | solution.py:99
  (54 shorter events, 1.4 us)
Async XLA Ops:
  0.0 7.6 %copy-start = (s32[8,4]{0,1:T(4,128)S(1)}, s32[8,4]{0,1:T(4,128)}, u32[]{:S(2)}) copy-start(s32[8,4]{0,1:T(4,128)} %param.8) | copy-start | bytes 388
  1.0 8.0 %copy-start.1 = (bf16[64,4096]{1,0:T(8,128)(2,1)S(1)}, bf16[64,4096]{1,0:T(8,128)(2,1)}, u32[]{:S(2)}) copy-start(bf16[64,4096]{1,0:T(8,128)(2,1)} %param.5) | copy-start | bytes 1572868
  1.8 11.4 %all-to-all-start = ((bf16[64,4,512]{2,0,1:T(8,128)(2,1)}), bf16[64,4,512]{2,0,1:T(8,128)(2,1)S(1)}, u32[]{:S(2)}, u32[]{:S(2)}) async-start(bf16[64,4,512]{2,0,1:T(8,128)(2,1)} %pad_maximum_fusion.3), calls=%async_computation | async-start | bytes 524288 | tf_op jit(solution)/shard_map/all_to_all | solution.py:140
  13.2 26.9 %all-to-all-start.1 = ((bf16[64,4,1024]{2,0,1:T(8,128)(2,1)}), bf16[64,4,1024]{2,0,1:T(8,128)(2,1)S(1)}, u32[]{:S(2)}, u32[]{:S(2)}) async-start(bf16[64,4,1024]{2,0,1:T(8,128)(2,1)} %bitcast.112), calls=%async_computation.1 | async-start | bytes 1048576 | tf_op jit(solution)/shard_map/all_to_all | solution.py:175
  17.3 3.1 %collective-permute-start = (bf16[2,2,64,128]{3,2,1,0:T(8,128)(2,1)S(1)}, bf16[2,2,64,128]{3,2,1,0:T(8,128)(2,1)S(1)}, u32[]{:S(2)}, u32[]{:S(2)}) collective-permute-start(bf16[2,2,64,128]{3,2,1,0:T(8,128)(2,1)S(1)} %bitcast.135), channel_id=1, source_target_pairs={{0,4},{4,0},{1,5},{5,1},{2,6},{6,2},{3,7},{7,3},{8,12},{12,8},{9,1... | collective-permute-start | bytes 196616 | tf_op jit(solution)/shard_map/ppermute | solution.py:174
  19.6 24.4 %copy-start.3 = (s32[2,5]{1,0:T(2,128)}, s32[2,5]{1,0:T(2,128)S(1)}, u32[]{:S(2)}) copy-start(s32[2,5]{1,0:T(2,128)S(1)} %concatenate.45.refs_0_) | copy-start | bytes 124
  20.4 11.8 %collective-permute-start.5 = (bf16[2,1,2,64,128]{4,3,2,0,1:T(8,128)(2,1)S(1)}, bf16[2,1,2,64,128]{4,3,2,0,1:T(8,128)(2,1)S(1)}, u32[]{:S(2)}, u32[]{:S(2)}) collective-permute-start(bf16[2,1,2,64,128]{4,3,2,0,1:T(8,128)(2,1)S(1)} %get-tuple-element.45), channel_id=1, source_target_pairs={{0,64},{8,72},{16,80},{24,88},{32,96},{40,104},{48,112},{56,120},{... | collective-permute-start | bytes 196616 | tf_op jit(solution)/shard_map/ppermute | solution.py:184
  23.4 9.3 %collective-permute-start.4 = (bf16[2,1,2,64,128]{4,3,2,0,1:T(8,128)(2,1)S(1)}, bf16[2,1,2,64,128]{4,3,2,0,1:T(8,128)(2,1)S(1)}, u32[]{:S(2)}, u32[]{:S(2)}) collective-permute-start(bf16[2,1,2,64,128]{4,3,2,0,1:T(8,128)(2,1)S(1)} %get-tuple-element.45), channel_id=1, source_target_pairs={{0,32},{8,40},{16,48},{24,56},{32,64},{40,72},{48,80},{56,88},{64,... | collective-permute-start | bytes 196616 | tf_op jit(solution)/shard_map/ppermute | solution.py:184
  23.8 11.5 %collective-permute-start.6 = (bf16[2,1,2,64,128]{4,3,2,0,1:T(8,128)(2,1)S(1)}, bf16[2,1,2,64,128]{4,3,2,0,1:T(8,128)(2,1)S(1)}, u32[]{:S(2)}, u32[]{:S(2)}) collective-permute-start(bf16[2,1,2,64,128]{4,3,2,0,1:T(8,128)(2,1)S(1)} %get-tuple-element.45), channel_id=1, source_target_pairs={{0,96},{8,104},{16,112},{24,120},{32,0},{40,8},{48,16},{56,24},{64... | collective-permute-start | bytes 196616 | tf_op jit(solution)/shard_map/ppermute | solution.py:184
  26.1 14.0 %collective-permute-start.8 = (bf16[256,256]{1,0:T(8,128)(2,1)S(1)}, bf16[256,256]{1,0:T(8,128)(2,1)S(1)}, u32[]{:S(2)}, u32[]{:S(2)}) collective-permute-start(bf16[256,256]{1,0:T(8,128)(2,1)S(1)} %get-tuple-element.41), channel_id=1, source_target_pairs={{0,4},{4,8},{8,12},{12,16},{16,20},{20,24},{24,28},{28,32},{32,36}... | collective-permute-start | bytes 393224 | tf_op jit(solution)/shard_map/ppermute | solution.py:19
  30.3 9.8 %collective-permute-start.7 = (bf16[256,256]{1,0:T(8,128)(2,1)S(1)}, bf16[256,256]{1,0:T(8,128)(2,1)S(1)}, u32[]{:S(2)}, u32[]{:S(2)}) collective-permute-start(bf16[256,256]{1,0:T(8,128)(2,1)S(1)} %get-tuple-element.44), channel_id=1, source_target_pairs={{0,4},{4,8},{8,12},{12,16},{16,20},{20,24},{24,28},{28,32},{32,36}... | collective-permute-start | bytes 393224 | tf_op jit(solution)/shard_map/ppermute | solution.py:19
  32.2 3.4 %collective-permute-start.3 = (bf16[2,1,2,64,128]{4,3,2,0,1:T(8,128)(2,1)S(1)}, bf16[2,1,2,64,128]{4,3,2,0,1:T(8,128)(2,1)S(1)}, u32[]{:S(2)}, u32[]{:S(2)}) collective-permute-start(bf16[2,1,2,64,128]{4,3,2,0,1:T(8,128)(2,1)S(1)} %get-tuple-element.46), channel_id=1, source_target_pairs={{0,24},{8,0},{16,8},{24,16},{32,56},{40,32},{48,40},{56,48},{64,88... | collective-permute-start | bytes 196616 | tf_op jit(solution)/shard_map/ppermute | solution.py:184
  32.6 5.0 %collective-permute-start.2 = (bf16[2,1,2,64,128]{4,3,2,0,1:T(8,128)(2,1)S(1)}, bf16[2,1,2,64,128]{4,3,2,0,1:T(8,128)(2,1)S(1)}, u32[]{:S(2)}, u32[]{:S(2)}) collective-permute-start(bf16[2,1,2,64,128]{4,3,2,0,1:T(8,128)(2,1)S(1)} %get-tuple-element.46), channel_id=1, source_target_pairs={{0,16},{8,24},{16,0},{24,8},{32,48},{40,56},{48,32},{56,40},{64,80... | collective-permute-start | bytes 196616 | tf_op jit(solution)/shard_map/ppermute | solution.py:184
  35.3 4.7 %collective-permute-start.1 = (bf16[2,1,2,64,128]{4,3,2,0,1:T(8,128)(2,1)S(1)}, bf16[2,1,2,64,128]{4,3,2,0,1:T(8,128)(2,1)S(1)}, u32[]{:S(2)}, u32[]{:S(2)}) collective-permute-start(bf16[2,1,2,64,128]{4,3,2,0,1:T(8,128)(2,1)S(1)} %get-tuple-element.46), channel_id=1, source_target_pairs={{0,8},{8,16},{16,24},{24,0},{32,40},{40,48},{48,56},{56,32},{64,72... | collective-permute-start | bytes 196616 | tf_op jit(solution)/shard_map/ppermute | solution.py:184
  40.1 9.2 %copy-start.2 = (bf16[64,4,1024]{2,0,1:T(8,128)(2,1)}, bf16[64,4,1024]{2,0,1:T(8,128)(2,1)S(1)}, u32[]{:S(2)}) copy-start(bf16[64,4,1024]{2,0,1:T(8,128)(2,1)S(1)} %all-to-all-done.1) | copy-start | bytes 1572868
  40.1 7.7 %collective-permute-start.13 = (bf16[4,2,1,2,64,128]{5,4,3,1,0,2:T(8,128)(2,1)S(1)}, bf16[4,2,1,2,64,128]{5,4,3,1,0,2:T(8,128)(2,1)S(1)}, u32[]{:S(2)}, u32[]{:S(2)}) collective-permute-start(bf16[4,2,1,2,64,128]{5,4,3,1,0,2:T(8,128)(2,1)S(1)} %bitcast.119), channel_id=1, source_target_pairs={{0,16},{8,24},{16,0},{24,8},{32,48},{40,56},{48,32},{56,40},{64,80... | collective-permute-start | bytes 786440 | tf_op jit(solution)/shard_map/ppermute | solution.py:184
  40.2 14.9 %collective-permute-start.12 = (bf16[4,2,1,2,64,128]{5,4,3,1,0,2:T(8,128)(2,1)S(1)}, bf16[4,2,1,2,64,128]{5,4,3,1,0,2:T(8,128)(2,1)S(1)}, u32[]{:S(2)}, u32[]{:S(2)}) collective-permute-start(bf16[4,2,1,2,64,128]{5,4,3,1,0,2:T(8,128)(2,1)S(1)} %bitcast.120), channel_id=1, source_target_pairs={{0,8},{8,16},{16,24},{24,0},{32,40},{40,48},{48,56},{56,32},{64,72... | collective-permute-start | bytes 786440 | tf_op jit(solution)/shard_map/ppermute | solution.py:184
  40.9 14.2 %collective-permute-start.14 = (bf16[4,2,1,2,64,128]{5,4,3,1,2,0:T(8,128)(2,1)S(1)}, bf16[4,2,1,2,64,128]{5,4,3,1,2,0:T(8,128)(2,1)S(1)}, u32[]{:S(2)}, u32[]{:S(2)}) collective-permute-start(bf16[4,2,1,2,64,128]{5,4,3,1,2,0:T(8,128)(2,1)S(1)} %pad_maximum_fusion.5), channel_id=1, source_target_pairs={{0,24},{8,0},{16,8},{24,16},{32,56},{40,32},{48,40},{56,48},{64,88... | collective-permute-start | bytes 786440 | tf_op jit(solution)/shard_map/ppermute | solution.py:184
  42.9 12.3 %collective-permute-start.11 = (bf16[4,2,1,2,64,128]{5,4,3,1,0,2:T(8,128)(2,1)S(1)}, bf16[4,2,1,2,64,128]{5,4,3,1,0,2:T(8,128)(2,1)S(1)}, u32[]{:S(2)}, u32[]{:S(2)}) collective-permute-start(bf16[4,2,1,2,64,128]{5,4,3,1,0,2:T(8,128)(2,1)S(1)} %pad_maximum_fusion.4), channel_id=1, source_target_pairs={{0,96},{8,104},{16,112},{24,120},{32,0},{40,8},{48,16},{56,24},{64... | collective-permute-start | bytes 786440 | tf_op jit(solution)/shard_map/ppermute | solution.py:184
  42.9 12.3 %collective-permute-start.10 = (bf16[4,2,1,2,64,128]{5,4,3,1,0,2:T(8,128)(2,1)S(1)}, bf16[4,2,1,2,64,128]{5,4,3,1,0,2:T(8,128)(2,1)}, u32[]{:S(2)}, u32[]{:S(2)}) collective-permute-start(bf16[4,2,1,2,64,128]{5,4,3,1,0,2:T(8,128)(2,1)S(1)} %pad_maximum_fusion.4), channel_id=1, source_target_pairs={{0,64},{8,72},{16,80},{24,88},{32,96},{40,104},{48,112},{56,120},{... | collective-permute-start | bytes 786440 | tf_op jit(solution)/shard_map/ppermute | solution.py:184
  47.8 8.0 %collective-permute-start.9 = (bf16[4,2,1,2,64,128]{5,4,3,1,0,2:T(8,128)(2,1)S(1)}, bf16[4,2,1,2,64,128]{5,4,3,1,0,2:T(8,128)(2,1)S(1)}, u32[]{:S(2)}, u32[]{:S(2)}) collective-permute-start(bf16[4,2,1,2,64,128]{5,4,3,1,0,2:T(8,128)(2,1)S(1)} %pad_maximum_fusion.4), channel_id=1, source_target_pairs={{0,32},{8,40},{16,48},{24,56},{32,64},{40,72},{48,80},{56,88},{64,... | collective-permute-start | bytes 786440 | tf_op jit(solution)/shard_map/ppermute | solution.py:184
  58.5 6.7 %collective-permute-start.15 = (bf16[2,2048,128]{2,1,0:T(8,128)(2,1)S(1)}, bf16[2,2048,128]{2,1,0:T(8,128)(2,1)S(1)}, u32[]{:S(2)}, u32[]{:S(2)}) collective-permute-start(bf16[2,2048,128]{2,1,0:T(8,128)(2,1)S(1)} %pad_maximum_fusion.2), channel_id=1, source_target_pairs={{0,4},{4,0},{1,5},{5,1},{2,6},{6,2},{3,7},{7,3},{8,12},{12,8},{9,1... | collective-permute-start | bytes 3145736 | tf_op jit(solution)/shard_map/ppermute | solution.py:216

commit v16 on v15

--- a/solution.py
+++ b/solution.py
@@ -20,9 +20,10 @@
 
 
 def attend_kernel(
-    off_ref, q_ref, wk_ref, wv_ref, kv_ref, vv_ref, ms_ref, mv_ref, o_ref, *, group, scale, nbd
+    off_ref, q_ref, wk_ref, wv_ref, kv_ref, vv_ref, ms_ref, mv_ref, *rest, group, scale, nbd, head
 ):
-    g = pl.program_id(0)
+    o_ref = rest[-1]
+    g = head
     i = pl.program_id(1)
     rows = BLOCK_TOKENS * group
     picked_k, picked_v = [], []
@@ -67,42 +68,49 @@
         ]
 
 
-def attend(offsets, q_all, win_k, win_v, kv, vv, ms, mv, group, scale):
-    kv_local, nbd = ms.shape[0], ms.shape[1]
+def attend(offsets, q_all, win_k, win_v, kv, vv, ms, mv, group, scale, head, prior):
+    nbd = ms.shape[1]
     slash_rows = ms.shape[3]
     vert_rows = kv.shape[1]
     window_rows = win_k.shape[0]
     cols = group * HEAD_WIDTH
     rows = BLOCK_TOKENS * group
-    steps = kv_local * nbd
-    flops = steps * 4 * rows * (slash_rows + vert_rows) * HEAD_WIDTH
+    flops = nbd * 4 * rows * (slash_rows + vert_rows) * HEAD_WIDTH
     cost = pl.CostEstimate(
         flops=flops,
-        transcendentals=steps * rows * (slash_rows + vert_rows),
-        bytes_accessed=2 * (2 * q_all.size + win_k.size + win_v.size + kv.size + vv.size),
-    )
-    kernel = lambda *refs: attend_kernel(*refs, group=group, scale=scale, nbd=nbd)
+        transcendentals=nbd * rows * (slash_rows + vert_rows),
+        bytes_accessed=2 * (q_all.size + win_k.size // 2 + kv.size + vv.size),
+    )
+    kernel = lambda *refs: attend_kernel(*refs, group=group, scale=scale, nbd=nbd, head=head)
+    in_specs = [
+        pl.BlockSpec((BLOCK_TOKENS, cols), lambda g, i, off: (i, head)),
+        pl.BlockSpec((window_rows, HEAD_WIDTH), lambda g, i, off: (0, head)),
+        pl.BlockSpec((window_rows, HEAD_WIDTH), lambda g, i, off: (0, head)),
+        pl.BlockSpec((1, vert_rows, HEAD_WIDTH), lambda g, i, off: (0, 0, 0)),
+        pl.BlockSpec((1, vert_rows, HEAD_WIDTH), lambda g, i, off: (0, 0, 0)),
+        pl.BlockSpec((1, 1, 1, slash_rows), lambda g, i, off: (head, i, 0, 0)),
+        pl.BlockSpec((1, 1, 1, vert_rows), lambda g, i, off: (head, i, 0, 0)),
+    ]
+    operands = [offsets, q_all, win_k, win_v, kv, vv, ms, mv]
+    aliases = {}
+    if prior is not None:
+        in_specs.append(pl.BlockSpec(memory_space=pl.ANY))
+        aliases = {len(operands): 0}
+        operands.append(prior)
     grid_spec = pltpu.PrefetchScalarGridSpec(
         num_scalar_prefetch=1,
-        grid=(kv_local, nbd),
-        in_specs=[
-            pl.BlockSpec((BLOCK_TOKENS, cols), lambda g, i, off: (i, g)),
-            pl.BlockSpec((window_rows, HEAD_WIDTH), lambda g, i, off: (0, g)),
-            pl.BlockSpec((window_rows, HEAD_WIDTH), lambda g, i, off: (0, g)),
-            pl.BlockSpec((1, vert_rows, HEAD_WIDTH), lambda g, i, off: (g, 0, 0)),
-            pl.BlockSpec((1, vert_rows, HEAD_WIDTH), lambda g, i, off: (g, 0, 0)),
-            pl.BlockSpec((1, 1, 1, slash_rows), lambda g, i, off: (g, i, 0, 0)),
-            pl.BlockSpec((1, 1, 1, vert_rows), lambda g, i, off: (g, i, 0, 0)),
-        ],
-        out_specs=pl.BlockSpec((BLOCK_TOKENS, cols), lambda g, i, off: (i, g)),
+        grid=(1, nbd),
+        in_specs=in_specs,
+        out_specs=pl.BlockSpec((BLOCK_TOKENS, cols), lambda g, i, off: (i, head)),
     )
     return pl.pallas_call(
         kernel,
         grid_spec=grid_spec,
         out_shape=jax.ShapeDtypeStruct(q_all.shape, q_all.dtype),
         cost_estimate=cost,
+        input_output_aliases=aliases,
         interpret=INTERPRET,
-    )(offsets, q_all, win_k, win_v, kv, vv, ms, mv)
+    )(*operands)
 
 
 def side_inputs(prev_k, prev_v, k_all, v_all, diagonal_offsets, local_vert, seq_index, nbd):
@@ -205,21 +213,21 @@
     dx = (chip_index % side - owner_chip % side) % side
     heads_idx = jnp.arange(kv_local)[:, None]
     dc = (owner_core + core_index) % cores
-    part = jnp.stack(
-        [
-            across[dy[0], dx[0], dc[0], 0, rank[0]],
-            down[dx[1], dy[1], dc[1], 0, rank[1]],
-        ],
-        0,
-    )
-    part = part.reshape(kv_local, listed * BLOCK_TOKENS, HEAD_WIDTH)
-    other = lax.ppermute(part, "core", swap)
-    vert_keys = jnp.where(core_index == 0, part, other)
-    vert_vals = jnp.where(core_index == 0, other, part)
-    return attend(
-        diagonal_offsets, q_all, window_k, window_v, vert_keys, vert_vals, ms, mv,
-        query_group, softmax_scale,
-    )
+    gathered = [
+        across[dy[0], dx[0], dc[0], 0, rank[0]],
+        down[dx[1], dy[1], dc[1], 0, rank[1]],
+    ]
+    result = None
+    for head in range(kv_local):
+        part = gathered[head].reshape(1, listed * BLOCK_TOKENS, HEAD_WIDTH)
+        other = lax.ppermute(part, "core", swap)
+        vert_keys = jnp.where(core_index == 0, part, other)
+        vert_vals = jnp.where(core_index == 0, other, part)
+        result = attend(
+            diagonal_offsets, q_all, window_k, window_v, vert_keys, vert_vals, ms, mv,
+            query_group, softmax_scale, head, result,
+        )
+    return result
 
 
 def solution(mesh):

time: 80.9 us -> 79.9 us (0.988)
  starting transfers between devices: 34.9 us -> 30.9 us
  Pallas kernels: 13.6 us -> 16.2 us
    pallas_call x1 -> x2, Pallas kernels: 13.6 us -> 16.2 us  [attend(): pl.pallas_call(kernel, grid_spec=grid_spec, out_shape=jax.ShapeDtypeStruc...]
    ppermute x12, waiting for transfers between devices: 12.2 us -> 14.6 us  [shift(): return lax.ppermute(value, 'chip', pairs)]
    ppermute x12, starting transfers between devices: 12.9 us -> 10.5 us  [shift(): return lax.ppermute(value, 'chip', pairs)]
    ppermute x1 -> x2, starting transfers between devices: 4.44 us -> 2.51 us  [local(): other = lax.ppermute(part, 'core', swap)]
    ppermute x1 -> x2, waiting for transfers between devices: 2.29 us -> 0.71 us  [local(): other = lax.ppermute(part, 'core', swap)]
    another operation x4, other arithmetic: 1.28 us -> 0.34 us  [ring(): jnp.stack([value] + [shift(value, stride, s) for s in range(1, side)], 0)]
    select_n x1 -> x2, other arithmetic: 1.61 us -> 2.2 us  [local(): vert_vals = jnp.where(core_index == 0, other, part)]
  transfers between devices with their start and end apart: 18 -> 19, of which waited for: 8 -> 9; matrix products, arithmetic and copies ran while one was open for 10% -> 12% of each run, Pallas kernels for 0% -> 10%
where the time goes in v16:
time: 79.9 us; the launch traced here: 79.4 us
  starting transfers between devices  30.9 us (39%)
  waiting for transfers between devices  18.8 us (24%)
  Pallas kernels  16.2 us (20%)
  other arithmetic  7.62 us (10%)
  local copies, waits for them, and re-layouts  5.63 us (7%)
    pallas_call x2, Pallas kernels, attend(): pl.pallas_call(kernel, grid_spec=grid_spec, out_shape=jax.ShapeDtypeStruc...  16.2 us
    ppermute x12, waiting for transfers between devices, shift(): return lax.ppermute(value, 'chip', pairs)  14.6 us
    ppermute x12, starting transfers between devices, shift(): return lax.ppermute(value, 'chip', pairs)  10.5 us
    ppermute x2, starting transfers between devices, shifted(): return lax.ppermute(value, axis, pairs)  6.42 us
    all_to_all x1, starting transfers between devices, local(): lax.all_to_all(joined, 'head', split_axis=1, concat_axis=0, tiled=True)  5.84 us
    all_to_all x1, starting transfers between devices, local(): lax.all_to_all(queries, 'head', split_axis=1, concat_axis=0, tiled=True)  3.47 us
    all_to_all x1, waiting for transfers between devices, local(): lax.all_to_all(joined, 'head', split_axis=1, concat_axis=0, tiled=True)  3.28 us
    ppermute x2, starting transfers between devices, local(): other = lax.ppermute(part, 'core', swap)  2.51 us
  transfers between devices with their start and end apart: 19, of which 9 were waited for; matrix products, arithmetic and copies ran while one was open for 12% of the time, Pallas kernels for 10%

profile of v16, /device:TPU:1, one launch (start us, length us, event | category | flops | bytes accessed | tf_op | source)
XLA Modules:
  0.0 79.4 jit_solution(8525064893757542435)
XLA Ops:
  0.0 1.0 %copy_bitcast_fusion.1 = (bf16[64,4,256]{2,0,1:T(8,128)(2,1)S(1)}, bf16[64,4,256]{2,0,1:T(8,128)(2,1)S(1)}) fusion(bf16[8,4,8,256]{3,2,1,0:T(8,128)(2,1)} %bitcast.141, bf16[8,4,8,256]{3,2,1,0:T(8,128)(2,1)} %bitcast.142), kind=kLoop, calls=%fused_computation.17 | loop fusion | bytes 524288 | tf_op jit(solution)/shard_map/reshape | solution.py:146
  1.0 0.7 pad_maximum_fusion.2
  1.7 5.8 %all-to-all-start = ((bf16[64,4,512]{2,0,1:T(8,128)(2,1)}), bf16[64,4,512]{2,0,1:T(8,128)(2,1)S(1)}, u32[]{:S(2)}, u32[]{:S(2)}) async-start(bf16[64,4,512]{2,0,1:T(8,128)(2,1)} %pad_maximum_fusion.2), calls=%async_computation | async-start | bytes 524288 | tf_op jit(solution)/shard_map/all_to_all | solution.py:148
  7.6 0.7 and_select_fusion.5
  8.4 0.2 convert_reduce_fusion
  8.6 0.2 fusion.1
  8.8 0.8 %copy.84 = bf16[8,4,8,1024]{3,2,0,1:T(8,128)(2,1)} copy(bf16[8,4,8,1024]{3,2,1,0:T(8,128)(2,1)S(1)} %bitcast.129) | data formatting | bytes 1048576 | tf_op jit(solution)/shard_map/all_to_all | solution.py:183
  9.7 0.1 copy.75
  9.9 3.3 %all-to-all-done = bf16[64,4,512]{2,0,1:T(8,128)(2,1)S(1)} async-done(((bf16[64,4,512]{2,0,1:T(8,128)(2,1)}), bf16[64,4,512]{2,0,1:T(8,128)(2,1)S(1)}, u32[]{:S(2)}, u32[]{:S(2)}) %all-to-all-start) | async-done | bytes 262176 | tf_op jit(solution)/shard_map/all_to_all | solution.py:148
  13.1 3.5 %all-to-all-start.1 = ((bf16[64,4,1024]{2,0,1:T(8,128)(2,1)}), bf16[64,4,1024]{2,0,1:T(8,128)(2,1)S(1)}, u32[]{:S(2)}, u32[]{:S(2)}) async-start(bf16[64,4,1024]{2,0,1:T(8,128)(2,1)} %bitcast.116), calls=%async_computation.1 | async-start | bytes 1048576 | tf_op jit(solution)/shard_map/all_to_all | solution.py:183
  16.7 0.6 gather_fusion.1
  17.3 2.2 %collective-permute-start = (bf16[2,2,64,128]{3,2,1,0:T(8,128)(2,1)S(1)}, bf16[2,2,64,128]{3,2,1,0:T(8,128)(2,1)S(1)}, u32[]{:S(2)}, u32[]{:S(2)}) collective-permute-start(bf16[2,2,64,128]{3,2,1,0:T(8,128)(2,1)S(1)} %bitcast.143), channel_id=1, source_target_pairs={{0,4},{4,0},{1,5},{5,1},{2,6},{6,2},{3,7},{7,3},{8,12},{12,8},{9,1... | collective-permute-start | bytes 196616 | tf_op jit(solution)/shard_map/ppermute | solution.py:182
  19.6 0.6 gather_fusion
  20.2 0.2 collective-permute-done
  20.4 2.5 %collective-permute-start.3 = (bf16[2,1,2,64,128]{4,3,2,0,1:T(8,128)(2,1)S(1)}, bf16[2,1,2,64,128]{4,3,2,0,1:T(8,128)(2,1)S(1)}, u32[]{:S(2)}, u32[]{:S(2)}) collective-permute-start(bf16[2,1,2,64,128]{4,3,2,0,1:T(8,128)(2,1)S(1)} %get-tuple-element.48), channel_id=1, source_target_pairs={{0,24},{8,0},{16,8},{24,16},{32,56},{40,32},{48,40},{56,48},{64,88... | collective-permute-start | bytes 196616 | tf_op jit(solution)/shard_map/ppermute | solution.py:192
  22.9 0.5 collective-permute-start.2
  23.5 0.6 collective-permute-start.1
  24.1 4.5 %collective-permute-start.7 = (bf16[256,256]{1,0:T(8,128)(2,1)S(1)}, bf16[256,256]{1,0:T(8,128)(2,1)S(1)}, u32[]{:S(2)}, u32[]{:S(2)}) collective-permute-start(bf16[256,256]{1,0:T(8,128)(2,1)S(1)} %get-tuple-element.46), channel_id=1, source_target_pairs={{0,4},{4,8},{8,12},{12,16},{16,20},{20,24},{24,28},{28,32},{32,36}... | collective-permute-start | bytes 393224 | tf_op jit(solution)/shard_map/ppermute | solution.py:19
  28.6 1.9 %collective-permute-start.8 = (bf16[256,256]{1,0:T(8,128)(2,1)S(1)}, bf16[256,256]{1,0:T(8,128)(2,1)S(1)}, u32[]{:S(2)}, u32[]{:S(2)}) collective-permute-start(bf16[256,256]{1,0:T(8,128)(2,1)S(1)} %get-tuple-element.43), channel_id=1, source_target_pairs={{0,4},{4,8},{8,12},{12,16},{16,20},{20,24},{24,28},{28,32},{32,36}... | collective-permute-start | bytes 393224 | tf_op jit(solution)/shard_map/ppermute | solution.py:19
  30.5 2.8 %collective-permute-start.6 = (bf16[2,1,2,64,128]{4,3,2,0,1:T(8,128)(2,1)S(1)}, bf16[2,1,2,64,128]{4,3,2,0,1:T(8,128)(2,1)S(1)}, u32[]{:S(2)}, u32[]{:S(2)}) collective-permute-start(bf16[2,1,2,64,128]{4,3,2,0,1:T(8,128)(2,1)S(1)} %get-tuple-element.47), channel_id=1, source_target_pairs={{0,96},{8,104},{16,112},{24,120},{32,0},{40,8},{48,16},{56,24},{64... | collective-permute-start | bytes 196616 | tf_op jit(solution)/shard_map/ppermute | solution.py:192
  33.3 0.3 collective-permute-start.5
  33.7 0.7 collective-permute-start.4
  34.4 0.2 collective-permute-done.6
  34.6 3.5 %collective-permute-done.5 = bf16[2,1,2,64,128]{4,3,2,0,1:T(8,128)(2,1)S(1)} collective-permute-done((bf16[2,1,2,64,128]{4,3,2,0,1:T(8,128)(2,1)S(1)}, bf16[2,1,2,64,128]{4,3,2,0,1:T(8,128)(2,1)S(1)}, u32[]{:S(2)}, u32[]{:S(2)}) %collective-permute-start.5) | collective-permute-done | bytes 65568 | tf_op jit(solution)/shard_map/ppermute | solution.py:192
  38.1 1.6 %collective-permute-done.4 = bf16[2,1,2,64,128]{4,3,2,0,1:T(8,128)(2,1)S(1)} collective-permute-done((bf16[2,1,2,64,128]{4,3,2,0,1:T(8,128)(2,1)S(1)}, bf16[2,1,2,64,128]{4,3,2,0,1:T(8,128)(2,1)S(1)}, u32[]{:S(2)}, u32[]{:S(2)}) %collective-permute-start.4) | collective-permute-done | bytes 65568 | tf_op jit(solution)/shard_map/ppermute | solution.py:192
  39.9 0.4 collective-permute-start.10
  40.3 1.0 %collective-permute-start.9 = (bf16[4,2,1,2,64,128]{5,4,3,1,0,2:T(8,128)(2,1)S(1)}, bf16[4,2,1,2,64,128]{5,4,3,1,0,2:T(8,128)(2,1)S(1)}, u32[]{:S(2)}, u32[]{:S(2)}) collective-permute-start(bf16[4,2,1,2,64,128]{5,4,3,1,0,2:T(8,128)(2,1)S(1)} %bitcast.126), channel_id=1, source_target_pairs={{0,32},{8,40},{16,48},{24,56},{32,64},{40,72},{48,80},{56,88},{64,... | collective-permute-start | bytes 786440 | tf_op jit(solution)/shard_map/ppermute | solution.py:192
  41.4 0.7 collective-permute-start.14
  42.0 0.8 %collective-permute-start.13 = (bf16[4,2,1,2,64,128]{5,4,3,1,0,2:T(8,128)(2,1)S(1)}, bf16[4,2,1,2,64,128]{5,4,3,1,0,2:T(8,128)(2,1)S(1)}, u32[]{:S(2)}, u32[]{:S(2)}) collective-permute-start(bf16[4,2,1,2,64,128]{5,4,3,1,0,2:T(8,128)(2,1)S(1)} %pad_maximum_fusion.4), channel_id=1, source_target_pairs={{0,16},{8,24},{16,0},{24,8},{32,48},{40,56},{48,32},{56,40},{64,80... | collective-permute-start | bytes 786440 | tf_op jit(solution)/shard_map/ppermute | solution.py:192
  43.7 0.1 stack.110
  43.9 0.1 stack.109
  44.0 0.7 copy_convert_fusion.refs_7_
  44.7 0.6 copy_convert_fusion.1.refs_6_
  45.3 1.4 %collective-permute-done.11 = bf16[4,2,1,2,64,128]{5,4,3,1,2,0:T(8,128)(2,1)S(1)} collective-permute-done((bf16[4,2,1,2,64,128]{5,4,3,1,2,0:T(8,128)(2,1)S(1)}, bf16[4,2,1,2,64,128]{5,4,3,1,2,0:T(8,128)(2,1)S(1)}, u32[]{:S(2)}, u32[]{:S(2)}) %collective-permute-start.11) | collective-permute-done | bytes 262176 | tf_op jit(solution)/shard_map/ppermute | solution.py:192
  46.7 0.7 pad_maximum_fusion.5.refs_2_
  47.5 0.7 pad_maximum_fusion.6.refs_3_
  48.2 7.2 %collective-permute-done.9 = bf16[4,2,1,2,64,128]{5,4,3,1,0,2:T(8,128)(2,1)S(1)} collective-permute-done((bf16[4,2,1,2,64,128]{5,4,3,1,0,2:T(8,128)(2,1)S(1)}, bf16[4,2,1,2,64,128]{5,4,3,1,0,2:T(8,128)(2,1)S(1)}, u32[]{:S(2)}, u32[]{:S(2)}) %collective-permute-start.9) | collective-permute-done | bytes 262176 | tf_op jit(solution)/shard_map/ppermute | solution.py:192
  55.3 0.1 pad_maximum_fusion
  55.5 0.7 collective-permute-done.12
  56.2 0.1 pad_maximum_fusion.1
  56.4 0.7 gather_fusion.3
  57.1 2.4 %collective-permute-start.16 = (bf16[1,2048,128]{2,1,0:T(8,128)(2,1)S(1)}, bf16[1,2048,128]{2,1,0:T(8,128)(2,1)S(1)}, u32[]{:S(2)}, u32[]{:S(2)}) collective-permute-start(bf16[1,2048,128]{2,1,0:T(8,128)(2,1)S(1)} %bitcast.122), channel_id=1, source_target_pairs={{0,4},{4,0},{1,5},{5,1},{2,6},{6,2},{3,7},{7,3},{8,12},{12,8},{9,1... | collective-permute-start | bytes 1572872 | tf_op jit(solution)/shard_map/ppermute | solution.py:223
  59.5 0.7 gather_fusion.2
  60.4 0.7 collective-permute-done.16
  61.1 1.1 %broadcast_select_fusion = (bf16[1,2048,128]{2,1,0:T(8,128)(2,1)}, bf16[1,2048,128]{2,1,0:T(8,128)(2,1)}) fusion(bf16[1,2048,128]{2,1,0:T(8,128)(2,1)S(1)} %collective-permute-done.16, pred[]{:T(512)S(6)} %eq.39, bf16[1,2048,128]{2,1,0:T(8,128)(2,1)S(1)} %bitcast.123), kind=kLoop, calls=%fused_computation.7 | loop fusion | flops 524288 | bytes 2097153 | tf_op jit(solution)/shard_map/jit(_where)/select_n | solution.py:225
  62.2 8.1 %shard_map.55.refs_8_ = bf16[256,1024]{1,0:T(8,128)(2,1)} custom-call(s32[2,5]{1,0:T(2,128)} %copy-done.3, bf16[256,1024]{1,0:T(8,128)(2,1)} %bitcast.130, bf16[512,256]{1,0:T(8,128)(2,1)} %pad_maximum_fusion.5.refs_2_, bf16[512,256]{1,0:T(8,128)(2,1)} %pad_maximum_fusion.6.refs_3_, bf16[1,2048,128]{2,1,0:T(8,128)(2,1)} %get-tuple-element.40.refs_4_, ...), custom_call_target="tpu_custom_call" | custom-call | flops 1275068416 | bytes 1703936 | tf_op jit(solution)/shard_map/pallas_call | solution.py:106
  70.2 1.1 %broadcast_select_fusion.2 = (bf16[1,2048,128]{2,1,0:T(8,128)(2,1)}, bf16[1,2048,128]{2,1,0:T(8,128)(2,1)}) fusion(bf16[1,2048,128]{2,1,0:T(8,128)(2,1)S(1)} %collective-permute-done.15, pred[]{:T(512)S(6)} %eq.39, bf16[1,2048,128]{2,1,0:T(8,128)(2,1)S(1)} %bitcast.121), kind=kLoop, calls=%fused_computation.9 | loop fusion | flops 524288 | bytes 2097153 | tf_op jit(solution)/shard_map/jit(_where)/select_n | solution.py:225
  71.3 8.1 %shard_map.56 = bf16[256,1024]{1,0:T(8,128)(2,1)} custom-call(s32[2,5]{1,0:T(2,128)} %copy-done.3, bf16[256,1024]{1,0:T(8,128)(2,1)} %bitcast.131, bf16[512,256]{1,0:T(8,128)(2,1)} %pad_maximum_fusion.5.refs_2_, bf16[512,256]{1,0:T(8,128)(2,1)} %pad_maximum_fusion.6.refs_3_, ...), custom_call_target="tpu_custom_call", output_to_operand_aliasing={{}: (8, {})} | custom-call | flops 1275068416 | bytes 1703936 | tf_op jit(solution)/shard_map/pallas_call | solution.py:106
  (57 shorter events, 1.7 us)
Async XLA Ops:
  0.0 9.7 %copy-start = (s32[8,4]{0,1:T(4,128)S(1)}, s32[8,4]{0,1:T(4,128)}, u32[]{:S(2)}) copy-start(s32[8,4]{0,1:T(4,128)} %param.8) | copy-start | bytes 388
  1.0 7.8 %copy-start.1 = (bf16[64,4096]{1,0:T(8,128)(2,1)S(1)}, bf16[64,4096]{1,0:T(8,128)(2,1)}, u32[]{:S(2)}) copy-start(bf16[64,4096]{1,0:T(8,128)(2,1)} %param.5) | copy-start | bytes 1572868
  1.7 11.4 %all-to-all-start = ((bf16[64,4,512]{2,0,1:T(8,128)(2,1)}), bf16[64,4,512]{2,0,1:T(8,128)(2,1)S(1)}, u32[]{:S(2)}, u32[]{:S(2)}) async-start(bf16[64,4,512]{2,0,1:T(8,128)(2,1)} %pad_maximum_fusion.2), calls=%async_computation | async-start | bytes 524288 | tf_op jit(solution)/shard_map/all_to_all | solution.py:148
  13.1 26.7 %all-to-all-start.1 = ((bf16[64,4,1024]{2,0,1:T(8,128)(2,1)}), bf16[64,4,1024]{2,0,1:T(8,128)(2,1)S(1)}, u32[]{:S(2)}, u32[]{:S(2)}) async-start(bf16[64,4,1024]{2,0,1:T(8,128)(2,1)} %bitcast.116), calls=%async_computation.1 | async-start | bytes 1048576 | tf_op jit(solution)/shard_map/all_to_all | solution.py:183
  17.3 3.1 %collective-permute-start = (bf16[2,2,64,128]{3,2,1,0:T(8,128)(2,1)S(1)}, bf16[2,2,64,128]{3,2,1,0:T(8,128)(2,1)S(1)}, u32[]{:S(2)}, u32[]{:S(2)}) collective-permute-start(bf16[2,2,64,128]{3,2,1,0:T(8,128)(2,1)S(1)} %bitcast.143), channel_id=1, source_target_pairs={{0,4},{4,0},{1,5},{5,1},{2,6},{6,2},{3,7},{7,3},{8,12},{12,8},{9,1... | collective-permute-start | bytes 196616 | tf_op jit(solution)/shard_map/ppermute | solution.py:182
  19.5 23.3 %copy-start.3 = (s32[2,5]{1,0:T(2,128)}, s32[2,5]{1,0:T(2,128)S(1)}, u32[]{:S(2)}) copy-start(s32[2,5]{1,0:T(2,128)S(1)} %concatenate.44.refs_0_) | copy-start | bytes 124
  20.4 10.1 %collective-permute-start.3 = (bf16[2,1,2,64,128]{4,3,2,0,1:T(8,128)(2,1)S(1)}, bf16[2,1,2,64,128]{4,3,2,0,1:T(8,128)(2,1)S(1)}, u32[]{:S(2)}, u32[]{:S(2)}) collective-permute-start(bf16[2,1,2,64,128]{4,3,2,0,1:T(8,128)(2,1)S(1)} %get-tuple-element.48), channel_id=1, source_target_pairs={{0,24},{8,0},{16,8},{24,16},{32,56},{40,32},{48,40},{56,48},{64,88... | collective-permute-start | bytes 196616 | tf_op jit(solution)/shard_map/ppermute | solution.py:192
  22.9 10.4 %collective-permute-start.2 = (bf16[2,1,2,64,128]{4,3,2,0,1:T(8,128)(2,1)S(1)}, bf16[2,1,2,64,128]{4,3,2,0,1:T(8,128)(2,1)S(1)}, u32[]{:S(2)}, u32[]{:S(2)}) collective-permute-start(bf16[2,1,2,64,128]{4,3,2,0,1:T(8,128)(2,1)S(1)} %get-tuple-element.48), channel_id=1, source_target_pairs={{0,16},{8,24},{16,0},{24,8},{32,48},{40,56},{48,32},{56,40},{64,80... | collective-permute-start | bytes 196616 | tf_op jit(solution)/shard_map/ppermute | solution.py:192
  23.5 10.2 %collective-permute-start.1 = (bf16[2,1,2,64,128]{4,3,2,0,1:T(8,128)(2,1)S(1)}, bf16[2,1,2,64,128]{4,3,2,0,1:T(8,128)(2,1)S(1)}, u32[]{:S(2)}, u32[]{:S(2)}) collective-permute-start(bf16[2,1,2,64,128]{4,3,2,0,1:T(8,128)(2,1)S(1)} %get-tuple-element.48), channel_id=1, source_target_pairs={{0,8},{8,16},{16,24},{24,0},{32,40},{40,48},{48,56},{56,32},{64,72... | collective-permute-start | bytes 196616 | tf_op jit(solution)/shard_map/ppermute | solution.py:192
  24.1 15.7 %collective-permute-start.7 = (bf16[256,256]{1,0:T(8,128)(2,1)S(1)}, bf16[256,256]{1,0:T(8,128)(2,1)S(1)}, u32[]{:S(2)}, u32[]{:S(2)}) collective-permute-start(bf16[256,256]{1,0:T(8,128)(2,1)S(1)} %get-tuple-element.46), channel_id=1, source_target_pairs={{0,4},{4,8},{8,12},{12,16},{16,20},{20,24},{24,28},{28,32},{32,36}... | collective-permute-start | bytes 393224 | tf_op jit(solution)/shard_map/ppermute | solution.py:19
  28.6 11.2 %collective-permute-start.8 = (bf16[256,256]{1,0:T(8,128)(2,1)S(1)}, bf16[256,256]{1,0:T(8,128)(2,1)S(1)}, u32[]{:S(2)}, u32[]{:S(2)}) collective-permute-start(bf16[256,256]{1,0:T(8,128)(2,1)S(1)} %get-tuple-element.43), channel_id=1, source_target_pairs={{0,4},{4,8},{8,12},{12,16},{16,20},{20,24},{24,28},{28,32},{32,36}... | collective-permute-start | bytes 393224 | tf_op jit(solution)/shard_map/ppermute | solution.py:19
  30.5 4.1 %collective-permute-start.6 = (bf16[2,1,2,64,128]{4,3,2,0,1:T(8,128)(2,1)S(1)}, bf16[2,1,2,64,128]{4,3,2,0,1:T(8,128)(2,1)S(1)}, u32[]{:S(2)}, u32[]{:S(2)}) collective-permute-start(bf16[2,1,2,64,128]{4,3,2,0,1:T(8,128)(2,1)S(1)} %get-tuple-element.47), channel_id=1, source_target_pairs={{0,96},{8,104},{16,112},{24,120},{32,0},{40,8},{48,16},{56,24},{64... | collective-permute-start | bytes 196616 | tf_op jit(solution)/shard_map/ppermute | solution.py:192
  33.3 4.8 %collective-permute-start.5 = (bf16[2,1,2,64,128]{4,3,2,0,1:T(8,128)(2,1)S(1)}, bf16[2,1,2,64,128]{4,3,2,0,1:T(8,128)(2,1)S(1)}, u32[]{:S(2)}, u32[]{:S(2)}) collective-permute-start(bf16[2,1,2,64,128]{4,3,2,0,1:T(8,128)(2,1)S(1)} %get-tuple-element.47), channel_id=1, source_target_pairs={{0,64},{8,72},{16,80},{24,88},{32,96},{40,104},{48,112},{56,120},{... | collective-permute-start | bytes 196616 | tf_op jit(solution)/shard_map/ppermute | solution.py:192
  33.7 6.1 %collective-permute-start.4 = (bf16[2,1,2,64,128]{4,3,2,0,1:T(8,128)(2,1)S(1)}, bf16[2,1,2,64,128]{4,3,2,0,1:T(8,128)(2,1)S(1)}, u32[]{:S(2)}, u32[]{:S(2)}) collective-permute-start(bf16[2,1,2,64,128]{4,3,2,0,1:T(8,128)(2,1)S(1)} %get-tuple-element.47), channel_id=1, source_target_pairs={{0,32},{8,40},{16,48},{24,56},{32,64},{40,72},{48,80},{56,88},{64,... | collective-permute-start | bytes 196616 | tf_op jit(solution)/shard_map/ppermute | solution.py:192
  39.8 8.4 %copy-start.2 = (bf16[64,4,1024]{2,0,1:T(8,128)(2,1)}, bf16[64,4,1024]{2,0,1:T(8,128)(2,1)S(1)}, u32[]{:S(2)}) copy-start(bf16[64,4,1024]{2,0,1:T(8,128)(2,1)S(1)} %all-to-all-done.1) | copy-start | bytes 1572868
  39.8 6.9 %collective-permute-start.11 = (bf16[4,2,1,2,64,128]{5,4,3,1,2,0:T(8,128)(2,1)S(1)}, bf16[4,2,1,2,64,128]{5,4,3,1,2,0:T(8,128)(2,1)S(1)}, u32[]{:S(2)}, u32[]{:S(2)}) collective-permute-start(bf16[4,2,1,2,64,128]{5,4,3,1,2,0:T(8,128)(2,1)S(1)} %pad_maximum_fusion.3), channel_id=1, source_target_pairs={{0,96},{8,104},{16,112},{24,120},{32,0},{40,8},{48,16},{56,24},{64... | collective-permute-start | bytes 786440 | tf_op jit(solution)/shard_map/ppermute | solution.py:192
  39.9 8.3 %collective-permute-start.10 = (bf16[4,2,1,2,64,128]{5,4,3,1,0,2:T(8,128)(2,1)S(1)}, bf16[4,2,1,2,64,128]{5,4,3,1,0,2:T(8,128)(2,1)S(1)}, u32[]{:S(2)}, u32[]{:S(2)}) collective-permute-start(bf16[4,2,1,2,64,128]{5,4,3,1,0,2:T(8,128)(2,1)S(1)} %bitcast.125), channel_id=1, source_target_pairs={{0,64},{8,72},{16,80},{24,88},{32,96},{40,104},{48,112},{56,120},{... | collective-permute-start | bytes 786440 | tf_op jit(solution)/shard_map/ppermute | solution.py:192
  40.3 15.0 %collective-permute-start.9 = (bf16[4,2,1,2,64,128]{5,4,3,1,0,2:T(8,128)(2,1)S(1)}, bf16[4,2,1,2,64,128]{5,4,3,1,0,2:T(8,128)(2,1)S(1)}, u32[]{:S(2)}, u32[]{:S(2)}) collective-permute-start(bf16[4,2,1,2,64,128]{5,4,3,1,0,2:T(8,128)(2,1)S(1)} %bitcast.126), channel_id=1, source_target_pairs={{0,32},{8,40},{16,48},{24,56},{32,64},{40,72},{48,80},{56,88},{64,... | collective-permute-start | bytes 786440 | tf_op jit(solution)/shard_map/ppermute | solution.py:192
  41.4 14.1 %collective-permute-start.14 = (bf16[4,2,1,2,64,128]{5,4,3,1,0,2:T(8,128)(2,1)S(1)}, bf16[4,2,1,2,64,128]{5,4,3,1,0,2:T(8,128)(2,1)S(1)}, u32[]{:S(2)}, u32[]{:S(2)}) collective-permute-start(bf16[4,2,1,2,64,128]{5,4,3,1,0,2:T(8,128)(2,1)S(1)} %pad_maximum_fusion.4), channel_id=1, source_target_pairs={{0,24},{8,0},{16,8},{24,16},{32,56},{40,32},{48,40},{56,48},{64,88... | collective-permute-start | bytes 786440 | tf_op jit(solution)/shard_map/ppermute | solution.py:192
  42.0 13.4 %collective-permute-start.13 = (bf16[4,2,1,2,64,128]{5,4,3,1,0,2:T(8,128)(2,1)S(1)}, bf16[4,2,1,2,64,128]{5,4,3,1,0,2:T(8,128)(2,1)S(1)}, u32[]{:S(2)}, u32[]{:S(2)}) collective-permute-start(bf16[4,2,1,2,64,128]{5,4,3,1,0,2:T(8,128)(2,1)S(1)} %pad_maximum_fusion.4), channel_id=1, source_target_pairs={{0,16},{8,24},{16,0},{24,8},{32,48},{40,56},{48,32},{56,40},{64,80... | collective-permute-start | bytes 786440 | tf_op jit(solution)/shard_map/ppermute | solution.py:192
  46.7 9.5 %collective-permute-start.12 = (bf16[4,2,1,2,64,128]{5,4,3,1,0,2:T(8,128)(2,1)S(1)}, bf16[4,2,1,2,64,128]{5,4,3,1,0,2:T(8,128)(2,1)S(1)}, u32[]{:S(2)}, u32[]{:S(2)}) collective-permute-start(bf16[4,2,1,2,64,128]{5,4,3,1,0,2:T(8,128)(2,1)S(1)} %pad_maximum_fusion.4), channel_id=1, source_target_pairs={{0,8},{8,16},{16,24},{24,0},{32,40},{40,48},{48,56},{56,32},{64,72... | collective-permute-start | bytes 786440 | tf_op jit(solution)/shard_map/ppermute | solution.py:192
  57.1 4.0 %collective-permute-start.16 = (bf16[1,2048,128]{2,1,0:T(8,128)(2,1)S(1)}, bf16[1,2048,128]{2,1,0:T(8,128)(2,1)S(1)}, u32[]{:S(2)}, u32[]{:S(2)}) collective-permute-start(bf16[1,2048,128]{2,1,0:T(8,128)(2,1)S(1)} %bitcast.122), channel_id=1, source_target_pairs={{0,4},{4,0},{1,5},{5,1},{2,6},{6,2},{3,7},{7,3},{8,12},{12,8},{9,1... | collective-permute-start | bytes 1572872 | tf_op jit(solution)/shard_map/ppermute | solution.py:223
  60.3 10.0 %collective-permute-start.15 = (bf16[1,2048,128]{2,1,0:T(8,128)(2,1)S(1)}, bf16[1,2048,128]{2,1,0:T(8,128)(2,1)S(1)}, u32[]{:S(2)}, u32[]{:S(2)}) collective-permute-start(bf16[1,2048,128]{2,1,0:T(8,128)(2,1)S(1)} %bitcast.120), channel_id=1, source_target_pairs={{0,4},{4,0},{1,5},{5,1},{2,6},{6,2},{3,7},{7,3},{8,12},{12,8},{9,1... | collective-permute-start | bytes 1572872 | tf_op jit(solution)/shard_map/ppermute | solution.py:223

commit v17 on v16

--- a/solution.py
+++ b/solution.py
@@ -20,10 +20,10 @@
 
 
 def attend_kernel(
-    off_ref, q_ref, wk_ref, wv_ref, kv_ref, vv_ref, ms_ref, mv_ref, *rest, group, scale, nbd, head
+    off_ref, head_ref, q_ref, wk_ref, wv_ref, kv_ref, vv_ref, ms_ref, mv_ref, *rest, group, scale, nbd
 ):
     o_ref = rest[-1]
-    g = head
+    g = head_ref[0]
     i = pl.program_id(1)
     rows = BLOCK_TOKENS * group
     picked_k, picked_v = [], []
@@ -68,7 +68,7 @@
         ]
 
 
-def attend(offsets, q_all, win_k, win_v, kv, vv, ms, mv, group, scale, head, prior):
+def attend(offsets, head, q_all, win_k, win_v, kv, vv, ms, mv, group, scale, prior):
     nbd = ms.shape[1]
     slash_rows = ms.shape[3]
     vert_rows = kv.shape[1]
@@ -81,27 +81,27 @@
         transcendentals=nbd * rows * (slash_rows + vert_rows),
         bytes_accessed=2 * (q_all.size + win_k.size // 2 + kv.size + vv.size),
     )
-    kernel = lambda *refs: attend_kernel(*refs, group=group, scale=scale, nbd=nbd, head=head)
+    kernel = lambda *refs: attend_kernel(*refs, group=group, scale=scale, nbd=nbd)
     in_specs = [
-        pl.BlockSpec((BLOCK_TOKENS, cols), lambda g, i, off: (i, head)),
-        pl.BlockSpec((window_rows, HEAD_WIDTH), lambda g, i, off: (0, head)),
-        pl.BlockSpec((window_rows, HEAD_WIDTH), lambda g, i, off: (0, head)),
-        pl.BlockSpec((1, vert_rows, HEAD_WIDTH), lambda g, i, off: (0, 0, 0)),
-        pl.BlockSpec((1, vert_rows, HEAD_WIDTH), lambda g, i, off: (0, 0, 0)),
-        pl.BlockSpec((1, 1, 1, slash_rows), lambda g, i, off: (head, i, 0, 0)),
-        pl.BlockSpec((1, 1, 1, vert_rows), lambda g, i, off: (head, i, 0, 0)),
+        pl.BlockSpec((BLOCK_TOKENS, cols), lambda g, i, off, hd: (i, hd[0])),
+        pl.BlockSpec((window_rows, HEAD_WIDTH), lambda g, i, off, hd: (0, hd[0])),
+        pl.BlockSpec((window_rows, HEAD_WIDTH), lambda g, i, off, hd: (0, hd[0])),
+        pl.BlockSpec((1, vert_rows, HEAD_WIDTH), lambda g, i, off, hd: (0, 0, 0)),
+        pl.BlockSpec((1, vert_rows, HEAD_WIDTH), lambda g, i, off, hd: (0, 0, 0)),
+        pl.BlockSpec((1, 1, 1, slash_rows), lambda g, i, off, hd: (hd[0], i, 0, 0)),
+        pl.BlockSpec((1, 1, 1, vert_rows), lambda g, i, off, hd: (hd[0], i, 0, 0)),
     ]
-    operands = [offsets, q_all, win_k, win_v, kv, vv, ms, mv]
+    operands = [offsets, head, q_all, win_k, win_v, kv, vv, ms, mv]
     aliases = {}
     if prior is not None:
         in_specs.append(pl.BlockSpec(memory_space=pl.ANY))
         aliases = {len(operands): 0}
         operands.append(prior)
     grid_spec = pltpu.PrefetchScalarGridSpec(
-        num_scalar_prefetch=1,
+        num_scalar_prefetch=2,
         grid=(1, nbd),
         in_specs=in_specs,
-        out_specs=pl.BlockSpec((BLOCK_TOKENS, cols), lambda g, i, off: (i, head)),
+        out_specs=pl.BlockSpec((BLOCK_TOKENS, cols), lambda g, i, off, hd: (i, hd[0])),
     )
     return pl.pallas_call(
         kernel,
@@ -177,8 +177,9 @@
     chip_index = lax.axis_index("chip")
     swap = [(c, cores - 1 - c) for c in range(cores)]
     heads_col = jnp.arange(kv_local)[:, None]
-    mine = jnp.where(core_index == 0, own_k, own_v)[pieces, :, heads_col]
-    sent = jnp.where(core_index == 0, own_v, own_k)[pieces, :, heads_col]
+    both = jnp.stack([own_k[pieces, :, heads_col], own_v[pieces, :, heads_col]], 1)
+    mine = lax.dynamic_index_in_dim(both, core_index, 0, keepdims=False)
+    sent = lax.dynamic_index_in_dim(both, cores - 1 - core_index, 0, keepdims=False)
     stage = jnp.stack([mine, lax.ppermute(sent, "core", swap)], 0)
     q_all = lax.all_to_all(queries, "head", split_axis=1, concat_axis=0, tiled=True)
     def shift(value, stride, step):
@@ -213,21 +214,21 @@
     dx = (chip_index % side - owner_chip % side) % side
     heads_idx = jnp.arange(kv_local)[:, None]
     dc = (owner_core + core_index) % cores
-    gathered = [
-        across[dy[0], dx[0], dc[0], 0, rank[0]],
-        down[dx[1], dy[1], dc[1], 0, rank[1]],
-    ]
-    result = None
-    for head in range(kv_local):
-        part = gathered[head].reshape(1, listed * BLOCK_TOKENS, HEAD_WIDTH)
-        other = lax.ppermute(part, "core", swap)
-        vert_keys = jnp.where(core_index == 0, part, other)
-        vert_vals = jnp.where(core_index == 0, other, part)
-        result = attend(
-            diagonal_offsets, q_all, window_k, window_v, vert_keys, vert_vals, ms, mv,
-            query_group, softmax_scale, head, result,
-        )
-    return result
+    pick_head = lambda table: lax.dynamic_index_in_dim(table, core_index, 0, keepdims=False)
+    dyc, dxc, dcc, rankc = pick_head(dy), pick_head(dx), pick_head(dc), pick_head(rank)
+    shape = (1, listed * BLOCK_TOKENS, HEAD_WIDTH)
+    own_keys = across[dyc, dxc, dcc, 0, rankc].reshape(shape)
+    own_vals = down[dxc, dyc, dcc, 0, rankc].reshape(shape)
+    other_keys, other_vals = lax.ppermute((own_keys, own_vals), "core", swap)
+    first = jnp.reshape(core_index, (1,)).astype(jnp.int32)
+    result = attend(
+        diagonal_offsets, first, q_all, window_k, window_v, own_keys, own_vals, ms, mv,
+        query_group, softmax_scale, None,
+    )
+    return attend(
+        diagonal_offsets, cores - 1 - first, q_all, window_k, window_v, other_keys, other_vals,
+        ms, mv, query_group, softmax_scale, result,
+    )
 
 
 def solution(mesh):

time: 79.9 us -> 80.3 us (level)
  local copies, waits for them, and re-layouts: 5.63 us -> 8 us
  other arithmetic: 7.62 us -> 5.4 us
    unnamed x9 -> x17, local copies, waits for them, and re-layouts: 0.11 us -> 2.45 us
    select_n x3 -> x1, other arithmetic: 2.21 us -> 0.02 us  [local(): dy = (chip_index // side - owner_chip // side) % side]
  transfers between devices with their start and end apart: 19 -> 19, of which waited for: 9 -> 8; matrix products, arithmetic and copies ran while one was open for 12% -> 11% of each run, Pallas kernels for 10% -> 10%
where the time goes in v17:
time: 80.3 us; the launch traced here: 79.9 us
  starting transfers between devices  30.9 us (38%)
  waiting for transfers between devices  18.8 us (23%)
  Pallas kernels  16.5 us (21%)
  local copies, waits for them, and re-layouts  8 us (10%)
  other arithmetic  5.4 us (7%)
    pallas_call x2, Pallas kernels, attend(): pl.pallas_call(kernel, grid_spec=grid_spec, out_shape=jax.ShapeDtypeStruc...  16.5 us
    ppermute x12, waiting for transfers between devices, shift(): return lax.ppermute(value, 'chip', pairs)  14.7 us
    ppermute x12, starting transfers between devices, shift(): return lax.ppermute(value, 'chip', pairs)  10.5 us
    ppermute x2, starting transfers between devices, shifted(): return lax.ppermute(value, axis, pairs)  6.42 us
    all_to_all x1, starting transfers between devices, local(): lax.all_to_all(joined, 'head', split_axis=1, concat_axis=0, tiled=True)  5.84 us
    all_to_all x1, starting transfers between devices, local(): lax.all_to_all(queries, 'head', split_axis=1, concat_axis=0, tiled=True)  3.47 us
    all_to_all x1, waiting for transfers between devices, local(): lax.all_to_all(joined, 'head', split_axis=1, concat_axis=0, tiled=True)  3.21 us
    ppermute x2, starting transfers between devices, local(): other_keys, other_vals = lax.ppermute((own_keys, own_vals), 'core', swap)  2.5 us
  transfers between devices with their start and end apart: 19, of which 8 were waited for; matrix products, arithmetic and copies ran while one was open for 11% of the time, Pallas kernels for 10%

profile of v17, /device:TPU:1, one launch (start us, length us, event | category | flops | bytes accessed | tf_op | source)
XLA Modules:
  0.0 79.9 jit_solution(10475136552136991075)
XLA Ops:
  0.0 1.0 %copy_bitcast_fusion.1 = (bf16[64,4,256]{2,0,1:T(8,128)(2,1)S(1)}, bf16[64,4,256]{2,0,1:T(8,128)(2,1)S(1)}) fusion(bf16[8,4,8,256]{3,2,1,0:T(8,128)(2,1)} %bitcast.145, bf16[8,4,8,256]{3,2,1,0:T(8,128)(2,1)} %bitcast.146), kind=kLoop, calls=%fused_computation.17 | loop fusion | bytes 524288 | tf_op jit(solution)/shard_map/reshape | solution.py:146
  1.0 0.7 pad_maximum_fusion.2
  1.7 5.8 %all-to-all-start = ((bf16[64,4,512]{2,0,1:T(8,128)(2,1)}), bf16[64,4,512]{2,0,1:T(8,128)(2,1)S(1)}, u32[]{:S(2)}, u32[]{:S(2)}) async-start(bf16[64,4,512]{2,0,1:T(8,128)(2,1)} %pad_maximum_fusion.2), calls=%async_computation | async-start | bytes 524288 | tf_op jit(solution)/shard_map/all_to_all | solution.py:148
  7.6 0.7 and_select_fusion.1
  8.4 0.2 convert_reduce_fusion
  8.6 0.1 fusion.4
  8.8 0.8 %copy.77 = bf16[8,4,8,1024]{3,2,0,1:T(8,128)(2,1)} copy(bf16[8,4,8,1024]{3,2,1,0:T(8,128)(2,1)S(1)} %bitcast.128) | data formatting | bytes 1048576 | tf_op jit(solution)/shard_map/all_to_all | solution.py:184
  9.8 0.1 copy.68
  9.9 3.2 %all-to-all-done = bf16[64,4,512]{2,0,1:T(8,128)(2,1)S(1)} async-done(((bf16[64,4,512]{2,0,1:T(8,128)(2,1)}), bf16[64,4,512]{2,0,1:T(8,128)(2,1)S(1)}, u32[]{:S(2)}, u32[]{:S(2)}) %all-to-all-start) | async-done | bytes 262176 | tf_op jit(solution)/shard_map/all_to_all | solution.py:148
  13.1 3.5 %all-to-all-start.1 = ((bf16[64,4,1024]{2,0,1:T(8,128)(2,1)}), bf16[64,4,1024]{2,0,1:T(8,128)(2,1)S(1)}, u32[]{:S(2)}, u32[]{:S(2)}) async-start(bf16[64,4,1024]{2,0,1:T(8,128)(2,1)} %bitcast.121), calls=%async_computation.1 | async-start | bytes 1048576 | tf_op jit(solution)/shard_map/all_to_all | solution.py:184
  16.8 0.6 gather_fusion
  17.4 0.6 gather_fusion.1
  18.0 2.2 %collective-permute-start = (bf16[2,2,64,128]{3,2,1,0:T(8,128)(2,1)S(1)}, bf16[2,2,64,128]{3,2,1,0:T(8,128)(2,1)S(1)}, u32[]{:S(2)}, u32[]{:S(2)}) collective-permute-start(bf16[2,2,64,128]{3,2,1,0:T(8,128)(2,1)S(1)} %get-tuple-element.46), channel_id=1, source_target_pairs={{0,4},{4,0},{1,5},{5,1},{2,6},{6,2},{3,7},{7,3},{8,12},{12,8},{9,1... | collective-permute-start | bytes 196616 | tf_op jit(solution)/shard_map/ppermute | solution.py:183
  20.2 0.9 %collective-permute-done = bf16[2,2,64,128]{3,2,1,0:T(8,128)(2,1)S(1)} collective-permute-done((bf16[2,2,64,128]{3,2,1,0:T(8,128)(2,1)S(1)}, bf16[2,2,64,128]{3,2,1,0:T(8,128)(2,1)S(1)}, u32[]{:S(2)}, u32[]{:S(2)}) %collective-permute-start) | collective-permute-done | bytes 65568 | tf_op jit(solution)/shard_map/ppermute | solution.py:183
  21.1 2.5 %collective-permute-start.3 = (bf16[2,1,2,64,128]{4,3,2,0,1:T(8,128)(2,1)S(1)}, bf16[2,1,2,64,128]{4,3,2,0,1:T(8,128)(2,1)S(1)}, u32[]{:S(2)}, u32[]{:S(2)}) collective-permute-start(bf16[2,1,2,64,128]{4,3,2,0,1:T(8,128)(2,1)S(1)} %get-tuple-element.45), channel_id=1, source_target_pairs={{0,24},{8,0},{16,8},{24,16},{32,56},{40,32},{48,40},{56,48},{64,88... | collective-permute-start | bytes 196616 | tf_op jit(solution)/shard_map/ppermute | solution.py:193
  23.6 0.5 collective-permute-start.2
  24.1 0.6 collective-permute-start.1
  24.7 4.5 %collective-permute-start.7 = (bf16[256,256]{1,0:T(8,128)(2,1)S(1)}, bf16[256,256]{1,0:T(8,128)(2,1)S(1)}, u32[]{:S(2)}, u32[]{:S(2)}) collective-permute-start(bf16[256,256]{1,0:T(8,128)(2,1)S(1)} %get-tuple-element.41), channel_id=1, source_target_pairs={{0,4},{4,8},{8,12},{12,16},{16,20},{20,24},{24,28},{28,32},{32,36}... | collective-permute-start | bytes 393224 | tf_op jit(solution)/shard_map/ppermute | solution.py:19
  29.2 1.9 %collective-permute-start.8 = (bf16[256,256]{1,0:T(8,128)(2,1)S(1)}, bf16[256,256]{1,0:T(8,128)(2,1)S(1)}, u32[]{:S(2)}, u32[]{:S(2)}) collective-permute-start(bf16[256,256]{1,0:T(8,128)(2,1)S(1)} %get-tuple-element.40), channel_id=1, source_target_pairs={{0,4},{4,8},{8,12},{12,16},{16,20},{20,24},{24,28},{28,32},{32,36}... | collective-permute-start | bytes 393224 | tf_op jit(solution)/shard_map/ppermute | solution.py:19
  31.2 2.8 %collective-permute-start.6 = (bf16[2,1,2,64,128]{4,3,2,0,1:T(8,128)(2,1)S(1)}, bf16[2,1,2,64,128]{4,3,2,0,1:T(8,128)(2,1)S(1)}, u32[]{:S(2)}, u32[]{:S(2)}) collective-permute-start(bf16[2,1,2,64,128]{4,3,2,0,1:T(8,128)(2,1)S(1)} %get-tuple-element.44), channel_id=1, source_target_pairs={{0,96},{8,104},{16,112},{24,120},{32,0},{40,8},{48,16},{56,24},{64... | collective-permute-start | bytes 196616 | tf_op jit(solution)/shard_map/ppermute | solution.py:193
  34.0 0.3 collective-permute-start.5
  34.3 0.7 collective-permute-start.4
  35.1 0.2 collective-permute-done.6
  35.3 3.5 %collective-permute-done.5 = bf16[2,1,2,64,128]{4,3,2,0,1:T(8,128)(2,1)S(1)} collective-permute-done((bf16[2,1,2,64,128]{4,3,2,0,1:T(8,128)(2,1)S(1)}, bf16[2,1,2,64,128]{4,3,2,0,1:T(8,128)(2,1)S(1)}, u32[]{:S(2)}, u32[]{:S(2)}) %collective-permute-start.5) | collective-permute-done | bytes 65568 | tf_op jit(solution)/shard_map/ppermute | solution.py:193
  38.8 1.6 %collective-permute-done.4 = bf16[2,1,2,64,128]{4,3,2,0,1:T(8,128)(2,1)S(1)} collective-permute-done((bf16[2,1,2,64,128]{4,3,2,0,1:T(8,128)(2,1)S(1)}, bf16[2,1,2,64,128]{4,3,2,0,1:T(8,128)(2,1)S(1)}, u32[]{:S(2)}, u32[]{:S(2)}) %collective-permute-start.4) | collective-permute-done | bytes 65568 | tf_op jit(solution)/shard_map/ppermute | solution.py:193
  40.6 0.4 collective-permute-start.10
  41.0 1.0 %collective-permute-start.9 = (bf16[4,2,1,2,64,128]{5,4,3,1,0,2:T(8,128)(2,1)S(1)}, bf16[4,2,1,2,64,128]{5,4,3,1,0,2:T(8,128)(2,1)S(1)}, u32[]{:S(2)}, u32[]{:S(2)}) collective-permute-start(bf16[4,2,1,2,64,128]{5,4,3,1,0,2:T(8,128)(2,1)S(1)} %pad_maximum_fusion.3), channel_id=1, source_target_pairs={{0,32},{8,40},{16,48},{24,56},{32,64},{40,72},{48,80},{56,88},{64,... | collective-permute-start | bytes 786440 | tf_op jit(solution)/shard_map/ppermute | solution.py:193
  42.0 0.7 collective-permute-start.14
  42.7 0.8 %collective-permute-start.13 = (bf16[4,2,1,2,64,128]{5,4,3,1,0,2:T(8,128)(2,1)S(1)}, bf16[4,2,1,2,64,128]{5,4,3,1,0,2:T(8,128)(2,1)S(1)}, u32[]{:S(2)}, u32[]{:S(2)}) collective-permute-start(bf16[4,2,1,2,64,128]{5,4,3,1,0,2:T(8,128)(2,1)S(1)} %bitcast.125), channel_id=1, source_target_pairs={{0,16},{8,24},{16,0},{24,8},{32,48},{40,56},{48,32},{56,40},{64,80... | collective-permute-start | bytes 786440 | tf_op jit(solution)/shard_map/ppermute | solution.py:193
  44.4 0.1 stack.119
  44.6 0.1 stack.118
  44.7 0.7 copy_convert_fusion.refs_8_
  45.4 0.6 copy_convert_fusion.1.refs_7_
  46.0 1.4 %collective-permute-done.11 = bf16[4,2,1,2,64,128]{5,4,3,1,0,2:T(8,128)(2,1)S(1)} collective-permute-done((bf16[4,2,1,2,64,128]{5,4,3,1,0,2:T(8,128)(2,1)S(1)}, bf16[4,2,1,2,64,128]{5,4,3,1,0,2:T(8,128)(2,1)S(1)}, u32[]{:S(2)}, u32[]{:S(2)}) %collective-permute-start.11) | collective-permute-done | bytes 262176 | tf_op jit(solution)/shard_map/ppermute | solution.py:193
  47.4 0.7 pad_maximum_fusion.5.refs_3_
  48.1 0.7 pad_maximum_fusion.6.refs_4_
  48.9 7.1 %collective-permute-done.9 = bf16[4,2,1,2,64,128]{5,4,3,1,0,2:T(8,128)(2,1)S(1)} collective-permute-done((bf16[4,2,1,2,64,128]{5,4,3,1,0,2:T(8,128)(2,1)S(1)}, bf16[4,2,1,2,64,128]{5,4,3,1,0,2:T(8,128)(2,1)S(1)}, u32[]{:S(2)}, u32[]{:S(2)}) %collective-permute-start.9) | collective-permute-done | bytes 262176 | tf_op jit(solution)/shard_map/ppermute | solution.py:193
  56.0 0.1 pad_maximum_fusion
  56.2 0.8 collective-permute-done.12
  56.9 0.1 pad_maximum_fusion.1
  57.1 0.7 gather_fusion.2
  57.8 2.4 %collective-permute-start.15 = (bf16[1,2048,128]{2,1,0:T(8,128)(2,1)S(1)}, bf16[1,2048,128]{2,1,0:T(8,128)(2,1)S(1)}, u32[]{:S(2)}, u32[]{:S(2)}) collective-permute-start(bf16[1,2048,128]{2,1,0:T(8,128)(2,1)S(1)} %bitcast.131), channel_id=1, source_target_pairs={{0,4},{4,0},{1,5},{5,1},{2,6},{6,2},{3,7},{7,3},{8,12},{12,8},{9,1... | collective-permute-start | bytes 1572872 | tf_op jit(solution)/shard_map/ppermute | solution.py:222
  60.2 0.7 gather_fusion.3
  61.1 0.7 copy-done.4
  61.8 8.2 %shard_map.55.refs_9_ = bf16[256,1024]{1,0:T(8,128)(2,1)} custom-call(s32[2,5]{1,0:T(2,128)} %copy-done.5, s32[1]{0:T(128)} %bitcast.25.refs_1_, bf16[256,1024]{1,0:T(8,128)(2,1)} %bitcast.129, bf16[512,256]{1,0:T(8,128)(2,1)} %pad_maximum_fusion.5.refs_3_, bf16[512,256]{1,0:T(8,128)(2,1)} %pad_maximum_fusion.6.refs_4_, bf16[1,2048,128]{2,1,0:T(8,128)(2,1)} %bitcast.132, ...), custom_call_target="tpu_custom_call" | custom-call | flops 1275068416 | bytes 1703936 | tf_op jit(solution)/shard_map/pallas_call | solution.py:106
  70.0 0.8 copy-done.6
  70.8 0.8 %copy-done.7 = bf16[1,2048,128]{2,1,0:T(8,128)(2,1)} copy-done((bf16[1,2048,128]{2,1,0:T(8,128)(2,1)}, bf16[1,2048,128]{2,1,0:T(8,128)(2,1)S(1)}, u32[]{:S(2)}) %copy-start.7) | copy-done | bytes 524312
  71.6 8.2 %shard_map.56 = bf16[256,1024]{1,0:T(8,128)(2,1)} custom-call(s32[2,5]{1,0:T(2,128)} %copy-done.5, s32[1]{0:T(128)S(6)} %sub.102.refs_1_, bf16[256,1024]{1,0:T(8,128)(2,1)} %bitcast.130, bf16[512,256]{1,0:T(8,128)(2,1)} %pad_maximum_fusion.5.refs_3_, bf16[512,256]{1,0:T(8,128)(2,1)} %pad_maximum_fusion.6.refs_4_, ...), custom_call_target="tpu_custom_call", output_to_operand_aliasing={{}: (9, {})} | custom-call | flops 1275068416 | bytes 1703936 | tf_op jit(solution)/shard_map/pallas_call | solution.py:106
  (64 shorter events, 1.8 us)
Async XLA Ops:
  0.0 9.7 %copy-start = (s32[8,4]{0,1:T(4,128)S(1)}, s32[8,4]{0,1:T(4,128)}, u32[]{:S(2)}) copy-start(s32[8,4]{0,1:T(4,128)} %param.8) | copy-start | bytes 388
  1.0 7.8 %copy-start.1 = (bf16[64,4096]{1,0:T(8,128)(2,1)S(1)}, bf16[64,4096]{1,0:T(8,128)(2,1)}, u32[]{:S(2)}) copy-start(bf16[64,4096]{1,0:T(8,128)(2,1)} %param.5) | copy-start | bytes 1572868
  1.7 11.4 %all-to-all-start = ((bf16[64,4,512]{2,0,1:T(8,128)(2,1)}), bf16[64,4,512]{2,0,1:T(8,128)(2,1)S(1)}, u32[]{:S(2)}, u32[]{:S(2)}) async-start(bf16[64,4,512]{2,0,1:T(8,128)(2,1)} %pad_maximum_fusion.2), calls=%async_computation | async-start | bytes 524288 | tf_op jit(solution)/shard_map/all_to_all | solution.py:148
  9.9 33.6 %copy-start.5 = (s32[2,5]{1,0:T(2,128)}, s32[2,5]{1,0:T(2,128)S(1)}, u32[]{:S(2)}) copy-start(s32[2,5]{1,0:T(2,128)S(1)} %concatenate.44.refs_0_) | copy-start | bytes 124
  13.1 27.3 %all-to-all-start.1 = ((bf16[64,4,1024]{2,0,1:T(8,128)(2,1)}), bf16[64,4,1024]{2,0,1:T(8,128)(2,1)S(1)}, u32[]{:S(2)}, u32[]{:S(2)}) async-start(bf16[64,4,1024]{2,0,1:T(8,128)(2,1)} %bitcast.121), calls=%async_computation.1 | async-start | bytes 1048576 | tf_op jit(solution)/shard_map/all_to_all | solution.py:184
  18.0 3.1 %collective-permute-start = (bf16[2,2,64,128]{3,2,1,0:T(8,128)(2,1)S(1)}, bf16[2,2,64,128]{3,2,1,0:T(8,128)(2,1)S(1)}, u32[]{:S(2)}, u32[]{:S(2)}) collective-permute-start(bf16[2,2,64,128]{3,2,1,0:T(8,128)(2,1)S(1)} %get-tuple-element.46), channel_id=1, source_target_pairs={{0,4},{4,0},{1,5},{5,1},{2,6},{6,2},{3,7},{7,3},{8,12},{12,8},{9,1... | collective-permute-start | bytes 196616 | tf_op jit(solution)/shard_map/ppermute | solution.py:183
  21.1 10.1 %collective-permute-start.3 = (bf16[2,1,2,64,128]{4,3,2,0,1:T(8,128)(2,1)S(1)}, bf16[2,1,2,64,128]{4,3,2,0,1:T(8,128)(2,1)S(1)}, u32[]{:S(2)}, u32[]{:S(2)}) collective-permute-start(bf16[2,1,2,64,128]{4,3,2,0,1:T(8,128)(2,1)S(1)} %get-tuple-element.45), channel_id=1, source_target_pairs={{0,24},{8,0},{16,8},{24,16},{32,56},{40,32},{48,40},{56,48},{64,88... | collective-permute-start | bytes 196616 | tf_op jit(solution)/shard_map/ppermute | solution.py:193
  23.6 10.4 %collective-permute-start.2 = (bf16[2,1,2,64,128]{4,3,2,0,1:T(8,128)(2,1)S(1)}, bf16[2,1,2,64,128]{4,3,2,0,1:T(8,128)(2,1)S(1)}, u32[]{:S(2)}, u32[]{:S(2)}) collective-permute-start(bf16[2,1,2,64,128]{4,3,2,0,1:T(8,128)(2,1)S(1)} %get-tuple-element.45), channel_id=1, source_target_pairs={{0,16},{8,24},{16,0},{24,8},{32,48},{40,56},{48,32},{56,40},{64,80... | collective-permute-start | bytes 196616 | tf_op jit(solution)/shard_map/ppermute | solution.py:193
  24.1 10.2 %collective-permute-start.1 = (bf16[2,1,2,64,128]{4,3,2,0,1:T(8,128)(2,1)S(1)}, bf16[2,1,2,64,128]{4,3,2,0,1:T(8,128)(2,1)S(1)}, u32[]{:S(2)}, u32[]{:S(2)}) collective-permute-start(bf16[2,1,2,64,128]{4,3,2,0,1:T(8,128)(2,1)S(1)} %get-tuple-element.45), channel_id=1, source_target_pairs={{0,8},{8,16},{16,24},{24,0},{32,40},{40,48},{48,56},{56,32},{64,72... | collective-permute-start | bytes 196616 | tf_op jit(solution)/shard_map/ppermute | solution.py:193
  24.7 15.7 %collective-permute-start.7 = (bf16[256,256]{1,0:T(8,128)(2,1)S(1)}, bf16[256,256]{1,0:T(8,128)(2,1)S(1)}, u32[]{:S(2)}, u32[]{:S(2)}) collective-permute-start(bf16[256,256]{1,0:T(8,128)(2,1)S(1)} %get-tuple-element.41), channel_id=1, source_target_pairs={{0,4},{4,8},{8,12},{12,16},{16,20},{20,24},{24,28},{28,32},{32,36}... | collective-permute-start | bytes 393224 | tf_op jit(solution)/shard_map/ppermute | solution.py:19
  29.2 11.2 %collective-permute-start.8 = (bf16[256,256]{1,0:T(8,128)(2,1)S(1)}, bf16[256,256]{1,0:T(8,128)(2,1)S(1)}, u32[]{:S(2)}, u32[]{:S(2)}) collective-permute-start(bf16[256,256]{1,0:T(8,128)(2,1)S(1)} %get-tuple-element.40), channel_id=1, source_target_pairs={{0,4},{4,8},{8,12},{12,16},{16,20},{20,24},{24,28},{28,32},{32,36}... | collective-permute-start | bytes 393224 | tf_op jit(solution)/shard_map/ppermute | solution.py:19
  31.2 4.1 %collective-permute-start.6 = (bf16[2,1,2,64,128]{4,3,2,0,1:T(8,128)(2,1)S(1)}, bf16[2,1,2,64,128]{4,3,2,0,1:T(8,128)(2,1)S(1)}, u32[]{:S(2)}, u32[]{:S(2)}) collective-permute-start(bf16[2,1,2,64,128]{4,3,2,0,1:T(8,128)(2,1)S(1)} %get-tuple-element.44), channel_id=1, source_target_pairs={{0,96},{8,104},{16,112},{24,120},{32,0},{40,8},{48,16},{56,24},{64... | collective-permute-start | bytes 196616 | tf_op jit(solution)/shard_map/ppermute | solution.py:193
  34.0 4.8 %collective-permute-start.5 = (bf16[2,1,2,64,128]{4,3,2,0,1:T(8,128)(2,1)S(1)}, bf16[2,1,2,64,128]{4,3,2,0,1:T(8,128)(2,1)S(1)}, u32[]{:S(2)}, u32[]{:S(2)}) collective-permute-start(bf16[2,1,2,64,128]{4,3,2,0,1:T(8,128)(2,1)S(1)} %get-tuple-element.44), channel_id=1, source_target_pairs={{0,64},{8,72},{16,80},{24,88},{32,96},{40,104},{48,112},{56,120},{... | collective-permute-start | bytes 196616 | tf_op jit(solution)/shard_map/ppermute | solution.py:193
  34.3 6.1 %collective-permute-start.4 = (bf16[2,1,2,64,128]{4,3,2,0,1:T(8,128)(2,1)S(1)}, bf16[2,1,2,64,128]{4,3,2,0,1:T(8,128)(2,1)S(1)}, u32[]{:S(2)}, u32[]{:S(2)}) collective-permute-start(bf16[2,1,2,64,128]{4,3,2,0,1:T(8,128)(2,1)S(1)} %get-tuple-element.44), channel_id=1, source_target_pairs={{0,32},{8,40},{16,48},{24,56},{32,64},{40,72},{48,80},{56,88},{64,... | collective-permute-start | bytes 196616 | tf_op jit(solution)/shard_map/ppermute | solution.py:193
  40.5 8.4 %copy-start.2 = (bf16[64,4,1024]{2,0,1:T(8,128)(2,1)}, bf16[64,4,1024]{2,0,1:T(8,128)(2,1)S(1)}, u32[]{:S(2)}) copy-start(bf16[64,4,1024]{2,0,1:T(8,128)(2,1)S(1)} %all-to-all-done.1) | copy-start | bytes 1572868
  40.5 6.9 %collective-permute-start.11 = (bf16[4,2,1,2,64,128]{5,4,3,1,0,2:T(8,128)(2,1)S(1)}, bf16[4,2,1,2,64,128]{5,4,3,1,0,2:T(8,128)(2,1)S(1)}, u32[]{:S(2)}, u32[]{:S(2)}) collective-permute-start(bf16[4,2,1,2,64,128]{5,4,3,1,0,2:T(8,128)(2,1)S(1)} %pad_maximum_fusion.3), channel_id=1, source_target_pairs={{0,96},{8,104},{16,112},{24,120},{32,0},{40,8},{48,16},{56,24},{64... | collective-permute-start | bytes 786440 | tf_op jit(solution)/shard_map/ppermute | solution.py:193
  40.6 8.3 %collective-permute-start.10 = (bf16[4,2,1,2,64,128]{5,4,3,1,0,2:T(8,128)(2,1)S(1)}, bf16[4,2,1,2,64,128]{5,4,3,1,0,2:T(8,128)(2,1)S(1)}, u32[]{:S(2)}, u32[]{:S(2)}) collective-permute-start(bf16[4,2,1,2,64,128]{5,4,3,1,0,2:T(8,128)(2,1)S(1)} %pad_maximum_fusion.3), channel_id=1, source_target_pairs={{0,64},{8,72},{16,80},{24,88},{32,96},{40,104},{48,112},{56,120},{... | collective-permute-start | bytes 786440 | tf_op jit(solution)/shard_map/ppermute | solution.py:193
  41.0 15.0 %collective-permute-start.9 = (bf16[4,2,1,2,64,128]{5,4,3,1,0,2:T(8,128)(2,1)S(1)}, bf16[4,2,1,2,64,128]{5,4,3,1,0,2:T(8,128)(2,1)S(1)}, u32[]{:S(2)}, u32[]{:S(2)}) collective-permute-start(bf16[4,2,1,2,64,128]{5,4,3,1,0,2:T(8,128)(2,1)S(1)} %pad_maximum_fusion.3), channel_id=1, source_target_pairs={{0,32},{8,40},{16,48},{24,56},{32,64},{40,72},{48,80},{56,88},{64,... | collective-permute-start | bytes 786440 | tf_op jit(solution)/shard_map/ppermute | solution.py:193
  42.0 14.1 %collective-permute-start.14 = (bf16[4,2,1,2,64,128]{5,4,3,1,2,0:T(8,128)(2,1)S(1)}, bf16[4,2,1,2,64,128]{5,4,3,1,2,0:T(8,128)(2,1)S(1)}, u32[]{:S(2)}, u32[]{:S(2)}) collective-permute-start(bf16[4,2,1,2,64,128]{5,4,3,1,2,0:T(8,128)(2,1)S(1)} %pad_maximum_fusion.4), channel_id=1, source_target_pairs={{0,24},{8,0},{16,8},{24,16},{32,56},{40,32},{48,40},{56,48},{64,88... | collective-permute-start | bytes 786440 | tf_op jit(solution)/shard_map/ppermute | solution.py:193
  42.7 13.4 %collective-permute-start.13 = (bf16[4,2,1,2,64,128]{5,4,3,1,0,2:T(8,128)(2,1)S(1)}, bf16[4,2,1,2,64,128]{5,4,3,1,0,2:T(8,128)(2,1)S(1)}, u32[]{:S(2)}, u32[]{:S(2)}) collective-permute-start(bf16[4,2,1,2,64,128]{5,4,3,1,0,2:T(8,128)(2,1)S(1)} %bitcast.125), channel_id=1, source_target_pairs={{0,16},{8,24},{16,0},{24,8},{32,48},{40,56},{48,32},{56,40},{64,80... | collective-permute-start | bytes 786440 | tf_op jit(solution)/shard_map/ppermute | solution.py:193
  47.4 9.5 %collective-permute-start.12 = (bf16[4,2,1,2,64,128]{5,4,3,1,0,2:T(8,128)(2,1)S(1)}, bf16[4,2,1,2,64,128]{5,4,3,1,0,2:T(8,128)(2,1)S(1)}, u32[]{:S(2)}, u32[]{:S(2)}) collective-permute-start(bf16[4,2,1,2,64,128]{5,4,3,1,0,2:T(8,128)(2,1)S(1)} %bitcast.126), channel_id=1, source_target_pairs={{0,8},{8,16},{16,24},{24,0},{32,40},{40,48},{48,56},{56,32},{64,72... | collective-permute-start | bytes 786440 | tf_op jit(solution)/shard_map/ppermute | solution.py:193
  57.8 3.2 %copy-start.3 = (bf16[32,64,128]{2,1,0:T(8,128)(2,1)}, bf16[32,64,128]{2,1,0:T(8,128)(2,1)S(1)}, u32[]{:S(2)}) copy-start(bf16[32,64,128]{2,1,0:T(8,128)(2,1)S(1)} %gather_fusion.2) | copy-start | bytes 1572868
  57.8 12.2 %collective-permute-start.15 = (bf16[1,2048,128]{2,1,0:T(8,128)(2,1)S(1)}, bf16[1,2048,128]{2,1,0:T(8,128)(2,1)S(1)}, u32[]{:S(2)}, u32[]{:S(2)}) collective-permute-start(bf16[1,2048,128]{2,1,0:T(8,128)(2,1)S(1)} %bitcast.131), channel_id=1, source_target_pairs={{0,4},{4,0},{1,5},{5,1},{2,6},{6,2},{3,7},{7,3},{8,12},{12,8},{9,1... | collective-permute-start | bytes 1572872 | tf_op jit(solution)/shard_map/ppermute | solution.py:222
  61.0 0.8 %copy-start.4 = (bf16[32,64,128]{2,1,0:T(8,128)(2,1)}, bf16[32,64,128]{2,1,0:T(8,128)(2,1)S(1)}, u32[]{:S(2)}) copy-start(bf16[32,64,128]{2,1,0:T(8,128)(2,1)S(1)} %gather_fusion.3) | copy-start | bytes 1572868
  61.0 9.1 %collective-permute-start.16 = (bf16[1,2048,128]{2,1,0:T(8,128)(2,1)S(1)}, bf16[1,2048,128]{2,1,0:T(8,128)(2,1)S(1)}, u32[]{:S(2)}, u32[]{:S(2)}) collective-permute-start(bf16[1,2048,128]{2,1,0:T(8,128)(2,1)S(1)} %bitcast.133), channel_id=1, source_target_pairs={{0,4},{4,0},{1,5},{5,1},{2,6},{6,2},{3,7},{7,3},{8,12},{12,8},{9,1... | collective-permute-start | bytes 1572872 | tf_op jit(solution)/shard_map/ppermute | solution.py:222
  70.0 0.8 %copy-start.6 = (bf16[1,2048,128]{2,1,0:T(8,128)(2,1)}, bf16[1,2048,128]{2,1,0:T(8,128)(2,1)S(1)}, u32[]{:S(2)}) copy-start(bf16[1,2048,128]{2,1,0:T(8,128)(2,1)S(1)} %collective-permute-done.15.refs_5_) | copy-start | bytes 1572868
  70.8 0.8 %copy-start.7 = (bf16[1,2048,128]{2,1,0:T(8,128)(2,1)}, bf16[1,2048,128]{2,1,0:T(8,128)(2,1)S(1)}, u32[]{:S(2)}) copy-start(bf16[1,2048,128]{2,1,0:T(8,128)(2,1)S(1)} %collective-permute-done.16.refs_6_) | copy-start | bytes 1572868
